TPU v7x, 32 devices: a whole 2x2x4 slice. The times are simulated.
32 devices in a mesh: groups: 2 (over x), batch: 4 (over z), head: 4 (over y, core).
Axes of the slice: x: 2, y: 2, z: 4, core: 2. Of those that a mesh axis runs over, the one named last changes fastest.
Arguments:
- tier_feed_tensor: bfloat16 [4, 64, 4096], P(None, 'groups', 'batch'), parts along dimension 1, may hold values from -6 to 6
- preceding_feed_each_stream: bfloat16 [64, 4096], P('groups', 'batch'), parts along dimension 0, may hold values from -6 to 6
- stream_kept_tableaux: float32 [64, 64, 4096], P(('groups', 'batch'), 'head'), parts along dimension 0, may hold values from -6 to 6
- position_mapping_target: int32 [64], P('groups'), parts along dimension 0, may hold values from 0 to 31, as said below
- lagging_mixture_weights: float32 [6, 4096], P(None, 'batch'), may hold values from 0 to 1
- lagging_narrow_lowering: bfloat16 [4096, 320], P('batch'), may hold values from -0.09375 to 0.09375
- lagging_narrow_raising: bfloat16 [5, 64, 4096], P(None, None, 'batch'), may hold values from -0.75 to 0.75
- fourfold_linear_maps: bfloat16 [4, 4096, 4096], P(None, 'batch', 'head'), may hold values from -0.09375 to 0.09375
- attenuation_narrow_lowering: bfloat16 [4096, 128], P('batch'), may hold values from -0.09375 to 0.09375
- attenuation_narrow_raising: bfloat16 [128, 4096], P(None, 'head'), may hold values from -0.5 to 0.5
- attenuation_doublelog_anchor: float32 [4096], P('head'), may hold values from -6 to 1
- instant_premium: float32 [4096], P('head'), may hold values from -4 to 4
- norming_multiplier: float32 [4096], P('head'), may hold values from 0.5 to 1.5
- norming_intercept: float32 [4096], P('head'), may hold values from -3 to 3
- outgoing_linear_map: bfloat16 [4096, 4096], P('head', 'batch'), may hold values from -0.09375 to 0.09375
Outputs:
- y_first: bfloat16 [2, 64, 4096], P(None, ('groups', 'head'), 'batch'), parts along dimension 1
- y_second: bfloat16 [2, 64, 4096], P(None, ('groups', 'head'), 'batch'), parts along dimension 1
- final_state: float32 [256, 16, 4096], P(('groups', 'batch', 'head')), parts along dimension 0
There are 2 independent parts, one for each index of `groups`. A program takes and returns all parts, laid end to end along the dimension named above; an argument that names none is the same for every part. Nothing has to cross between parts.
Inputs may be any that keep to these rules, and one draw needn't show every extreme that they name: position_mapping_target is a permutation of 0 to 31. For every aligned block of 8 sessions and every aligned block of 8 slots, the number of sessions of the former that have slots in the latter is exactly 2.
All inputs are finite; a program needn't handle non-finite values.
Results may differ from a plain program's by a relative error of at most 0.035.
Values may be sent and summed in bfloat16 or wider, within the bound.
No kernel may reach another device: no remote copies, remote signals or barrier semaphores. Data moves between devices by JAX's collectives and lax.ppermute only.
A program may use at most 128 MiB of HBM per device.

v0:
```python
import jax
import jax.numpy as jnp
from jax import lax
from jax.sharding import PartitionSpec as P

SUBSPACE_EXTENT = 64
STEPS_A = 2
MIX_MAPS = 5
NORMALIZER_GUARD = 0.00064


def route_to_slots(value, position_mapping_target, batch_index, head_index):
    batch_count = lax.axis_size("batch")
    head_count = lax.axis_size("head")
    local_rows, heads_here, width = value.shape
    cluster_number = head_count // 4
    slots_dev = local_rows // cluster_number
    per_pair = slots_dev // batch_count
    quarter = heads_here // 4
    own_map = lax.dynamic_slice_in_dim(
        position_mapping_target, batch_index * local_rows, local_rows
    )
    send_order = jnp.argsort(own_map // slots_dev, stable=True)
    packed = jnp.take(value, send_order, axis=0)
    packed = packed.reshape(batch_count, cluster_number, per_pair, 4, quarter, width)
    packed = packed.transpose(0, 3, 1, 2, 4, 5).reshape(
        batch_count * head_count, per_pair, quarter, width
    )
    arrived = lax.all_to_all(packed, ("batch", "head"), split_axis=0, concat_axis=0, tiled=True)
    arrived = arrived.reshape(batch_count, head_count, per_pair, quarter, width)
    arrived = arrived.transpose(0, 2, 1, 3, 4).reshape(slots_dev, head_count * quarter, width)
    target = batch_index * cluster_number + head_index % cluster_number
    arrivals = lax.dynamic_slice_in_dim(
        jnp.argsort(position_mapping_target // slots_dev, stable=True),
        target * slots_dev,
        slots_dev,
    )
    placing = jnp.argsort(jnp.take(position_mapping_target, arrivals) % slots_dev)
    return jnp.take(arrived, placing, axis=0)


def per_device(
    tier_feed_tensor,
    preceding_feed_each_stream,
    stream_kept_tableaux,
    position_mapping_target,
    lagging_mixture_weights,
    lagging_narrow_lowering,
    lagging_narrow_raising,
    fourfold_linear_maps,
    attenuation_narrow_lowering,
    attenuation_narrow_raising,
    attenuation_doublelog_anchor,
    instant_premium,
    norming_multiplier,
    norming_intercept,
    outgoing_linear_map,
):
    batch_count = lax.axis_size("batch")
    batch_index = lax.axis_index("batch")
    head_index = lax.axis_index("head")
    steps, sessions, feats = tier_feed_tensor.shape
    local_rows = sessions // batch_count
    heads_here = stream_kept_tableaux.shape[1]
    width = heads_here * SUBSPACE_EXTENT
    f32 = jnp.float32
    bf16 = jnp.bfloat16

    moved_state = route_to_slots(
        stream_kept_tableaux.astype(bf16), position_mapping_target, batch_index, head_index
    )

    previous = jnp.concatenate([preceding_feed_each_stream[None], tier_feed_tensor[:-1]], axis=0)

    def by_block(value):
        return value.reshape(steps, batch_count, local_rows, feats).transpose(1, 0, 2, 3).reshape(
            batch_count * steps * local_rows, feats
        )

    x_float = by_block(tier_feed_tensor).astype(f32)
    shifted = by_block(previous).astype(f32) - x_float
    rows = x_float.shape[0]
    base_mix = (x_float + shifted * lagging_mixture_weights[0]).astype(bf16)
    partial_value = jnp.dot(base_mix, lagging_narrow_lowering, preferred_element_type=f32)
    hidden = jnp.tanh(lax.psum(partial_value.astype(bf16), "batch").astype(f32)).astype(bf16)
    hidden = hidden.reshape(rows, MIX_MAPS, lagging_narrow_raising.shape[1])
    offsets = jnp.einsum(
        "nim,imd->ind", hidden, lagging_narrow_raising, preferred_element_type=f32
    )
    mixed = (
        x_float[None] + shifted[None] * (lagging_mixture_weights[1:, None, :] + offsets)
    ).astype(bf16)
    main_part = jnp.einsum(
        "inf,ifc->nic", mixed[:4], fourfold_linear_maps, preferred_element_type=f32
    )
    decay_part = jnp.dot(mixed[4], attenuation_narrow_lowering, preferred_element_type=f32)
    aggregated = lax.psum_scatter(
        jnp.concatenate([main_part.reshape(rows, -1), decay_part], axis=1).astype(bf16),
        "batch",
        scatter_dimension=0,
        tiled=True,
    ).astype(f32)
    aggregated = aggregated.reshape(steps, local_rows, -1)

    def heads_of(value):
        return value.reshape(steps, local_rows, heads_here, SUBSPACE_EXTENT)

    recept = heads_of(aggregated[..., :width])
    key_vec = heads_of(aggregated[..., width : 2 * width])
    valued = heads_of(aggregated[..., 2 * width : 3 * width])
    gate_act = jax.nn.silu(aggregated[..., 3 * width : 4 * width])
    low_rank = jnp.tanh(aggregated[..., 4 * width :]).astype(bf16)
    decay_rate = heads_of(
        jnp.exp(
            -jnp.exp(
                attenuation_doublelog_anchor
                + jnp.dot(low_rank, attenuation_narrow_raising, preferred_element_type=f32)
            )
        )
    )
    bonus_term = jnp.sum(
        recept * instant_premium.reshape(heads_here, SUBSPACE_EXTENT) * key_vec, axis=-1
    )

    prefix = [jnp.ones_like(decay_rate[0])]
    for t in range(steps):
        prefix.append(prefix[-1] * decay_rate[t])
    query = jnp.stack([recept[t] * prefix[t] for t in range(steps)])
    state = stream_kept_tableaux.reshape(
        local_rows, heads_here, SUBSPACE_EXTENT, SUBSPACE_EXTENT
    )
    from_state = jnp.einsum(
        "tnhi,nhij->tnhj", query, state, precision=lax.Precision.HIGHEST
    )
    outputs = []
    for t in range(steps):
        total = bonus_term[t][..., None] * valued[t] + from_state[t]
        for s in range(t):
            factor = key_vec[s]
            for u in range(s + 1, t):
                factor = factor * decay_rate[u]
            total = total + jnp.sum(recept[t] * factor, axis=-1, keepdims=True) * valued[s]
        outputs.append(total)
    wkv_out = jnp.stack(outputs)

    tails = []
    for s in range(steps):
        factor = key_vec[s]
        for u in range(s + 1, steps):
            factor = factor * decay_rate[u]
        tails.append(factor)
    payload = jnp.concatenate([prefix[steps]] + tails + [valued[s] for s in range(steps)], axis=-1)
    moved_terms = route_to_slots(
        payload.astype(bf16), position_mapping_target, batch_index, head_index
    ).astype(f32)
    slots_dev, columns, _ = moved_terms.shape
    moved_terms = moved_terms.reshape(slots_dev, columns, 1 + 2 * steps, SUBSPACE_EXTENT)
    final_state = moved_terms[:, :, 0, :, None] * moved_state.astype(f32).reshape(
        slots_dev, columns, SUBSPACE_EXTENT, SUBSPACE_EXTENT
    )
    for s in range(steps):
        final_state = (
            final_state
            + moved_terms[:, :, 1 + s, :, None] * moved_terms[:, :, 1 + steps + s, None, :]
        )
    final_state = final_state.reshape(slots_dev, columns, SUBSPACE_EXTENT * SUBSPACE_EXTENT)

    average = jnp.mean(wkv_out, axis=-1, keepdims=True)
    demeaned = wkv_out - average
    spread_squared = jnp.mean(demeaned * demeaned, axis=-1, keepdims=True)
    standardized = (demeaned * lax.rsqrt(spread_squared + NORMALIZER_GUARD)).reshape(
        steps, local_rows, width
    ) * norming_multiplier + norming_intercept
    combined_response = (standardized * gate_act).astype(bf16)

    gathered = lax.all_gather(combined_response, "batch", axis=1, tiled=True)
    inverse = jnp.argsort(position_mapping_target)
    arranged = jnp.concatenate(
        [gathered[:STEPS_A], jnp.take(gathered[STEPS_A:], inverse, axis=1)], axis=0
    )
    partial_y = jnp.einsum(
        "tnf,fo->tno", arranged, outgoing_linear_map, preferred_element_type=f32
    ).astype(bf16)
    produced = lax.psum_scatter(partial_y, "head", scatter_dimension=1, tiled=True)
    return (produced[:STEPS_A], produced[STEPS_A:], final_state)


def solution(mesh):
    in_specs = (
        P(None, "groups", "batch"),
        P("groups", "batch"),
        P(("groups", "batch"), "head", None),
        P("groups"),
        P(None, "batch"),
        P("batch", None),
        P(None, None, "batch"),
        P(None, "batch", "head"),
        P("batch", None),
        P(None, "head"),
        P("head"),
        P("head"),
        P("head"),
        P("head"),
        P("head", "batch"),
    )
    out_specs = (
        P(None, ("groups", "head"), "batch"),
        P(None, ("groups", "head"), "batch"),
        P(("groups", "batch", "head"), None, None),
    )
    return jax.shard_map(
        per_device, mesh=mesh, in_specs=in_specs, out_specs=out_specs, check_vma=False
    )
```

profile of v0, /device:TPU:0, one launch (start us, length us, event | category | flops | bytes accessed | tf_op | source)
XLA Modules:
  0.0 220.4 jit_solution(10291202828699283689)
XLA Ops:
  7.2 1.1 convert_bitcast_fusion
  8.4 0.9 slice_bitcast_fusion.2
  9.6 0.8 copy-done.4
  10.4 1.0 convolution_convert_fusion.1
  11.5 1.6 sort.76
  13.2 1.0 sort.75
  14.2 2.7 %convert_element_type.81 = bf16[8,16,4096]{2,1,0:T(8,128)(2,1)} convert(f32[8,16,4096]{2,1,0:T(8,128)} %param.23) | non-fusion elementwise | flops 524288 | bytes 3145728 | tf_op jit(solution)/shard_map/convert_element_type | solution.py:70
  17.5 2.8 %gather_fusion.4 = bf16[8,16,4096]{2,1,0:T(8,128)(2,1)} fusion(bf16[8,16,4096]{2,1,0:T(8,128)(2,1)} %convert_element_type.81, s32[1024]{0:T(1024)S(1)} %pad_clamp_fusion.1), kind=kCustom, calls=%fused_computation.2.clone | custom fusion | bytes 2097184 | tf_op jit(solution)/shard_map/jit(_take)/gather | solution.py:24
  20.3 28.0 %all-reduce.2.cloned.1.call-done = bf16[128,320]{0,1:T(8,128)(2,1)} async-done(((bf16[128,320]{0,1:T(8,128)(2,1)}), bf16[128,320]{0,1:T(8,128)(2,1)}) %all-reduce.2.cloned.1.call-update) | async-done | bytes 81936 | tf_op jit(solution)/shard_map/psum | solution.py:85
  48.3 0.9 tanh_convert_fusion
  49.3 1.7 add_convert_fusion
  51.3 4.8 %fusion.2 = bf16[128,4,1024]{2,0,1:T(8,128)(2,1)S(1)} fusion(bf16[5,128,1024]{2,1,0:T(8,128)(2,1)S(1)} %add_convert_fusion, bf16[4,1024,1024]{2,1,0:T(8,128)(2,1)} %param.28), kind=kOutput, calls=%fused_computation.15 | convolution fusion | flops 1074266112 | bytes 10747904 | tf_op jit(solution)/shard_map/inf,ifc->nic/dot_general | solution.py:93
  56.1 1.3 copy.116
  57.4 1.3 pad_maximum_fusion
  58.7 1.6 copy.129
  60.4 1.4 broadcast_select_fusion
  61.8 1.2 reshape.401
  63.0 2.8 %copy.127 = bf16[4,1,2,4,4,4096]{5,4,2,3,0,1:T(4,128)(2,1)} copy(bf16[4,1,2,4,4,4096]{5,4,3,2,0,1:T(4,128)(2,1)} %reshape.401) | data formatting | bytes 2097152 | tf_op jit(solution)/shard_map/reshape | solution.py:25
  65.8 4.7 %all-to-all-start.1 = ((bf16[16,2,4,4096]{3,2,1,0:T(4,128)(2,1)}), bf16[16,2,4,4096]{3,2,1,0:T(4,128)(2,1)S(1)}, u32[]{:S(2)}, u32[]{:S(2)}) async-start(bf16[16,2,4,4096]{3,2,1,0:T(4,128)(2,1)} %bitcast.108), calls=%async_computation.1 | async-start | bytes 2097152 | tf_op jit(solution)/shard_map/all_to_all | solution.py:29
  70.6 4.6 %reshape.394 = f32[8,16,64,64]{3,2,1,0:T(8,128)} reshape(f32[8,16,4096]{2,1,0:T(8,128)} %param.23) | data formatting | bytes 4194304 | tf_op jit(solution)/shard_map/reshape | solution.py:129
  75.8 1.6 sort.74
  78.1 1.0 sort.77
  80.8 25.1 %all-to-all-done.1 = bf16[16,2,4,4096]{3,2,1,0:T(4,128)(2,1)S(1)} async-done(((bf16[16,2,4,4096]{3,2,1,0:T(4,128)(2,1)}), bf16[16,2,4,4096]{3,2,1,0:T(4,128)(2,1)S(1)}, u32[]{:S(2)}, u32[]{:S(2)}) %all-to-all-start.1) | async-done | bytes 1048608 | tf_op jit(solution)/shard_map/all_to_all | solution.py:29
  105.9 1.4 copy.142
  107.3 1.4 reshape.404
  108.7 1.7 gather_fusion.5
  110.4 1.0 bitcast_convert_fusion
  112.9 0.7 fusion.42
  113.9 5.3 %fusion.9 = f32[8,16,4,64]{3,2,1,0:T(4,128)S(1)} fusion(f32[8,16,64,64]{3,2,1,0:T(8,128)} %reshape.394, f32[1,8,16,64]{3,0,2,1:T(1,128)S(1)} %bitcast.128, f32[1,8,16,64]{3,0,2,1:T(1,128)S(1)} %bitcast.129, f32[1,8,16,64]{3,0,2,1:T(1,128)S(1)} %bitcast.130, f32[1,8,16,64]{3,0,2,1:T(1,128)S(1)} %bitcast.131), kind=kOutput, calls=%fused_computation.31 | convolution fusion | flops 25264128 | bytes 2359296 | tf_op jit(solution)/shard_map/tnhi,nhij->tnhj/dot_general | solution.py:132
  119.3 0.7 squeeze.27
  119.9 0.7 squeeze.26
  120.6 0.7 squeeze.28
  121.5 0.7 reduce_sum.84
  122.2 0.7 reduce_sum.83
  123.0 1.0 reshape.392
  124.0 0.8 multiply_reduce_fusion.1
  124.8 0.8 mul.557
  125.8 0.8 mul.553
  126.7 0.8 mul.548
  127.6 0.8 squeeze.29
  128.5 0.8 mul.528
  129.4 1.1 fusion.33
  132.5 0.8 fusion.27
  133.3 17.0 %all_gather.3 = bf16[4,32,1024]{2,1,0:T(8,128)(2,1)S(1)} all-gather(bf16[4,8,1024]{2,1,0:T(8,128)(2,1)S(1)} %fusion.27), channel_id=1, replica_groups=mesh['groups'=2,'batch'=4,'head'=4] {'batch'}, dimensions={1}, use_global_device_ids=true | all-gather | bytes 327680 | tf_op jit(solution)/shard_map/all_gather | solution.py:176
  150.8 0.7 slice.293
  152.2 0.7 gather_fusion.1
  153.0 0.7 copy.125
  153.8 4.6 %all-to-all-start = ((bf16[16,2,4,576]{3,2,1,0:T(4,128)(2,1)}), bf16[16,2,4,576]{3,2,1,0:T(4,128)(2,1)S(1)}, u32[]{:S(2)}, u32[]{:S(2)}) async-start(bf16[16,2,4,576]{3,2,1,0:T(4,128)(2,1)} %bitcast.26), calls=%async_computation | async-start | bytes 327680 | tf_op jit(solution)/shard_map/all_to_all | solution.py:29
  158.4 0.9 gather_fusion
  160.1 0.8 copy.135
  160.9 5.9 %all-to-all-done = bf16[16,2,4,576]{3,2,1,0:T(4,128)(2,1)S(1)} async-done(((bf16[16,2,4,576]{3,2,1,0:T(4,128)(2,1)}), bf16[16,2,4,576]{3,2,1,0:T(4,128)(2,1)S(1)}, u32[]{:S(2)}, u32[]{:S(2)}) %all-to-all-start) | async-done | bytes 147488 | tf_op jit(solution)/shard_map/all_to_all | solution.py:29
  167.0 0.7 gather_fusion.3
  168.4 2.6 %broadcast_multiply_fusion = f32[8,16,64,64]{3,2,1,0:T(8,128)} fusion(f32[8,16,64]{2,1,0:T(8,128)S(1)} %bitcast.126, f32[8,16,64]{2,1,0:T(8,128)S(1)} %bitcast.127), kind=kLoop, calls=%fused_computation.9 | loop fusion | flops 524288 | bytes 2162688 | tf_op jit(solution)/shard_map/mul | solution.py:164
  170.9 4.8 %mul.604 = f32[8,16,4096]{2,1,0:T(8,128)} reshape(f32[8,16,64,64]{3,2,1,0:T(8,128)} %broadcast_multiply_fusion) | data formatting | bytes 4194304 | tf_op jit(solution)/shard_map/mul | solution.py:164
  175.7 2.5 %broadcast_multiply_fusion.1 = f32[8,16,64,64]{3,2,1,0:T(8,128)} fusion(f32[8,16,64]{2,1,0:T(8,128)S(1)} %bitcast.124, f32[8,16,64]{2,1,0:T(8,128)S(1)} %bitcast.125), kind=kLoop, calls=%fused_computation.11 | loop fusion | flops 524288 | bytes 2162688 | tf_op jit(solution)/shard_map/mul | solution.py:164
  178.3 4.8 %mul.598 = f32[8,16,4096]{2,1,0:T(8,128)} reshape(f32[8,16,64,64]{3,2,1,0:T(8,128)} %broadcast_multiply_fusion.1) | data formatting | bytes 4194304 | tf_op jit(solution)/shard_map/mul | solution.py:164
  183.0 2.5 %broadcast_multiply_fusion.2 = f32[8,16,64,64]{3,2,1,0:T(8,128)} fusion(f32[8,16,64]{2,1,0:T(8,128)S(1)} %bitcast.122, f32[8,16,64]{2,1,0:T(8,128)S(1)} %bitcast.123), kind=kLoop, calls=%fused_computation.12 | loop fusion | flops 524288 | bytes 2162688 | tf_op jit(solution)/shard_map/mul | solution.py:164
  185.6 4.8 %mul.592 = f32[8,16,4096]{2,1,0:T(8,128)} reshape(f32[8,16,64,64]{3,2,1,0:T(8,128)} %broadcast_multiply_fusion.2) | data formatting | bytes 4194304 | tf_op jit(solution)/shard_map/mul | solution.py:164
  190.4 2.5 %broadcast_multiply_fusion.3 = f32[8,16,64,64]{3,2,1,0:T(8,128)} fusion(f32[8,16,64]{2,1,0:T(8,128)S(1)} %bitcast.120, f32[8,16,64]{2,1,0:T(8,128)S(1)} %bitcast.121), kind=kLoop, calls=%fused_computation.13 | loop fusion | flops 524288 | bytes 2162688 | tf_op jit(solution)/shard_map/mul | solution.py:164
  192.9 4.8 %mul.586 = f32[8,16,4096]{2,1,0:T(8,128)} reshape(f32[8,16,64,64]{3,2,1,0:T(8,128)} %broadcast_multiply_fusion.3) | data formatting | bytes 4194304 | tf_op jit(solution)/shard_map/mul | solution.py:164
  197.6 2.5 %mul.578 = f32[8,16,64,64]{3,2,1,0:T(8,128)} broadcast(f32[8,16,64]{2,1,0:T(8,128)S(1)} %bitcast.119), dimensions={0,1,2} | broadcast | bytes 2129920 | tf_op jit(solution)/shard_map/mul | solution.py:158
  200.2 4.9 %mul.579 = f32[8,16,4096]{2,1,0:T(8,128)} reshape(f32[8,16,64,64]{3,2,1,0:T(8,128)} %mul.578) | data formatting | bytes 4194304 | tf_op jit(solution)/shard_map/mul | solution.py:158
  205.0 6.7 %add_add_fusion = f32[8,16,4096]{2,1,0:T(8,128)} fusion(f32[8,16,4096]{2,1,0:T(8,128)} %mul.604, f32[8,16,4096]{2,1,0:T(8,128)} %mul.598, f32[8,16,4096]{2,1,0:T(8,128)} %mul.592, f32[8,16,4096]{2,1,0:T(8,128)} %mul.586, f32[8,16,4096]{2,1,0:T(8,128)} %mul.579, bf16[8,16,4096]{2,1,0:T(8,128)(2,1)S(1)} %copy-done.3, pred[8]{0:T(512)(128)(4,1)S(1)} %copy-done.17), kind=kLoop, calls=%fused_computation.10 | loop fusion | flops 3670016 | bytes 13631496 | tf_op jit(solution)/shard_map/add | solution.py:163
  211.7 0.9 reshape.479
  (132 shorter events, 12.9 us)
Async XLA Ops:
  7.2 152.3 %copy-start = (bf16[1024,1024]{1,0:T(8,128)(2,1)S(1)}, bf16[1024,1024]{1,0:T(8,128)(2,1)}, u32[]{:S(2)}) copy-start(bf16[1024,1024]{1,0:T(8,128)(2,1)} %param.35) | copy-start | bytes 6291460
  7.2 2.2 %copy-start.7 = (bf16[32,1024]{1,0:T(8,128)(2,1)S(1)}, bf16[32,1024]{1,0:T(8,128)(2,1)}, u32[]{:S(2)}) copy-start(bf16[32,1024]{1,0:T(8,128)(2,1)} %param.22) | copy-start | bytes 196612
  7.2 41.1 %all-reduce.2.cloned.1.call-start = ((), (), s32[]{:S(2)}) async-start(), calls=%async_computation.4 | async-start | bytes 163840 | tf_op jit(solution)/shard_map/psum | solution.py:85
  9.3 1.1 copy-start.4
  9.3 1.1 slice-start
  9.5 2.0 copy-start.12
  9.5 2.0 copy-start.2
  11.4 98.9 %reduce-scatter.7.cloned.1.call-start = ((), (), s32[]{:S(2)}) async-start(), calls=%async_computation.5 | async-start | bytes 1351680 | tf_op jit(solution)/shard_map/reduce_scatter | solution.py:97
  14.2 46.1 %copy-start.18 = (pred[8]{0:T(512)(128)(4,1)}, pred[8]{0:T(512)(128)(4,1)S(1)}, u32[]{:S(2)}) copy-start(pred[8]{0:T(512)(128)(4,1)S(1)} %compare_and_fusion.1) | copy-start | bytes 28
  16.9 0.6 copy-start.13
  20.3 30.6 %copy-start.5 = (bf16[1024,128]{1,0:T(8,128)(2,1)S(1)}, bf16[1024,128]{1,0:T(8,128)(2,1)}, u32[]{:S(2)}) copy-start(bf16[1024,128]{1,0:T(8,128)(2,1)} %param.29) | copy-start | bytes 786436
  65.8 40.1 %all-to-all-start.1 = ((bf16[16,2,4,4096]{3,2,1,0:T(4,128)(2,1)}), bf16[16,2,4,4096]{3,2,1,0:T(4,128)(2,1)S(1)}, u32[]{:S(2)}, u32[]{:S(2)}) async-start(bf16[16,2,4,4096]{3,2,1,0:T(4,128)(2,1)} %bitcast.108), calls=%async_computation.1 | async-start | bytes 2097152 | tf_op jit(solution)/shard_map/all_to_all | solution.py:29
  70.5 4.6 %copy-start.16 = (f32[1024]{0:T(1024)S(1)}, f32[1024]{0:T(1024)}, u32[]{:S(2)}) copy-start(f32[1024]{0:T(1024)} %param.32) | copy-start | bytes 12292
  79.7 30.7 %copy-start.14 = (s32[1024]{0:T(1024)}, s32[1024]{0:T(1024)S(1)}, u32[]{:S(2)}) copy-start(s32[1024]{0:T(1024)S(1)} %pad_clamp_fusion) | copy-start | bytes 12292
  107.3 4.1 %copy-start.6 = (bf16[128,1024]{1,0:T(8,128)(2,1)S(1)}, bf16[128,1024]{1,0:T(8,128)(2,1)}, u32[]{:S(2)}) copy-start(bf16[128,1024]{1,0:T(8,128)(2,1)} %param.30) | copy-start | bytes 786436
  107.3 4.1 %copy-start.15 = (f32[1024]{0:T(1024)S(1)}, f32[1024]{0:T(1024)}, u32[]{:S(2)}) copy-start(f32[1024]{0:T(1024)} %param.31) | copy-start | bytes 12292
  130.6 19.9 %copy-start.10 = (bf16[1,8,1024]{2,1,0:T(8,128)(2,1)S(1)}, bf16[1,8,1024]{2,1,0:T(8,128)(2,1)}, u32[]{:S(2)}) copy-start(bf16[1,8,1024]{2,1,0:T(8,128)(2,1)} %get-tuple-element.27) | copy-start | bytes 49156
  130.7 19.9 %copy-start.9 = (bf16[1,8,1024]{2,1,0:T(8,128)(2,1)S(1)}, bf16[1,8,1024]{2,1,0:T(8,128)(2,1)}, u32[]{:S(2)}) copy-start(bf16[1,8,1024]{2,1,0:T(8,128)(2,1)} %get-tuple-element.28) | copy-start | bytes 49156
  130.7 20.0 %copy-start.8 = (bf16[1,8,1024]{2,1,0:T(8,128)(2,1)S(1)}, bf16[1,8,1024]{2,1,0:T(8,128)(2,1)}, u32[]{:S(2)}) copy-start(bf16[1,8,1024]{2,1,0:T(8,128)(2,1)} %get-tuple-element.23) | copy-start | bytes 49156
  131.9 19.7 %copy-start.11 = (bf16[1,8,1024]{2,1,0:T(8,128)(2,1)S(1)}, bf16[1,8,1024]{2,1,0:T(8,128)(2,1)}, u32[]{:S(2)}) copy-start(bf16[1,8,1024]{2,1,0:T(8,128)(2,1)} %get-tuple-element.33) | copy-start | bytes 49156
  132.0 20.9 %copy-start.19 = (pred[8]{0:T(512)(128)(4,1)S(1)}, pred[8]{0:T(512)(128)(4,1)}, u32[]{:S(2)}) copy-start(pred[8]{0:T(512)(128)(4,1)} %copy-done.18) | copy-start | bytes 28
  132.5 26.9 %copy-start.20 = (pred[32]{0:T(512)(128)(4,1)S(1)}, pred[32]{0:T(512)(128)(4,1)}, u32[]{:S(2)}) copy-start(pred[32]{0:T(512)(128)(4,1)} %compare_and_fusion.2) | copy-start | bytes 100
  153.8 13.1 %all-to-all-start = ((bf16[16,2,4,576]{3,2,1,0:T(4,128)(2,1)}), bf16[16,2,4,576]{3,2,1,0:T(4,128)(2,1)S(1)}, u32[]{:S(2)}, u32[]{:S(2)}) async-start(bf16[16,2,4,576]{3,2,1,0:T(4,128)(2,1)} %bitcast.26), calls=%async_computation | async-start | bytes 327680 | tf_op jit(solution)/shard_map/all_to_all | solution.py:29
  158.4 53.3 %reduce-scatter.9.cloned.1.call-start = ((), (), s32[]{:S(2)}) async-start(), calls=%async_computation.6 | async-start | bytes 327680
  159.5 8.2 %copy-start.17 = (pred[8]{0:T(512)(128)(4,1)S(1)}, pred[8]{0:T(512)(128)(4,1)}, u32[]{:S(2)}) copy-start(pred[8]{0:T(512)(128)(4,1)} %compare_and_fusion) | copy-start | bytes 28
  200.2 4.9 %copy-start.3 = (bf16[8,16,4096]{2,1,0:T(8,128)(2,1)S(1)}, bf16[8,16,4096]{2,1,0:T(8,128)(2,1)}, u32[]{:S(2)}) copy-start(bf16[8,16,4096]{2,1,0:T(8,128)(2,1)} %gather_fusion.5) | copy-start | bytes 3145732
  205.0 8.8 %copy-start.1 = (bf16[1024,1024]{1,0:T(8,128)(2,1)S(1)}, bf16[1024,1024]{1,0:T(8,128)(2,1)}, u32[]{:S(2)}) copy-start(bf16[1024,1024]{1,0:T(8,128)(2,1)} %param.35) | copy-start | bytes 6291460
Sparse Core Ops, SparseCore 0:
  11.6 36.7 all-reduce.1
  60.5 40.1 reduce-scatter.6
  161.8 21.3 reduce-scatter.8
where the time goes:
time: 222 us; the launch traced here: 220 us
  local copies, waits for them, and re-layouts  68 us (31%)
  waiting for transfers between devices  59 us (27%)
  other arithmetic  38.8 us (17%)
  blocking collectives  17 us (8%)
  between operations  14.4 us (6%)
  matrix products  13.8 us (6%)
  starting transfers between devices  9.43 us (4%)
    all_to_all x2, waiting for transfers between devices, route_to_slots(): lax.all_to_all(packed, ('batch', 'head'), split_axis=0, concat_axis=0, ti...  31 us
    psum x1, waiting for transfers between devices, per_device(): lax.psum(partial_value.astype(bf16), 'batch').astype(f32)  28 us
    mul x4, local copies, waits for them, and re-layouts, per_device(): moved_terms[:, :, 1 + s, :, None]  19.1 us
    all_gather x1, blocking collectives, per_device(): gathered = lax.all_gather(combined_response, 'batch', axis=1, tiled=True)  17 us
    mul x4, other arithmetic, per_device(): moved_terms[:, :, 1 + s, :, None]  10.2 us
    all_to_all x2, starting transfers between devices, route_to_slots(): lax.all_to_all(packed, ('batch', 'head'), split_axis=0, concat_axis=0, ti...  9.3 us
    mul x2, local copies, waits for them, and re-layouts, per_device(): moved_terms[:, :, 0, :, None]  7.39 us
    add x1, other arithmetic, per_device(): final_state + moved_terms[:, :, 1 + s, :, None] * moved_terms[:, :, 1 + s...  6.66 us
  transfers between devices with their start and end apart: 5, of which 3 were waited for; matrix products, arithmetic and copies ran while one was open for 34% of the time, Pallas kernels for 0%

commit v1 on v0

--- a/solution.py
+++ b/solution.py
@@ -1,6 +1,10 @@
+import functools
+
 import jax
 import jax.numpy as jnp
 from jax import lax
+from jax.experimental import pallas as pl
+from jax.experimental.pallas import tpu as pltpu
 from jax.sharding import PartitionSpec as P
 
 SUBSPACE_EXTENT = 64
@@ -37,6 +41,53 @@
     )
     placing = jnp.argsort(jnp.take(position_mapping_target, arrivals) % slots_dev)
     return jnp.take(arrived, placing, axis=0)
+
+
+def rebuild_kernel(steps, state_ref, terms_ref, out_ref, spread_ref, tile_ref):
+    extent = SUBSPACE_EXTENT
+
+    @pl.when(pl.program_id(0) == 0)
+    def _():
+        lane = lax.broadcasted_iota(jnp.int32, spread_ref.shape, 1)
+        row = lax.broadcasted_iota(jnp.int32, spread_ref.shape, 0)
+        spread_ref[...] = (lane // extent == row).astype(spread_ref.dtype)
+        tile_ref[...] = (lane % extent == row).astype(tile_ref.dtype)
+
+    spread = spread_ref[...]
+    tile = tile_ref[...]
+    total = jnp.dot(terms_ref[0], spread, preferred_element_type=jnp.float32) * state_ref[...].astype(
+        jnp.float32
+    )
+    for s in range(steps):
+        total = total + jnp.dot(
+            terms_ref[1 + s], spread, preferred_element_type=jnp.float32
+        ) * jnp.dot(terms_ref[1 + steps + s], tile, preferred_element_type=jnp.float32)
+    out_ref[...] = total
+
+
+def rebuild_state(moved_state, moved_terms, steps):
+    slots_dev, columns, flat = moved_state.shape
+    pieces = moved_terms.shape[1]
+    extent = SUBSPACE_EXTENT
+    return pl.pallas_call(
+        functools.partial(rebuild_kernel, steps),
+        grid=(slots_dev,),
+        in_specs=[
+            pl.BlockSpec((None, columns, flat), lambda n: (n, 0, 0)),
+            pl.BlockSpec((None, pieces, columns, extent), lambda n: (n, 0, 0, 0)),
+        ],
+        out_specs=pl.BlockSpec((None, columns, flat), lambda n: (n, 0, 0)),
+        out_shape=jax.ShapeDtypeStruct((slots_dev, columns, flat), jnp.float32),
+        scratch_shapes=[
+            pltpu.VMEM((extent, flat), jnp.bfloat16),
+            pltpu.VMEM((extent, flat), jnp.bfloat16),
+        ],
+        cost_estimate=pl.CostEstimate(
+            flops=2 * slots_dev * columns * extent * flat * (1 + 2 * steps),
+            transcendentals=0,
+            bytes_accessed=slots_dev * columns * (flat * 6 + pieces * extent * 2),
+        ),
+    )(moved_state, moved_terms)
 
 
 def per_device(
@@ -152,18 +203,12 @@
     payload = jnp.concatenate([prefix[steps]] + tails + [valued[s] for s in range(steps)], axis=-1)
     moved_terms = route_to_slots(
         payload.astype(bf16), position_mapping_target, batch_index, head_index
-    ).astype(f32)
+    )
     slots_dev, columns, _ = moved_terms.shape
-    moved_terms = moved_terms.reshape(slots_dev, columns, 1 + 2 * steps, SUBSPACE_EXTENT)
-    final_state = moved_terms[:, :, 0, :, None] * moved_state.astype(f32).reshape(
-        slots_dev, columns, SUBSPACE_EXTENT, SUBSPACE_EXTENT
-    )
-    for s in range(steps):
-        final_state = (
-            final_state
-            + moved_terms[:, :, 1 + s, :, None] * moved_terms[:, :, 1 + steps + s, None, :]
-        )
-    final_state = final_state.reshape(slots_dev, columns, SUBSPACE_EXTENT * SUBSPACE_EXTENT)
+    moved_terms = moved_terms.reshape(slots_dev, columns, 1 + 2 * steps, SUBSPACE_EXTENT).transpose(
+        0, 2, 1, 3
+    )
+    final_state = rebuild_state(moved_state, moved_terms, steps)
 
     average = jnp.mean(wkv_out, axis=-1, keepdims=True)
     demeaned = wkv_out - average

time: 222 us -> 192 us (0.86)
  local copies, waits for them, and re-layouts: 68 us -> 44 us
  other arithmetic: 38.8 us -> 23.7 us
  Pallas kernels: 0 us -> 8.54 us
    mul x6 -> x0, local copies, waits for them, and re-layouts: 26.5 us -> none  [the longest x4 19.1 us: per_device(): moved_terms[:, :, 1 + s, :, None]]
    mul x4 -> x0, other arithmetic: 10.2 us -> none  [per_device(): moved_terms[:, :, 1 + s, :, None]]
    pallas_call x0 -> x1, Pallas kernels: none -> 8.54 us  [rebuild_state(): pl.pallas_call(functools.partial(rebuild_kernel, steps), grid=(slots_dev,...]
    add x1 -> x0, other arithmetic: 6.66 us -> none  [per_device(): final_state + moved_terms[:, :, 1 + s, :, None] * moved_terms[:, :, 1 + s...]
    unnamed x48 -> x50, local copies, waits for them, and re-layouts: 6.24 us -> 6.27 us
  transfers between devices with their start and end apart: 5 -> 5, of which waited for: 3 -> 3; matrix products, arithmetic and copies ran while one was open for 34% -> 20% of each run, Pallas kernels for 0% -> 4%
where the time goes in v1:
time: 192 us; the launch traced here: 191 us
  waiting for transfers between devices  59.7 us (31%)
  local copies, waits for them, and re-layouts  44 us (23%)
  other arithmetic  23.7 us (12%)
  blocking collectives  17 us (9%)
  between operations  14.4 us (8%)
  matrix products  13.8 us (7%)
  starting transfers between devices  9.42 us (5%)
  Pallas kernels  8.54 us (4%)
    all_to_all x2, waiting for transfers between devices, route_to_slots(): lax.all_to_all(packed, ('batch', 'head'), split_axis=0, concat_axis=0, ti...  31.7 us
    psum x1, waiting for transfers between devices, per_device(): lax.psum(partial_value.astype(bf16), 'batch').astype(f32)  28 us
    all_gather x1, blocking collectives, per_device(): gathered = lax.all_gather(combined_response, 'batch', axis=1, tiled=True)  17 us
    all_to_all x2, starting transfers between devices, route_to_slots(): lax.all_to_all(packed, ('batch', 'head'), split_axis=0, concat_axis=0, ti...  9.3 us
    pallas_call x1, Pallas kernels, rebuild_state(): pl.pallas_call(functools.partial(rebuild_kernel, steps), grid=(slots_dev,...  8.54 us
    unnamed x50, local copies, waits for them, and re-layouts  6.27 us
    dot_general x1, matrix products, per_device(): jnp.einsum('tnhi,nhij->tnhj', query, state, precision=lax.Precision.HIGHEST)  5.34 us
    dot_general x1, matrix products, per_device(): jnp.einsum('inf,ifc->nic', mixed[:4], fourfold_linear_maps, preferred_ele...  4.83 us
  transfers between devices with their start and end apart: 5, of which 3 were waited for; matrix products, arithmetic and copies ran while one was open for 20% of the time, Pallas kernels for 4%

profile of v1, /device:TPU:0, one launch (start us, length us, event | category | flops | bytes accessed | tf_op | source)
XLA Modules:
  0.0 190.6 jit_solution(14477822667708076964)
XLA Ops:
  7.2 1.1 convert_bitcast_fusion
  8.4 0.9 slice_bitcast_fusion.2
  9.6 0.8 copy-done.3
  10.4 1.0 convolution_convert_fusion.1
  11.5 1.6 sort.76
  13.2 1.0 sort.75
  14.2 2.7 %convert_element_type.77 = bf16[8,16,4096]{2,1,0:T(8,128)(2,1)} convert(f32[8,16,4096]{2,1,0:T(8,128)} %param.23) | non-fusion elementwise | flops 524288 | bytes 3145728 | tf_op jit(solution)/shard_map/convert_element_type | solution.py:121
  17.5 2.8 %gather_fusion.1 = bf16[8,16,4096]{2,1,0:T(8,128)(2,1)} fusion(bf16[8,16,4096]{2,1,0:T(8,128)(2,1)} %convert_element_type.77, s32[1024]{0:T(1024)S(1)} %pad_clamp_fusion.1), kind=kCustom, calls=%fused_computation.clone | custom fusion | bytes 2097184 | tf_op jit(solution)/shard_map/jit(_take)/gather | solution.py:28
  20.3 28.0 %all-reduce.2.cloned.1.call-done = bf16[128,320]{0,1:T(8,128)(2,1)} async-done(((bf16[128,320]{0,1:T(8,128)(2,1)}), bf16[128,320]{0,1:T(8,128)(2,1)}) %all-reduce.2.cloned.1.call-update) | async-done | bytes 81936 | tf_op jit(solution)/shard_map/psum | solution.py:136
  48.3 0.9 tanh_convert_fusion
  49.2 1.7 add_convert_fusion
  51.2 4.8 %fusion.2 = bf16[128,4,1024]{2,0,1:T(8,128)(2,1)S(1)} fusion(bf16[5,128,1024]{2,1,0:T(8,128)(2,1)S(1)} %add_convert_fusion, bf16[4,1024,1024]{2,1,0:T(8,128)(2,1)} %param.28), kind=kOutput, calls=%fused_computation.10 | convolution fusion | flops 1074266112 | bytes 10747904 | tf_op jit(solution)/shard_map/inf,ifc->nic/dot_general | solution.py:144
  56.1 1.3 copy.119
  57.4 1.3 pad_maximum_fusion
  58.7 1.6 copy.133
  60.3 1.4 broadcast_select_fusion.1
  61.7 1.2 reshape.372
  63.0 2.8 %copy.128 = bf16[4,1,2,4,4,4096]{5,4,2,3,0,1:T(4,128)(2,1)} copy(bf16[4,1,2,4,4,4096]{5,4,3,2,0,1:T(4,128)(2,1)} %reshape.372) | data formatting | bytes 2097152 | tf_op jit(solution)/shard_map/reshape | solution.py:29
  65.8 4.7 %all-to-all-start = ((bf16[16,2,4,4096]{3,2,1,0:T(4,128)(2,1)}), bf16[16,2,4,4096]{3,2,1,0:T(4,128)(2,1)S(1)}, u32[]{:S(2)}, u32[]{:S(2)}) async-start(bf16[16,2,4,4096]{3,2,1,0:T(4,128)(2,1)} %bitcast.92), calls=%async_computation | async-start | bytes 2097152 | tf_op jit(solution)/shard_map/all_to_all | solution.py:33
  70.6 4.6 %reshape.371 = f32[8,16,64,64]{3,2,1,0:T(8,128)} reshape(f32[8,16,4096]{2,1,0:T(8,128)} %param.23) | data formatting | bytes 4194304 | tf_op jit(solution)/shard_map/reshape | solution.py:180
  75.2 0.7 mul.412
  75.9 1.6 sort.74
  77.5 0.6 gather_fusion.2
  78.1 1.0 sort.77
  80.9 25.0 %all-to-all-done = bf16[16,2,4,4096]{3,2,1,0:T(4,128)(2,1)S(1)} async-done(((bf16[16,2,4,4096]{3,2,1,0:T(4,128)(2,1)}), bf16[16,2,4,4096]{3,2,1,0:T(4,128)(2,1)S(1)}, u32[]{:S(2)}, u32[]{:S(2)}) %all-to-all-start) | async-done | bytes 1048608 | tf_op jit(solution)/shard_map/all_to_all | solution.py:33
  105.9 1.4 copy.147
  107.3 1.4 reshape.375
  108.7 1.6 gather_fusion.3
  110.3 1.0 bitcast_convert_fusion
  111.5 0.7 slice_multiply_fusion.4
  112.1 0.7 multiply_convert_fusion
  112.8 0.7 fusion.41
  113.8 5.3 %fusion.9 = f32[8,16,4,64]{3,2,1,0:T(4,128)S(1)} fusion(f32[8,16,64,64]{3,2,1,0:T(8,128)} %reshape.371, f32[1,8,16,64]{3,0,2,1:T(1,128)S(1)} %bitcast.104, f32[1,8,16,64]{3,0,2,1:T(1,128)S(1)} %bitcast.105, f32[1,8,16,64]{3,0,2,1:T(1,128)S(1)} %bitcast.106, f32[1,8,16,64]{3,0,2,1:T(1,128)S(1)} %bitcast.107), kind=kOutput, calls=%fused_computation.28 | convolution fusion | flops 25264128 | bytes 2359296 | tf_op jit(solution)/shard_map/tnhi,nhij->tnhj/dot_general | solution.py:183
  119.2 0.7 squeeze.27
  119.9 0.7 squeeze.26
  120.6 0.7 squeeze.28
  121.4 0.7 reduce_sum.84
  122.1 0.7 reduce_sum.83
  122.9 1.0 reshape.369
  123.9 0.8 multiply_reduce_fusion.1
  124.8 0.8 mul.460
  125.7 0.8 mul.456
  126.6 0.8 mul.451
  127.6 0.8 squeeze.29
  128.4 0.8 mul.431
  129.3 1.1 fusion.33
  132.5 17.0 %all_gather.3 = bf16[4,32,1024]{2,1,0:T(8,128)(2,1)S(1)} all-gather(bf16[4,8,1024]{2,1,0:T(8,128)(2,1)S(1)} %fusion.27), channel_id=1, replica_groups=mesh['groups'=2,'batch'=4,'head'=4] {'batch'}, dimensions={1}, use_global_device_ids=true | all-gather | bytes 327680 | tf_op jit(solution)/shard_map/all_gather | solution.py:221
  149.6 0.9 gather_fusion
  151.4 0.8 copy.139
  152.7 0.7 slice.257
  153.7 0.7 squeeze.33
  154.4 0.7 squeeze.34
  155.1 0.9 concatenate.25
  156.0 0.7 gather_fusion.4
  156.7 0.7 broadcast_select_fusion.3
  157.5 0.7 copy.130
  158.2 4.6 %all-to-all-start.1 = ((bf16[16,2,4,576]{3,2,1,0:T(4,128)(2,1)}), bf16[16,2,4,576]{3,2,1,0:T(4,128)(2,1)S(1)}, u32[]{:S(2)}, u32[]{:S(2)}) async-start(bf16[16,2,4,576]{3,2,1,0:T(4,128)(2,1)} %bitcast.30), calls=%async_computation.1 | async-start | bytes 327680 | tf_op jit(solution)/shard_map/all_to_all | solution.py:33
  162.8 1.8 broadcast_select_fusion.state_ref
  164.6 6.7 %all-to-all-done.1 = bf16[16,2,4,576]{3,2,1,0:T(4,128)(2,1)S(1)} async-done(((bf16[16,2,4,576]{3,2,1,0:T(4,128)(2,1)}), bf16[16,2,4,576]{3,2,1,0:T(4,128)(2,1)S(1)}, u32[]{:S(2)}, u32[]{:S(2)}) %all-to-all-start.1) | async-done | bytes 147488 | tf_op jit(solution)/shard_map/all_to_all | solution.py:33
  171.4 0.7 gather_fusion.5
  172.5 0.8 copy.148
  173.3 8.5 %shard_map.166 = f32[8,16,4096]{2,1,0:T(8,128)} custom-call(bf16[8,16,4096]{2,1,0:T(8,128)(2,1)} %broadcast_select_fusion.state_ref, bf16[8,9,16,64]{3,2,1,0:T(8,128)(2,1)} %bitcast.95), custom_call_target="tpu_custom_call" | custom-call | flops 603979776 | bytes 3293184 | tf_op jit(solution)/shard_map/pallas_call | solution.py:72
  181.9 0.9 reshape.453
  182.8 0.6 copy.137
  (125 shorter events, 9.0 us)
Async XLA Ops:
  7.2 143.5 %copy-start = (bf16[1024,1024]{1,0:T(8,128)(2,1)S(1)}, bf16[1024,1024]{1,0:T(8,128)(2,1)}, u32[]{:S(2)}) copy-start(bf16[1024,1024]{1,0:T(8,128)(2,1)} %param.35) | copy-start | bytes 6291460
  7.2 2.2 %copy-start.6 = (bf16[32,1024]{1,0:T(8,128)(2,1)S(1)}, bf16[32,1024]{1,0:T(8,128)(2,1)}, u32[]{:S(2)}) copy-start(bf16[32,1024]{1,0:T(8,128)(2,1)} %param.22) | copy-start | bytes 196612
  7.2 41.1 %all-reduce.2.cloned.1.call-start = ((), (), s32[]{:S(2)}) async-start(), calls=%async_computation.4 | async-start | bytes 163840 | tf_op jit(solution)/shard_map/psum | solution.py:136
  9.3 1.1 copy-start.3
  9.3 1.1 slice-start
  9.5 2.0 %copy-start.12 = (f32[6,1024]{1,0:T(8,128)S(1)}, f32[6,1024]{1,0:T(8,128)}, u32[]{:S(2)}) copy-start(f32[6,1024]{1,0:T(8,128)} %param.25) | copy-start | bytes 73732
  9.5 2.0 %copy-start.1 = (s32[32]{0:T(128)S(1)}, s32[32]{0:T(128)}, u32[]{:S(2)}) copy-start(s32[32]{0:T(128)} %param.24) | copy-start | bytes 388
  11.4 98.8 %reduce-scatter.7.cloned.1.call-start = ((), (), s32[]{:S(2)}) async-start(), calls=%async_computation.5 | async-start | bytes 1351680 | tf_op jit(solution)/shard_map/reduce_scatter | solution.py:148
  14.2 46.1 %copy-start.19 = (pred[8]{0:T(512)(128)(4,1)}, pred[8]{0:T(512)(128)(4,1)S(1)}, u32[]{:S(2)}) copy-start(pred[8]{0:T(512)(128)(4,1)S(1)} %compare_and_fusion.1) | copy-start | bytes 28
  16.9 0.6 copy-start.13
  20.3 30.6 %copy-start.4 = (bf16[1024,128]{1,0:T(8,128)(2,1)S(1)}, bf16[1024,128]{1,0:T(8,128)(2,1)}, u32[]{:S(2)}) copy-start(bf16[1024,128]{1,0:T(8,128)(2,1)} %param.29) | copy-start | bytes 786436
  65.8 40.1 %all-to-all-start = ((bf16[16,2,4,4096]{3,2,1,0:T(4,128)(2,1)}), bf16[16,2,4,4096]{3,2,1,0:T(4,128)(2,1)S(1)}, u32[]{:S(2)}, u32[]{:S(2)}) async-start(bf16[16,2,4,4096]{3,2,1,0:T(4,128)(2,1)} %bitcast.92), calls=%async_computation | async-start | bytes 2097152 | tf_op jit(solution)/shard_map/all_to_all | solution.py:33
  70.5 4.7 %copy-start.18 = (f32[1024]{0:T(1024)S(1)}, f32[1024]{0:T(1024)}, u32[]{:S(2)}) copy-start(f32[1024]{0:T(1024)} %param.32) | copy-start | bytes 12292
  70.5 111.3 %reduce-scatter.9.cloned.1.call-start = ((), (), s32[]{:S(2)}) async-start(), calls=%async_computation.6 | async-start | bytes 327680
  79.7 29.0 %copy-start.14 = (s32[1024]{0:T(1024)}, s32[1024]{0:T(1024)S(1)}, u32[]{:S(2)}) copy-start(s32[1024]{0:T(1024)S(1)} %pad_clamp_fusion) | copy-start | bytes 12292
  107.3 4.0 %copy-start.5 = (bf16[128,1024]{1,0:T(8,128)(2,1)S(1)}, bf16[128,1024]{1,0:T(8,128)(2,1)}, u32[]{:S(2)}) copy-start(bf16[128,1024]{1,0:T(8,128)(2,1)} %param.30) | copy-start | bytes 786436
  107.3 4.0 %copy-start.15 = (f32[1024]{0:T(1024)S(1)}, f32[1024]{0:T(1024)}, u32[]{:S(2)}) copy-start(f32[1024]{0:T(1024)} %param.31) | copy-start | bytes 12292
  125.6 6.8 %copy-start.16 = (f32[1024]{0:T(1024)S(1)}, f32[1024]{0:T(1024)}, u32[]{:S(2)}) copy-start(f32[1024]{0:T(1024)} %param.34) | copy-start | bytes 12292
  125.6 6.8 %copy-start.17 = (f32[1024]{0:T(1024)S(1)}, f32[1024]{0:T(1024)}, u32[]{:S(2)}) copy-start(f32[1024]{0:T(1024)} %param.33) | copy-start | bytes 12292
  130.9 19.7 %copy-start.21 = (pred[32]{0:T(512)(128)(4,1)S(1)}, pred[32]{0:T(512)(128)(4,1)}, u32[]{:S(2)}) copy-start(pred[32]{0:T(512)(128)(4,1)} %compare_and_fusion.2) | copy-start | bytes 100
  150.6 1.8 copy-start.9
  150.6 1.9 copy-start.8
  150.7 1.9 copy-start.7
  150.7 2.9 %copy-start.11 = (bf16[1,8,1024]{2,1,0:T(8,128)(2,1)S(1)}, bf16[1,8,1024]{2,1,0:T(8,128)(2,1)}, u32[]{:S(2)}) copy-start(bf16[1,8,1024]{2,1,0:T(8,128)(2,1)} %get-tuple-element.25) | copy-start | bytes 49156
  150.7 3.0 %copy-start.10 = (bf16[1,8,1024]{2,1,0:T(8,128)(2,1)S(1)}, bf16[1,8,1024]{2,1,0:T(8,128)(2,1)}, u32[]{:S(2)}) copy-start(bf16[1,8,1024]{2,1,0:T(8,128)(2,1)} %get-tuple-element.26) | copy-start | bytes 49156
  151.2 11.6 %copy-start.2 = (bf16[8,16,4096]{2,1,0:T(8,128)(2,1)S(1)}, bf16[8,16,4096]{2,1,0:T(8,128)(2,1)}, u32[]{:S(2)}) copy-start(bf16[8,16,4096]{2,1,0:T(8,128)(2,1)} %gather_fusion.3) | copy-start | bytes 3145732
  157.4 14.7 %copy-start.20 = (pred[8]{0:T(512)(128)(4,1)S(1)}, pred[8]{0:T(512)(128)(4,1)}, u32[]{:S(2)}) copy-start(pred[8]{0:T(512)(128)(4,1)} %compare_and_fusion) | copy-start | bytes 28
  158.2 13.1 %all-to-all-start.1 = ((bf16[16,2,4,576]{3,2,1,0:T(4,128)(2,1)}), bf16[16,2,4,576]{3,2,1,0:T(4,128)(2,1)S(1)}, u32[]{:S(2)}, u32[]{:S(2)}) async-start(bf16[16,2,4,576]{3,2,1,0:T(4,128)(2,1)} %bitcast.30), calls=%async_computation.1 | async-start | bytes 327680 | tf_op jit(solution)/shard_map/all_to_all | solution.py:33
Sparse Core Ops, SparseCore 0:
  11.5 36.7 all-reduce.1
  60.4 40.1 reduce-scatter.6
  152.4 20.3 reduce-scatter.8

commit v2 on v1

--- a/solution.py
+++ b/solution.py
@@ -41,6 +41,21 @@
     )
     placing = jnp.argsort(jnp.take(position_mapping_target, arrivals) % slots_dev)
     return jnp.take(arrived, placing, axis=0)
+
+
+def exchange_sum(pieces, axis_name):
+    arrived = lax.all_to_all(pieces, axis_name, split_axis=0, concat_axis=0, tiled=True)
+    return jnp.sum(arrived.astype(jnp.float32), axis=0)
+
+
+def exchange_copies(value, axis_name):
+    count = lax.axis_size(axis_name)
+    copies = jnp.broadcast_to(value[None], (count,) + value.shape)
+    return lax.all_to_all(copies, axis_name, split_axis=0, concat_axis=0, tiled=True)
+
+
+def widen(value):
+    return value.astype(jnp.bfloat16).astype(jnp.float32)
 
 
 def rebuild_kernel(steps, state_ref, terms_ref, out_ref, spread_ref, tile_ref):
@@ -133,7 +148,9 @@
     rows = x_float.shape[0]
     base_mix = (x_float + shifted * lagging_mixture_weights[0]).astype(bf16)
     partial_value = jnp.dot(base_mix, lagging_narrow_lowering, preferred_element_type=f32)
-    hidden = jnp.tanh(lax.psum(partial_value.astype(bf16), "batch").astype(f32)).astype(bf16)
+    hidden = jnp.tanh(
+        jnp.sum(exchange_copies(partial_value.astype(bf16), "batch").astype(f32), axis=0)
+    ).astype(bf16)
     hidden = hidden.reshape(rows, MIX_MAPS, lagging_narrow_raising.shape[1])
     offsets = jnp.einsum(
         "nim,imd->ind", hidden, lagging_narrow_raising, preferred_element_type=f32
@@ -145,20 +162,19 @@
         "inf,ifc->nic", mixed[:4], fourfold_linear_maps, preferred_element_type=f32
     )
     decay_part = jnp.dot(mixed[4], attenuation_narrow_lowering, preferred_element_type=f32)
-    aggregated = lax.psum_scatter(
-        jnp.concatenate([main_part.reshape(rows, -1), decay_part], axis=1).astype(bf16),
+    aggregated = exchange_sum(
+        jnp.concatenate([main_part.reshape(rows, -1), decay_part], axis=1)
+        .astype(bf16)
+        .reshape(batch_count, steps, local_rows, -1),
         "batch",
-        scatter_dimension=0,
-        tiled=True,
-    ).astype(f32)
-    aggregated = aggregated.reshape(steps, local_rows, -1)
+    )
 
     def heads_of(value):
         return value.reshape(steps, local_rows, heads_here, SUBSPACE_EXTENT)
 
-    recept = heads_of(aggregated[..., :width])
-    key_vec = heads_of(aggregated[..., width : 2 * width])
-    valued = heads_of(aggregated[..., 2 * width : 3 * width])
+    recept = heads_of(widen(aggregated[..., :width]))
+    key_vec = heads_of(widen(aggregated[..., width : 2 * width]))
+    valued = heads_of(widen(aggregated[..., 2 * width : 3 * width]))
     gate_act = jax.nn.silu(aggregated[..., 3 * width : 4 * width])
     low_rank = jnp.tanh(aggregated[..., 4 * width :]).astype(bf16)
     decay_rate = heads_of(
@@ -218,7 +234,8 @@
     ) * norming_multiplier + norming_intercept
     combined_response = (standardized * gate_act).astype(bf16)
 
-    gathered = lax.all_gather(combined_response, "batch", axis=1, tiled=True)
+    gathered = exchange_copies(combined_response, "batch").transpose(1, 0, 2, 3)
+    gathered = gathered.reshape(steps, sessions, width)
     inverse = jnp.argsort(position_mapping_target)
     arranged = jnp.concatenate(
         [gathered[:STEPS_A], jnp.take(gathered[STEPS_A:], inverse, axis=1)], axis=0
@@ -226,7 +243,11 @@
     partial_y = jnp.einsum(
         "tnf,fo->tno", arranged, outgoing_linear_map, preferred_element_type=f32
     ).astype(bf16)
-    produced = lax.psum_scatter(partial_y, "head", scatter_dimension=1, tiled=True)
+    head_count = lax.axis_size("head")
+    produced = exchange_sum(
+        partial_y.reshape(steps, head_count, sessions // head_count, -1).transpose(1, 0, 2, 3),
+        "head",
+    ).astype(bf16)
     return (produced[:STEPS_A], produced[STEPS_A:], final_state)
 
 

time: 192 us -> 159 us (0.83)
  waiting for transfers between devices: 59.7 us -> 26.9 us
  starting transfers between devices: 9.42 us -> 29.8 us
  blocking collectives: 17 us -> 0 us
  between operations: 14.4 us -> 1.28 us
  local copies, waits for them, and re-layouts: 44 us -> 52.2 us
    psum x1 -> x0, waiting for transfers between devices: 28 us -> none  [per_device(): lax.psum(partial_value.astype(bf16), 'batch').astype(f32)]
    all_to_all x0 -> x4, starting transfers between devices: none -> 19.5 us  [the longest x2 9.74 us: exchange_sum(): lax.all_to_all(pieces, axis_name, split_axis=0, concat_axis=0, tiled=True)]
    all_to_all x2, waiting for transfers between devices: 31.7 us -> 13.2 us  [route_to_slots(): lax.all_to_all(packed, ('batch', 'head'), split_axis=0, concat_axis=0, ti...]
    all_gather x1 -> x0, blocking collectives: 17 us -> none  [per_device(): gathered = lax.all_gather(combined_response, 'batch', axis=1, tiled=True)]
    all_to_all x0 -> x4, waiting for transfers between devices: none -> 13.7 us  [the longest x2 8.66 us: exchange_sum(): lax.all_to_all(pieces, axis_name, split_axis=0, concat_axis=0, tiled=True)]
    unnamed x50 -> x36, local copies, waits for them, and re-layouts: 6.27 us -> 0.91 us
    mul x6, local copies, waits for them, and re-layouts: 3.49 us -> 0.46 us  [per_device(): recept[t] * factor]
    reshape x3, local copies, waits for them, and re-layouts: 4.11 us -> 6.82 us  [route_to_slots(): packed.reshape(batch_count, cluster_number, per_pair, 4, quarter, width)]
  transfers between devices with their start and end apart: 5 -> 6, of which waited for: 3 -> 4; matrix products, arithmetic and copies ran while one was open for 20% -> 36% of each run, Pallas kernels for 4% -> 5%
where the time goes in v2:
time: 159 us; the launch traced here: 157 us
  local copies, waits for them, and re-layouts  52.2 us (33%)
  starting transfers between devices  29.8 us (19%)
  waiting for transfers between devices  26.9 us (17%)
  other arithmetic  23.1 us (15%)
  matrix products  14.7 us (9%)
  Pallas kernels  8.54 us (5%)
    all_to_all x2, waiting for transfers between devices, route_to_slots(): lax.all_to_all(packed, ('batch', 'head'), split_axis=0, concat_axis=0, ti...  13.2 us
    all_to_all x2, starting transfers between devices, route_to_slots(): lax.all_to_all(packed, ('batch', 'head'), split_axis=0, concat_axis=0, ti...  10.4 us
    all_to_all x2, starting transfers between devices, exchange_sum(): lax.all_to_all(pieces, axis_name, split_axis=0, concat_axis=0, tiled=True)  9.74 us
    all_to_all x2, starting transfers between devices, exchange_copies(): lax.all_to_all(copies, axis_name, split_axis=0, concat_axis=0, tiled=True)  9.73 us
    all_to_all x2, waiting for transfers between devices, exchange_sum(): lax.all_to_all(pieces, axis_name, split_axis=0, concat_axis=0, tiled=True)  8.66 us
    pallas_call x1, Pallas kernels, rebuild_state(): pl.pallas_call(functools.partial(rebuild_kernel, steps), grid=(slots_dev,...  8.54 us
    reshape x3, local copies, waits for them, and re-layouts, route_to_slots(): packed.reshape(batch_count, cluster_number, per_pair, 4, quarter, width)  6.82 us
    dot_general x1, matrix products, per_device(): jnp.einsum('tnhi,nhij->tnhj', query, state, precision=lax.Precision.HIGHEST)  5.34 us
  transfers between devices with their start and end apart: 6, of which 4 were waited for; matrix products, arithmetic and copies ran while one was open for 36% of the time, Pallas kernels for 5%

profile of v2, /device:TPU:0, one launch (start us, length us, event | category | flops | bytes accessed | tf_op | source)
XLA Modules:
  0.0 156.6 jit_solution(5747400579801737663)
XLA Ops:
  0.7 1.2 convert_bitcast_fusion
  1.8 0.9 slice_bitcast_fusion
  3.0 0.8 copy-done.4
  4.2 0.8 broadcast_in_dim.34
  5.0 6.3 %all-to-all-start = ((bf16[4,128,320]{1,2,0:T(8,128)(2,1)}), bf16[4,128,320]{1,2,0:T(8,128)(2,1)S(1)}, u32[]{:S(2)}, u32[]{:S(2)}) async-start(bf16[4,128,320]{1,2,0:T(8,128)(2,1)} %broadcast_in_dim.34), calls=%async_computation | async-start | bytes 655360 | tf_op jit(solution)/shard_map/all_to_all | solution.py:54
  11.4 1.6 %sort.76 = (s32[32]{0:T(128)}, s32[32]{0:T(128)S(1)}) sort(s32[32]{0:T(128)S(1)} %and_select_fusion.2, s32[32]{0:T(128)S(1)} %iota.21), dimensions={0}, to_apply=%region_14.16 | sort | flops 160 | bytes 512 | tf_op jit(solution)/shard_map/jit(argsort)/sort | solution.py:38
  13.1 1.0 sort.75
  14.1 2.7 %convert_element_type.103 = bf16[8,16,4096]{2,1,0:T(8,128)(2,1)} convert(f32[8,16,4096]{2,1,0:T(8,128)} %param.23) | non-fusion elementwise | flops 524288 | bytes 3145728 | tf_op jit(solution)/shard_map/convert_element_type | solution.py:136
  16.8 2.8 %gather_fusion.1 = bf16[8,16,4096]{2,1,0:T(8,128)(2,1)} fusion(bf16[8,16,4096]{2,1,0:T(8,128)(2,1)} %convert_element_type.103, s32[1024]{0:T(1024)S(1)} %pad_clamp_fusion.1), kind=kCustom, calls=%fused_computation.clone | custom fusion | bytes 2097184 | tf_op jit(solution)/shard_map/jit(_take)/gather | solution.py:28
  19.6 2.4 %broadcast_select_fusion.1 = bf16[8,16,4096]{2,1,0:T(8,128)(2,1)} fusion(bf16[8,16,4096]{2,1,0:T(8,128)(2,1)} %gather_fusion.1, pred[8]{0:T(512)(128)(4,1)S(1)} %compare_and_fusion.1), kind=kLoop, calls=%fused_computation.23 | loop fusion | flops 524288 | bytes 2097160 | tf_op jit(solution)/shard_map/jit(_take)/select_n | solution.py:28
  22.0 2.3 %reshape.376 = bf16[4,1,2,4,4,4096]{5,4,3,2,0,1:T(4,128)(2,1)} reshape(bf16[8,16,4096]{2,1,0:T(8,128)(2,1)} %broadcast_select_fusion.1) | data formatting | bytes 2097152 | tf_op jit(solution)/shard_map/reshape | solution.py:29
  24.2 2.8 %copy.130 = bf16[4,1,2,4,4,4096]{5,4,2,3,0,1:T(4,128)(2,1)} copy(bf16[4,1,2,4,4,4096]{5,4,3,2,0,1:T(4,128)(2,1)} %reshape.376) | data formatting | bytes 2097152 | tf_op jit(solution)/shard_map/reshape | solution.py:29
  27.1 6.2 %all-to-all-start.4 = ((bf16[16,2,4,4096]{3,2,1,0:T(4,128)(2,1)}), bf16[16,2,4,4096]{3,2,1,0:T(4,128)(2,1)}, u32[]{:S(2)}, u32[]{:S(2)}) async-start(bf16[16,2,4,4096]{3,2,1,0:T(4,128)(2,1)} %bitcast.98), calls=%async_computation.4 | async-start | bytes 2097152 | tf_op jit(solution)/shard_map/all_to_all | solution.py:33
  33.4 1.7 %add_convert_fusion = bf16[5,128,1024]{2,1,0:T(8,128)(2,1)S(1)} fusion(bf16[128,5,64]{0,2,1:T(8,128)(2,1)S(1)} %bitcast.109, bf16[5,64,1024]{2,1,0:T(8,128)(2,1)} %param.27, f32[5,1024]{1,0:T(8,128)S(1)} %slice.176, f32[128,1024]{1,0:T(8,128)S(1)} %bitcast_subtract_fusion, f32[128,1024]{1,0:T(8,128)S(1)} %bitcast.97), kind=kOutput, calls=%fused_computation.6 | convolution fusion | flops 86507520 | bytes 3117056 | tf_op jit(solution)/shard_map/nim,imd->ind/dot_general | solution.py:155
  35.1 4.8 %fusion.2 = bf16[128,4,1024]{2,0,1:T(8,128)(2,1)S(1)} fusion(bf16[5,128,1024]{2,1,0:T(8,128)(2,1)S(1)} %add_convert_fusion, bf16[4,1024,1024]{2,1,0:T(8,128)(2,1)} %param.28), kind=kOutput, calls=%fused_computation.11 | convolution fusion | flops 1074266112 | bytes 10747904 | tf_op jit(solution)/shard_map/inf,ifc->nic/dot_general | solution.py:161
  40.0 1.8 %copy.120 = bf16[128,4,1024]{2,1,0:T(4,128)(2,1)} copy(bf16[128,4,1024]{2,0,1:T(8,128)(2,1)S(1)} %fusion.2) | data formatting | bytes 2097152 | tf_op jit(solution)/shard_map/inf,ifc->nic/transpose | solution.py:161
  41.8 1.8 %concatenate.26 = bf16[4,4,8,4096]{3,2,1,0:T(8,128)(2,1)S(1)} reshape(bf16[128,4,1024]{2,1,0:T(4,128)(2,1)} %copy.120) | data formatting | bytes 2097152 | tf_op jit(solution)/shard_map/concatenate | solution.py:166
  43.6 1.2 convolution_convert_fusion.2
  44.8 1.1 pad_maximum_fusion
  45.8 10.5 %all-to-all-done.4 = bf16[16,2,4,4096]{3,2,1,0:T(4,128)(2,1)} async-done(((bf16[16,2,4,4096]{3,2,1,0:T(4,128)(2,1)}), bf16[16,2,4,4096]{3,2,1,0:T(4,128)(2,1)}, u32[]{:S(2)}, u32[]{:S(2)}) %all-to-all-start.4) | async-done | bytes 1048608 | tf_op jit(solution)/shard_map/all_to_all | solution.py:33
  56.3 6.3 %all-to-all-start.1 = ((bf16[4,4,8,4224]{3,2,1,0:T(8,128)(2,1)}), bf16[4,4,8,4224]{3,2,1,0:T(8,128)(2,1)S(1)}, u32[]{:S(2)}, u32[]{:S(2)}) async-start(bf16[4,4,8,4224]{3,2,1,0:T(8,128)(2,1)} %pad_maximum_fusion), calls=%async_computation.1 | async-start | bytes 2162688 | tf_op jit(solution)/shard_map/all_to_all | solution.py:47
  62.6 4.6 %reshape.374 = f32[8,16,64,64]{3,2,1,0:T(8,128)} reshape(f32[8,16,4096]{2,1,0:T(8,128)} %param.23) | data formatting | bytes 4194304 | tf_op jit(solution)/shard_map/reshape | solution.py:196
  67.3 1.6 %sort.74 = (s32[32]{0:T(128)}, s32[32]{0:T(128)S(1)}) sort(s32[32]{0:T(128)S(1)} %copy-done.1, s32[32]{0:T(128)S(1)} %iota.19), dimensions={0}, to_apply=%region_11.12 | sort | flops 160 | bytes 512 | tf_op jit(solution)/shard_map/jit(argsort)/sort | solution.py:239
  69.6 1.0 sort.77
  72.4 2.9 %copy.145 = bf16[4,4,2,4,4096]{4,3,1,2,0:T(4,128)(2,1)} copy(bf16[4,4,2,4,4096]{4,3,2,1,0:T(4,128)(2,1)} %bitcast.32) | data formatting | bytes 2097152 | tf_op jit(solution)/shard_map/reshape | solution.py:34
  75.2 2.2 %reshape.379 = bf16[8,16,4096]{2,1,0:T(8,128)(2,1)} reshape(bf16[4,2,4,4,4096]{4,3,2,1,0:T(4,128)(2,1)} %bitcast.99) | data formatting | bytes 2097152 | tf_op jit(solution)/shard_map/reshape | solution.py:35
  77.4 2.9 %gather_fusion.3 = bf16[8,16,4096]{2,1,0:T(8,128)(2,1)} fusion(bf16[8,16,4096]{2,1,0:T(8,128)(2,1)} %reshape.379, s32[1024]{0:T(1024)S(1)} %pad_clamp_fusion), kind=kCustom, calls=%fused_computation.3.clone | custom fusion | bytes 2097184 | tf_op jit(solution)/shard_map/jit(_take)/gather | solution.py:43
  80.3 8.7 %all-to-all-done.1 = bf16[4,4,8,4224]{3,2,1,0:T(8,128)(2,1)S(1)} async-done(((bf16[4,4,8,4224]{3,2,1,0:T(8,128)(2,1)}), bf16[4,4,8,4224]{3,2,1,0:T(8,128)(2,1)S(1)}, u32[]{:S(2)}, u32[]{:S(2)}) %all-to-all-start.1) | async-done | bytes 1081376 | tf_op jit(solution)/shard_map/all_to_all | solution.py:47
  89.2 0.7 slice.234
  89.9 0.9 fusion.11
  94.1 0.8 mul.426
  95.1 0.8 slice.186
  95.9 5.3 %fusion.12 = f32[8,16,4,64]{3,2,1,0:T(4,128)S(1)} fusion(f32[8,16,64,64]{3,2,1,0:T(8,128)} %reshape.374, f32[1,8,16,64]{3,0,2,1:T(1,128)S(1)} %bitcast.110, f32[1,8,16,64]{3,0,2,1:T(1,128)S(1)} %bitcast.111, f32[1,8,16,64]{3,0,2,1:T(1,128)S(1)} %bitcast.112, f32[1,8,16,64]{3,0,2,1:T(1,128)S(1)} %bitcast.113), kind=kOutput, calls=%fused_computation.30 | convolution fusion | flops 25264128 | bytes 2359296 | tf_op jit(solution)/shard_map/tnhi,nhij->tnhj/dot_general | solution.py:199
  103.3 0.9 multiply_reduce_fusion
  104.5 0.8 mul.479
  105.3 0.8 squeeze.27
  106.1 0.8 squeeze.28
  106.9 0.8 squeeze.29
  107.7 0.8 squeeze.30
  108.6 0.8 squeeze.31
  109.5 0.7 gather_fusion.4
  110.2 1.4 broadcast_select_fusion.3
  111.6 1.7 %reshape.380 = bf16[4,1,2,4,4,576]{5,4,3,2,0,1:T(4,128)(2,1)} reshape(bf16[8,16,576]{2,1,0:T(8,128)(2,1)} %broadcast_select_fusion.3) | data formatting | bytes 294912 | tf_op jit(solution)/shard_map/reshape | solution.py:29
  113.3 1.6 %copy.132 = bf16[4,4,1,2,4,576]{5,4,3,1,0,2:T(4,128)(2,1)} copy(bf16[4,4,1,2,4,576]{5,4,1,3,0,2:T(4,128)(2,1)} %bitcast.105) | data formatting | bytes 294912 | tf_op jit(solution)/shard_map/transpose | solution.py:30
  114.9 4.2 %all-to-all-start.5 = ((bf16[16,2,4,576]{3,2,1,0:T(4,128)(2,1)}), bf16[16,2,4,576]{3,2,1,0:T(4,128)(2,1)}, u32[]{:S(2)}, u32[]{:S(2)}) async-start(bf16[16,2,4,576]{3,2,1,0:T(4,128)(2,1)} %bitcast.104), calls=%async_computation.5 | async-start | bytes 327680 | tf_op jit(solution)/shard_map/all_to_all | solution.py:33
  119.1 0.7 add_rsqrt_fusion
  119.8 0.7 stack.27
  120.5 0.7 stack.26
  121.2 0.7 stack.25
  121.9 0.7 stack.24
  123.0 0.8 sub.35
  123.8 1.1 fusion.31
  124.8 2.7 %all-to-all-done.5 = bf16[16,2,4,576]{3,2,1,0:T(4,128)(2,1)} async-done(((bf16[16,2,4,576]{3,2,1,0:T(4,128)(2,1)}), bf16[16,2,4,576]{3,2,1,0:T(4,128)(2,1)}, u32[]{:S(2)}, u32[]{:S(2)}) %all-to-all-start.5) | async-done | bytes 147488 | tf_op jit(solution)/shard_map/all_to_all | solution.py:33
  127.6 0.7 broadcast_in_dim.35
  128.3 3.4 %all-to-all-start.2 = ((bf16[4,4,8,1024]{3,2,1,0:T(8,128)(2,1)}), bf16[4,4,8,1024]{3,2,1,0:T(8,128)(2,1)S(1)}, u32[]{:S(2)}, u32[]{:S(2)}) async-start(bf16[4,4,8,1024]{3,2,1,0:T(8,128)(2,1)} %broadcast_in_dim.35), calls=%async_computation.2 | async-start | bytes 524288 | tf_op jit(solution)/shard_map/all_to_all | solution.py:54
  131.7 1.8 %broadcast_select_fusion.state_ref = bf16[8,16,4096]{2,1,0:T(8,128)(2,1)} fusion(bf16[8,16,4096]{2,1,0:T(8,128)(2,1)S(1)} %copy-done.2, pred[8]{0:T(512)(128)(4,1)} %compare_and_fusion), kind=kLoop, calls=%fused_computation.22 | loop fusion | flops 524288 | bytes 2097160 | tf_op jit(solution)/shard_map/jit(_take)/select_n | solution.py:43
  133.5 1.0 copy.149
  134.6 0.7 gather_fusion.5
  135.3 5.0 %all-to-all-done.2 = bf16[4,4,8,1024]{3,2,1,0:T(8,128)(2,1)S(1)} async-done(((bf16[4,4,8,1024]{3,2,1,0:T(8,128)(2,1)}), bf16[4,4,8,1024]{3,2,1,0:T(8,128)(2,1)S(1)}, u32[]{:S(2)}, u32[]{:S(2)}) %all-to-all-start.2) | async-done | bytes 262176 | tf_op jit(solution)/shard_map/all_to_all | solution.py:54
  140.5 0.9 gather_fusion
  142.0 0.7 copy.147
  142.8 3.4 %all-to-all-start.3 = ((bf16[4,4,8,1024]{3,2,1,0:T(8,128)(2,1)}), bf16[4,4,8,1024]{3,2,1,0:T(8,128)(2,1)S(1)}, u32[]{:S(2)}, u32[]{:S(2)}) async-start(bf16[4,4,8,1024]{3,2,1,0:T(8,128)(2,1)} %bitcast.92), calls=%async_computation.3 | async-start | bytes 524288 | tf_op jit(solution)/shard_map/all_to_all | solution.py:47
  146.5 0.8 copy.146
  147.4 8.5 %shard_map.166 = f32[8,16,4096]{2,1,0:T(8,128)} custom-call(bf16[8,16,4096]{2,1,0:T(8,128)(2,1)} %broadcast_select_fusion.state_ref, bf16[8,9,16,64]{3,2,1,0:T(8,128)(2,1)} %bitcast.100), custom_call_target="tpu_custom_call" | custom-call | flops 603979776 | bytes 3293184 | tf_op jit(solution)/shard_map/pallas_call | solution.py:87
  (118 shorter events, 11.5 us)
Async XLA Ops:
  0.6 140.9 %copy-start = (bf16[1024,1024]{1,0:T(8,128)(2,1)S(1)}, bf16[1024,1024]{1,0:T(8,128)(2,1)}, u32[]{:S(2)}) copy-start(bf16[1024,1024]{1,0:T(8,128)(2,1)} %param.35) | copy-start | bytes 6291460
  0.6 2.2 %copy-start.7 = (bf16[32,1024]{1,0:T(8,128)(2,1)S(1)}, bf16[32,1024]{1,0:T(8,128)(2,1)}, u32[]{:S(2)}) copy-start(bf16[32,1024]{1,0:T(8,128)(2,1)} %param.22) | copy-start | bytes 196612
  2.8 1.1 copy-start.4
  2.8 1.1 slice-start
  3.0 8.4 %copy-start.11 = (f32[6,1024]{1,0:T(8,128)S(1)}, f32[6,1024]{1,0:T(8,128)}, u32[]{:S(2)}) copy-start(f32[6,1024]{1,0:T(8,128)} %param.25) | copy-start | bytes 73732
  3.0 8.4 %copy-start.1 = (s32[32]{0:T(128)S(1)}, s32[32]{0:T(128)}, u32[]{:S(2)}) copy-start(s32[32]{0:T(128)} %param.24) | copy-start | bytes 388
  5.0 22.1 %all-to-all-start = ((bf16[4,128,320]{1,2,0:T(8,128)(2,1)}), bf16[4,128,320]{1,2,0:T(8,128)(2,1)S(1)}, u32[]{:S(2)}, u32[]{:S(2)}) async-start(bf16[4,128,320]{1,2,0:T(8,128)(2,1)} %broadcast_in_dim.34), calls=%async_computation | async-start | bytes 655360 | tf_op jit(solution)/shard_map/all_to_all | solution.py:54
  14.1 5.5 %copy-start.16 = (pred[8]{0:T(512)(128)(4,1)}, pred[8]{0:T(512)(128)(4,1)S(1)}, u32[]{:S(2)}) copy-start(pred[8]{0:T(512)(128)(4,1)S(1)} %compare_and_fusion.1) | copy-start | bytes 28
  16.8 7.5 %copy-start.12 = (s32[1024]{0:T(1024)}, s32[1024]{0:T(1024)S(1)}, u32[]{:S(2)}) copy-start(s32[1024]{0:T(1024)S(1)} %pad_clamp_fusion.1) | copy-start | bytes 12292
  27.1 29.2 %all-to-all-start.4 = ((bf16[16,2,4,4096]{3,2,1,0:T(4,128)(2,1)}), bf16[16,2,4,4096]{3,2,1,0:T(4,128)(2,1)}, u32[]{:S(2)}, u32[]{:S(2)}) async-start(bf16[16,2,4,4096]{3,2,1,0:T(4,128)(2,1)} %bitcast.98), calls=%async_computation.4 | async-start | bytes 2097152 | tf_op jit(solution)/shard_map/all_to_all | solution.py:33
  56.3 32.6 %all-to-all-start.1 = ((bf16[4,4,8,4224]{3,2,1,0:T(8,128)(2,1)}), bf16[4,4,8,4224]{3,2,1,0:T(8,128)(2,1)S(1)}, u32[]{:S(2)}, u32[]{:S(2)}) async-start(bf16[4,4,8,4224]{3,2,1,0:T(8,128)(2,1)} %pad_maximum_fusion), calls=%async_computation.1 | async-start | bytes 2162688 | tf_op jit(solution)/shard_map/all_to_all | solution.py:47
  62.6 4.6 %copy-start.14 = (f32[1024]{0:T(1024)S(1)}, f32[1024]{0:T(1024)}, u32[]{:S(2)}) copy-start(f32[1024]{0:T(1024)} %param.32) | copy-start | bytes 12292
  71.2 9.1 %copy-start.13 = (s32[1024]{0:T(1024)}, s32[1024]{0:T(1024)S(1)}, u32[]{:S(2)}) copy-start(s32[1024]{0:T(1024)S(1)} %pad_clamp_fusion) | copy-start | bytes 12292
  77.4 12.5 %copy-start.5 = (bf16[128,1024]{1,0:T(8,128)(2,1)S(1)}, bf16[128,1024]{1,0:T(8,128)(2,1)}, u32[]{:S(2)}) copy-start(bf16[128,1024]{1,0:T(8,128)(2,1)} %param.30) | copy-start | bytes 786436
  89.1 0.8 copy-start.3
  101.3 1.3 copy-start.6
  101.3 2.9 %copy-start.8 = (bf16[1,8,1024]{2,1,0:T(8,128)(2,1)S(1)}, bf16[1,8,1024]{2,1,0:T(8,128)(2,1)}, u32[]{:S(2)}) copy-start(bf16[1,8,1024]{2,1,0:T(8,128)(2,1)} %get-tuple-element.42) | copy-start | bytes 49156
  101.3 3.0 %copy-start.10 = (bf16[1,8,1024]{2,1,0:T(8,128)(2,1)S(1)}, bf16[1,8,1024]{2,1,0:T(8,128)(2,1)}, u32[]{:S(2)}) copy-start(bf16[1,8,1024]{2,1,0:T(8,128)(2,1)} %get-tuple-element.25) | copy-start | bytes 49156
  101.3 3.1 %copy-start.9 = (bf16[1,8,1024]{2,1,0:T(8,128)(2,1)S(1)}, bf16[1,8,1024]{2,1,0:T(8,128)(2,1)}, u32[]{:S(2)}) copy-start(bf16[1,8,1024]{2,1,0:T(8,128)(2,1)} %get-tuple-element.26) | copy-start | bytes 49156
  111.6 20.1 %copy-start.2 = (bf16[8,16,4096]{2,1,0:T(8,128)(2,1)S(1)}, bf16[8,16,4096]{2,1,0:T(8,128)(2,1)}, u32[]{:S(2)}) copy-start(bf16[8,16,4096]{2,1,0:T(8,128)(2,1)} %gather_fusion.3) | copy-start | bytes 3145732
  114.9 12.6 %all-to-all-start.5 = ((bf16[16,2,4,576]{3,2,1,0:T(4,128)(2,1)}), bf16[16,2,4,576]{3,2,1,0:T(4,128)(2,1)}, u32[]{:S(2)}, u32[]{:S(2)}) async-start(bf16[16,2,4,576]{3,2,1,0:T(4,128)(2,1)} %bitcast.104), calls=%async_computation.5 | async-start | bytes 327680 | tf_op jit(solution)/shard_map/all_to_all | solution.py:33
  128.3 12.0 %all-to-all-start.2 = ((bf16[4,4,8,1024]{3,2,1,0:T(8,128)(2,1)}), bf16[4,4,8,1024]{3,2,1,0:T(8,128)(2,1)S(1)}, u32[]{:S(2)}, u32[]{:S(2)}) async-start(bf16[4,4,8,1024]{3,2,1,0:T(8,128)(2,1)} %broadcast_in_dim.35), calls=%async_computation.2 | async-start | bytes 524288 | tf_op jit(solution)/shard_map/all_to_all | solution.py:54
  131.7 9.8 %copy-start.17 = (pred[32]{0:T(512)(128)(4,1)S(1)}, pred[32]{0:T(512)(128)(4,1)}, u32[]{:S(2)}) copy-start(pred[32]{0:T(512)(128)(4,1)} %compare_and_fusion.2) | copy-start | bytes 100
  140.5 5.7 %copy-start.15 = (pred[8]{0:T(512)(128)(4,1)S(1)}, pred[8]{0:T(512)(128)(4,1)}, u32[]{:S(2)}) copy-start(pred[8]{0:T(512)(128)(4,1)} %compare_and_fusion) | copy-start | bytes 28
  142.8 13.1 %all-to-all-start.3 = ((bf16[4,4,8,1024]{3,2,1,0:T(8,128)(2,1)}), bf16[4,4,8,1024]{3,2,1,0:T(8,128)(2,1)S(1)}, u32[]{:S(2)}, u32[]{:S(2)}) async-start(bf16[4,4,8,1024]{3,2,1,0:T(8,128)(2,1)} %bitcast.92), calls=%async_computation.3 | async-start | bytes 524288 | tf_op jit(solution)/shard_map/all_to_all | solution.py:47

commit v3 on v2

--- a/solution.py
+++ b/solution.py
@@ -25,23 +25,41 @@
         position_mapping_target, batch_index * local_rows, local_rows
     )
     send_order = jnp.argsort(own_map // slots_dev, stable=True)
-    packed = jnp.take(value, send_order, axis=0)
-    packed = packed.reshape(batch_count, cluster_number, per_pair, 4, quarter, width)
-    packed = packed.transpose(0, 3, 1, 2, 4, 5).reshape(
-        batch_count * head_count, per_pair, quarter, width
-    )
+    dest = jnp.arange(batch_count * head_count, dtype=jnp.int32)
+    dest_block = (dest // head_count) * cluster_number + dest % cluster_number
+    quad = (dest % head_count) // cluster_number
+    pair = jnp.arange(per_pair, dtype=jnp.int32)
+    within = jnp.arange(quarter, dtype=jnp.int32)
+    sent_sessions = jnp.take(
+        send_order, dest_block[:, None] * per_pair + pair[None, :], mode="clip"
+    )
+    sent_rows = (
+        sent_sessions[:, :, None] * heads_here
+        + (quad * quarter)[:, None, None]
+        + within[None, None, :]
+    )
+    packed = jnp.take(
+        value.reshape(local_rows * heads_here, width), sent_rows.reshape(-1), axis=0, mode="clip"
+    ).reshape(batch_count * head_count, per_pair * quarter, width)
     arrived = lax.all_to_all(packed, ("batch", "head"), split_axis=0, concat_axis=0, tiled=True)
-    arrived = arrived.reshape(batch_count, head_count, per_pair, quarter, width)
-    arrived = arrived.transpose(0, 2, 1, 3, 4).reshape(slots_dev, head_count * quarter, width)
     target = batch_index * cluster_number + head_index % cluster_number
     arrivals = lax.dynamic_slice_in_dim(
         jnp.argsort(position_mapping_target // slots_dev, stable=True),
         target * slots_dev,
         slots_dev,
     )
-    placing = jnp.argsort(jnp.take(position_mapping_target, arrivals) % slots_dev)
-    return jnp.take(arrived, placing, axis=0)
-
+    placing = jnp.argsort(jnp.take(position_mapping_target, arrivals, mode="clip") % slots_dev)
+    source_head = jnp.arange(head_count, dtype=jnp.int32)
+    kept_rows = (
+        (
+            (placing[:, None, None] // per_pair) * head_count + source_head[None, :, None]
+        )
+        * per_pair
+        + placing[:, None, None] % per_pair
+    ) * quarter + within[None, None, :]
+    return jnp.take(
+        arrived.reshape(-1, width), kept_rows.reshape(-1), axis=0, mode="clip"
+    ).reshape(slots_dev, head_count * quarter, width)
 
 def exchange_sum(pieces, axis_name):
     arrived = lax.all_to_all(pieces, axis_name, split_axis=0, concat_axis=0, tiled=True)
@@ -238,7 +256,7 @@
     gathered = gathered.reshape(steps, sessions, width)
     inverse = jnp.argsort(position_mapping_target)
     arranged = jnp.concatenate(
-        [gathered[:STEPS_A], jnp.take(gathered[STEPS_A:], inverse, axis=1)], axis=0
+        [gathered[:STEPS_A], jnp.take(gathered[STEPS_A:], inverse, axis=1, mode="clip")], axis=0
     )
     partial_y = jnp.einsum(
         "tnf,fo->tno", arranged, outgoing_linear_map, preferred_element_type=f32

time: 159 us -> 166 us (1.044)
  local copies, waits for them, and re-layouts: 52.2 us -> 63.1 us
  waiting for transfers between devices: 26.9 us -> 22.5 us
    reshape x9 -> x0, local copies, waits for them, and re-layouts: 14 us -> none  [the longest x3 6.82 us: route_to_slots(): packed.reshape(batch_count, cluster_number, per_pair, 4, quarter, width)]
    all_to_all x2, waiting for transfers between devices: 13.2 us -> 2.17 us  [route_to_slots(): lax.all_to_all(packed, ('batch', 'head'), split_axis=0, concat_axis=0, ti...]
    all_to_all x2, waiting for transfers between devices: 8.66 us -> 18.4 us  [exchange_sum(): lax.all_to_all(pieces, axis_name, split_axis=0, concat_axis=0, tiled=True)]
    select_n x10 -> x2, other arithmetic: 5.81 us -> 0.1 us  [the longest x1 0.09 us: route_to_slots(): send_order = jnp.argsort(own_map // slots_dev, stable=True)]
    mul x6, local copies, waits for them, and re-layouts: 0.46 us -> 5.62 us  [per_device(): recept[t] * factor]
    mul x3, local copies, waits for them, and re-layouts: 0.99 us -> 4.37 us  [per_device(): query = jnp.stack([recept[t] * prefix[t] for t in range(steps)])]
    all_to_all x2, waiting for transfers between devices: 5.03 us -> 1.92 us  [exchange_copies(): lax.all_to_all(copies, axis_name, split_axis=0, concat_axis=0, tiled=True)]
    slice x2, local copies, waits for them, and re-layouts: 0.03 us -> 2.56 us  [per_device(): gathered[:STEPS_A]]
  transfers between devices with their start and end apart: 6 -> 6, of which waited for: 4 -> 3; matrix products, arithmetic and copies ran while one was open for 36% -> 49% of each run, Pallas kernels for 5% -> 5%
where the time goes in v3:
time: 166 us; the launch traced here: 163 us
  local copies, waits for them, and re-layouts  63.1 us (38%)
  starting transfers between devices  29.5 us (18%)
  waiting for transfers between devices  22.5 us (14%)
  other arithmetic  22.3 us (13%)
  matrix products  15.7 us (9%)
  Pallas kernels  8.54 us (5%)
    all_to_all x2, waiting for transfers between devices, exchange_sum(): lax.all_to_all(pieces, axis_name, split_axis=0, concat_axis=0, tiled=True)  18.4 us
    all_to_all x2, starting transfers between devices, exchange_copies(): lax.all_to_all(copies, axis_name, split_axis=0, concat_axis=0, tiled=True)  11.2 us
    all_to_all x2, starting transfers between devices, route_to_slots(): lax.all_to_all(packed, ('batch', 'head'), split_axis=0, concat_axis=0, ti...  9.97 us
    pallas_call x1, Pallas kernels, rebuild_state(): pl.pallas_call(functools.partial(rebuild_kernel, steps), grid=(slots_dev,...  8.54 us
    all_to_all x2, starting transfers between devices, exchange_sum(): lax.all_to_all(pieces, axis_name, split_axis=0, concat_axis=0, tiled=True)  8.28 us
    dot_general x1, matrix products, per_device(): jnp.einsum('tnhi,nhij->tnhj', query, state, precision=lax.Precision.HIGHEST)  6.68 us
    mul x6, local copies, waits for them, and re-layouts, per_device(): recept[t] * factor  5.62 us
    squeeze x4, local copies, waits for them, and re-layouts, per_device(): total = bonus_term[t][..., None] * valued[t] + from_state[t]  5.19 us
  transfers between devices with their start and end apart: 6, of which 3 were waited for; matrix products, arithmetic and copies ran while one was open for 49% of the time, Pallas kernels for 5%

profile of v3, /device:TPU:0, one launch (start us, length us, event | category | flops | bytes accessed | tf_op | source)
XLA Modules:
  0.0 162.8 jit_solution(17074158766200899296)
XLA Ops:
  0.7 1.2 convert_bitcast_fusion
  1.8 0.9 slice_bitcast_fusion
  3.0 1.1 copy-done.7
  5.3 6.3 %all-to-all-start = ((bf16[4,128,320]{1,2,0:T(8,128)(2,1)}), bf16[4,128,320]{1,2,0:T(8,128)(2,1)S(1)}, u32[]{:S(2)}, u32[]{:S(2)}) async-start(bf16[4,128,320]{1,2,0:T(8,128)(2,1)} %broadcast_in_dim.20), calls=%async_computation | async-start | bytes 655360 | tf_op jit(solution)/shard_map/all_to_all | solution.py:72
  11.6 4.6 %reshape.581 = f32[8,16,64,64]{3,2,1,0:T(8,128)} reshape(f32[8,16,4096]{2,1,0:T(8,128)} %param.17) | data formatting | bytes 4194304 | tf_op jit(solution)/shard_map/reshape | solution.py:214
  16.2 1.7 %convert_element_type.104 = bf16[8,16,4096]{2,1,0:T(8,128)(2,1)S(1)} convert(f32[8,16,4096]{2,1,0:T(8,128)} %param.17) | non-fusion elementwise | flops 524288 | bytes 3145728 | tf_op jit(solution)/shard_map/convert_element_type | solution.py:154
  18.3 1.0 sort.75
  20.0 1.9 %all-to-all-done = bf16[4,128,320]{1,2,0:T(8,128)(2,1)S(1)} async-done(((bf16[4,128,320]{1,2,0:T(8,128)(2,1)}), bf16[4,128,320]{1,2,0:T(8,128)(2,1)S(1)}, u32[]{:S(2)}, u32[]{:S(2)}) %all-to-all-start) | async-done | bytes 327712 | tf_op jit(solution)/shard_map/all_to_all | solution.py:72
  22.0 2.0 %add_convert_fusion = bf16[5,128,1024]{2,1,0:T(8,128)(2,1)S(1)} fusion(bf16[128,5,64]{0,2,1:T(8,128)(2,1)S(1)} %bitcast.106, bf16[5,64,1024]{2,1,0:T(8,128)(2,1)} %param.21, f32[5,1024]{1,0:T(8,128)S(1)} %slice.176, f32[128,1024]{1,0:T(8,128)} %copy-done.3, f32[128,1024]{1,0:T(8,128)} %bitcast.96), kind=kOutput, calls=%fused_computation.7 | convolution fusion | flops 86507520 | bytes 3117056 | tf_op jit(solution)/shard_map/nim,imd->ind/dot_general | solution.py:173
  24.0 4.9 %fusion.2 = bf16[128,4,1024]{2,0,1:T(8,128)(2,1)S(1)} fusion(bf16[5,128,1024]{2,1,0:T(8,128)(2,1)S(1)} %add_convert_fusion, bf16[4,1024,1024]{2,1,0:T(8,128)(2,1)} %param.22), kind=kOutput, calls=%fused_computation.12 | convolution fusion | flops 1074266112 | bytes 10747904 | tf_op jit(solution)/shard_map/inf,ifc->nic/dot_general | solution.py:179
  28.9 1.8 %copy.86 = bf16[128,4,1024]{2,1,0:T(4,128)(2,1)} copy(bf16[128,4,1024]{2,0,1:T(8,128)(2,1)S(1)} %fusion.2) | data formatting | bytes 2097152 | tf_op jit(solution)/shard_map/inf,ifc->nic/transpose | solution.py:179
  30.7 2.6 %concatenate.37 = bf16[4,4,8,4096]{3,2,1,0:T(8,128)(2,1)} reshape(bf16[128,4,1024]{2,1,0:T(4,128)(2,1)} %copy.86) | data formatting | bytes 2097152 | tf_op jit(solution)/shard_map/concatenate | solution.py:184
  33.3 1.2 convolution_convert_fusion.2
  34.4 2.3 %pad_maximum_fusion = bf16[4,4,8,4224]{3,2,1,0:T(8,128)(2,1)} fusion(bf16[4,4,8,128]{3,2,1,0:T(8,128)(2,1)S(1)} %convolution_convert_fusion.2, bf16[4,4,8,4096]{3,2,1,0:T(8,128)(2,1)} %concatenate.37), kind=kLoop, calls=%fused_computation.21 | loop fusion | flops 2162688 | bytes 2162688 | tf_op jit(solution)/shard_map/concatenate | solution.py:184
  36.7 4.2 %all-to-all-start.1 = ((bf16[4,4,8,4224]{3,2,1,0:T(8,128)(2,1)}), bf16[4,4,8,4224]{3,2,1,0:T(8,128)(2,1)}, u32[]{:S(2)}, u32[]{:S(2)}) async-start(bf16[4,4,8,4224]{3,2,1,0:T(8,128)(2,1)} %pad_maximum_fusion), calls=%async_computation.1 | async-start | bytes 2162688 | tf_op jit(solution)/shard_map/all_to_all | solution.py:65
  41.4 1.6 sort.76
  43.7 2.2 %gather_fusion.2 = bf16[128,4096]{1,0:T(8,128)(2,1)} fusion(bf16[128,4096]{1,0:T(8,128)(2,1)S(1)} %bitcast.92, s32[1024]{0:T(1024)S(1)} %pad_clamp_fusion.2), kind=kCustom, calls=%fused_computation.2 | custom fusion | bytes 2097664 | tf_op jit(solution)/shard_map/jit(_take)/gather | solution.py:41
  46.0 1.0 sort.77
  47.5 18.4 %all-to-all-done.1 = bf16[4,4,8,4224]{3,2,1,0:T(8,128)(2,1)} async-done(((bf16[4,4,8,4224]{3,2,1,0:T(8,128)(2,1)}), bf16[4,4,8,4224]{3,2,1,0:T(8,128)(2,1)}, u32[]{:S(2)}, u32[]{:S(2)}) %all-to-all-start.1) | async-done | bytes 1081376 | tf_op jit(solution)/shard_map/all_to_all | solution.py:65
  65.9 3.9 %all-to-all-start.4 = ((bf16[16,8,4096]{2,1,0:T(8,128)(2,1)}), bf16[16,8,4096]{2,1,0:T(8,128)(2,1)S(1)}, u32[]{:S(2)}, u32[]{:S(2)}) async-start(bf16[16,8,4096]{2,1,0:T(8,128)(2,1)} %bitcast.97), calls=%async_computation.4 | async-start | bytes 2097152 | tf_op jit(solution)/shard_map/all_to_all | solution.py:44
  69.8 1.5 convert_reduce_fusion
  73.6 1.5 mul.487
  75.1 1.5 mul.484
  76.5 1.5 mul.481
  78.0 1.5 slice.186
  79.5 6.7 %fusion.12 = f32[8,16,4,64]{3,2,1,0:T(4,128)} fusion(f32[8,16,64,64]{3,2,1,0:T(8,128)} %reshape.581, f32[1,8,16,64]{3,0,2,1:T(1,128)} %bitcast.107, f32[1,8,16,64]{3,0,2,1:T(1,128)} %bitcast.108, f32[1,8,16,64]{3,0,2,1:T(1,128)} %bitcast.109, f32[1,8,16,64]{3,0,2,1:T(1,128)} %bitcast.110), kind=kOutput, calls=%fused_computation.28 | convolution fusion | flops 25264128 | bytes 2359296 | tf_op jit(solution)/shard_map/tnhi,nhij->tnhj/dot_general | solution.py:217
  87.0 0.8 reshape.579
  87.8 1.7 %copy.105 = f32[8,16,4,64]{3,1,0,2:T(8,128)} copy(f32[8,16,4,64]{3,2,1,0:T(4,128)} %fusion.12) | data formatting | bytes 262144 | tf_op jit(solution)/shard_map/tnhi,nhij->tnhj/dot_general | solution.py:217
  89.4 1.4 fusion.48
  90.9 1.4 squeeze.9
  92.3 1.5 squeeze.8
  93.8 1.5 squeeze.10
  95.2 1.4 mul.504
  97.4 0.8 mul.500
  98.2 0.9 reduce_sum.116
  99.2 0.8 mul.521
  100.2 0.8 mul.517
  101.1 0.8 mul.512
  102.0 0.8 squeeze.11
  102.9 0.8 mul.492
  103.8 1.2 multiply_reduce_fusion.1
  105.0 1.3 fusion.36
  110.7 0.8 sub.46
  112.4 1.2 fusion.31
  114.3 4.9 %all-to-all-start.2 = ((bf16[4,4,8,1024]{3,2,1,0:T(8,128)(2,1)}), bf16[4,4,8,1024]{3,2,1,0:T(8,128)(2,1)}, u32[]{:S(2)}, u32[]{:S(2)}) async-start(bf16[4,4,8,1024]{3,2,1,0:T(8,128)(2,1)} %broadcast_in_dim.21), calls=%async_computation.2 | async-start | bytes 524288 | tf_op jit(solution)/shard_map/all_to_all | solution.py:72
  119.9 1.6 sort.74
  122.2 0.8 mul.540
  123.0 0.8 mul.542
  123.9 0.8 mul.544
  124.7 1.4 mul.546
  127.2 0.9 concatenate.45
  128.1 1.5 gather_fusion.5
  129.7 6.1 %all-to-all-start.5 = ((bf16[16,8,576]{2,1,0:T(8,128)(2,1)}), bf16[16,8,576]{2,1,0:T(8,128)(2,1)S(1)}, u32[]{:S(2)}, u32[]{:S(2)}) async-start(bf16[16,8,576]{2,1,0:T(8,128)(2,1)} %bitcast.34), calls=%async_computation.5 | async-start | bytes 327680 | tf_op jit(solution)/shard_map/all_to_all | solution.py:44
  135.8 1.6 %fusion.46 = (bf16[2,4,8,1024]{3,2,0,1:T(8,128)(2,1)}, bf16[2,4,8,1024]{3,2,0,1:T(8,128)(2,1)S(1)}) fusion(bf16[4,4,8,1024]{3,2,0,1:T(8,128)(2,1)} %bitcast.23), kind=kLoop, calls=%fused_computation.139 | loop fusion | bytes 524288 | tf_op jit(solution)/shard_map/slice | solution.py:259
  137.6 1.4 gather_fusion
  139.0 0.9 copy.106
  139.9 0.9 copy.107
  142.1 2.2 %all-to-all-done.5 = bf16[16,8,576]{2,1,0:T(8,128)(2,1)S(1)} async-done(((bf16[16,8,576]{2,1,0:T(8,128)(2,1)}), bf16[16,8,576]{2,1,0:T(8,128)(2,1)S(1)}, u32[]{:S(2)}, u32[]{:S(2)}) %all-to-all-start.5) | async-done | bytes 147488 | tf_op jit(solution)/shard_map/all_to_all | solution.py:44
  144.2 4.0 %all-to-all-start.3 = ((bf16[4,4,8,1024]{3,2,1,0:T(8,128)(2,1)}), bf16[4,4,8,1024]{3,2,1,0:T(8,128)(2,1)}, u32[]{:S(2)}, u32[]{:S(2)}) async-start(bf16[4,4,8,1024]{3,2,1,0:T(8,128)(2,1)} %bitcast.101), calls=%async_computation.3 | async-start | bytes 524288 | tf_op jit(solution)/shard_map/all_to_all | solution.py:65
  148.5 2.2 %gather_fusion.4 = bf16[128,4096]{1,0:T(8,128)(2,1)} fusion(bf16[128,4096]{1,0:T(8,128)(2,1)S(1)} %bitcast.93, s32[1024]{0:T(1024)S(1)} %pad_clamp_fusion), kind=kCustom, calls=%fused_computation.4 | custom fusion | bytes 2097664 | tf_op jit(solution)/shard_map/jit(_take)/gather | solution.py:60
  150.7 0.9 gather_fusion.6
  151.8 0.8 copy.103
  152.6 8.5 %shard_map.166 = f32[8,16,4096]{2,1,0:T(8,128)} custom-call(bf16[8,16,4096]{2,1,0:T(8,128)(2,1)} %bitcast.98, bf16[8,9,16,64]{3,2,1,0:T(8,128)(2,1)} %bitcast.99), custom_call_target="tpu_custom_call" | custom-call | flops 603979776 | bytes 3293184 | tf_op jit(solution)/shard_map/pallas_call | solution.py:105
  161.2 1.0 reduce_sum.122
  (110 shorter events, 19.3 us)
Async XLA Ops:
  0.6 140.2 %copy-start = (bf16[1024,1024]{1,0:T(8,128)(2,1)S(1)}, bf16[1024,1024]{1,0:T(8,128)(2,1)}, u32[]{:S(2)}) copy-start(bf16[1024,1024]{1,0:T(8,128)(2,1)} %param.29) | copy-start | bytes 6291460
  0.6 2.2 %copy-start.10 = (bf16[32,1024]{1,0:T(8,128)(2,1)S(1)}, bf16[32,1024]{1,0:T(8,128)(2,1)}, u32[]{:S(2)}) copy-start(bf16[32,1024]{1,0:T(8,128)(2,1)} %param.16) | copy-start | bytes 196612
  2.8 1.4 copy-start.7
  2.8 1.3 slice-start
  2.8 1.6 %copy-start.2 = (f32[4,4,8,1024]{3,2,1,0:T(8,128)}, f32[4,4,8,1024]{3,2,1,0:T(8,128)S(1)}, u32[]{:S(2)}) copy-start(f32[4,4,8,1024]{3,2,1,0:T(8,128)S(1)} %copy.84) | copy-start | bytes 1572868
  3.0 8.6 %copy-start.11 = (f32[6,1024]{1,0:T(8,128)S(1)}, f32[6,1024]{1,0:T(8,128)}, u32[]{:S(2)}) copy-start(f32[6,1024]{1,0:T(8,128)} %param.19) | copy-start | bytes 73732
  3.0 8.6 %copy-start.3 = (f32[128,1024]{1,0:T(8,128)}, f32[128,1024]{1,0:T(8,128)S(1)}, u32[]{:S(2)}) copy-start(f32[128,1024]{1,0:T(8,128)S(1)} %bitcast_subtract_fusion) | copy-start | bytes 1572868
  5.3 16.6 %all-to-all-start = ((bf16[4,128,320]{1,2,0:T(8,128)(2,1)}), bf16[4,128,320]{1,2,0:T(8,128)(2,1)S(1)}, u32[]{:S(2)}, u32[]{:S(2)}) async-start(bf16[4,128,320]{1,2,0:T(8,128)(2,1)} %broadcast_in_dim.20), calls=%async_computation | async-start | bytes 655360 | tf_op jit(solution)/shard_map/all_to_all | solution.py:72
  16.2 1.8 %copy-start.13 = (f32[1024]{0:T(1024)S(1)}, f32[1024]{0:T(1024)}, u32[]{:S(2)}) copy-start(f32[1024]{0:T(1024)} %param.26) | copy-start | bytes 12292
  16.2 2.0 %copy-start.1 = (s32[32]{0:T(128)S(1)}, s32[32]{0:T(128)}, u32[]{:S(2)}) copy-start(s32[32]{0:T(128)} %param.18) | copy-start | bytes 388
  36.7 29.2 %all-to-all-start.1 = ((bf16[4,4,8,4224]{3,2,1,0:T(8,128)(2,1)}), bf16[4,4,8,4224]{3,2,1,0:T(8,128)(2,1)}, u32[]{:S(2)}, u32[]{:S(2)}) async-start(bf16[4,4,8,4224]{3,2,1,0:T(8,128)(2,1)} %pad_maximum_fusion), calls=%async_computation.1 | async-start | bytes 2162688 | tf_op jit(solution)/shard_map/all_to_all | solution.py:65
  65.9 47.7 %all-to-all-start.4 = ((bf16[16,8,4096]{2,1,0:T(8,128)(2,1)}), bf16[16,8,4096]{2,1,0:T(8,128)(2,1)S(1)}, u32[]{:S(2)}, u32[]{:S(2)}) async-start(bf16[16,8,4096]{2,1,0:T(8,128)(2,1)} %bitcast.97), calls=%async_computation.4 | async-start | bytes 2097152 | tf_op jit(solution)/shard_map/all_to_all | solution.py:44
  69.8 3.0 %copy-start.8 = (bf16[128,1024]{1,0:T(8,128)(2,1)S(1)}, bf16[128,1024]{1,0:T(8,128)(2,1)}, u32[]{:S(2)}) copy-start(bf16[128,1024]{1,0:T(8,128)(2,1)} %param.24) | copy-start | bytes 786436
  69.8 3.0 %copy-start.12 = (f32[1024]{0:T(1024)S(1)}, f32[1024]{0:T(1024)}, u32[]{:S(2)}) copy-start(f32[1024]{0:T(1024)} %param.25) | copy-start | bytes 12292
  71.3 1.5 copy-start.4
  71.3 1.6 copy-start.5
  105.0 14.2 %copy-start.14 = (s32[8]{0:T(128)S(1)}, s32[8]{0:T(128)}, u32[]{:S(2)}) copy-start(s32[8]{0:T(128)} %get-tuple-element.53) | copy-start | bytes 100
  106.3 20.5 %copy-start.6 = (f32[4,8,1024]{2,1,0:T(8,128)S(1)}, f32[4,8,1024]{2,1,0:T(8,128)}, u32[]{:S(2)}) copy-start(f32[4,8,1024]{2,1,0:T(8,128)} %get-tuple-element.19) | copy-start | bytes 393220
  109.2 0.6 copy-start.9
  114.3 15.4 %all-to-all-start.2 = ((bf16[4,4,8,1024]{3,2,1,0:T(8,128)(2,1)}), bf16[4,4,8,1024]{3,2,1,0:T(8,128)(2,1)}, u32[]{:S(2)}, u32[]{:S(2)}) async-start(bf16[4,4,8,1024]{3,2,1,0:T(8,128)(2,1)} %broadcast_in_dim.21), calls=%async_computation.2 | async-start | bytes 524288 | tf_op jit(solution)/shard_map/all_to_all | solution.py:72
  129.7 14.6 %all-to-all-start.5 = ((bf16[16,8,576]{2,1,0:T(8,128)(2,1)}), bf16[16,8,576]{2,1,0:T(8,128)(2,1)S(1)}, u32[]{:S(2)}, u32[]{:S(2)}) async-start(bf16[16,8,576]{2,1,0:T(8,128)(2,1)} %bitcast.34), calls=%async_computation.5 | async-start | bytes 327680 | tf_op jit(solution)/shard_map/all_to_all | solution.py:44
  144.2 16.9 %all-to-all-start.3 = ((bf16[4,4,8,1024]{3,2,1,0:T(8,128)(2,1)}), bf16[4,4,8,1024]{3,2,1,0:T(8,128)(2,1)}, u32[]{:S(2)}, u32[]{:S(2)}) async-start(bf16[4,4,8,1024]{3,2,1,0:T(8,128)(2,1)} %bitcast.101), calls=%async_computation.3 | async-start | bytes 524288 | tf_op jit(solution)/shard_map/all_to_all | solution.py:65

commit v4 on v3

--- a/solution.py
+++ b/solution.py
@@ -121,6 +121,92 @@
             bytes_accessed=slots_dev * columns * (flat * 6 + pieces * extent * 2),
         ),
     )(moved_state, moved_terms)
+
+
+def recurrence_kernel(steps, proj_ref, params_ref, state_ref, mixed_ref, payload_ref, spread_ref):
+    extent = SUBSPACE_EXTENT
+
+    @pl.when(pl.program_id(0) == 0)
+    def _():
+        lane = lax.broadcasted_iota(jnp.int32, spread_ref.shape, 1)
+        row = lax.broadcasted_iota(jnp.int32, spread_ref.shape, 0)
+        spread_ref[...] = (lane // extent == row).astype(spread_ref.dtype)
+
+    spread = spread_ref[...]
+    state = state_ref[...]
+    premium = params_ref[0]
+    gain = params_ref[1]
+    bias = params_ref[2]
+    recept = [proj_ref[0, t] for t in range(steps)]
+    key_vec = [proj_ref[1, t] for t in range(steps)]
+    valued = [proj_ref[2, t] for t in range(steps)]
+    decay_rate = [proj_ref[3, t] for t in range(steps)]
+    flat = state.shape[-1]
+    prefix = jnp.ones_like(recept[0])
+    for t in range(steps):
+        query = recept[t] * prefix
+        high = query.astype(jnp.bfloat16)
+        rest = query - high.astype(jnp.float32)
+        middle = rest.astype(jnp.bfloat16)
+        low = (rest - middle.astype(jnp.float32)).astype(jnp.bfloat16)
+        spread_query = (
+            jnp.dot(high, spread, preferred_element_type=jnp.float32)
+            + jnp.dot(middle, spread, preferred_element_type=jnp.float32)
+            + jnp.dot(low, spread, preferred_element_type=jnp.float32)
+        )
+        weighted = spread_query * state
+        folded = weighted[:, 0:128]
+        for c in range(1, flat // 128):
+            folded = folded + weighted[:, 128 * c : 128 * (c + 1)]
+        from_state = folded[:, :extent] + folded[:, extent:]
+        bonus_term = jnp.sum(recept[t] * premium * key_vec[t], axis=-1, keepdims=True)
+        total = bonus_term * valued[t] + from_state
+        for s in range(t):
+            factor = key_vec[s]
+            for u in range(s + 1, t):
+                factor = factor * decay_rate[u]
+            total = total + jnp.sum(recept[t] * factor, axis=-1, keepdims=True) * valued[s]
+        average = jnp.mean(total, axis=-1, keepdims=True)
+        demeaned = total - average
+        spread_squared = jnp.mean(demeaned * demeaned, axis=-1, keepdims=True)
+        standardized = demeaned * lax.rsqrt(spread_squared + NORMALIZER_GUARD) * gain + bias
+        mixed_ref[t] = (standardized * proj_ref[4, t]).astype(mixed_ref.dtype)
+        prefix = prefix * decay_rate[t]
+    payload_ref[0] = prefix.astype(payload_ref.dtype)
+    for s in range(steps):
+        factor = key_vec[s]
+        for u in range(s + 1, steps):
+            factor = factor * decay_rate[u]
+        payload_ref[1 + s] = factor.astype(payload_ref.dtype)
+        payload_ref[1 + steps + s] = valued[s].astype(payload_ref.dtype)
+
+
+def run_recurrence(projected, params, state):
+    pieces, steps, local_rows, heads_here, extent = projected.shape
+    flat = state.shape[-1]
+    return pl.pallas_call(
+        functools.partial(recurrence_kernel, steps),
+        grid=(local_rows,),
+        in_specs=[
+            pl.BlockSpec((pieces, steps, None, heads_here, extent), lambda n: (0, 0, n, 0, 0)),
+            pl.BlockSpec((3, heads_here, extent), lambda n: (0, 0, 0)),
+            pl.BlockSpec((None, heads_here, flat), lambda n: (n, 0, 0)),
+        ],
+        out_specs=[
+            pl.BlockSpec((steps, None, heads_here, extent), lambda n: (0, n, 0, 0)),
+            pl.BlockSpec((None, 1 + 2 * steps, heads_here, extent), lambda n: (n, 0, 0, 0)),
+        ],
+        out_shape=[
+            jax.ShapeDtypeStruct((steps, local_rows, heads_here, extent), jnp.bfloat16),
+            jax.ShapeDtypeStruct((local_rows, 1 + 2 * steps, heads_here, extent), jnp.bfloat16),
+        ],
+        scratch_shapes=[pltpu.VMEM((extent, flat), jnp.bfloat16)],
+        cost_estimate=pl.CostEstimate(
+            flops=2 * local_rows * heads_here * extent * flat * 3 * steps,
+            transcendentals=steps * local_rows * heads_here,
+            bytes_accessed=local_rows * heads_here * (flat * 4 + extent * (pieces * steps * 4 + steps * 2 + (1 + 2 * steps) * 2)),
+        ),
+    )(projected, params, state)
 
 
 def per_device(
@@ -203,54 +289,24 @@
             )
         )
     )
-    bonus_term = jnp.sum(
-        recept * instant_premium.reshape(heads_here, SUBSPACE_EXTENT) * key_vec, axis=-1
-    )
-
-    prefix = [jnp.ones_like(decay_rate[0])]
-    for t in range(steps):
-        prefix.append(prefix[-1] * decay_rate[t])
-    query = jnp.stack([recept[t] * prefix[t] for t in range(steps)])
-    state = stream_kept_tableaux.reshape(
-        local_rows, heads_here, SUBSPACE_EXTENT, SUBSPACE_EXTENT
-    )
-    from_state = jnp.einsum(
-        "tnhi,nhij->tnhj", query, state, precision=lax.Precision.HIGHEST
-    )
-    outputs = []
-    for t in range(steps):
-        total = bonus_term[t][..., None] * valued[t] + from_state[t]
-        for s in range(t):
-            factor = key_vec[s]
-            for u in range(s + 1, t):
-                factor = factor * decay_rate[u]
-            total = total + jnp.sum(recept[t] * factor, axis=-1, keepdims=True) * valued[s]
-        outputs.append(total)
-    wkv_out = jnp.stack(outputs)
-
-    tails = []
-    for s in range(steps):
-        factor = key_vec[s]
-        for u in range(s + 1, steps):
-            factor = factor * decay_rate[u]
-        tails.append(factor)
-    payload = jnp.concatenate([prefix[steps]] + tails + [valued[s] for s in range(steps)], axis=-1)
+    projected = jnp.stack([recept, key_vec, valued, decay_rate, heads_of(gate_act)])
+    params = jnp.stack([instant_premium, norming_multiplier, norming_intercept]).reshape(
+        3, heads_here, SUBSPACE_EXTENT
+    )
+    mixed_heads, payload = run_recurrence(projected, params, stream_kept_tableaux)
+    combined_response = mixed_heads.reshape(steps, local_rows, width)
+    pieces = payload.shape[1]
     moved_terms = route_to_slots(
-        payload.astype(bf16), position_mapping_target, batch_index, head_index
+        payload.transpose(0, 2, 1, 3).reshape(local_rows, heads_here, pieces * SUBSPACE_EXTENT),
+        position_mapping_target,
+        batch_index,
+        head_index,
     )
     slots_dev, columns, _ = moved_terms.shape
-    moved_terms = moved_terms.reshape(slots_dev, columns, 1 + 2 * steps, SUBSPACE_EXTENT).transpose(
+    moved_terms = moved_terms.reshape(slots_dev, columns, pieces, SUBSPACE_EXTENT).transpose(
         0, 2, 1, 3
     )
     final_state = rebuild_state(moved_state, moved_terms, steps)
-
-    average = jnp.mean(wkv_out, axis=-1, keepdims=True)
-    demeaned = wkv_out - average
-    spread_squared = jnp.mean(demeaned * demeaned, axis=-1, keepdims=True)
-    standardized = (demeaned * lax.rsqrt(spread_squared + NORMALIZER_GUARD)).reshape(
-        steps, local_rows, width
-    ) * norming_multiplier + norming_intercept
-    combined_response = (standardized * gate_act).astype(bf16)
 
     gathered = exchange_copies(combined_response, "batch").transpose(1, 0, 2, 3)
     gathered = gathered.reshape(steps, sessions, width)

time: 166 us -> 145 us (0.87); the launches traced: 163 us -> 143 us
  local copies, waits for them, and re-layouts: 63.1 us -> 39.2 us
  Pallas kernels: 8.54 us -> 20.1 us
  waiting for transfers between devices: 22.5 us -> 31.3 us
  other arithmetic: 22.3 us -> 14.5 us
  matrix products: 15.7 us -> 10.1 us
  starting transfers between devices: 29.5 us -> 27.2 us
    mul x17 -> x0, local copies, waits for them, and re-layouts: 14.8 us -> none  [the longest x6 5.62 us: per_device(): recept[t] * factor]
    all_to_all x2, waiting for transfers between devices: 1.92 us -> 14.8 us  [exchange_copies(): lax.all_to_all(copies, axis_name, split_axis=0, concat_axis=0, tiled=True)]
    pallas_call x0 -> x1, Pallas kernels: none -> 11.5 us  [run_recurrence(): pl.pallas_call(functools.partial(recurrence_kernel, steps), grid=(local_r...]
    dot_general x1 -> x0, matrix products: 6.68 us -> none  [per_device(): jnp.einsum('tnhi,nhij->tnhj', query, state, precision=lax.Precision.HIGHEST)]
    reshape x3 -> x0, local copies, waits for them, and re-layouts: 6.23 us -> none  [the longest x1 4.62 us: per_device(): stream_kept_tableaux.reshape(local_rows, heads_here, SUBSPACE_EXTENT, SUB...]
    squeeze x4 -> x0, local copies, waits for them, and re-layouts: 5.19 us -> none  [per_device(): total = bonus_term[t][..., None] * valued[t] + from_state[t]]
    unnamed x30, local copies, waits for them, and re-layouts: 1.47 us -> 6.59 us
    another operation x6 -> x12, local copies, waits for them, and re-layouts: 3.84 us -> 8.47 us  [the longest x6 5.84 us: per_device(): jnp.stack([recept, key_vec, valued, decay_rate, heads_of(gate_act)])]
  transfers between devices with their start and end apart: 6 -> 6, of which waited for: 3 -> 4; matrix products, arithmetic and copies ran while one was open for 49% -> 30% of each run, Pallas kernels for 5% -> 14%
where the time goes in v4:
time: 145 us; the launch traced here: 143 us
  local copies, waits for them, and re-layouts  39.2 us (27%)
  waiting for transfers between devices  31.3 us (22%)
  starting transfers between devices  27.2 us (19%)
  Pallas kernels  20.1 us (14%)
  other arithmetic  14.5 us (10%)
  matrix products  10.1 us (7%)
    all_to_all x2, waiting for transfers between devices, exchange_copies(): lax.all_to_all(copies, axis_name, split_axis=0, concat_axis=0, tiled=True)  14.8 us
    all_to_all x2, waiting for transfers between devices, exchange_sum(): lax.all_to_all(pieces, axis_name, split_axis=0, concat_axis=0, tiled=True)  14.3 us
    pallas_call x1, Pallas kernels, run_recurrence(): pl.pallas_call(functools.partial(recurrence_kernel, steps), grid=(local_r...  11.5 us
    all_to_all x2, starting transfers between devices, exchange_copies(): lax.all_to_all(copies, axis_name, split_axis=0, concat_axis=0, tiled=True)  11.3 us
    pallas_call x1, Pallas kernels, rebuild_state(): pl.pallas_call(functools.partial(rebuild_kernel, steps), grid=(slots_dev,...  8.54 us
    all_to_all x2, starting transfers between devices, exchange_sum(): lax.all_to_all(pieces, axis_name, split_axis=0, concat_axis=0, tiled=True)  8.42 us
    all_to_all x2, starting transfers between devices, route_to_slots(): lax.all_to_all(packed, ('batch', 'head'), split_axis=0, concat_axis=0, ti...  7.49 us
    unnamed x30, local copies, waits for them, and re-layouts  6.59 us
  transfers between devices with their start and end apart: 6, of which 4 were waited for; matrix products, arithmetic and copies ran while one was open for 30% of the time, Pallas kernels for 14%

profile of v4, /device:TPU:0, one launch (start us, length us, event | category | flops | bytes accessed | tf_op | source)
XLA Modules:
  0.0 143.5 jit_solution(13303716537573189736)
XLA Ops:
  0.7 1.2 convert_bitcast_fusion
  1.8 0.9 slice_bitcast_fusion
  3.0 1.0 copy-done.6
  4.0 0.4 convolution_convert_fusion.1
  4.3 0.8 broadcast_in_dim.22
  5.1 6.3 %all-to-all-start = ((bf16[4,128,320]{1,2,0:T(8,128)(2,1)}), bf16[4,128,320]{1,2,0:T(8,128)(2,1)S(1)}, u32[]{:S(2)}, u32[]{:S(2)}) async-start(bf16[4,128,320]{1,2,0:T(8,128)(2,1)} %broadcast_in_dim.22), calls=%async_computation | async-start | bytes 655360 | tf_op jit(solution)/shard_map/all_to_all | solution.py:72
  11.4 10.3 %all-to-all-done = bf16[4,128,320]{1,2,0:T(8,128)(2,1)S(1)} async-done(((bf16[4,128,320]{1,2,0:T(8,128)(2,1)}), bf16[4,128,320]{1,2,0:T(8,128)(2,1)S(1)}, u32[]{:S(2)}, u32[]{:S(2)}) %all-to-all-start) | async-done | bytes 327712 | tf_op jit(solution)/shard_map/all_to_all | solution.py:72
  21.8 1.7 %add_convert_fusion = bf16[5,128,1024]{2,1,0:T(8,128)(2,1)S(1)} fusion(bf16[128,5,64]{0,2,1:T(8,128)(2,1)S(1)} %bitcast.80, bf16[5,64,1024]{2,1,0:T(8,128)(2,1)} %param.21, f32[5,1024]{1,0:T(8,128)S(1)} %slice.52, f32[128,1024]{1,0:T(8,128)S(1)} %bitcast_subtract_fusion, f32[128,1024]{1,0:T(8,128)S(1)} %bitcast.71), kind=kOutput, calls=%fused_computation.7 | convolution fusion | flops 86507520 | bytes 3117056 | tf_op jit(solution)/shard_map/nim,imd->ind/dot_general | solution.py:259
  23.5 5.3 %fusion.2 = bf16[128,4,1024]{2,0,1:T(8,128)(2,1)S(1)} fusion(bf16[5,128,1024]{2,1,0:T(8,128)(2,1)S(1)} %add_convert_fusion, bf16[4,1024,1024]{2,1,0:T(8,128)(2,1)} %param.22), kind=kOutput, calls=%fused_computation.12 | convolution fusion | flops 1074266112 | bytes 10747904 | tf_op jit(solution)/shard_map/inf,ifc->nic/dot_general | solution.py:265
  28.8 1.8 %copy.31 = bf16[128,4,1024]{2,1,0:T(4,128)(2,1)} copy(bf16[128,4,1024]{2,0,1:T(8,128)(2,1)S(1)} %fusion.2) | data formatting | bytes 2097152 | tf_op jit(solution)/shard_map/inf,ifc->nic/transpose | solution.py:265
  30.6 1.9 %concatenate.22 = bf16[4,4,8,4096]{3,2,1,0:T(8,128)(2,1)S(1)} reshape(bf16[128,4,1024]{2,1,0:T(4,128)(2,1)} %copy.31) | data formatting | bytes 2097152 | tf_op jit(solution)/shard_map/concatenate | solution.py:270
  32.5 1.2 convolution_convert_fusion.2
  33.7 1.1 pad_maximum_fusion
  34.7 4.4 %all-to-all-start.1 = ((bf16[4,4,8,4224]{3,2,1,0:T(8,128)(2,1)}), bf16[4,4,8,4224]{3,2,1,0:T(8,128)(2,1)}, u32[]{:S(2)}, u32[]{:S(2)}) async-start(bf16[4,4,8,4224]{3,2,1,0:T(8,128)(2,1)} %pad_maximum_fusion), calls=%async_computation.1 | async-start | bytes 2162688 | tf_op jit(solution)/shard_map/all_to_all | solution.py:65
  39.4 1.7 %convert_element_type.89 = bf16[8,16,4096]{2,1,0:T(8,128)(2,1)S(1)} convert(f32[8,16,4096]{2,1,0:T(8,128)} %state_ref.1) | non-fusion elementwise | flops 524288 | bytes 3145728 | tf_op jit(solution)/shard_map/convert_element_type | solution.py:240
  41.3 1.6 %sort.74 = (s32[32]{0:T(128)}, s32[32]{0:T(128)S(1)}) sort(s32[32]{0:T(128)S(1)} %copy-done.1, s32[32]{0:T(128)S(1)} %iota.51), dimensions={0}, to_apply=%region_2.3 | sort | flops 160 | bytes 512 | tf_op jit(solution)/shard_map/jit(argsort)/sort | solution.py:313
  42.9 1.6 %sort.76 = (s32[32]{0:T(128)}, s32[32]{0:T(128)S(1)}) sort(s32[32]{0:T(128)S(1)} %and_select_fusion.3, s32[32]{0:T(128)S(1)} %iota.54), dimensions={0}, to_apply=%region_5.6 | sort | flops 160 | bytes 512 | tf_op jit(solution)/shard_map/jit(argsort)/sort | solution.py:47
  44.7 1.0 sort.75
  45.7 0.7 gather_fusion.1
  46.8 0.6 gather_fusion.3
  47.4 2.2 %gather_fusion.2 = bf16[128,4096]{1,0:T(8,128)(2,1)} fusion(bf16[128,4096]{1,0:T(8,128)(2,1)S(1)} %bitcast.67, s32[1024]{0:T(1024)S(1)} %get-tuple-element.25), kind=kCustom, calls=%fused_computation.2 | custom fusion | bytes 2097664 | tf_op jit(solution)/shard_map/jit(_take)/gather | solution.py:41
  49.6 14.3 %all-to-all-done.1 = bf16[4,4,8,4224]{3,2,1,0:T(8,128)(2,1)} async-done(((bf16[4,4,8,4224]{3,2,1,0:T(8,128)(2,1)}), bf16[4,4,8,4224]{3,2,1,0:T(8,128)(2,1)}, u32[]{:S(2)}, u32[]{:S(2)}) %all-to-all-start.1) | async-done | bytes 1081376 | tf_op jit(solution)/shard_map/all_to_all | solution.py:65
  64.0 3.8 %all-to-all-start.4 = ((bf16[16,8,4096]{2,1,0:T(8,128)(2,1)}), bf16[16,8,4096]{2,1,0:T(8,128)(2,1)S(1)}, u32[]{:S(2)}, u32[]{:S(2)}) async-start(bf16[16,8,4096]{2,1,0:T(8,128)(2,1)} %bitcast.72), calls=%async_computation.4 | async-start | bytes 2097152 | tf_op jit(solution)/shard_map/all_to_all | solution.py:44
  67.8 1.0 sort.77
  68.8 0.6 pad_maximum_fusion.1.params_ref
  69.4 1.4 %convert_reduce_fusion = f32[4,8,4224]{2,1,0:T(8,128)S(1)} fusion(bf16[4,4,8,4224]{3,2,1,0:T(8,128)(2,1)} %all-to-all-done.1), kind=kLoop, calls=%fused_computation.8 | loop fusion | flops 946176 | bytes 1622016 | tf_op jit(solution)/shard_map/reduce_sum | solution.py:66
  70.8 0.8 copy-done.2
  71.6 0.7 slice_convert_fusion
  72.4 1.0 reshape.289
  73.4 1.7 %reshape.290 = f32[1,4,8,16,64]{4,3,2,1,0:T(8,128)} reshape(f32[4,8,1024]{2,1,0:T(8,128)} %get-tuple-element.16) | data formatting | bytes 262144 | tf_op jit(solution)/shard_map/stack;reshape | solution.py:292
  75.1 0.8 reshape.291
  75.9 1.2 fusion.11
  77.0 0.8 stack_reshape.30
  77.8 0.9 divide_multiply_fusion
  78.8 0.8 stack_reshape.31
  79.6 0.7 constant_dynamic-update-slice_fusion.4
  80.3 1.7 %constant_dynamic-update-slice_fusion.3 = f32[5,4,8,16,64]{4,3,2,1,0:T(8,128)} fusion(f32[5,4,8,16,64]{4,3,2,1,0:T(8,128)} %constant_dynamic-update-slice_fusion.4, f32[1,4,8,16,64]{4,3,2,1,0:T(8,128)} %reshape.290), kind=kLoop, calls=%fused_computation.51 | loop fusion | bytes 524288
  82.0 1.7 %constant_dynamic-update-slice_fusion.2 = f32[5,4,8,16,64]{4,3,2,1,0:T(8,128)} fusion(f32[5,4,8,16,64]{4,3,2,1,0:T(8,128)} %constant_dynamic-update-slice_fusion.3, f32[1,4,8,16,64]{4,3,2,1,0:T(8,128)} %reshape.291), kind=kLoop, calls=%fused_computation.50 | loop fusion | bytes 524288
  83.7 0.7 constant_dynamic-update-slice_fusion.1
  84.4 0.7 constant_dynamic-update-slice_fusion.proj_ref
  85.1 11.5 %shard_map.166 = (bf16[4,8,16,64]{3,2,1,0:T(8,128)(2,1)}, bf16[8,9,16,64]{3,2,1,0:T(8,128)(2,1)}) custom-call(f32[5,4,8,16,64]{4,3,2,1,0:T(8,128)} %constant_dynamic-update-slice_fusion.proj_ref, f32[3,16,64]{2,1,0:T(8,128)} %pad_maximum_fusion.1.params_ref, f32[8,16,4096]{2,1,0:T(8,128)} %state_ref.1), custom_call_target="tpu_custom_call" | custom-call | flops 805306368 | bytes 2965504 | tf_op jit(solution)/shard_map/pallas_call | solution.py:187
  96.6 1.0 broadcast_in_dim.23
  97.7 0.7 broadcast_in_dim.24
  98.4 5.0 %all-to-all-start.2 = ((bf16[4,4,8,1024]{3,2,1,0:T(8,128)(2,1)}), bf16[4,4,8,1024]{3,2,1,0:T(8,128)(2,1)}, u32[]{:S(2)}, u32[]{:S(2)}) async-start(bf16[4,4,8,1024]{3,2,1,0:T(8,128)(2,1)} %broadcast_in_dim.24), calls=%async_computation.2 | async-start | bytes 524288 | tf_op jit(solution)/shard_map/all_to_all | solution.py:72
  103.5 1.9 %copy.36 = bf16[8,16,9,64]{3,2,1,0:T(8,128)(2,1)} copy(bf16[8,16,9,64]{3,1,2,0:T(8,128)(2,1)} %bitcast.81) | data formatting | bytes 294912 | tf_op jit(solution)/shard_map/transpose | solution.py:300
  105.4 1.4 reshape_reshape.6
  106.7 1.5 %gather_fusion.5 = bf16[128,576]{1,0:T(8,128)(2,1)} fusion(bf16[128,576]{1,0:T(8,128)(2,1)S(1)} %reshape_reshape.6, s32[1024]{0:T(1024)S(1)} %get-tuple-element.25), kind=kCustom, calls=%fused_computation.5 | custom fusion | bytes 295424 | tf_op jit(solution)/shard_map/jit(_take)/gather | solution.py:41
  108.3 4.5 %all-to-all-done.2 = bf16[4,4,8,1024]{3,2,1,0:T(8,128)(2,1)} async-done(((bf16[4,4,8,1024]{3,2,1,0:T(8,128)(2,1)}), bf16[4,4,8,1024]{3,2,1,0:T(8,128)(2,1)}, u32[]{:S(2)}, u32[]{:S(2)}) %all-to-all-start.2) | async-done | bytes 262176 | tf_op jit(solution)/shard_map/all_to_all | solution.py:72
  112.7 3.7 %all-to-all-start.5 = ((bf16[16,8,576]{2,1,0:T(8,128)(2,1)}), bf16[16,8,576]{2,1,0:T(8,128)(2,1)S(1)}, u32[]{:S(2)}, u32[]{:S(2)}) async-start(bf16[16,8,576]{2,1,0:T(8,128)(2,1)} %bitcast.26), calls=%async_computation.5 | async-start | bytes 327680 | tf_op jit(solution)/shard_map/all_to_all | solution.py:44
  116.4 1.6 %fusion.25 = (bf16[2,4,8,1024]{3,2,0,1:T(8,128)(2,1)}, bf16[2,4,8,1024]{3,2,0,1:T(8,128)(2,1)S(1)}) fusion(bf16[4,4,8,1024]{3,2,0,1:T(8,128)(2,1)} %bitcast.14), kind=kLoop, calls=%fused_computation.88 | loop fusion | bytes 524288 | tf_op jit(solution)/shard_map/slice | solution.py:315
  118.2 1.5 %gather_fusion = bf16[32,2,1024]{2,1,0:T(2,128)(2,1)} fusion(bf16[2,32,1024]{2,0,1:T(2,128)(2,1)S(1)} %bitcast.79, s32[1024]{0:T(1024)S(1)} %pad_clamp_fusion.4), kind=kCustom, calls=%fused_computation | custom fusion | bytes 262272 | tf_op jit(solution)/shard_map/jit(_take)/gather | solution.py:315
  119.7 0.9 copy.45
  120.6 0.9 copy.46
  121.5 0.4 fusion.6
  122.0 0.7 copy.44
  122.7 2.2 %all-to-all-done.5 = bf16[16,8,576]{2,1,0:T(8,128)(2,1)S(1)} async-done(((bf16[16,8,576]{2,1,0:T(8,128)(2,1)}), bf16[16,8,576]{2,1,0:T(8,128)(2,1)S(1)}, u32[]{:S(2)}, u32[]{:S(2)}) %all-to-all-start.5) | async-done | bytes 147488 | tf_op jit(solution)/shard_map/all_to_all | solution.py:44
  124.9 4.0 %all-to-all-start.3 = ((bf16[4,4,8,1024]{3,2,1,0:T(8,128)(2,1)}), bf16[4,4,8,1024]{3,2,1,0:T(8,128)(2,1)}, u32[]{:S(2)}, u32[]{:S(2)}) async-start(bf16[4,4,8,1024]{3,2,1,0:T(8,128)(2,1)} %bitcast.76), calls=%async_computation.3 | async-start | bytes 524288 | tf_op jit(solution)/shard_map/all_to_all | solution.py:65
  129.2 2.2 %gather_fusion.4 = bf16[128,4096]{1,0:T(8,128)(2,1)} fusion(bf16[128,4096]{1,0:T(8,128)(2,1)S(1)} %bitcast.68, s32[1024]{0:T(1024)S(1)} %pad_clamp_fusion), kind=kCustom, calls=%fused_computation.4 | custom fusion | bytes 2097664 | tf_op jit(solution)/shard_map/jit(_take)/gather | solution.py:60
  131.3 0.9 gather_fusion.6
  132.2 0.2 reshape_reshape.7
  132.5 0.8 copy.43
  133.3 8.5 %shard_map.167 = f32[8,16,4096]{2,1,0:T(8,128)} custom-call(bf16[8,16,4096]{2,1,0:T(8,128)(2,1)} %bitcast.73, bf16[8,9,16,64]{3,2,1,0:T(8,128)(2,1)} %bitcast.75), custom_call_target="tpu_custom_call" | custom-call | flops 603979776 | bytes 3293184 | tf_op jit(solution)/shard_map/pallas_call | solution.py:105
  141.8 1.0 reduce_sum.32
  142.8 0.6 fusion.26
  (67 shorter events, 1.7 us)
Async XLA Ops:
  0.6 120.9 %copy-start = (bf16[1024,1024]{1,0:T(8,128)(2,1)S(1)}, bf16[1024,1024]{1,0:T(8,128)(2,1)}, u32[]{:S(2)}) copy-start(bf16[1024,1024]{1,0:T(8,128)(2,1)} %param.29) | copy-start | bytes 6291460
  0.6 2.2 %copy-start.7 = (bf16[32,1024]{1,0:T(8,128)(2,1)S(1)}, bf16[32,1024]{1,0:T(8,128)(2,1)}, u32[]{:S(2)}) copy-start(bf16[32,1024]{1,0:T(8,128)(2,1)} %param.16) | copy-start | bytes 196612
  2.9 1.1 copy-start.6
  2.9 1.1 slice-start.1
  4.0 7.4 %copy-start.8 = (f32[6,1024]{1,0:T(8,128)S(1)}, f32[6,1024]{1,0:T(8,128)}, u32[]{:S(2)}) copy-start(f32[6,1024]{1,0:T(8,128)} %param.19) | copy-start | bytes 73732
  5.1 16.6 %all-to-all-start = ((bf16[4,128,320]{1,2,0:T(8,128)(2,1)}), bf16[4,128,320]{1,2,0:T(8,128)(2,1)S(1)}, u32[]{:S(2)}, u32[]{:S(2)}) async-start(bf16[4,128,320]{1,2,0:T(8,128)(2,1)} %broadcast_in_dim.22), calls=%async_computation | async-start | bytes 655360 | tf_op jit(solution)/shard_map/all_to_all | solution.py:72
  23.5 5.3 %copy-start.3 = (bf16[5,128,1024]{2,1,0:T(8,128)(2,1)}, bf16[5,128,1024]{2,1,0:T(8,128)(2,1)S(1)}, u32[]{:S(2)}) copy-start(bf16[5,128,1024]{2,1,0:T(8,128)(2,1)S(1)} %add_convert_fusion) | copy-start | bytes 3932164
  30.6 1.9 %slice-start = ((bf16[5,128,1024]{2,1,0:T(8,128)(2,1)}), bf16[1,128,1024]{2,1,0:T(8,128)(2,1)S(1)}, s32[]{:S(2)}) async-start(bf16[5,128,1024]{2,1,0:T(8,128)(2,1)} %copy-done.3), calls=%async_computation.6 | async-start | bytes 524288 | tf_op jit(solution)/shard_map/slice | solution.py:268
  34.7 4.4 %copy-start.10 = (f32[1024]{0:T(1024)S(1)}, f32[1024]{0:T(1024)}, u32[]{:S(2)}) copy-start(f32[1024]{0:T(1024)} %param.28) | copy-start | bytes 12292
  34.7 4.5 %copy-start.11 = (f32[1024]{0:T(1024)S(1)}, f32[1024]{0:T(1024)}, u32[]{:S(2)}) copy-start(f32[1024]{0:T(1024)} %param.27) | copy-start | bytes 12292
  34.7 4.6 %copy-start.12 = (f32[1024]{0:T(1024)S(1)}, f32[1024]{0:T(1024)}, u32[]{:S(2)}) copy-start(f32[1024]{0:T(1024)} %param.26) | copy-start | bytes 12292
  34.7 29.2 %all-to-all-start.1 = ((bf16[4,4,8,4224]{3,2,1,0:T(8,128)(2,1)}), bf16[4,4,8,4224]{3,2,1,0:T(8,128)(2,1)}, u32[]{:S(2)}, u32[]{:S(2)}) async-start(bf16[4,4,8,4224]{3,2,1,0:T(8,128)(2,1)} %pad_maximum_fusion), calls=%async_computation.1 | async-start | bytes 2162688 | tf_op jit(solution)/shard_map/all_to_all | solution.py:65
  39.4 1.9 %copy-start.1 = (s32[32]{0:T(128)S(1)}, s32[32]{0:T(128)}, u32[]{:S(2)}) copy-start(s32[32]{0:T(128)} %param.18) | copy-start | bytes 388
  64.0 33.7 %all-to-all-start.4 = ((bf16[16,8,4096]{2,1,0:T(8,128)(2,1)}), bf16[16,8,4096]{2,1,0:T(8,128)(2,1)S(1)}, u32[]{:S(2)}, u32[]{:S(2)}) async-start(bf16[16,8,4096]{2,1,0:T(8,128)(2,1)} %bitcast.72), calls=%async_computation.4 | async-start | bytes 2097152 | tf_op jit(solution)/shard_map/all_to_all | solution.py:44
  70.8 0.8 copy-start.2
  71.6 4.3 %copy-start.9 = (f32[1024]{0:T(1024)S(1)}, f32[1024]{0:T(1024)}, u32[]{:S(2)}) copy-start(f32[1024]{0:T(1024)} %param.25) | copy-start | bytes 12292
  79.6 4.1 %copy-start.4 = (f32[1,4,8,16,64]{4,3,2,1,0:T(8,128)S(1)}, f32[1,4,8,16,64]{4,3,2,1,0:T(8,128)}, u32[]{:S(2)}) copy-start(f32[1,4,8,16,64]{4,3,2,1,0:T(8,128)} %stack_reshape.30) | copy-start | bytes 393220
  79.6 4.8 %copy-start.5 = (f32[1,4,8,16,64]{4,3,2,1,0:T(8,128)S(1)}, f32[1,4,8,16,64]{4,3,2,1,0:T(8,128)}, u32[]{:S(2)}) copy-start(f32[1,4,8,16,64]{4,3,2,1,0:T(8,128)} %stack_reshape.31) | copy-start | bytes 393220
  98.4 14.3 %all-to-all-start.2 = ((bf16[4,4,8,1024]{3,2,1,0:T(8,128)(2,1)}), bf16[4,4,8,1024]{3,2,1,0:T(8,128)(2,1)}, u32[]{:S(2)}, u32[]{:S(2)}) async-start(bf16[4,4,8,1024]{3,2,1,0:T(8,128)(2,1)} %broadcast_in_dim.24), calls=%async_computation.2 | async-start | bytes 524288 | tf_op jit(solution)/shard_map/all_to_all | solution.py:72
  112.7 12.2 %all-to-all-start.5 = ((bf16[16,8,576]{2,1,0:T(8,128)(2,1)}), bf16[16,8,576]{2,1,0:T(8,128)(2,1)S(1)}, u32[]{:S(2)}, u32[]{:S(2)}) async-start(bf16[16,8,576]{2,1,0:T(8,128)(2,1)} %bitcast.26), calls=%async_computation.5 | async-start | bytes 327680 | tf_op jit(solution)/shard_map/all_to_all | solution.py:44
  124.9 16.9 %all-to-all-start.3 = ((bf16[4,4,8,1024]{3,2,1,0:T(8,128)(2,1)}), bf16[4,4,8,1024]{3,2,1,0:T(8,128)(2,1)}, u32[]{:S(2)}, u32[]{:S(2)}) async-start(bf16[4,4,8,1024]{3,2,1,0:T(8,128)(2,1)} %bitcast.76), calls=%async_computation.3 | async-start | bytes 524288 | tf_op jit(solution)/shard_map/all_to_all | solution.py:65

commit v5 on v4

--- a/solution.py
+++ b/solution.py
@@ -123,7 +123,19 @@
     )(moved_state, moved_terms)
 
 
-def recurrence_kernel(steps, proj_ref, params_ref, state_ref, mixed_ref, payload_ref, spread_ref):
+def recurrence_kernel(
+    steps,
+    recept_ref,
+    key_ref,
+    value_ref,
+    decay_ref,
+    gate_ref,
+    params_ref,
+    state_ref,
+    mixed_ref,
+    payload_ref,
+    spread_ref,
+):
     extent = SUBSPACE_EXTENT
 
     @pl.when(pl.program_id(0) == 0)
@@ -137,10 +149,10 @@
     premium = params_ref[0]
     gain = params_ref[1]
     bias = params_ref[2]
-    recept = [proj_ref[0, t] for t in range(steps)]
-    key_vec = [proj_ref[1, t] for t in range(steps)]
-    valued = [proj_ref[2, t] for t in range(steps)]
-    decay_rate = [proj_ref[3, t] for t in range(steps)]
+    recept = [recept_ref[t] for t in range(steps)]
+    key_vec = [key_ref[t] for t in range(steps)]
+    valued = [value_ref[t] for t in range(steps)]
+    decay_rate = [decay_ref[t] for t in range(steps)]
     flat = state.shape[-1]
     prefix = jnp.ones_like(recept[0])
     for t in range(steps):
@@ -170,7 +182,7 @@
         demeaned = total - average
         spread_squared = jnp.mean(demeaned * demeaned, axis=-1, keepdims=True)
         standardized = demeaned * lax.rsqrt(spread_squared + NORMALIZER_GUARD) * gain + bias
-        mixed_ref[t] = (standardized * proj_ref[4, t]).astype(mixed_ref.dtype)
+        mixed_ref[t] = (standardized * gate_ref[t]).astype(mixed_ref.dtype)
         prefix = prefix * decay_rate[t]
     payload_ref[0] = prefix.astype(payload_ref.dtype)
     for s in range(steps):
@@ -182,13 +194,14 @@
 
 
 def run_recurrence(projected, params, state):
-    pieces, steps, local_rows, heads_here, extent = projected.shape
+    pieces = len(projected)
+    steps, local_rows, heads_here, extent = projected[0].shape
     flat = state.shape[-1]
     return pl.pallas_call(
         functools.partial(recurrence_kernel, steps),
         grid=(local_rows,),
         in_specs=[
-            pl.BlockSpec((pieces, steps, None, heads_here, extent), lambda n: (0, 0, n, 0, 0)),
+            *[pl.BlockSpec((steps, None, heads_here, extent), lambda n: (0, n, 0, 0))] * pieces,
             pl.BlockSpec((3, heads_here, extent), lambda n: (0, 0, 0)),
             pl.BlockSpec((None, heads_here, flat), lambda n: (n, 0, 0)),
         ],
@@ -206,7 +219,7 @@
             transcendentals=steps * local_rows * heads_here,
             bytes_accessed=local_rows * heads_here * (flat * 4 + extent * (pieces * steps * 4 + steps * 2 + (1 + 2 * steps) * 2)),
         ),
-    )(projected, params, state)
+    )(*projected, params, state)
 
 
 def per_device(
@@ -289,7 +302,7 @@
             )
         )
     )
-    projected = jnp.stack([recept, key_vec, valued, decay_rate, heads_of(gate_act)])
+    projected = (recept, key_vec, valued, decay_rate, heads_of(gate_act))
     params = jnp.stack([instant_premium, norming_multiplier, norming_intercept]).reshape(
         3, heads_here, SUBSPACE_EXTENT
     )

time: 145 us -> 143 us (0.986)
  local copies, waits for them, and re-layouts: 39.2 us -> 33.6 us
  waiting for transfers between devices: 31.3 us -> 35.5 us
    another operation x6 -> x0, local copies, waits for them, and re-layouts: 5.84 us -> none  [per_device(): jnp.stack([recept, key_vec, valued, decay_rate, heads_of(gate_act)])]
    reshape x0 -> x5, local copies, waits for them, and re-layouts: none -> 5.83 us  [heads_of(): return value.reshape(steps, local_rows, heads_here, SUBSPACE_EXTENT)]
    unnamed x30 -> x20, local copies, waits for them, and re-layouts: 6.59 us -> 0.8 us
    all_to_all x2, waiting for transfers between devices: 14.3 us -> 18.5 us  [exchange_sum(): lax.all_to_all(pieces, axis_name, split_axis=0, concat_axis=0, tiled=True)]
    slice x2, local copies, waits for them, and re-layouts: 2.54 us -> 1 us  [per_device(): gathered[:STEPS_A]]
  transfers between devices with their start and end apart: 6 -> 6, of which waited for: 4 -> 4; matrix products, arithmetic and copies ran while one was open for 30% -> 27% of each run, Pallas kernels for 14% -> 14%
where the time goes in v5:
time: 143 us; the launch traced here: 142 us
  waiting for transfers between devices  35.5 us (25%)
  local copies, waits for them, and re-layouts  33.6 us (23%)
  starting transfers between devices  27.1 us (19%)
  Pallas kernels  20.3 us (14%)
  other arithmetic  14.4 us (10%)
  matrix products  10.1 us (7%)
    all_to_all x2, waiting for transfers between devices, exchange_sum(): lax.all_to_all(pieces, axis_name, split_axis=0, concat_axis=0, tiled=True)  18.5 us
    all_to_all x2, waiting for transfers between devices, exchange_copies(): lax.all_to_all(copies, axis_name, split_axis=0, concat_axis=0, tiled=True)  14.8 us
    pallas_call x1, Pallas kernels, run_recurrence(): pl.pallas_call(functools.partial(recurrence_kernel, steps), grid=(local_r...  11.8 us
    all_to_all x2, starting transfers between devices, exchange_copies(): lax.all_to_all(copies, axis_name, split_axis=0, concat_axis=0, tiled=True)  11.3 us
    pallas_call x1, Pallas kernels, rebuild_state(): pl.pallas_call(functools.partial(rebuild_kernel, steps), grid=(slots_dev,...  8.54 us
    all_to_all x2, starting transfers between devices, exchange_sum(): lax.all_to_all(pieces, axis_name, split_axis=0, concat_axis=0, tiled=True)  8.29 us
    all_to_all x2, starting transfers between devices, route_to_slots(): lax.all_to_all(packed, ('batch', 'head'), split_axis=0, concat_axis=0, ti...  7.5 us
    reshape x5, local copies, waits for them, and re-layouts, heads_of(): return value.reshape(steps, local_rows, heads_here, SUBSPACE_EXTENT)  5.83 us
  transfers between devices with their start and end apart: 6, of which 4 were waited for; matrix products, arithmetic and copies ran while one was open for 27% of the time, Pallas kernels for 14%

profile of v5, /device:TPU:0, one launch (start us, length us, event | category | flops | bytes accessed | tf_op | source)
XLA Modules:
  0.0 141.9 jit_solution(148849501927146092)
XLA Ops:
  0.6 1.1 slice_bitcast_fusion
  1.7 1.0 convert_bitcast_fusion
  2.8 0.9 convert_bitcast_fusion.1
  3.9 0.4 convolution_convert_fusion.1
  4.3 0.8 broadcast_in_dim.22
  5.0 6.3 %all-to-all-start = ((bf16[4,128,320]{1,2,0:T(8,128)(2,1)}), bf16[4,128,320]{1,2,0:T(8,128)(2,1)S(1)}, u32[]{:S(2)}, u32[]{:S(2)}) async-start(bf16[4,128,320]{1,2,0:T(8,128)(2,1)} %broadcast_in_dim.22), calls=%async_computation | async-start | bytes 655360 | tf_op jit(solution)/shard_map/all_to_all | solution.py:72
  11.4 10.3 %all-to-all-done = bf16[4,128,320]{1,2,0:T(8,128)(2,1)S(1)} async-done(((bf16[4,128,320]{1,2,0:T(8,128)(2,1)}), bf16[4,128,320]{1,2,0:T(8,128)(2,1)S(1)}, u32[]{:S(2)}, u32[]{:S(2)}) %all-to-all-start) | async-done | bytes 327712 | tf_op jit(solution)/shard_map/all_to_all | solution.py:72
  21.7 1.7 %add_convert_fusion = bf16[5,128,1024]{2,1,0:T(8,128)(2,1)S(1)} fusion(bf16[128,5,64]{0,2,1:T(8,128)(2,1)S(1)} %bitcast.80, bf16[5,64,1024]{2,1,0:T(8,128)(2,1)} %param.21, f32[5,1024]{1,0:T(8,128)S(1)} %slice.52, f32[128,1024]{1,0:T(8,128)S(1)} %bitcast_subtract_fusion, f32[128,1024]{1,0:T(8,128)S(1)} %bitcast.71), kind=kOutput, calls=%fused_computation.7 | convolution fusion | flops 86507520 | bytes 3117056 | tf_op jit(solution)/shard_map/nim,imd->ind/dot_general | solution.py:272
  23.4 5.3 %fusion.2 = bf16[128,4,1024]{2,0,1:T(8,128)(2,1)S(1)} fusion(bf16[5,128,1024]{2,1,0:T(8,128)(2,1)S(1)} %add_convert_fusion, bf16[4,1024,1024]{2,1,0:T(8,128)(2,1)} %param.22), kind=kOutput, calls=%fused_computation.12 | convolution fusion | flops 1074266112 | bytes 10747904 | tf_op jit(solution)/shard_map/inf,ifc->nic/dot_general | solution.py:278
  28.7 1.8 %copy.31 = bf16[128,4,1024]{2,1,0:T(4,128)(2,1)} copy(bf16[128,4,1024]{2,0,1:T(8,128)(2,1)S(1)} %fusion.2) | data formatting | bytes 2097152 | tf_op jit(solution)/shard_map/inf,ifc->nic/transpose | solution.py:278
  30.6 1.9 %concatenate.22 = bf16[4,4,8,4096]{3,2,1,0:T(8,128)(2,1)S(1)} reshape(bf16[128,4,1024]{2,1,0:T(4,128)(2,1)} %copy.31) | data formatting | bytes 2097152 | tf_op jit(solution)/shard_map/concatenate | solution.py:283
  32.4 1.2 convolution_convert_fusion.2
  33.6 1.1 pad_maximum_fusion
  34.7 4.3 %all-to-all-start.1 = ((bf16[4,4,8,4224]{3,2,1,0:T(8,128)(2,1)}), bf16[4,4,8,4224]{3,2,1,0:T(8,128)(2,1)}, u32[]{:S(2)}, u32[]{:S(2)}) async-start(bf16[4,4,8,4224]{3,2,1,0:T(8,128)(2,1)} %pad_maximum_fusion), calls=%async_computation.1 | async-start | bytes 2162688 | tf_op jit(solution)/shard_map/all_to_all | solution.py:65
  39.0 0.1 reshape.335
  39.1 0.1 and_select_fusion.6
  39.2 1.0 sort.75
  40.2 0.7 gather_fusion.1
  40.9 0.1 reshape.389
  41.1 0.1 iota_add_fusion.1
  41.2 0.1 reshape.343
  41.3 1.7 %convert_element_type.89 = bf16[8,16,4096]{2,1,0:T(8,128)(2,1)S(1)} convert(f32[8,16,4096]{2,1,0:T(8,128)} %state_ref.1) | non-fusion elementwise | flops 524288 | bytes 3145728 | tf_op jit(solution)/shard_map/convert_element_type | solution.py:253
  43.0 2.2 %gather_fusion.2 = bf16[128,4096]{1,0:T(8,128)(2,1)} fusion(bf16[128,4096]{1,0:T(8,128)(2,1)S(1)} %bitcast.67, s32[1024]{0:T(1024)S(1)} %pad_clamp_fusion.2), kind=kCustom, calls=%fused_computation.2 | custom fusion | bytes 2097664 | tf_op jit(solution)/shard_map/jit(_take)/gather | solution.py:41
  45.2 18.5 %all-to-all-done.1 = bf16[4,4,8,4224]{3,2,1,0:T(8,128)(2,1)} async-done(((bf16[4,4,8,4224]{3,2,1,0:T(8,128)(2,1)}), bf16[4,4,8,4224]{3,2,1,0:T(8,128)(2,1)}, u32[]{:S(2)}, u32[]{:S(2)}) %all-to-all-start.1) | async-done | bytes 1081376 | tf_op jit(solution)/shard_map/all_to_all | solution.py:65
  63.8 3.8 %all-to-all-start.4 = ((bf16[16,8,4096]{2,1,0:T(8,128)(2,1)}), bf16[16,8,4096]{2,1,0:T(8,128)(2,1)S(1)}, u32[]{:S(2)}, u32[]{:S(2)}) async-start(bf16[16,8,4096]{2,1,0:T(8,128)(2,1)} %bitcast.72), calls=%async_computation.4 | async-start | bytes 2097152 | tf_op jit(solution)/shard_map/all_to_all | solution.py:44
  67.6 1.6 %sort.76 = (s32[32]{0:T(128)}, s32[32]{0:T(128)S(1)}) sort(s32[32]{0:T(128)S(1)} %and_select_fusion.3, s32[32]{0:T(128)S(1)} %iota.54), dimensions={0}, to_apply=%region_5.6 | sort | flops 160 | bytes 512 | tf_op jit(solution)/shard_map/jit(argsort)/sort | solution.py:47
  69.3 1.6 %sort.74 = (s32[32]{0:T(128)}, s32[32]{0:T(128)S(1)}) sort(s32[32]{0:T(128)S(1)} %copy-done.1, s32[32]{0:T(128)S(1)} %iota.51), dimensions={0}, to_apply=%region_2.3 | sort | flops 160 | bytes 512 | tf_op jit(solution)/shard_map/jit(argsort)/sort | solution.py:326
  70.9 0.6 gather_fusion.3
  71.8 1.0 sort.77
  72.7 0.6 pad_maximum_fusion.1.params_ref
  73.3 1.4 %convert_reduce_fusion = f32[4,8,4224]{2,1,0:T(8,128)S(1)} fusion(bf16[4,4,8,4224]{3,2,1,0:T(8,128)(2,1)} %all-to-all-done.1), kind=kLoop, calls=%fused_computation.8 | loop fusion | flops 946176 | bytes 1622016 | tf_op jit(solution)/shard_map/reduce_sum | solution.py:66
  74.8 0.8 copy-done.2
  75.6 0.8 reshape.308.gate_ref
  76.4 0.7 slice_convert_fusion
  77.2 1.7 %reshape.323.value_ref = f32[4,8,16,64]{3,2,1,0:T(8,128)} reshape(f32[4,8,1024]{2,1,0:T(8,128)} %get-tuple-element.15) | data formatting | bytes 262144 | tf_op jit(solution)/shard_map/reshape | solution.py:290
  78.8 1.1 fusion.11
  80.0 0.8 reshape.307.decay_ref
  80.8 1.7 %reshape.321.key_ref = f32[4,8,16,64]{3,2,1,0:T(8,128)} reshape(f32[4,8,1024]{2,1,0:T(8,128)} %get-tuple-element.16) | data formatting | bytes 262144 | tf_op jit(solution)/shard_map/reshape | solution.py:290
  82.5 0.8 reshape.319.recept_ref
  83.3 11.8 %shard_map.166 = (bf16[4,8,16,64]{3,2,1,0:T(8,128)(2,1)}, bf16[8,9,16,64]{3,2,1,0:T(8,128)(2,1)}) custom-call(f32[4,8,16,64]{3,2,1,0:T(8,128)} %reshape.319.recept_ref, f32[4,8,16,64]{3,2,1,0:T(8,128)} %reshape.321.key_ref, f32[4,8,16,64]{3,2,1,0:T(8,128)} %reshape.323.value_ref, f32[4,8,16,64]{3,2,1,0:T(8,128)} %reshape.307.decay_ref, ...), custom_call_target="tpu_custom_call" | custom-call | flops 805306368 | bytes 2965504 | tf_op jit(solution)/shard_map/pallas_call | solution.py:200
  95.1 1.0 broadcast_in_dim.23
  96.2 0.7 broadcast_in_dim.24
  96.9 5.0 %all-to-all-start.2 = ((bf16[4,4,8,1024]{3,2,1,0:T(8,128)(2,1)}), bf16[4,4,8,1024]{3,2,1,0:T(8,128)(2,1)}, u32[]{:S(2)}, u32[]{:S(2)}) async-start(bf16[4,4,8,1024]{3,2,1,0:T(8,128)(2,1)} %broadcast_in_dim.24), calls=%async_computation.2 | async-start | bytes 524288 | tf_op jit(solution)/shard_map/all_to_all | solution.py:72
  102.0 1.9 %copy.36 = bf16[8,16,9,64]{3,2,1,0:T(8,128)(2,1)} copy(bf16[8,16,9,64]{3,1,2,0:T(8,128)(2,1)} %bitcast.81) | data formatting | bytes 294912 | tf_op jit(solution)/shard_map/transpose | solution.py:313
  103.8 1.4 reshape_reshape.6
  105.2 1.5 %gather_fusion.5 = bf16[128,576]{1,0:T(8,128)(2,1)} fusion(bf16[128,576]{1,0:T(8,128)(2,1)S(1)} %reshape_reshape.6, s32[1024]{0:T(1024)S(1)} %pad_clamp_fusion.2), kind=kCustom, calls=%fused_computation.5 | custom fusion | bytes 295424 | tf_op jit(solution)/shard_map/jit(_take)/gather | solution.py:41
  106.7 4.5 %all-to-all-done.2 = bf16[4,4,8,1024]{3,2,1,0:T(8,128)(2,1)} async-done(((bf16[4,4,8,1024]{3,2,1,0:T(8,128)(2,1)}), bf16[4,4,8,1024]{3,2,1,0:T(8,128)(2,1)}, u32[]{:S(2)}, u32[]{:S(2)}) %all-to-all-start.2) | async-done | bytes 262176 | tf_op jit(solution)/shard_map/all_to_all | solution.py:72
  111.2 3.7 %all-to-all-start.5 = ((bf16[16,8,576]{2,1,0:T(8,128)(2,1)}), bf16[16,8,576]{2,1,0:T(8,128)(2,1)S(1)}, u32[]{:S(2)}, u32[]{:S(2)}) async-start(bf16[16,8,576]{2,1,0:T(8,128)(2,1)} %bitcast.26), calls=%async_computation.5 | async-start | bytes 327680 | tf_op jit(solution)/shard_map/all_to_all | solution.py:44
  114.9 1.0 fusion.25
  115.9 0.8 copy.33
  116.7 2.4 %gather_fusion = bf16[32,2,1024]{2,1,0:T(2,128)(2,1)} fusion(bf16[2,32,1024]{2,0,1:T(2,128)(2,1)} %bitcast.79, s32[1024]{0:T(1024)S(1)} %pad_clamp_fusion.4), kind=kCustom, calls=%fused_computation | custom fusion | bytes 262272 | tf_op jit(solution)/shard_map/jit(_take)/gather | solution.py:328
  119.1 0.9 copy.45
  120.0 0.4 fusion.6
  120.5 0.7 copy.44
  121.2 2.2 %all-to-all-done.5 = bf16[16,8,576]{2,1,0:T(8,128)(2,1)S(1)} async-done(((bf16[16,8,576]{2,1,0:T(8,128)(2,1)}), bf16[16,8,576]{2,1,0:T(8,128)(2,1)S(1)}, u32[]{:S(2)}, u32[]{:S(2)}) %all-to-all-start.5) | async-done | bytes 147488 | tf_op jit(solution)/shard_map/all_to_all | solution.py:44
  123.4 4.0 %all-to-all-start.3 = ((bf16[4,4,8,1024]{3,2,1,0:T(8,128)(2,1)}), bf16[4,4,8,1024]{3,2,1,0:T(8,128)(2,1)}, u32[]{:S(2)}, u32[]{:S(2)}) async-start(bf16[4,4,8,1024]{3,2,1,0:T(8,128)(2,1)} %bitcast.76), calls=%async_computation.3 | async-start | bytes 524288 | tf_op jit(solution)/shard_map/all_to_all | solution.py:65
  127.5 0.1 reshape.359
  127.6 2.2 %gather_fusion.4 = bf16[128,4096]{1,0:T(8,128)(2,1)} fusion(bf16[128,4096]{1,0:T(8,128)(2,1)S(1)} %bitcast.68, s32[1024]{0:T(1024)S(1)} %pad_clamp_fusion), kind=kCustom, calls=%fused_computation.4 | custom fusion | bytes 2097664 | tf_op jit(solution)/shard_map/jit(_take)/gather | solution.py:60
  129.8 0.9 gather_fusion.6
  130.7 0.2 reshape_reshape.7
  130.9 0.8 copy.43
  131.8 8.5 %shard_map.167 = f32[8,16,4096]{2,1,0:T(8,128)} custom-call(bf16[8,16,4096]{2,1,0:T(8,128)(2,1)} %bitcast.73, bf16[8,9,16,64]{3,2,1,0:T(8,128)(2,1)} %bitcast.75), custom_call_target="tpu_custom_call" | custom-call | flops 603979776 | bytes 3293184 | tf_op jit(solution)/shard_map/pallas_call | solution.py:105
  140.3 1.0 reduce_sum.32
  141.3 0.6 fusion.26
  (57 shorter events, 1.0 us)
Async XLA Ops:
  0.6 119.4 %copy-start = (bf16[1024,1024]{1,0:T(8,128)(2,1)S(1)}, bf16[1024,1024]{1,0:T(8,128)(2,1)}, u32[]{:S(2)}) copy-start(bf16[1024,1024]{1,0:T(8,128)(2,1)} %param.29) | copy-start | bytes 6291460
  2.7 1.1 copy-start.4
  2.8 1.1 slice-start.1
  3.8 7.5 %copy-start.5 = (f32[6,1024]{1,0:T(8,128)S(1)}, f32[6,1024]{1,0:T(8,128)}, u32[]{:S(2)}) copy-start(f32[6,1024]{1,0:T(8,128)} %param.19) | copy-start | bytes 73732
  5.0 16.6 %all-to-all-start = ((bf16[4,128,320]{1,2,0:T(8,128)(2,1)}), bf16[4,128,320]{1,2,0:T(8,128)(2,1)S(1)}, u32[]{:S(2)}, u32[]{:S(2)}) async-start(bf16[4,128,320]{1,2,0:T(8,128)(2,1)} %broadcast_in_dim.22), calls=%async_computation | async-start | bytes 655360 | tf_op jit(solution)/shard_map/all_to_all | solution.py:72
  23.4 5.3 %copy-start.3 = (bf16[5,128,1024]{2,1,0:T(8,128)(2,1)}, bf16[5,128,1024]{2,1,0:T(8,128)(2,1)S(1)}, u32[]{:S(2)}) copy-start(bf16[5,128,1024]{2,1,0:T(8,128)(2,1)S(1)} %add_convert_fusion) | copy-start | bytes 3932164
  30.5 1.9 %slice-start = ((bf16[5,128,1024]{2,1,0:T(8,128)(2,1)}), bf16[1,128,1024]{2,1,0:T(8,128)(2,1)S(1)}, s32[]{:S(2)}) async-start(bf16[5,128,1024]{2,1,0:T(8,128)(2,1)} %copy-done.3), calls=%async_computation.6 | async-start | bytes 524288 | tf_op jit(solution)/shard_map/slice | solution.py:281
  33.6 5.5 %copy-start.1 = (s32[32]{0:T(128)S(1)}, s32[32]{0:T(128)}, u32[]{:S(2)}) copy-start(s32[32]{0:T(128)} %param.18) | copy-start | bytes 388
  34.7 29.1 %all-to-all-start.1 = ((bf16[4,4,8,4224]{3,2,1,0:T(8,128)(2,1)}), bf16[4,4,8,4224]{3,2,1,0:T(8,128)(2,1)}, u32[]{:S(2)}, u32[]{:S(2)}) async-start(bf16[4,4,8,4224]{3,2,1,0:T(8,128)(2,1)} %pad_maximum_fusion), calls=%async_computation.1 | async-start | bytes 2162688 | tf_op jit(solution)/shard_map/all_to_all | solution.py:65
  45.2 26.3 %copy-start.6 = (f32[1024]{0:T(1024)S(1)}, f32[1024]{0:T(1024)}, u32[]{:S(2)}) copy-start(f32[1024]{0:T(1024)} %param.26) | copy-start | bytes 12292
  45.2 26.4 %copy-start.7 = (f32[1024]{0:T(1024)S(1)}, f32[1024]{0:T(1024)}, u32[]{:S(2)}) copy-start(f32[1024]{0:T(1024)} %param.27) | copy-start | bytes 12292
  45.2 26.4 %copy-start.8 = (f32[1024]{0:T(1024)S(1)}, f32[1024]{0:T(1024)}, u32[]{:S(2)}) copy-start(f32[1024]{0:T(1024)} %param.28) | copy-start | bytes 12292
  63.8 32.4 %all-to-all-start.4 = ((bf16[16,8,4096]{2,1,0:T(8,128)(2,1)}), bf16[16,8,4096]{2,1,0:T(8,128)(2,1)S(1)}, u32[]{:S(2)}, u32[]{:S(2)}) async-start(bf16[16,8,4096]{2,1,0:T(8,128)(2,1)} %bitcast.72), calls=%async_computation.4 | async-start | bytes 2097152 | tf_op jit(solution)/shard_map/all_to_all | solution.py:44
  74.8 0.8 copy-start.2
  83.3 18.5 %copy-start.9 = (s32[8]{0:T(128)S(1)}, s32[8]{0:T(128)}, u32[]{:S(2)}) copy-start(s32[8]{0:T(128)} %get-tuple-element.13) | copy-start | bytes 100
  96.9 14.3 %all-to-all-start.2 = ((bf16[4,4,8,1024]{3,2,1,0:T(8,128)(2,1)}), bf16[4,4,8,1024]{3,2,1,0:T(8,128)(2,1)}, u32[]{:S(2)}, u32[]{:S(2)}) async-start(bf16[4,4,8,1024]{3,2,1,0:T(8,128)(2,1)} %broadcast_in_dim.24), calls=%async_computation.2 | async-start | bytes 524288 | tf_op jit(solution)/shard_map/all_to_all | solution.py:72
  111.2 12.2 %all-to-all-start.5 = ((bf16[16,8,576]{2,1,0:T(8,128)(2,1)}), bf16[16,8,576]{2,1,0:T(8,128)(2,1)S(1)}, u32[]{:S(2)}, u32[]{:S(2)}) async-start(bf16[16,8,576]{2,1,0:T(8,128)(2,1)} %bitcast.26), calls=%async_computation.5 | async-start | bytes 327680 | tf_op jit(solution)/shard_map/all_to_all | solution.py:44
  123.4 16.9 %all-to-all-start.3 = ((bf16[4,4,8,1024]{3,2,1,0:T(8,128)(2,1)}), bf16[4,4,8,1024]{3,2,1,0:T(8,128)(2,1)}, u32[]{:S(2)}, u32[]{:S(2)}) async-start(bf16[4,4,8,1024]{3,2,1,0:T(8,128)(2,1)} %bitcast.76), calls=%async_computation.3 | async-start | bytes 524288 | tf_op jit(solution)/shard_map/all_to_all | solution.py:65

commit v6 on v5

--- a/solution.py
+++ b/solution.py
@@ -76,7 +76,7 @@
     return value.astype(jnp.bfloat16).astype(jnp.float32)
 
 
-def rebuild_kernel(steps, state_ref, terms_ref, out_ref, spread_ref, tile_ref):
+def fill_tables(spread_ref, tile_ref=None):
     extent = SUBSPACE_EXTENT
 
     @pl.when(pl.program_id(0) == 0)
@@ -84,43 +84,8 @@
         lane = lax.broadcasted_iota(jnp.int32, spread_ref.shape, 1)
         row = lax.broadcasted_iota(jnp.int32, spread_ref.shape, 0)
         spread_ref[...] = (lane // extent == row).astype(spread_ref.dtype)
-        tile_ref[...] = (lane % extent == row).astype(tile_ref.dtype)
-
-    spread = spread_ref[...]
-    tile = tile_ref[...]
-    total = jnp.dot(terms_ref[0], spread, preferred_element_type=jnp.float32) * state_ref[...].astype(
-        jnp.float32
-    )
-    for s in range(steps):
-        total = total + jnp.dot(
-            terms_ref[1 + s], spread, preferred_element_type=jnp.float32
-        ) * jnp.dot(terms_ref[1 + steps + s], tile, preferred_element_type=jnp.float32)
-    out_ref[...] = total
-
-
-def rebuild_state(moved_state, moved_terms, steps):
-    slots_dev, columns, flat = moved_state.shape
-    pieces = moved_terms.shape[1]
-    extent = SUBSPACE_EXTENT
-    return pl.pallas_call(
-        functools.partial(rebuild_kernel, steps),
-        grid=(slots_dev,),
-        in_specs=[
-            pl.BlockSpec((None, columns, flat), lambda n: (n, 0, 0)),
-            pl.BlockSpec((None, pieces, columns, extent), lambda n: (n, 0, 0, 0)),
-        ],
-        out_specs=pl.BlockSpec((None, columns, flat), lambda n: (n, 0, 0)),
-        out_shape=jax.ShapeDtypeStruct((slots_dev, columns, flat), jnp.float32),
-        scratch_shapes=[
-            pltpu.VMEM((extent, flat), jnp.bfloat16),
-            pltpu.VMEM((extent, flat), jnp.bfloat16),
-        ],
-        cost_estimate=pl.CostEstimate(
-            flops=2 * slots_dev * columns * extent * flat * (1 + 2 * steps),
-            transcendentals=0,
-            bytes_accessed=slots_dev * columns * (flat * 6 + pieces * extent * 2),
-        ),
-    )(moved_state, moved_terms)
+        if tile_ref is not None:
+            tile_ref[...] = (lane % extent == row).astype(tile_ref.dtype)
 
 
 def recurrence_kernel(
@@ -137,13 +102,7 @@
     spread_ref,
 ):
     extent = SUBSPACE_EXTENT
-
-    @pl.when(pl.program_id(0) == 0)
-    def _():
-        lane = lax.broadcasted_iota(jnp.int32, spread_ref.shape, 1)
-        row = lax.broadcasted_iota(jnp.int32, spread_ref.shape, 0)
-        spread_ref[...] = (lane // extent == row).astype(spread_ref.dtype)
-
+    fill_tables(spread_ref)
     spread = spread_ref[...]
     state = state_ref[...]
     premium = params_ref[0]
@@ -193,33 +152,78 @@
         payload_ref[1 + steps + s] = valued[s].astype(payload_ref.dtype)
 
 
+def row_block(rows):
+    return 64 if rows % 64 == 0 else rows
+
+
 def run_recurrence(projected, params, state):
     pieces = len(projected)
-    steps, local_rows, heads_here, extent = projected[0].shape
+    steps, rows, extent = projected[0].shape
     flat = state.shape[-1]
+    block = row_block(rows)
     return pl.pallas_call(
         functools.partial(recurrence_kernel, steps),
-        grid=(local_rows,),
+        grid=(rows // block,),
         in_specs=[
-            *[pl.BlockSpec((steps, None, heads_here, extent), lambda n: (0, n, 0, 0))] * pieces,
-            pl.BlockSpec((3, heads_here, extent), lambda n: (0, 0, 0)),
-            pl.BlockSpec((None, heads_here, flat), lambda n: (n, 0, 0)),
+            *[pl.BlockSpec((steps, block, extent), lambda n: (0, n, 0))] * pieces,
+            pl.BlockSpec((3, block, extent), lambda n: (0, n, 0)),
+            pl.BlockSpec((block, flat), lambda n: (n, 0)),
         ],
         out_specs=[
-            pl.BlockSpec((steps, None, heads_here, extent), lambda n: (0, n, 0, 0)),
-            pl.BlockSpec((None, 1 + 2 * steps, heads_here, extent), lambda n: (n, 0, 0, 0)),
+            pl.BlockSpec((steps, block, extent), lambda n: (0, n, 0)),
+            pl.BlockSpec((1 + 2 * steps, block, extent), lambda n: (0, n, 0)),
         ],
         out_shape=[
-            jax.ShapeDtypeStruct((steps, local_rows, heads_here, extent), jnp.bfloat16),
-            jax.ShapeDtypeStruct((local_rows, 1 + 2 * steps, heads_here, extent), jnp.bfloat16),
+            jax.ShapeDtypeStruct((steps, rows, extent), jnp.bfloat16),
+            jax.ShapeDtypeStruct((1 + 2 * steps, rows, extent), jnp.bfloat16),
         ],
         scratch_shapes=[pltpu.VMEM((extent, flat), jnp.bfloat16)],
         cost_estimate=pl.CostEstimate(
-            flops=2 * local_rows * heads_here * extent * flat * 3 * steps,
-            transcendentals=steps * local_rows * heads_here,
-            bytes_accessed=local_rows * heads_here * (flat * 4 + extent * (pieces * steps * 4 + steps * 2 + (1 + 2 * steps) * 2)),
+            flops=2 * rows * extent * flat * 3 * steps,
+            transcendentals=steps * rows,
+            bytes_accessed=rows * (flat * 4 + extent * (pieces * steps * 4 + 3 * 4 + steps * 2 + (1 + 2 * steps) * 2)),
         ),
     )(*projected, params, state)
+
+
+def rebuild_kernel(steps, state_ref, terms_ref, out_ref, spread_ref, tile_ref):
+    fill_tables(spread_ref, tile_ref)
+    spread = spread_ref[...]
+    tile = tile_ref[...]
+    total = jnp.dot(terms_ref[0], spread, preferred_element_type=jnp.float32) * state_ref[...].astype(
+        jnp.float32
+    )
+    for s in range(steps):
+        total = total + jnp.dot(
+            terms_ref[1 + s], spread, preferred_element_type=jnp.float32
+        ) * jnp.dot(terms_ref[1 + steps + s], tile, preferred_element_type=jnp.float32)
+    out_ref[...] = total
+
+
+def rebuild_state(moved_state, moved_terms, steps):
+    rows, flat = moved_state.shape
+    pieces = moved_terms.shape[0]
+    extent = SUBSPACE_EXTENT
+    block = row_block(rows)
+    return pl.pallas_call(
+        functools.partial(rebuild_kernel, steps),
+        grid=(rows // block,),
+        in_specs=[
+            pl.BlockSpec((block, flat), lambda n: (n, 0)),
+            pl.BlockSpec((pieces, block, extent), lambda n: (0, n, 0)),
+        ],
+        out_specs=pl.BlockSpec((block, flat), lambda n: (n, 0)),
+        out_shape=jax.ShapeDtypeStruct((rows, flat), jnp.float32),
+        scratch_shapes=[
+            pltpu.VMEM((extent, flat), jnp.bfloat16),
+            pltpu.VMEM((extent, flat), jnp.bfloat16),
+        ],
+        cost_estimate=pl.CostEstimate(
+            flops=2 * rows * extent * flat * (1 + 2 * steps),
+            transcendentals=0,
+            bytes_accessed=rows * (flat * 6 + pieces * extent * 2),
+        ),
+    )(moved_state, moved_terms)
 
 
 def per_device(
@@ -302,24 +306,40 @@
             )
         )
     )
-    projected = (recept, key_vec, valued, decay_rate, heads_of(gate_act))
-    params = jnp.stack([instant_premium, norming_multiplier, norming_intercept]).reshape(
-        3, heads_here, SUBSPACE_EXTENT
-    )
-    mixed_heads, payload = run_recurrence(projected, params, stream_kept_tableaux)
-    combined_response = mixed_heads.reshape(steps, local_rows, width)
-    pieces = payload.shape[1]
+    rows_here = local_rows * heads_here
+
+    def by_row(value):
+        return value.reshape(steps, rows_here, SUBSPACE_EXTENT)
+
+    projected = tuple(by_row(value) for value in (recept, key_vec, valued, decay_rate, gate_act))
+    params = jnp.broadcast_to(
+        jnp.stack([instant_premium, norming_multiplier, norming_intercept]).reshape(
+            3, 1, heads_here, SUBSPACE_EXTENT
+        ),
+        (3, local_rows, heads_here, SUBSPACE_EXTENT),
+    ).reshape(3, rows_here, SUBSPACE_EXTENT)
+    mixed_rows, payload = run_recurrence(
+        projected, params, stream_kept_tableaux.reshape(rows_here, -1)
+    )
+    combined_response = mixed_rows.reshape(steps, local_rows, width)
+    pieces = payload.shape[0]
     moved_terms = route_to_slots(
-        payload.transpose(0, 2, 1, 3).reshape(local_rows, heads_here, pieces * SUBSPACE_EXTENT),
+        payload.reshape(pieces, local_rows, heads_here, SUBSPACE_EXTENT)
+        .transpose(1, 2, 0, 3)
+        .reshape(local_rows, heads_here, pieces * SUBSPACE_EXTENT),
         position_mapping_target,
         batch_index,
         head_index,
     )
     slots_dev, columns, _ = moved_terms.shape
-    moved_terms = moved_terms.reshape(slots_dev, columns, pieces, SUBSPACE_EXTENT).transpose(
-        0, 2, 1, 3
-    )
-    final_state = rebuild_state(moved_state, moved_terms, steps)
+    moved_terms = (
+        moved_terms.reshape(slots_dev, columns, pieces, SUBSPACE_EXTENT)
+        .transpose(2, 0, 1, 3)
+        .reshape(pieces, slots_dev * columns, SUBSPACE_EXTENT)
+    )
+    final_state = rebuild_state(
+        moved_state.reshape(slots_dev * columns, -1), moved_terms, steps
+    ).reshape(slots_dev, columns, -1)
 
     gathered = exchange_copies(combined_response, "batch").transpose(1, 0, 2, 3)
     gathered = gathered.reshape(steps, sessions, width)

time: 143 us -> 136 us (0.951)
  Pallas kernels: 20.3 us -> 11.4 us
  local copies, waits for them, and re-layouts: 33.6 us -> 35.1 us
    pallas_call x2, Pallas kernels: 20.3 us -> 11.4 us  [the longest x1 6.4 us: run_recurrence(): pl.pallas_call(functools.partial(recurrence_kernel, steps), grid=(rows //...]
    another operation x0 -> x4, local copies, waits for them, and re-layouts: none -> 5.04 us  [by_row(): return value.reshape(steps, rows_here, SUBSPACE_EXTENT)]
    reshape x5 -> x2, local copies, waits for them, and re-layouts: 5.83 us -> 2.77 us  [the longest x1 1.98 us: per_device(): payload.reshape(pieces, local_rows, heads_here, SUBSPACE_EXTENT)]
  transfers between devices with their start and end apart: 6 -> 6, of which waited for: 4 -> 4; matrix products, arithmetic and copies ran while one was open for 27% -> 29% of each run, Pallas kernels for 14% -> 8%
where the time goes in v6:
time: 136 us; the launch traced here: 135 us
  waiting for transfers between devices  35.4 us (26%)
  local copies, waits for them, and re-layouts  35.1 us (26%)
  starting transfers between devices  27.3 us (20%)
  other arithmetic  14.4 us (11%)
  Pallas kernels  11.4 us (8%)
  matrix products  10.1 us (7%)
    all_to_all x2, waiting for transfers between devices, exchange_sum(): lax.all_to_all(pieces, axis_name, split_axis=0, concat_axis=0, tiled=True)  18.5 us
    all_to_all x2, waiting for transfers between devices, exchange_copies(): lax.all_to_all(copies, axis_name, split_axis=0, concat_axis=0, tiled=True)  14.7 us
    all_to_all x2, starting transfers between devices, exchange_copies(): lax.all_to_all(copies, axis_name, split_axis=0, concat_axis=0, tiled=True)  11.3 us
    all_to_all x2, starting transfers between devices, exchange_sum(): lax.all_to_all(pieces, axis_name, split_axis=0, concat_axis=0, tiled=True)  8.47 us
    all_to_all x2, starting transfers between devices, route_to_slots(): lax.all_to_all(packed, ('batch', 'head'), split_axis=0, concat_axis=0, ti...  7.52 us
    pallas_call x1, Pallas kernels, run_recurrence(): pl.pallas_call(functools.partial(recurrence_kernel, steps), grid=(rows //...  6.4 us
    dot_general x1, matrix products, per_device(): jnp.einsum('inf,ifc->nic', mixed[:4], fourfold_linear_maps, preferred_ele...  5.3 us
    another operation x4, local copies, waits for them, and re-layouts, by_row(): return value.reshape(steps, rows_here, SUBSPACE_EXTENT)  5.04 us
  transfers between devices with their start and end apart: 6, of which 4 were waited for; matrix products, arithmetic and copies ran while one was open for 29% of the time, Pallas kernels for 8%

profile of v6, /device:TPU:0, one launch (start us, length us, event | category | flops | bytes accessed | tf_op | source)
XLA Modules:
  0.0 134.6 jit_solution(210994383083301167)
XLA Ops:
  0.6 1.1 slice_bitcast_fusion
  1.7 1.0 convert_bitcast_fusion
  2.8 0.9 convert_bitcast_fusion.1
  3.9 0.4 convolution_convert_fusion.1
  4.3 0.8 broadcast_in_dim.26
  5.0 6.3 %all-to-all-start = ((bf16[4,128,320]{1,2,0:T(8,128)(2,1)}), bf16[4,128,320]{1,2,0:T(8,128)(2,1)S(1)}, u32[]{:S(2)}, u32[]{:S(2)}) async-start(bf16[4,128,320]{1,2,0:T(8,128)(2,1)} %broadcast_in_dim.26), calls=%async_computation | async-start | bytes 655360 | tf_op jit(solution)/shard_map/all_to_all | solution.py:72
  11.4 10.3 %all-to-all-done = bf16[4,128,320]{1,2,0:T(8,128)(2,1)S(1)} async-done(((bf16[4,128,320]{1,2,0:T(8,128)(2,1)}), bf16[4,128,320]{1,2,0:T(8,128)(2,1)S(1)}, u32[]{:S(2)}, u32[]{:S(2)}) %all-to-all-start) | async-done | bytes 327712 | tf_op jit(solution)/shard_map/all_to_all | solution.py:72
  21.8 1.7 %add_convert_fusion = bf16[5,128,1024]{2,1,0:T(8,128)(2,1)S(1)} fusion(bf16[128,5,64]{0,2,1:T(8,128)(2,1)S(1)} %bitcast.88, bf16[5,64,1024]{2,1,0:T(8,128)(2,1)} %param.21, f32[5,1024]{1,0:T(8,128)S(1)} %slice.52, f32[128,1024]{1,0:T(8,128)S(1)} %bitcast_subtract_fusion, f32[128,1024]{1,0:T(8,128)S(1)} %bitcast.76), kind=kOutput, calls=%fused_computation.7 | convolution fusion | flops 86507520 | bytes 3117056 | tf_op jit(solution)/shard_map/nim,imd->ind/dot_general | solution.py:276
  23.4 5.3 %fusion.2 = bf16[128,4,1024]{2,0,1:T(8,128)(2,1)S(1)} fusion(bf16[5,128,1024]{2,1,0:T(8,128)(2,1)S(1)} %add_convert_fusion, bf16[4,1024,1024]{2,1,0:T(8,128)(2,1)} %param.22), kind=kOutput, calls=%fused_computation.12 | convolution fusion | flops 1074266112 | bytes 10747904 | tf_op jit(solution)/shard_map/inf,ifc->nic/dot_general | solution.py:282
  28.8 1.8 %copy.33 = bf16[128,4,1024]{2,1,0:T(4,128)(2,1)} copy(bf16[128,4,1024]{2,0,1:T(8,128)(2,1)S(1)} %fusion.2) | data formatting | bytes 2097152 | tf_op jit(solution)/shard_map/inf,ifc->nic/transpose | solution.py:282
  30.6 1.9 %concatenate.22 = bf16[4,4,8,4096]{3,2,1,0:T(8,128)(2,1)S(1)} reshape(bf16[128,4,1024]{2,1,0:T(4,128)(2,1)} %copy.33) | data formatting | bytes 2097152 | tf_op jit(solution)/shard_map/concatenate | solution.py:287
  32.4 1.2 convolution_convert_fusion.2
  33.6 1.1 pad_maximum_fusion
  34.7 4.3 %all-to-all-start.1 = ((bf16[4,4,8,4224]{3,2,1,0:T(8,128)(2,1)}), bf16[4,4,8,4224]{3,2,1,0:T(8,128)(2,1)}, u32[]{:S(2)}, u32[]{:S(2)}) async-start(bf16[4,4,8,4224]{3,2,1,0:T(8,128)(2,1)} %pad_maximum_fusion), calls=%async_computation.1 | async-start | bytes 2162688 | tf_op jit(solution)/shard_map/all_to_all | solution.py:65
  39.0 0.1 reshape.323
  39.1 0.1 and_select_fusion.6
  39.2 1.0 sort.75
  40.2 0.7 gather_fusion.1
  41.1 0.1 iota_add_fusion.1
  41.2 0.1 reshape.331
  41.3 1.7 %convert_element_type.89 = bf16[8,16,4096]{2,1,0:T(8,128)(2,1)S(1)} convert(f32[8,16,4096]{2,1,0:T(8,128)} %param.17) | non-fusion elementwise | flops 524288 | bytes 3145728 | tf_op jit(solution)/shard_map/convert_element_type | solution.py:257
  43.0 2.2 %gather_fusion.2 = bf16[128,4096]{1,0:T(8,128)(2,1)} fusion(bf16[128,4096]{1,0:T(8,128)(2,1)S(1)} %bitcast.71, s32[1024]{0:T(1024)S(1)} %pad_clamp_fusion.2), kind=kCustom, calls=%fused_computation.2 | custom fusion | bytes 2097664 | tf_op jit(solution)/shard_map/jit(_take)/gather | solution.py:41
  45.2 18.5 %all-to-all-done.1 = bf16[4,4,8,4224]{3,2,1,0:T(8,128)(2,1)} async-done(((bf16[4,4,8,4224]{3,2,1,0:T(8,128)(2,1)}), bf16[4,4,8,4224]{3,2,1,0:T(8,128)(2,1)}, u32[]{:S(2)}, u32[]{:S(2)}) %all-to-all-start.1) | async-done | bytes 1081376 | tf_op jit(solution)/shard_map/all_to_all | solution.py:65
  63.8 3.8 %all-to-all-start.4 = ((bf16[16,8,4096]{2,1,0:T(8,128)(2,1)}), bf16[16,8,4096]{2,1,0:T(8,128)(2,1)S(1)}, u32[]{:S(2)}, u32[]{:S(2)}) async-start(bf16[16,8,4096]{2,1,0:T(8,128)(2,1)} %bitcast.77), calls=%async_computation.4 | async-start | bytes 2097152 | tf_op jit(solution)/shard_map/all_to_all | solution.py:44
  67.6 1.6 %sort.76 = (s32[32]{0:T(128)}, s32[32]{0:T(128)S(1)}) sort(s32[32]{0:T(128)S(1)} %and_select_fusion.3, s32[32]{0:T(128)S(1)} %iota.54), dimensions={0}, to_apply=%region_5.6 | sort | flops 160 | bytes 512 | tf_op jit(solution)/shard_map/jit(argsort)/sort | solution.py:47
  69.3 1.6 %sort.74 = (s32[32]{0:T(128)}, s32[32]{0:T(128)S(1)}) sort(s32[32]{0:T(128)S(1)} %copy-done.1, s32[32]{0:T(128)S(1)} %iota.51), dimensions={0}, to_apply=%region_2.3 | sort | flops 160 | bytes 512 | tf_op jit(solution)/shard_map/jit(argsort)/sort | solution.py:346
  70.9 0.6 gather_fusion.3
  71.8 1.0 sort.77
  72.7 0.6 maximum_bitcast_fusion
  73.3 1.4 %convert_reduce_fusion = f32[4,8,4224]{2,1,0:T(8,128)S(1)} fusion(bf16[4,4,8,4224]{3,2,1,0:T(8,128)(2,1)} %all-to-all-done.1), kind=kLoop, calls=%fused_computation.8 | loop fusion | flops 946176 | bytes 1622016 | tf_op jit(solution)/shard_map/reduce_sum | solution.py:66
  74.8 0.8 copy-done.2
  75.6 0.8 reshape.295.gate_ref
  76.4 0.7 slice_convert_fusion
  77.1 1.7 %reshape.311.value_ref = f32[4,128,64]{2,1,0:T(8,128)} reshape(f32[4,8,1024]{2,1,0:T(8,128)} %get-tuple-element.15) | data formatting | bytes 262144 | tf_op jit(solution)/shard_map/reshape;reshape | solution.py:312
  78.8 1.1 fusion.11
  80.0 0.8 reshape_reshape.30.decay_ref
  80.8 1.7 %reshape.310.key_ref = f32[4,128,64]{2,1,0:T(8,128)} reshape(f32[4,8,1024]{2,1,0:T(8,128)} %get-tuple-element.16) | data formatting | bytes 262144 | tf_op jit(solution)/shard_map/reshape;reshape | solution.py:312
  82.5 0.8 reshape.309.recept_ref
  83.3 1.4 %broadcast_in_dim.28 = f32[3,8,16,64]{3,2,1,0:T(8,128)} broadcast(f32[3,16,64]{2,1,0:T(8,128)} %maximum_bitcast_fusion), dimensions={0,2,3} | broadcast | bytes 110592 | tf_op jit(solution)/shard_map/broadcast_in_dim | solution.py:315
  84.8 6.4 %shard_map.166 = (bf16[4,128,64]{2,1,0:T(8,128)(2,1)}, bf16[9,128,64]{2,1,0:T(8,128)(2,1)}) custom-call(f32[4,128,64]{2,1,0:T(8,128)} %reshape.309.recept_ref, f32[4,128,64]{2,1,0:T(8,128)} %reshape.310.key_ref, f32[4,128,64]{2,1,0:T(8,128)} %reshape.311.value_ref, f32[4,128,64]{2,1,0:T(8,128)} %reshape_reshape.30.decay_ref, ...), custom_call_target="tpu_custom_call" | custom-call | flops 805306368 | bytes 3063808 | tf_op jit(solution)/shard_map/pallas_call | solution.py:164
  91.2 1.0 broadcast_in_dim.29
  92.2 0.7 broadcast_in_dim.30
  92.9 5.0 %all-to-all-start.2 = ((bf16[4,4,8,1024]{3,2,1,0:T(8,128)(2,1)}), bf16[4,4,8,1024]{3,2,1,0:T(8,128)(2,1)}, u32[]{:S(2)}, u32[]{:S(2)}) async-start(bf16[4,4,8,1024]{3,2,1,0:T(8,128)(2,1)} %broadcast_in_dim.30), calls=%async_computation.2 | async-start | bytes 524288 | tf_op jit(solution)/shard_map/all_to_all | solution.py:72
  98.0 2.0 %copy.45 = bf16[9,8,16,64]{3,0,2,1:T(8,128)(2,1)} copy(bf16[9,8,16,64]{3,2,1,0:T(8,128)(2,1)} %bitcast.89) | data formatting | bytes 294912 | tf_op jit(solution)/shard_map/reshape | solution.py:327
  100.0 1.4 %reshape_reshape.31 = bf16[128,576]{1,0:T(8,128)(2,1)S(1)} reshape(bf16[8,16,9,64]{3,2,1,0:T(8,128)(2,1)} %bitcast.79) | data formatting | bytes 294912 | tf_op jit(solution)/shard_map/reshape;reshape | solution.py:42
  101.3 1.5 %gather_fusion.5 = bf16[128,576]{1,0:T(8,128)(2,1)} fusion(bf16[128,576]{1,0:T(8,128)(2,1)S(1)} %reshape_reshape.31, s32[1024]{0:T(1024)S(1)} %pad_clamp_fusion.2), kind=kCustom, calls=%fused_computation.5 | custom fusion | bytes 295424 | tf_op jit(solution)/shard_map/jit(_take)/gather | solution.py:41
  102.9 4.4 %all-to-all-done.2 = bf16[4,4,8,1024]{3,2,1,0:T(8,128)(2,1)} async-done(((bf16[4,4,8,1024]{3,2,1,0:T(8,128)(2,1)}), bf16[4,4,8,1024]{3,2,1,0:T(8,128)(2,1)}, u32[]{:S(2)}, u32[]{:S(2)}) %all-to-all-start.2) | async-done | bytes 262176 | tf_op jit(solution)/shard_map/all_to_all | solution.py:72
  107.3 3.7 %all-to-all-start.5 = ((bf16[16,8,576]{2,1,0:T(8,128)(2,1)}), bf16[16,8,576]{2,1,0:T(8,128)(2,1)S(1)}, u32[]{:S(2)}, u32[]{:S(2)}) async-start(bf16[16,8,576]{2,1,0:T(8,128)(2,1)} %bitcast.29), calls=%async_computation.5 | async-start | bytes 327680 | tf_op jit(solution)/shard_map/all_to_all | solution.py:44
  111.0 1.0 fusion.25
  112.0 0.8 copy.35
  112.8 2.4 %gather_fusion = bf16[32,2,1024]{2,1,0:T(2,128)(2,1)} fusion(bf16[2,32,1024]{2,0,1:T(2,128)(2,1)} %bitcast.87, s32[1024]{0:T(1024)S(1)} %pad_clamp_fusion.4), kind=kCustom, calls=%fused_computation | custom fusion | bytes 262272 | tf_op jit(solution)/shard_map/jit(_take)/gather | solution.py:348
  115.1 0.9 copy.47
  116.1 0.4 fusion.6
  116.5 0.7 copy.46
  117.3 2.2 %all-to-all-done.5 = bf16[16,8,576]{2,1,0:T(8,128)(2,1)S(1)} async-done(((bf16[16,8,576]{2,1,0:T(8,128)(2,1)}), bf16[16,8,576]{2,1,0:T(8,128)(2,1)S(1)}, u32[]{:S(2)}, u32[]{:S(2)}) %all-to-all-start.5) | async-done | bytes 147488 | tf_op jit(solution)/shard_map/all_to_all | solution.py:44
  119.5 4.2 %all-to-all-start.3 = ((bf16[4,4,8,1024]{3,2,1,0:T(8,128)(2,1)}), bf16[4,4,8,1024]{3,2,1,0:T(8,128)(2,1)}, u32[]{:S(2)}, u32[]{:S(2)}) async-start(bf16[4,4,8,1024]{3,2,1,0:T(8,128)(2,1)} %bitcast.83), calls=%async_computation.3 | async-start | bytes 524288 | tf_op jit(solution)/shard_map/all_to_all | solution.py:65
  123.8 0.1 reshape.347
  123.9 2.2 %gather_fusion.4 = bf16[128,4096]{1,0:T(8,128)(2,1)} fusion(bf16[128,4096]{1,0:T(8,128)(2,1)S(1)} %bitcast.72, s32[1024]{0:T(1024)S(1)} %pad_clamp_fusion), kind=kCustom, calls=%fused_computation.4 | custom fusion | bytes 2097664 | tf_op jit(solution)/shard_map/jit(_take)/gather | solution.py:60
  126.1 0.9 gather_fusion.6
  127.0 0.2 reshape_reshape.32
  127.2 0.8 copy.39
  128.0 5.0 %shard_map.167 = f32[128,4096]{1,0:T(8,128)} custom-call(bf16[128,4096]{1,0:T(8,128)(2,1)} %gather_fusion.4, bf16[9,128,64]{2,1,0:T(8,128)(2,1)} %bitcast.82), custom_call_target="tpu_custom_call" | custom-call | flops 603979776 | bytes 3293184 | tf_op jit(solution)/shard_map/pallas_call | solution.py:208
  133.0 1.0 reduce_sum.32
  134.0 0.6 fusion.26
  (58 shorter events, 1.1 us)
Async XLA Ops:
  0.6 115.4 %copy-start = (bf16[1024,1024]{1,0:T(8,128)(2,1)S(1)}, bf16[1024,1024]{1,0:T(8,128)(2,1)}, u32[]{:S(2)}) copy-start(bf16[1024,1024]{1,0:T(8,128)(2,1)} %param.29) | copy-start | bytes 6291460
  2.7 1.1 copy-start.4
  2.8 1.1 slice-start.1
  3.8 7.5 %copy-start.5 = (f32[6,1024]{1,0:T(8,128)S(1)}, f32[6,1024]{1,0:T(8,128)}, u32[]{:S(2)}) copy-start(f32[6,1024]{1,0:T(8,128)} %param.19) | copy-start | bytes 73732
  5.0 16.6 %all-to-all-start = ((bf16[4,128,320]{1,2,0:T(8,128)(2,1)}), bf16[4,128,320]{1,2,0:T(8,128)(2,1)S(1)}, u32[]{:S(2)}, u32[]{:S(2)}) async-start(bf16[4,128,320]{1,2,0:T(8,128)(2,1)} %broadcast_in_dim.26), calls=%async_computation | async-start | bytes 655360 | tf_op jit(solution)/shard_map/all_to_all | solution.py:72
  23.4 5.3 %copy-start.3 = (bf16[5,128,1024]{2,1,0:T(8,128)(2,1)}, bf16[5,128,1024]{2,1,0:T(8,128)(2,1)S(1)}, u32[]{:S(2)}) copy-start(bf16[5,128,1024]{2,1,0:T(8,128)(2,1)S(1)} %add_convert_fusion) | copy-start | bytes 3932164
  30.6 1.9 %slice-start = ((bf16[5,128,1024]{2,1,0:T(8,128)(2,1)}), bf16[1,128,1024]{2,1,0:T(8,128)(2,1)S(1)}, s32[]{:S(2)}) async-start(bf16[5,128,1024]{2,1,0:T(8,128)(2,1)} %copy-done.3), calls=%async_computation.6 | async-start | bytes 524288 | tf_op jit(solution)/shard_map/slice | solution.py:285
  33.6 5.5 %copy-start.1 = (s32[32]{0:T(128)S(1)}, s32[32]{0:T(128)}, u32[]{:S(2)}) copy-start(s32[32]{0:T(128)} %param.18) | copy-start | bytes 388
  34.7 29.1 %all-to-all-start.1 = ((bf16[4,4,8,4224]{3,2,1,0:T(8,128)(2,1)}), bf16[4,4,8,4224]{3,2,1,0:T(8,128)(2,1)}, u32[]{:S(2)}, u32[]{:S(2)}) async-start(bf16[4,4,8,4224]{3,2,1,0:T(8,128)(2,1)} %pad_maximum_fusion), calls=%async_computation.1 | async-start | bytes 2162688 | tf_op jit(solution)/shard_map/all_to_all | solution.py:65
  45.2 26.3 %copy-start.6 = (f32[1024]{0:T(1024)S(1)}, f32[1024]{0:T(1024)}, u32[]{:S(2)}) copy-start(f32[1024]{0:T(1024)} %param.26) | copy-start | bytes 12292
  45.2 26.4 %copy-start.7 = (f32[1024]{0:T(1024)S(1)}, f32[1024]{0:T(1024)}, u32[]{:S(2)}) copy-start(f32[1024]{0:T(1024)} %param.27) | copy-start | bytes 12292
  45.2 26.4 %copy-start.8 = (f32[1024]{0:T(1024)S(1)}, f32[1024]{0:T(1024)}, u32[]{:S(2)}) copy-start(f32[1024]{0:T(1024)} %param.28) | copy-start | bytes 12292
  63.8 28.4 %all-to-all-start.4 = ((bf16[16,8,4096]{2,1,0:T(8,128)(2,1)}), bf16[16,8,4096]{2,1,0:T(8,128)(2,1)S(1)}, u32[]{:S(2)}, u32[]{:S(2)}) async-start(bf16[16,8,4096]{2,1,0:T(8,128)(2,1)} %bitcast.77), calls=%async_computation.4 | async-start | bytes 2097152 | tf_op jit(solution)/shard_map/all_to_all | solution.py:44
  74.8 0.8 copy-start.2
  84.8 13.2 %copy-start.9 = (s32[8]{0:T(128)S(1)}, s32[8]{0:T(128)}, u32[]{:S(2)}) copy-start(s32[8]{0:T(128)} %get-tuple-element.13) | copy-start | bytes 100
  92.9 14.3 %all-to-all-start.2 = ((bf16[4,4,8,1024]{3,2,1,0:T(8,128)(2,1)}), bf16[4,4,8,1024]{3,2,1,0:T(8,128)(2,1)}, u32[]{:S(2)}, u32[]{:S(2)}) async-start(bf16[4,4,8,1024]{3,2,1,0:T(8,128)(2,1)} %broadcast_in_dim.30), calls=%async_computation.2 | async-start | bytes 524288 | tf_op jit(solution)/shard_map/all_to_all | solution.py:72
  107.3 12.2 %all-to-all-start.5 = ((bf16[16,8,576]{2,1,0:T(8,128)(2,1)}), bf16[16,8,576]{2,1,0:T(8,128)(2,1)S(1)}, u32[]{:S(2)}, u32[]{:S(2)}) async-start(bf16[16,8,576]{2,1,0:T(8,128)(2,1)} %bitcast.29), calls=%async_computation.5 | async-start | bytes 327680 | tf_op jit(solution)/shard_map/all_to_all | solution.py:44
  119.5 13.6 %all-to-all-start.3 = ((bf16[4,4,8,1024]{3,2,1,0:T(8,128)(2,1)}), bf16[4,4,8,1024]{3,2,1,0:T(8,128)(2,1)}, u32[]{:S(2)}, u32[]{:S(2)}) async-start(bf16[4,4,8,1024]{3,2,1,0:T(8,128)(2,1)} %bitcast.83), calls=%async_computation.3 | async-start | bytes 524288 | tf_op jit(solution)/shard_map/all_to_all | solution.py:65

commit v7 on v6

--- a/solution.py
+++ b/solution.py
@@ -90,11 +90,8 @@
 
 def recurrence_kernel(
     steps,
-    recept_ref,
-    key_ref,
-    value_ref,
+    fourway_ref,
     decay_ref,
-    gate_ref,
     params_ref,
     state_ref,
     mixed_ref,
@@ -108,9 +105,9 @@
     premium = params_ref[0]
     gain = params_ref[1]
     bias = params_ref[2]
-    recept = [recept_ref[t] for t in range(steps)]
-    key_vec = [key_ref[t] for t in range(steps)]
-    valued = [value_ref[t] for t in range(steps)]
+    recept = [widen(fourway_ref[0, t]) for t in range(steps)]
+    key_vec = [widen(fourway_ref[1, t]) for t in range(steps)]
+    valued = [widen(fourway_ref[2, t]) for t in range(steps)]
     decay_rate = [decay_ref[t] for t in range(steps)]
     flat = state.shape[-1]
     prefix = jnp.ones_like(recept[0])
@@ -141,7 +138,9 @@
         demeaned = total - average
         spread_squared = jnp.mean(demeaned * demeaned, axis=-1, keepdims=True)
         standardized = demeaned * lax.rsqrt(spread_squared + NORMALIZER_GUARD) * gain + bias
-        mixed_ref[t] = (standardized * gate_ref[t]).astype(mixed_ref.dtype)
+        gate_value = fourway_ref[3, t]
+        gate_act = gate_value / (1.0 + jnp.exp(-gate_value))
+        mixed_ref[t] = (standardized * gate_act).astype(mixed_ref.dtype)
         prefix = prefix * decay_rate[t]
     payload_ref[0] = prefix.astype(payload_ref.dtype)
     for s in range(steps):
@@ -156,16 +155,17 @@
     return 64 if rows % 64 == 0 else rows
 
 
-def run_recurrence(projected, params, state):
-    pieces = len(projected)
-    steps, rows, extent = projected[0].shape
+def run_recurrence(fourway, decay_rate, params, state):
+    pieces = fourway.shape[0] + 1
+    steps, rows, extent = decay_rate.shape
     flat = state.shape[-1]
     block = row_block(rows)
     return pl.pallas_call(
         functools.partial(recurrence_kernel, steps),
         grid=(rows // block,),
         in_specs=[
-            *[pl.BlockSpec((steps, block, extent), lambda n: (0, n, 0))] * pieces,
+            pl.BlockSpec((pieces - 1, steps, block, extent), lambda n: (0, 0, n, 0)),
+            pl.BlockSpec((steps, block, extent), lambda n: (0, n, 0)),
             pl.BlockSpec((3, block, extent), lambda n: (0, n, 0)),
             pl.BlockSpec((block, flat), lambda n: (n, 0)),
         ],
@@ -183,7 +183,7 @@
             transcendentals=steps * rows,
             bytes_accessed=rows * (flat * 4 + extent * (pieces * steps * 4 + 3 * 4 + steps * 2 + (1 + 2 * steps) * 2)),
         ),
-    )(*projected, params, state)
+    )(fourway, decay_rate, params, state)
 
 
 def rebuild_kernel(steps, state_ref, terms_ref, out_ref, spread_ref, tile_ref):
@@ -253,9 +253,6 @@
     f32 = jnp.float32
     bf16 = jnp.bfloat16
 
-    moved_state = route_to_slots(
-        stream_kept_tableaux.astype(bf16), position_mapping_target, batch_index, head_index
-    )
 
     previous = jnp.concatenate([preceding_feed_each_stream[None], tier_feed_tensor[:-1]], axis=0)
 
@@ -290,13 +287,14 @@
         "batch",
     )
 
+    kept_for_move, aggregated = lax.optimization_barrier((stream_kept_tableaux, aggregated))
+    moved_state = route_to_slots(
+        kept_for_move.astype(bf16), position_mapping_target, batch_index, head_index
+    )
+
     def heads_of(value):
         return value.reshape(steps, local_rows, heads_here, SUBSPACE_EXTENT)
 
-    recept = heads_of(widen(aggregated[..., :width]))
-    key_vec = heads_of(widen(aggregated[..., width : 2 * width]))
-    valued = heads_of(widen(aggregated[..., 2 * width : 3 * width]))
-    gate_act = jax.nn.silu(aggregated[..., 3 * width : 4 * width])
     low_rank = jnp.tanh(aggregated[..., 4 * width :]).astype(bf16)
     decay_rate = heads_of(
         jnp.exp(
@@ -311,7 +309,12 @@
     def by_row(value):
         return value.reshape(steps, rows_here, SUBSPACE_EXTENT)
 
-    projected = tuple(by_row(value) for value in (recept, key_vec, valued, decay_rate, gate_act))
+    fourway = (
+        aggregated[..., : 4 * width]
+        .reshape(steps, local_rows, 4, heads_here, SUBSPACE_EXTENT)
+        .transpose(2, 0, 1, 3, 4)
+        .reshape(4, steps, rows_here, SUBSPACE_EXTENT)
+    )
     params = jnp.broadcast_to(
         jnp.stack([instant_premium, norming_multiplier, norming_intercept]).reshape(
             3, 1, heads_here, SUBSPACE_EXTENT
@@ -319,8 +322,9 @@
         (3, local_rows, heads_here, SUBSPACE_EXTENT),
     ).reshape(3, rows_here, SUBSPACE_EXTENT)
     mixed_rows, payload = run_recurrence(
-        projected, params, stream_kept_tableaux.reshape(rows_here, -1)
-    )
+        fourway, by_row(decay_rate), params, stream_kept_tableaux.reshape(rows_here, -1)
+    )
+    moved_state, mixed_rows, payload = lax.optimization_barrier((moved_state, mixed_rows, payload))
     combined_response = mixed_rows.reshape(steps, local_rows, width)
     pieces = payload.shape[0]
     moved_terms = route_to_slots(
@@ -337,6 +341,7 @@
         .transpose(2, 0, 1, 3)
         .reshape(pieces, slots_dev * columns, SUBSPACE_EXTENT)
     )
+    combined_response, moved_terms = lax.optimization_barrier((combined_response, moved_terms))
     final_state = rebuild_state(
         moved_state.reshape(slots_dev * columns, -1), moved_terms, steps
     ).reshape(slots_dev, columns, -1)

time: 136 us -> 143 us (1.051)
  waiting for transfers between devices: 35.4 us -> 51.9 us
  local copies, waits for them, and re-layouts: 35.1 us -> 27.5 us
  other arithmetic: 14.4 us -> 12.1 us
    all_to_all x2, waiting for transfers between devices: 2.2 us -> 11.4 us  [route_to_slots(): lax.all_to_all(packed, ('batch', 'head'), split_axis=0, concat_axis=0, ti...]
    all_to_all x2, waiting for transfers between devices: 18.5 us -> 23.4 us  [exchange_sum(): lax.all_to_all(pieces, axis_name, split_axis=0, concat_axis=0, tiled=True)]
    another operation x4 -> x1, local copies, waits for them, and re-layouts: 5.04 us -> 0.83 us  [by_row(): return value.reshape(steps, rows_here, SUBSPACE_EXTENT)]
    reshape x1 -> x3, local copies, waits for them, and re-layouts: 0.79 us -> 4.95 us  [the longest x2 4.81 us: per_device(): fourway = aggregated[..., :4 * width].reshape(steps, local_rows, 4, heads...]
    all_to_all x2, starting transfers between devices: 7.52 us -> 10.8 us  [route_to_slots(): lax.all_to_all(packed, ('batch', 'head'), split_axis=0, concat_axis=0, ti...]
    all_to_all x2, waiting for transfers between devices: 14.7 us -> 17.1 us  [exchange_copies(): lax.all_to_all(copies, axis_name, split_axis=0, concat_axis=0, tiled=True)]
    gather x2, local copies, waits for them, and re-layouts: 3.29 us -> 0.84 us  [per_device(): jnp.take(gathered[STEPS_A:], inverse, axis=1, mode='clip')]
    slice x0 -> x1, local copies, waits for them, and re-layouts: none -> 1.89 us  [per_device(): aggregated[..., :4 * width]]
  transfers between devices with their start and end apart: 6 -> 6, of which waited for: 4 -> 6; matrix products, arithmetic and copies ran while one was open for 29% -> 12% of each run, Pallas kernels for 8% -> 8%
where the time goes in v7:
time: 143 us; the launch traced here: 141 us
  waiting for transfers between devices  51.9 us (36%)
  starting transfers between devices  27.6 us (19%)
  local copies, waits for them, and re-layouts  27.5 us (19%)
  other arithmetic  12.1 us (8%)
  Pallas kernels  11.3 us (8%)
  matrix products  9.93 us (7%)
    all_to_all x2, waiting for transfers between devices, exchange_sum(): lax.all_to_all(pieces, axis_name, split_axis=0, concat_axis=0, tiled=True)  23.4 us
    all_to_all x2, waiting for transfers between devices, exchange_copies(): lax.all_to_all(copies, axis_name, split_axis=0, concat_axis=0, tiled=True)  17.1 us
    all_to_all x2, waiting for transfers between devices, route_to_slots(): lax.all_to_all(packed, ('batch', 'head'), split_axis=0, concat_axis=0, ti...  11.4 us
    all_to_all x2, starting transfers between devices, route_to_slots(): lax.all_to_all(packed, ('batch', 'head'), split_axis=0, concat_axis=0, ti...  10.8 us
    all_to_all x2, starting transfers between devices, exchange_copies(): lax.all_to_all(copies, axis_name, split_axis=0, concat_axis=0, tiled=True)  9.9 us
    all_to_all x2, starting transfers between devices, exchange_sum(): lax.all_to_all(pieces, axis_name, split_axis=0, concat_axis=0, tiled=True)  6.92 us
    pallas_call x1, Pallas kernels, run_recurrence(): pl.pallas_call(functools.partial(recurrence_kernel, steps), grid=(rows //...  6.3 us
    dot_general x1, matrix products, per_device(): jnp.einsum('inf,ifc->nic', mixed[:4], fourfold_linear_maps, preferred_ele...  5.34 us
  transfers between devices with their start and end apart: 6, of which 6 were waited for; matrix products, arithmetic and copies ran while one was open for 12% of the time, Pallas kernels for 8%

profile of v7, /device:TPU:0, one launch (start us, length us, event | category | flops | bytes accessed | tf_op | source)
XLA Modules:
  0.0 141.5 jit_solution(401092127597751544)
XLA Ops:
  0.6 1.1 slice_bitcast_fusion
  1.7 1.0 convert_bitcast_fusion
  2.8 0.9 convert_bitcast_fusion.1
  3.9 0.4 convolution_convert_fusion.1
  4.3 0.8 broadcast_in_dim.24
  5.0 6.3 %all-to-all-start = ((bf16[4,128,320]{1,2,0:T(8,128)(2,1)}), bf16[4,128,320]{1,2,0:T(8,128)(2,1)S(1)}, u32[]{:S(2)}, u32[]{:S(2)}) async-start(bf16[4,128,320]{1,2,0:T(8,128)(2,1)} %broadcast_in_dim.24), calls=%async_computation | async-start | bytes 655360 | tf_op jit(solution)/shard_map/all_to_all | solution.py:72
  11.4 10.3 %all-to-all-done = bf16[4,128,320]{1,2,0:T(8,128)(2,1)S(1)} async-done(((bf16[4,128,320]{1,2,0:T(8,128)(2,1)}), bf16[4,128,320]{1,2,0:T(8,128)(2,1)S(1)}, u32[]{:S(2)}, u32[]{:S(2)}) %all-to-all-start) | async-done | bytes 327712 | tf_op jit(solution)/shard_map/all_to_all | solution.py:72
  21.8 1.7 %add_convert_fusion = bf16[5,128,1024]{2,1,0:T(8,128)(2,1)S(1)} fusion(bf16[128,5,64]{0,2,1:T(8,128)(2,1)S(1)} %bitcast.94, bf16[5,64,1024]{2,1,0:T(8,128)(2,1)} %param.21, f32[5,1024]{1,0:T(8,128)S(1)} %slice.40, f32[128,1024]{1,0:T(8,128)S(1)} %bitcast_subtract_fusion, f32[128,1024]{1,0:T(8,128)S(1)} %bitcast.81), kind=kOutput, calls=%fused_computation.7 | convolution fusion | flops 86507520 | bytes 3117056 | tf_op jit(solution)/shard_map/nim,imd->ind/dot_general | solution.py:273
  23.5 5.3 %fusion.2 = bf16[128,4,1024]{2,0,1:T(8,128)(2,1)S(1)} fusion(bf16[5,128,1024]{2,1,0:T(8,128)(2,1)S(1)} %add_convert_fusion, bf16[4,1024,1024]{2,1,0:T(8,128)(2,1)} %param.22), kind=kOutput, calls=%fused_computation.12 | convolution fusion | flops 1074266112 | bytes 10747904 | tf_op jit(solution)/shard_map/inf,ifc->nic/dot_general | solution.py:279
  28.8 1.8 %copy.35 = bf16[128,4,1024]{2,1,0:T(4,128)(2,1)} copy(bf16[128,4,1024]{2,0,1:T(8,128)(2,1)S(1)} %fusion.2) | data formatting | bytes 2097152 | tf_op jit(solution)/shard_map/inf,ifc->nic/transpose | solution.py:279
  30.6 1.9 %concatenate.22 = bf16[4,4,8,4096]{3,2,1,0:T(8,128)(2,1)S(1)} reshape(bf16[128,4,1024]{2,1,0:T(4,128)(2,1)} %copy.35) | data formatting | bytes 2097152 | tf_op jit(solution)/shard_map/concatenate | solution.py:284
  32.5 1.2 convolution_convert_fusion.2
  33.7 1.1 pad_maximum_fusion
  34.8 3.5 %all-to-all-start.1 = ((bf16[4,4,8,4224]{3,2,1,0:T(8,128)(2,1)}), bf16[4,4,8,4224]{3,2,1,0:T(8,128)(2,1)S(1)}, u32[]{:S(2)}, u32[]{:S(2)}) async-start(bf16[4,4,8,4224]{3,2,1,0:T(8,128)(2,1)} %pad_maximum_fusion), calls=%async_computation.1 | async-start | bytes 2162688 | tf_op jit(solution)/shard_map/all_to_all | solution.py:65
  38.4 0.1 reshape.328
  38.5 0.1 and_select_fusion.6
  38.6 1.0 sort.74
  39.5 0.7 gather_fusion
  40.2 0.1 reshape.390
  40.4 0.1 iota_add_fusion.1
  40.5 0.1 reshape.336
  40.6 22.4 %all-to-all-done.1 = bf16[4,4,8,4224]{3,2,1,0:T(8,128)(2,1)S(1)} async-done(((bf16[4,4,8,4224]{3,2,1,0:T(8,128)(2,1)}), bf16[4,4,8,4224]{3,2,1,0:T(8,128)(2,1)S(1)}, u32[]{:S(2)}, u32[]{:S(2)}) %all-to-all-start.1) | async-done | bytes 1081376 | tf_op jit(solution)/shard_map/all_to_all | solution.py:65
  63.0 1.0 convert_reduce_fusion
  64.0 1.7 %convert_element_type.81 = bf16[8,16,4096]{2,1,0:T(8,128)(2,1)S(1)} convert(f32[8,16,4096]{2,1,0:T(8,128)} %param.17) | non-fusion elementwise | flops 524288 | bytes 3145728 | tf_op jit(solution)/shard_map/convert_element_type | solution.py:292
  65.7 2.2 %gather_fusion.1 = bf16[128,4096]{1,0:T(8,128)(2,1)} fusion(bf16[128,4096]{1,0:T(8,128)(2,1)S(1)} %bitcast.76, s32[1024]{0:T(1024)S(1)} %pad_clamp_fusion.3), kind=kCustom, calls=%fused_computation.1 | custom fusion | bytes 2097664 | tf_op jit(solution)/shard_map/jit(_take)/gather | solution.py:41
  67.9 3.9 %all-to-all-start.2 = ((bf16[16,8,4096]{2,1,0:T(8,128)(2,1)}), bf16[16,8,4096]{2,1,0:T(8,128)(2,1)S(1)}, u32[]{:S(2)}, u32[]{:S(2)}) async-start(bf16[16,8,4096]{2,1,0:T(8,128)(2,1)} %bitcast.82), calls=%async_computation.2 | async-start | bytes 2097152 | tf_op jit(solution)/shard_map/all_to_all | solution.py:44
  71.9 1.6 %sort.75 = (s32[32]{0:T(128)}, s32[32]{0:T(128)S(1)}) sort(s32[32]{0:T(128)S(1)} %and_select_fusion.3, s32[32]{0:T(128)S(1)} %iota.53), dimensions={0}, to_apply=%region_3.4 | sort | flops 160 | bytes 512 | tf_op jit(solution)/shard_map/jit(argsort)/sort | solution.py:47
  73.5 0.1 dynamic_slice.9
  73.6 0.6 gather_fusion.2
  74.4 1.0 sort.76
  75.4 0.1 add_multiply_fusion
  75.5 0.1 iota_add_fusion
  75.6 0.1 reshape.352
  75.7 0.6 maximum_bitcast_fusion
  76.3 1.9 %slice.44 = f32[4,8,4096]{2,1,0:T(8,128)} slice(f32[4,8,4224]{2,1,0:T(8,128)} %convert_reduce_fusion), slice={[0:4], [0:8], [0:4096]} | slice | bytes 1048576 | tf_op jit(solution)/shard_map/slice | solution.py:313
  78.2 0.9 fusion.11
  79.1 0.8 reshape_reshape.9.decay_ref
  80.0 2.4 %reshape.311 = f32[4,8,4,16,64]{4,3,2,1,0:T(8,128)} reshape(f32[4,8,4096]{2,1,0:T(8,128)} %slice.44) | data formatting | bytes 1048576 | tf_op jit(solution)/shard_map/reshape | solution.py:314
  82.4 2.4 %copy.36 = f32[4,8,4,16,64]{4,3,1,0,2:T(8,128)} copy(f32[4,8,4,16,64]{4,3,2,1,0:T(8,128)} %reshape.311) | data formatting | bytes 1048576 | tf_op jit(solution)/shard_map/reshape | solution.py:314
  84.8 0.7 broadcast_in_dim.27
  85.5 6.3 %shard_map.166 = (bf16[4,128,64]{2,1,0:T(8,128)(2,1)}, bf16[9,128,64]{2,1,0:T(8,128)(2,1)}) custom-call(f32[4,4,128,64]{3,2,1,0:T(8,128)} %bitcast.83, f32[4,128,64]{2,1,0:T(8,128)} %reshape_reshape.9.decay_ref, f32[3,128,64]{2,1,0:T(8,128)} %bitcast.90, f32[128,4096]{1,0:T(8,128)} %bitcast.79), custom_call_target="tpu_custom_call" | custom-call | flops 805306368 | bytes 3063808 | tf_op jit(solution)/shard_map/pallas_call | solution.py:163
  91.8 3.0 %all-to-all-done.2 = bf16[16,8,4096]{2,1,0:T(8,128)(2,1)S(1)} async-done(((bf16[16,8,4096]{2,1,0:T(8,128)(2,1)}), bf16[16,8,4096]{2,1,0:T(8,128)(2,1)S(1)}, u32[]{:S(2)}, u32[]{:S(2)}) %all-to-all-start.2) | async-done | bytes 1048608 | tf_op jit(solution)/shard_map/all_to_all | solution.py:44
  94.8 2.2 %gather_fusion.3 = bf16[128,4096]{1,0:T(8,128)(2,1)} fusion(bf16[128,4096]{1,0:T(8,128)(2,1)S(1)} %bitcast.77, s32[1024]{0:T(1024)S(1)} %pad_clamp_fusion.1), kind=kCustom, calls=%fused_computation.3 | custom fusion | bytes 2097664 | tf_op jit(solution)/shard_map/jit(_take)/gather | solution.py:60
  97.0 0.2 copy.48
  97.2 0.3 reshape_reshape.10
  97.5 1.5 %gather_fusion.4 = bf16[128,576]{1,0:T(8,128)(2,1)} fusion(bf16[128,576]{1,0:T(8,128)(2,1)S(1)} %reshape_reshape.10, s32[1024]{0:T(1024)S(1)} %pad_clamp_fusion.3), kind=kCustom, calls=%fused_computation.4 | custom fusion | bytes 295424 | tf_op jit(solution)/shard_map/jit(_take)/gather | solution.py:41
  99.1 6.9 %all-to-all-start.3 = ((bf16[16,8,576]{2,1,0:T(8,128)(2,1)}), bf16[16,8,576]{2,1,0:T(8,128)(2,1)S(1)}, u32[]{:S(2)}, u32[]{:S(2)}) async-start(bf16[16,8,576]{2,1,0:T(8,128)(2,1)} %bitcast.25), calls=%async_computation.3 | async-start | bytes 327680 | tf_op jit(solution)/shard_map/all_to_all | solution.py:44
  105.9 0.1 reshape.315
  106.1 8.3 %all-to-all-done.3 = bf16[16,8,576]{2,1,0:T(8,128)(2,1)S(1)} async-done(((bf16[16,8,576]{2,1,0:T(8,128)(2,1)}), bf16[16,8,576]{2,1,0:T(8,128)(2,1)S(1)}, u32[]{:S(2)}, u32[]{:S(2)}) %all-to-all-start.3) | async-done | bytes 147488 | tf_op jit(solution)/shard_map/all_to_all | solution.py:44
  114.4 0.9 gather_fusion.5
  115.3 0.2 reshape_reshape.11
  115.5 0.8 copy.38
  116.4 0.7 broadcast_in_dim.28
  117.1 3.6 %all-to-all-start.4 = ((bf16[4,4,8,1024]{3,2,1,0:T(8,128)(2,1)}), bf16[4,4,8,1024]{3,2,1,0:T(8,128)(2,1)S(1)}, u32[]{:S(2)}, u32[]{:S(2)}) async-start(bf16[4,4,8,1024]{3,2,1,0:T(8,128)(2,1)} %broadcast_in_dim.28), calls=%async_computation.4 | async-start | bytes 524288 | tf_op jit(solution)/shard_map/all_to_all | solution.py:72
  120.7 1.6 %sort.77 = (s32[32]{0:T(128)}, s32[32]{0:T(128)S(1)}) sort(s32[32]{0:T(128)S(1)} %copy-done.1, s32[32]{0:T(128)S(1)} %iota.55), dimensions={0}, to_apply=%region_5.6 | sort | flops 160 | bytes 512 | tf_op jit(solution)/shard_map/jit(argsort)/sort | solution.py:351
  122.3 6.8 %all-to-all-done.4 = bf16[4,4,8,1024]{3,2,1,0:T(8,128)(2,1)S(1)} async-done(((bf16[4,4,8,1024]{3,2,1,0:T(8,128)(2,1)}), bf16[4,4,8,1024]{3,2,1,0:T(8,128)(2,1)S(1)}, u32[]{:S(2)}, u32[]{:S(2)}) %all-to-all-start.4) | async-done | bytes 262176 | tf_op jit(solution)/shard_map/all_to_all | solution.py:72
  129.2 0.1 copy.40
  129.3 0.8 gather_fusion.6
  130.2 0.5 fusion.6
  130.6 0.7 copy.49
  131.4 3.4 %all-to-all-start.5 = ((bf16[4,4,8,1024]{3,2,1,0:T(8,128)(2,1)}), bf16[4,4,8,1024]{3,2,1,0:T(8,128)(2,1)S(1)}, u32[]{:S(2)}, u32[]{:S(2)}) async-start(bf16[4,4,8,1024]{3,2,1,0:T(8,128)(2,1)} %bitcast.73), calls=%async_computation.5 | async-start | bytes 524288 | tf_op jit(solution)/shard_map/all_to_all | solution.py:65
  134.8 5.0 %shard_map.167 = f32[128,4096]{1,0:T(8,128)} custom-call(bf16[128,4096]{1,0:T(8,128)(2,1)} %gather_fusion.3, bf16[9,128,64]{2,1,0:T(8,128)(2,1)} %bitcast.88), custom_call_target="tpu_custom_call" | custom-call | flops 603979776 | bytes 3293184 | tf_op jit(solution)/shard_map/pallas_call | solution.py:208
  139.8 1.0 all-to-all-done.5
  140.8 0.6 fusion.24
  (60 shorter events, 0.8 us)
Async XLA Ops:
  0.6 129.5 %copy-start = (bf16[1024,1024]{1,0:T(8,128)(2,1)S(1)}, bf16[1024,1024]{1,0:T(8,128)(2,1)}, u32[]{:S(2)}) copy-start(bf16[1024,1024]{1,0:T(8,128)(2,1)} %param.29) | copy-start | bytes 6291460
  2.7 1.1 copy-start.3
  2.8 1.1 slice-start.1
  3.8 7.5 %copy-start.8 = (f32[6,1024]{1,0:T(8,128)S(1)}, f32[6,1024]{1,0:T(8,128)}, u32[]{:S(2)}) copy-start(f32[6,1024]{1,0:T(8,128)} %param.19) | copy-start | bytes 73732
  5.0 16.6 %all-to-all-start = ((bf16[4,128,320]{1,2,0:T(8,128)(2,1)}), bf16[4,128,320]{1,2,0:T(8,128)(2,1)S(1)}, u32[]{:S(2)}, u32[]{:S(2)}) async-start(bf16[4,128,320]{1,2,0:T(8,128)(2,1)} %broadcast_in_dim.24), calls=%async_computation | async-start | bytes 655360 | tf_op jit(solution)/shard_map/all_to_all | solution.py:72
  23.5 5.4 %copy-start.2 = (bf16[5,128,1024]{2,1,0:T(8,128)(2,1)}, bf16[5,128,1024]{2,1,0:T(8,128)(2,1)S(1)}, u32[]{:S(2)}) copy-start(bf16[5,128,1024]{2,1,0:T(8,128)(2,1)S(1)} %add_convert_fusion) | copy-start | bytes 3932164
  30.6 1.9 %slice-start = ((bf16[5,128,1024]{2,1,0:T(8,128)(2,1)}), bf16[1,128,1024]{2,1,0:T(8,128)(2,1)S(1)}, s32[]{:S(2)}) async-start(bf16[5,128,1024]{2,1,0:T(8,128)(2,1)} %copy-done.2), calls=%async_computation.6 | async-start | bytes 524288 | tf_op jit(solution)/shard_map/slice | solution.py:282
  33.7 4.8 %copy-start.1 = (s32[32]{0:T(128)S(1)}, s32[32]{0:T(128)}, u32[]{:S(2)}) copy-start(s32[32]{0:T(128)} %param.18) | copy-start | bytes 388
  34.8 28.3 %all-to-all-start.1 = ((bf16[4,4,8,4224]{3,2,1,0:T(8,128)(2,1)}), bf16[4,4,8,4224]{3,2,1,0:T(8,128)(2,1)S(1)}, u32[]{:S(2)}, u32[]{:S(2)}) async-start(bf16[4,4,8,4224]{3,2,1,0:T(8,128)(2,1)} %pad_maximum_fusion), calls=%async_computation.1 | async-start | bytes 2162688 | tf_op jit(solution)/shard_map/all_to_all | solution.py:65
  67.9 6.3 %copy-start.10 = (f32[1024]{0:T(1024)S(1)}, f32[1024]{0:T(1024)}, u32[]{:S(2)}) copy-start(f32[1024]{0:T(1024)} %param.26) | copy-start | bytes 12292
  67.9 6.4 %copy-start.11 = (f32[1024]{0:T(1024)S(1)}, f32[1024]{0:T(1024)}, u32[]{:S(2)}) copy-start(f32[1024]{0:T(1024)} %param.27) | copy-start | bytes 12292
  67.9 6.5 %copy-start.12 = (f32[1024]{0:T(1024)S(1)}, f32[1024]{0:T(1024)}, u32[]{:S(2)}) copy-start(f32[1024]{0:T(1024)} %param.28) | copy-start | bytes 12292
  67.9 10.3 %copy-start.5 = (bf16[128,1024]{1,0:T(8,128)(2,1)S(1)}, bf16[128,1024]{1,0:T(8,128)(2,1)}, u32[]{:S(2)}) copy-start(bf16[128,1024]{1,0:T(8,128)(2,1)} %param.24) | copy-start | bytes 786436
  67.9 10.3 %copy-start.9 = (f32[1024]{0:T(1024)S(1)}, f32[1024]{0:T(1024)}, u32[]{:S(2)}) copy-start(f32[1024]{0:T(1024)} %param.25) | copy-start | bytes 12292
  67.9 26.9 %all-to-all-start.2 = ((bf16[16,8,4096]{2,1,0:T(8,128)(2,1)}), bf16[16,8,4096]{2,1,0:T(8,128)(2,1)S(1)}, u32[]{:S(2)}, u32[]{:S(2)}) async-start(bf16[16,8,4096]{2,1,0:T(8,128)(2,1)} %bitcast.82), calls=%async_computation.2 | async-start | bytes 2097152 | tf_op jit(solution)/shard_map/all_to_all | solution.py:44
  79.1 5.6 %copy-start.7 = (f32[3,16,64]{2,1,0:T(8,128)S(1)}, f32[3,16,64]{2,1,0:T(8,128)}, u32[]{:S(2)}) copy-start(f32[3,16,64]{2,1,0:T(8,128)} %maximum_bitcast_fusion) | copy-start | bytes 36868
  94.8 2.2 %copy-start.4 = (bf16[9,128,64]{2,1,0:T(8,128)(2,1)S(1)}, bf16[9,128,64]{2,1,0:T(8,128)(2,1)}, u32[]{:S(2)}) copy-start(bf16[9,128,64]{2,1,0:T(8,128)(2,1)} %get-tuple-element.24) | copy-start | bytes 442372
  97.0 9.0 %copy-start.6 = (bf16[4,128,64]{2,1,0:T(8,128)(2,1)S(1)}, bf16[4,128,64]{2,1,0:T(8,128)(2,1)}, u32[]{:S(2)}) copy-start(bf16[4,128,64]{2,1,0:T(8,128)(2,1)} %get-tuple-element.23) | copy-start | bytes 196612
  99.1 15.3 %all-to-all-start.3 = ((bf16[16,8,576]{2,1,0:T(8,128)(2,1)}), bf16[16,8,576]{2,1,0:T(8,128)(2,1)S(1)}, u32[]{:S(2)}, u32[]{:S(2)}) async-start(bf16[16,8,576]{2,1,0:T(8,128)(2,1)} %bitcast.25), calls=%async_computation.3 | async-start | bytes 327680 | tf_op jit(solution)/shard_map/all_to_all | solution.py:44
  117.1 12.0 %all-to-all-start.4 = ((bf16[4,4,8,1024]{3,2,1,0:T(8,128)(2,1)}), bf16[4,4,8,1024]{3,2,1,0:T(8,128)(2,1)S(1)}, u32[]{:S(2)}, u32[]{:S(2)}) async-start(bf16[4,4,8,1024]{3,2,1,0:T(8,128)(2,1)} %broadcast_in_dim.28), calls=%async_computation.4 | async-start | bytes 524288 | tf_op jit(solution)/shard_map/all_to_all | solution.py:72
  131.4 9.4 %all-to-all-start.5 = ((bf16[4,4,8,1024]{3,2,1,0:T(8,128)(2,1)}), bf16[4,4,8,1024]{3,2,1,0:T(8,128)(2,1)S(1)}, u32[]{:S(2)}, u32[]{:S(2)}) async-start(bf16[4,4,8,1024]{3,2,1,0:T(8,128)(2,1)} %bitcast.73), calls=%async_computation.5 | async-start | bytes 524288 | tf_op jit(solution)/shard_map/all_to_all | solution.py:65

commit v8 on v6

--- a/solution.py
+++ b/solution.py
@@ -62,15 +62,27 @@
     ).reshape(slots_dev, head_count * quarter, width)
 
 def exchange_sum(pieces, axis_name):
-    arrived = lax.all_to_all(pieces, axis_name, split_axis=0, concat_axis=0, tiled=True)
-    return jnp.sum(arrived.astype(jnp.float32), axis=0)
+    count = lax.axis_size(axis_name)
+    index = lax.axis_index(axis_name)
+    total = lax.dynamic_index_in_dim(pieces, index, keepdims=False).astype(jnp.float32)
+    for shift in range(1, count):
+        sent = lax.dynamic_index_in_dim(pieces, (index + shift) % count, keepdims=False)
+        total = total + lax.ppermute(
+            sent, axis_name, [(i, (i + shift) % count) for i in range(count)]
+        ).astype(jnp.float32)
+    return total
 
 
 def exchange_copies(value, axis_name):
     count = lax.axis_size(axis_name)
-    copies = jnp.broadcast_to(value[None], (count,) + value.shape)
-    return lax.all_to_all(copies, axis_name, split_axis=0, concat_axis=0, tiled=True)
-
+    index = lax.axis_index(axis_name)
+    received = [value]
+    for shift in range(1, count):
+        received.append(
+            lax.ppermute(value, axis_name, [(i, (i + shift) % count) for i in range(count)])
+        )
+    shifts = (index - jnp.arange(count, dtype=jnp.int32)) % count
+    return jnp.take(jnp.stack(received), shifts, axis=0, mode="clip")
 
 def widen(value):
     return value.astype(jnp.bfloat16).astype(jnp.float32)

time: 136 us -> 155 us (1.14)
  waiting for transfers between devices: 35.4 us -> 50.2 us
  starting transfers between devices: 27.3 us -> 30.7 us
  other arithmetic: 14.4 us -> 17.1 us
    ppermute x0 -> x12, waiting for transfers between devices: none -> 48.3 us  [the longest x6 28.2 us: exchange_copies(): lax.ppermute(value, axis_name, [(i, (i + shift) % count) for i in range(c...]
    all_to_all x4 -> x0, waiting for transfers between devices: 33.2 us -> none  [the longest x2 18.5 us: exchange_sum(): lax.all_to_all(pieces, axis_name, split_axis=0, concat_axis=0, tiled=True)]
    all_to_all x4 -> x0, starting transfers between devices: 19.8 us -> none  [the longest x2 11.3 us: exchange_copies(): lax.all_to_all(copies, axis_name, split_axis=0, concat_axis=0, tiled=True)]
    ppermute x0 -> x12, starting transfers between devices: none -> 18.7 us  [the longest x6 11 us: exchange_copies(): lax.ppermute(value, axis_name, [(i, (i + shift) % count) for i in range(c...]
    another operation x1 -> x3, other arithmetic: 0.03 us -> 4.75 us  [the longest x2 2.7 us: exchange_copies(): return jnp.take(jnp.stack(received), shifts, axis=0, mode='clip')]
    all_to_all x2, starting transfers between devices: 7.52 us -> 11.9 us  [route_to_slots(): lax.all_to_all(packed, ('batch', 'head'), split_axis=0, concat_axis=0, ti...]
    gather x0 -> x2, local copies, waits for them, and re-layouts: none -> 3.53 us  [exchange_copies(): return jnp.take(jnp.stack(received), shifts, axis=0, mode='clip')]
    broadcast_in_dim x3 -> x0, local copies, waits for them, and re-layouts: 2.53 us -> none  [exchange_copies(): copies = jnp.broadcast_to(value[None], (count,) + value.shape)]
  transfers between devices with their start and end apart: 6 -> 14, of which waited for: 4 -> 9; matrix products, arithmetic and copies ran while one was open for 29% -> 17% of each run, Pallas kernels for 8% -> 0%
where the time goes in v8:
time: 155 us; the launch traced here: 154 us
  waiting for transfers between devices  50.2 us (32%)
  local copies, waits for them, and re-layouts  33.6 us (22%)
  starting transfers between devices  30.7 us (20%)
  other arithmetic  17.1 us (11%)
  Pallas kernels  11.4 us (7%)
  matrix products  9.93 us (6%)
    ppermute x6, waiting for transfers between devices, exchange_copies(): lax.ppermute(value, axis_name, [(i, (i + shift) % count) for i in range(c...  28.2 us
    ppermute x6, waiting for transfers between devices, exchange_sum(): lax.ppermute(sent, axis_name, [(i, (i + shift) % count) for i in range(co...  20.1 us
    all_to_all x2, starting transfers between devices, route_to_slots(): lax.all_to_all(packed, ('batch', 'head'), split_axis=0, concat_axis=0, ti...  11.9 us
    ppermute x6, starting transfers between devices, exchange_copies(): lax.ppermute(value, axis_name, [(i, (i + shift) % count) for i in range(c...  11 us
    ppermute x6, starting transfers between devices, exchange_sum(): lax.ppermute(sent, axis_name, [(i, (i + shift) % count) for i in range(co...  7.78 us
    pallas_call x1, Pallas kernels, run_recurrence(): pl.pallas_call(functools.partial(recurrence_kernel, steps), grid=(rows //...  6.38 us
    dot_general x1, matrix products, per_device(): jnp.einsum('inf,ifc->nic', mixed[:4], fourfold_linear_maps, preferred_ele...  5.34 us
    pallas_call x1, Pallas kernels, rebuild_state(): pl.pallas_call(functools.partial(rebuild_kernel, steps), grid=(rows // bl...  4.99 us
  transfers between devices with their start and end apart: 14, of which 9 were waited for; matrix products, arithmetic and copies ran while one was open for 17% of the time, Pallas kernels for 0%

profile of v8, /device:TPU:0, one launch (start us, length us, event | category | flops | bytes accessed | tf_op | source)
XLA Modules:
  0.0 154.0 jit_solution(18063891130264950763)
XLA Ops:
  0.6 1.1 slice_bitcast_fusion
  1.7 1.0 convert_bitcast_fusion
  2.8 0.9 convert_bitcast_fusion.1
  4.3 5.1 %collective-permute-start.2 = (bf16[128,320]{0,1:T(8,128)(2,1)S(1)}, bf16[128,320]{0,1:T(8,128)(2,1)S(1)}, u32[]{:S(2)}, u32[]{:S(2)}) collective-permute-start(bf16[128,320]{0,1:T(8,128)(2,1)S(1)} %convolution_convert_fusion.1), channel_id=1, source_target_pairs={{0,12},{4,0},{8,4},{12,8},{1,13},{5,1},{9,5},{13,9},{2,14},{6,2},{... | collective-permute-start | bytes 245768 | tf_op jit(solution)/shard_map/ppermute | solution.py:82
  9.4 1.0 collective-permute-start
  10.5 1.6 %sort.76 = (s32[32]{0:T(128)}, s32[32]{0:T(128)S(1)}) sort(s32[32]{0:T(128)S(1)} %and_select_fusion.3, s32[32]{0:T(128)S(1)} %iota.60), dimensions={0}, to_apply=%region_3.4 | sort | flops 160 | bytes 512 | tf_op jit(solution)/shard_map/jit(argsort)/sort | solution.py:47
  12.2 0.6 gather_fusion.5
  13.1 1.0 sort.75
  14.0 0.7 gather_fusion.3
  14.9 2.0 %collective-permute-done.1 = bf16[128,320]{0,1:T(8,128)(2,1)S(1)} collective-permute-done((bf16[128,320]{0,1:T(8,128)(2,1)S(1)}, bf16[128,320]{0,1:T(8,128)(2,1)S(1)}, u32[]{:S(2)}, u32[]{:S(2)}) %collective-permute-start.1) | collective-permute-done | bytes 81952 | tf_op jit(solution)/shard_map/ppermute | solution.py:82
  16.9 0.6 copy-done.8
  17.5 1.0 pad_maximum_fusion
  18.6 1.3 gather_fusion
  19.9 1.0 convert_reduce_fusion
  21.0 1.7 %add_convert_fusion = bf16[5,128,1024]{2,1,0:T(8,128)(2,1)S(1)} fusion(bf16[128,5,64]{0,2,1:T(8,128)(2,1)S(1)} %bitcast.116, bf16[5,64,1024]{2,1,0:T(8,128)(2,1)} %param.21, f32[5,1024]{1,0:T(8,128)S(1)} %slice.52, f32[128,1024]{1,0:T(8,128)S(1)} %bitcast_subtract_fusion, f32[128,1024]{1,0:T(8,128)S(1)} %bitcast.105), kind=kOutput, calls=%fused_computation.9 | convolution fusion | flops 86507520 | bytes 3117056 | tf_op jit(solution)/shard_map/nim,imd->ind/dot_general | solution.py:288
  22.7 5.3 %fusion.2 = bf16[128,4,1024]{2,0,1:T(8,128)(2,1)S(1)} fusion(bf16[5,128,1024]{2,1,0:T(8,128)(2,1)S(1)} %add_convert_fusion, bf16[4,1024,1024]{2,1,0:T(8,128)(2,1)} %param.22), kind=kOutput, calls=%fused_computation.17 | convolution fusion | flops 1074266112 | bytes 10747904 | tf_op jit(solution)/shard_map/inf,ifc->nic/dot_general | solution.py:294
  28.1 1.8 %copy.26 = bf16[128,4,1024]{2,1,0:T(4,128)(2,1)} copy(bf16[128,4,1024]{2,0,1:T(8,128)(2,1)S(1)} %fusion.2) | data formatting | bytes 2097152 | tf_op jit(solution)/shard_map/inf,ifc->nic/transpose | solution.py:294
  29.9 1.9 %concatenate.22 = bf16[4,4,8,4096]{3,2,1,0:T(8,128)(2,1)S(1)} reshape(bf16[128,4,1024]{2,1,0:T(4,128)(2,1)} %copy.26) | data formatting | bytes 2097152 | tf_op jit(solution)/shard_map/concatenate | solution.py:299
  31.7 1.2 convolution_convert_fusion.2
  32.9 0.9 fusion.19
  33.8 0.5 collective-permute-start.3
  34.4 2.2 %collective-permute-start.4 = (bf16[4,8,4224]{2,1,0:T(8,128)(2,1)}, bf16[4,8,4224]{2,1,0:T(8,128)(2,1)}, u32[]{:S(2)}, u32[]{:S(2)}) collective-permute-start(bf16[4,8,4224]{2,1,0:T(8,128)(2,1)} %get-tuple-element.18), channel_id=1, source_target_pairs={{0,8},{4,12},{8,0},{12,4},{1,9},{5,13},{9,1},{13,5},{2,10},{6,14},... | collective-permute-start | bytes 811016 | tf_op jit(solution)/shard_map/ppermute | solution.py:70
  36.5 1.8 %collective-permute-start.5 = (bf16[4,8,4224]{2,1,0:T(8,128)(2,1)}, bf16[4,8,4224]{2,1,0:T(8,128)(2,1)}, u32[]{:S(2)}, u32[]{:S(2)}) collective-permute-start(bf16[4,8,4224]{2,1,0:T(8,128)(2,1)} %get-tuple-element.19), channel_id=1, source_target_pairs={{0,12},{4,0},{8,4},{12,8},{1,13},{5,1},{9,5},{13,9},{2,14},{6,2},{... | collective-permute-start | bytes 811016 | tf_op jit(solution)/shard_map/ppermute | solution.py:70
  38.8 6.6 %collective-permute-done.3 = bf16[4,8,4224]{2,1,0:T(8,128)(2,1)} collective-permute-done((bf16[4,8,4224]{2,1,0:T(8,128)(2,1)}, bf16[4,8,4224]{2,1,0:T(8,128)(2,1)}, u32[]{:S(2)}, u32[]{:S(2)}) %collective-permute-start.3) | collective-permute-done | bytes 270368 | tf_op jit(solution)/shard_map/ppermute | solution.py:70
  45.4 10.4 %collective-permute-done.4 = bf16[4,8,4224]{2,1,0:T(8,128)(2,1)} collective-permute-done((bf16[4,8,4224]{2,1,0:T(8,128)(2,1)}, bf16[4,8,4224]{2,1,0:T(8,128)(2,1)}, u32[]{:S(2)}, u32[]{:S(2)}) %collective-permute-start.4) | collective-permute-done | bytes 270368 | tf_op jit(solution)/shard_map/ppermute | solution.py:70
  55.8 2.1 %fusion.40 = (bf16[4,8,4224]{2,1,0:T(8,128)(2,1)S(1)}, f32[4,8,4224]{2,1,0:T(8,128)}) fusion(bf16[4,8,4224]{2,1,0:T(8,128)(2,1)} %collective-permute-done.5, bf16[4,8,4224]{2,1,0:T(8,128)(2,1)} %collective-permute-done.4, bf16[4,8,4224]{2,1,0:T(8,128)(2,1)} %collective-permute-done.3, s32[]{:T(128)S(6)} %select_n.148, ...), kind=kLoop, calls=%fused_computation.117 | loop fusion | flops 1622016 | bytes 2703364 | tf_op jit(solution)/shard_map/convert.12
  57.9 0.8 reshape.366.value_ref
  58.7 0.9 divide_multiply_fusion
  59.6 0.8 reshape.348.gate_ref
  60.5 0.9 fusion.11
  61.4 0.8 reshape_reshape.30.decay_ref
  62.2 0.8 reshape.365.key_ref
  63.0 0.8 reshape.364.recept_ref
  63.8 0.7 broadcast_in_dim.24
  64.5 6.4 %shard_map.166 = (bf16[4,128,64]{2,1,0:T(8,128)(2,1)}, bf16[9,128,64]{2,1,0:T(8,128)(2,1)}) custom-call(f32[4,128,64]{2,1,0:T(8,128)} %reshape.364.recept_ref, f32[4,128,64]{2,1,0:T(8,128)} %reshape.365.key_ref, f32[4,128,64]{2,1,0:T(8,128)} %reshape.366.value_ref, f32[4,128,64]{2,1,0:T(8,128)} %reshape_reshape.30.decay_ref, ...), custom_call_target="tpu_custom_call" | custom-call | flops 805306368 | bytes 3063808 | tf_op jit(solution)/shard_map/pallas_call | solution.py:176
  70.8 1.2 copy.40
  72.4 1.5 gather_fusion.7
  73.9 7.9 %all-to-all-start.1 = ((bf16[16,8,576]{2,1,0:T(8,128)(2,1)}), bf16[16,8,576]{2,1,0:T(8,128)(2,1)S(1)}, u32[]{:S(2)}, u32[]{:S(2)}) async-start(bf16[16,8,576]{2,1,0:T(8,128)(2,1)} %bitcast.44), calls=%async_computation.1 | async-start | bytes 327680 | tf_op jit(solution)/shard_map/all_to_all | solution.py:44
  81.8 1.7 %convert_element_type.127 = bf16[8,16,4096]{2,1,0:T(8,128)(2,1)S(1)} convert(f32[8,16,4096]{2,1,0:T(8,128)} %param.17) | non-fusion elementwise | flops 524288 | bytes 3145728 | tf_op jit(solution)/shard_map/convert_element_type | solution.py:269
  83.5 1.6 %sort.74 = (s32[32]{0:T(128)}, s32[32]{0:T(128)S(1)}) sort(s32[32]{0:T(128)S(1)} %copy-done.1, s32[32]{0:T(128)S(1)} %iota.57), dimensions={0}, to_apply=%region_1.2 | sort | flops 160 | bytes 512 | tf_op jit(solution)/shard_map/jit(argsort)/sort | solution.py:358
  85.1 2.2 %gather_fusion.4 = bf16[128,4096]{1,0:T(8,128)(2,1)} fusion(bf16[128,4096]{1,0:T(8,128)(2,1)S(1)} %bitcast.100, s32[1024]{0:T(1024)S(1)} %pad_clamp_fusion.2), kind=kCustom, calls=%fused_computation.4 | custom fusion | bytes 2097664 | tf_op jit(solution)/shard_map/jit(_take)/gather | solution.py:41
  87.3 1.0 sort.77
  88.3 1.9 %all-to-all-done.1 = bf16[16,8,576]{2,1,0:T(8,128)(2,1)S(1)} async-done(((bf16[16,8,576]{2,1,0:T(8,128)(2,1)}), bf16[16,8,576]{2,1,0:T(8,128)(2,1)S(1)}, u32[]{:S(2)}, u32[]{:S(2)}) %all-to-all-start.1) | async-done | bytes 147488 | tf_op jit(solution)/shard_map/all_to_all | solution.py:44
  90.2 4.0 %all-to-all-start = ((bf16[16,8,4096]{2,1,0:T(8,128)(2,1)}), bf16[16,8,4096]{2,1,0:T(8,128)(2,1)S(1)}, u32[]{:S(2)}, u32[]{:S(2)}) async-start(bf16[16,8,4096]{2,1,0:T(8,128)(2,1)} %bitcast.106), calls=%async_computation | async-start | bytes 2097152 | tf_op jit(solution)/shard_map/all_to_all | solution.py:44
  94.6 0.8 reshape.351
  95.3 3.7 %collective-permute-start.8 = (bf16[4,8,1024]{2,1,0:T(8,128)(2,1)}, bf16[4,8,1024]{2,1,0:T(8,128)(2,1)}, u32[]{:S(2)}, u32[]{:S(2)}) collective-permute-start(bf16[4,8,1024]{2,1,0:T(8,128)(2,1)} %reshape.351), channel_id=1, source_target_pairs={{0,12},{4,0},{8,4},{12,8},{1,13},{5,1},{9,5},{13,9},{2,14},{6,2},{... | collective-permute-start | bytes 196616 | tf_op jit(solution)/shard_map/ppermute | solution.py:82
  99.1 1.1 collective-permute-start.6
  100.3 13.7 %collective-permute-done.8 = bf16[4,8,1024]{2,1,0:T(8,128)(2,1)} collective-permute-done((bf16[4,8,1024]{2,1,0:T(8,128)(2,1)}, bf16[4,8,1024]{2,1,0:T(8,128)(2,1)}, u32[]{:S(2)}, u32[]{:S(2)}) %collective-permute-start.8) | collective-permute-done | bytes 65568 | tf_op jit(solution)/shard_map/ppermute | solution.py:82
  114.0 12.5 %collective-permute-done.7 = bf16[4,8,1024]{2,1,0:T(8,128)(2,1)} collective-permute-done((bf16[4,8,1024]{2,1,0:T(8,128)(2,1)}, bf16[4,8,1024]{2,1,0:T(8,128)(2,1)}, u32[]{:S(2)}, u32[]{:S(2)}) %collective-permute-start.7) | collective-permute-done | bytes 65568 | tf_op jit(solution)/shard_map/ppermute | solution.py:82
  126.5 1.6 %pad_maximum_fusion.1 = bf16[4,4,8,1024]{3,2,1,0:T(8,128)(2,1)} fusion(bf16[1,4,8,1024]{3,2,1,0:T(8,128)(2,1)} %bitcast.28, bf16[1,4,8,1024]{3,2,1,0:T(8,128)(2,1)} %bitcast.27, bf16[1,4,8,1024]{3,2,1,0:T(8,128)(2,1)} %bitcast.26, bf16[1,4,8,1024]{3,2,1,0:T(8,128)(2,1)S(1)} %stack_reshape.3), kind=kLoop, calls=%fused_computation.48 | loop fusion | flops 393216 | bytes 524288 | tf_op jit(solution)/shard_map/stack | solution.py:85
  128.2 2.2 %gather_fusion.1 = bf16[4,4,8,1024]{3,2,1,0:T(8,128)(2,1)} fusion(bf16[4,4,8,1024]{3,2,1,0:T(8,128)(2,1)} %pad_maximum_fusion.1, s32[1024]{0:T(1024)S(1)} %pad_clamp_fusion.5), kind=kCustom, calls=%fused_computation.1 | custom fusion | bytes 524304 | tf_op jit(solution)/shard_map/jit(_take)/gather | solution.py:85
  130.4 1.0 fusion.42
  131.4 0.8 copy.29
  132.2 2.4 %gather_fusion.2 = bf16[32,2,1024]{2,1,0:T(2,128)(2,1)} fusion(bf16[2,32,1024]{2,0,1:T(2,128)(2,1)} %copy.29, s32[1024]{0:T(1024)S(1)} %pad_clamp_fusion.4), kind=kCustom, calls=%fused_computation.2 | custom fusion | bytes 262272 | tf_op jit(solution)/shard_map/jit(_take)/gather | solution.py:360
  134.6 0.9 copy.41
  136.1 1.7 %collective-permute-start.11 = (bf16[4,8,1024]{2,1,0:T(8,128)(2,1)S(1)}, bf16[4,8,1024]{2,1,0:T(8,128)(2,1)S(1)}, u32[]{:S(2)}, u32[]{:S(2)}) collective-permute-start(bf16[4,8,1024]{2,1,0:T(8,128)(2,1)S(1)} %get-tuple-element.24), channel_id=1, source_target_pairs={{0,3},{1,0},{2,1},{3,2},{4,7},{5,4},{6,5},{7,6},{8,11},{9,8},{10,9... | collective-permute-start | bytes 196616 | tf_op jit(solution)/shard_map/ppermute | solution.py:70
  137.8 1.5 collective-permute-start.10
  140.2 2.2 %collective-permute-done.10 = bf16[4,8,1024]{2,1,0:T(8,128)(2,1)S(1)} collective-permute-done((bf16[4,8,1024]{2,1,0:T(8,128)(2,1)S(1)}, bf16[4,8,1024]{2,1,0:T(8,128)(2,1)S(1)}, u32[]{:S(2)}, u32[]{:S(2)}) %collective-permute-start.10) | collective-permute-done | bytes 65568 | tf_op jit(solution)/shard_map/ppermute | solution.py:70
  142.4 0.6 fusion.43
  143.1 0.9 gather_fusion.8
  144.0 1.0 reshape_reshape.32
  145.0 1.9 %copy.33 = bf16[9,8,16,64]{3,2,1,0:T(8,128)(2,1)} copy(bf16[9,8,16,64]{3,0,2,1:T(8,128)(2,1)} %bitcast.109) | data formatting | bytes 294912 | tf_op jit(solution)/shard_map/transpose | solution.py:349
  146.9 2.2 %gather_fusion.6 = bf16[128,4096]{1,0:T(8,128)(2,1)} fusion(bf16[128,4096]{1,0:T(8,128)(2,1)S(1)} %bitcast.101, s32[1024]{0:T(1024)S(1)} %pad_clamp_fusion), kind=kCustom, calls=%fused_computation.6 | custom fusion | bytes 2097664 | tf_op jit(solution)/shard_map/jit(_take)/gather | solution.py:60
  149.0 5.0 %shard_map.167 = f32[128,4096]{1,0:T(8,128)} custom-call(bf16[128,4096]{1,0:T(8,128)(2,1)} %gather_fusion.6, bf16[9,128,64]{2,1,0:T(8,128)(2,1)} %bitcast.111), custom_call_target="tpu_custom_call" | custom-call | flops 603979776 | bytes 3293184 | tf_op jit(solution)/shard_map/pallas_call | solution.py:220
  (84 shorter events, 3.8 us)
Async XLA Ops:
  0.6 134.9 %copy-start = (bf16[1024,1024]{1,0:T(8,128)(2,1)S(1)}, bf16[1024,1024]{1,0:T(8,128)(2,1)}, u32[]{:S(2)}) copy-start(bf16[1024,1024]{1,0:T(8,128)(2,1)} %param.29) | copy-start | bytes 6291460
  2.7 1.2 copy-start.3
  2.8 1.2 slice-start.1
  3.8 6.7 %copy-start.9 = (f32[6,1024]{1,0:T(8,128)S(1)}, f32[6,1024]{1,0:T(8,128)}, u32[]{:S(2)}) copy-start(f32[6,1024]{1,0:T(8,128)} %param.19) | copy-start | bytes 73732
  3.8 6.7 %copy-start.1 = (s32[32]{0:T(128)S(1)}, s32[32]{0:T(128)}, u32[]{:S(2)}) copy-start(s32[32]{0:T(128)} %param.18) | copy-start | bytes 388
  4.3 10.5 %copy-start.5 = (bf16[128,320]{0,1:T(8,128)(2,1)}, bf16[128,320]{0,1:T(8,128)(2,1)S(1)}, u32[]{:S(2)}) copy-start(bf16[128,320]{0,1:T(8,128)(2,1)S(1)} %convolution_convert_fusion.1) | copy-start | bytes 245764
  4.3 10.6 %collective-permute-start.2 = (bf16[128,320]{0,1:T(8,128)(2,1)S(1)}, bf16[128,320]{0,1:T(8,128)(2,1)S(1)}, u32[]{:S(2)}, u32[]{:S(2)}) collective-permute-start(bf16[128,320]{0,1:T(8,128)(2,1)S(1)} %convolution_convert_fusion.1), channel_id=1, source_target_pairs={{0,12},{4,0},{8,4},{12,8},{1,13},{5,1},{9,5},{13,9},{2,14},{6,2},{... | collective-permute-start | bytes 245768 | tf_op jit(solution)/shard_map/ppermute | solution.py:82
  9.4 7.5 %collective-permute-start.1 = (bf16[128,320]{0,1:T(8,128)(2,1)S(1)}, bf16[128,320]{0,1:T(8,128)(2,1)S(1)}, u32[]{:S(2)}, u32[]{:S(2)}) collective-permute-start(bf16[128,320]{0,1:T(8,128)(2,1)S(1)} %convolution_convert_fusion.1), channel_id=1, source_target_pairs={{0,8},{4,12},{8,0},{12,4},{1,9},{5,13},{9,1},{13,5},{2,10},{6,14},... | collective-permute-start | bytes 245768 | tf_op jit(solution)/shard_map/ppermute | solution.py:82
  9.4 7.5 %collective-permute-start = (bf16[128,320]{0,1:T(8,128)(2,1)S(1)}, bf16[128,320]{0,1:T(8,128)(2,1)}, u32[]{:S(2)}, u32[]{:S(2)}) collective-permute-start(bf16[128,320]{0,1:T(8,128)(2,1)S(1)} %convolution_convert_fusion.1), channel_id=1, source_target_pairs={{0,4},{4,8},{8,12},{12,0},{1,5},{5,9},{9,13},{13,1},{2,6},{6,10},{... | collective-permute-start | bytes 245768 | tf_op jit(solution)/shard_map/ppermute | solution.py:82
  14.9 2.0 %copy-start.7 = (bf16[128,320]{0,1:T(8,128)(2,1)}, bf16[128,320]{0,1:T(8,128)(2,1)S(1)}, u32[]{:S(2)}) copy-start(bf16[128,320]{0,1:T(8,128)(2,1)S(1)} %collective-permute-done.2) | copy-start | bytes 245764
  16.9 0.6 copy-start.8
  22.7 5.4 %copy-start.2 = (bf16[5,128,1024]{2,1,0:T(8,128)(2,1)}, bf16[5,128,1024]{2,1,0:T(8,128)(2,1)S(1)}, u32[]{:S(2)}) copy-start(bf16[5,128,1024]{2,1,0:T(8,128)(2,1)S(1)} %add_convert_fusion) | copy-start | bytes 3932164
  29.8 1.9 %slice-start = ((bf16[5,128,1024]{2,1,0:T(8,128)(2,1)}), bf16[1,128,1024]{2,1,0:T(8,128)(2,1)S(1)}, s32[]{:S(2)}) async-start(bf16[5,128,1024]{2,1,0:T(8,128)(2,1)} %copy-done.2), calls=%async_computation.2 | async-start | bytes 524288 | tf_op jit(solution)/shard_map/slice | solution.py:297
  29.8 8.7 %copy-start.11 = (f32[1024]{0:T(1024)S(1)}, f32[1024]{0:T(1024)}, u32[]{:S(2)}) copy-start(f32[1024]{0:T(1024)} %param.26) | copy-start | bytes 12292
  29.9 8.8 %copy-start.12 = (f32[1024]{0:T(1024)S(1)}, f32[1024]{0:T(1024)}, u32[]{:S(2)}) copy-start(f32[1024]{0:T(1024)} %param.27) | copy-start | bytes 12292
  29.9 8.8 %copy-start.13 = (f32[1024]{0:T(1024)S(1)}, f32[1024]{0:T(1024)}, u32[]{:S(2)}) copy-start(f32[1024]{0:T(1024)} %param.28) | copy-start | bytes 12292
  33.8 11.6 %collective-permute-start.3 = (bf16[4,8,4224]{2,1,0:T(8,128)(2,1)}, bf16[4,8,4224]{2,1,0:T(8,128)(2,1)}, u32[]{:S(2)}, u32[]{:S(2)}) collective-permute-start(bf16[4,8,4224]{2,1,0:T(8,128)(2,1)} %get-tuple-element.17), channel_id=1, source_target_pairs={{0,4},{4,8},{8,12},{12,0},{1,5},{5,9},{9,13},{13,1},{2,6},{6,10},{... | collective-permute-start | bytes 811016 | tf_op jit(solution)/shard_map/ppermute | solution.py:70
  34.4 21.5 %collective-permute-start.4 = (bf16[4,8,4224]{2,1,0:T(8,128)(2,1)}, bf16[4,8,4224]{2,1,0:T(8,128)(2,1)}, u32[]{:S(2)}, u32[]{:S(2)}) collective-permute-start(bf16[4,8,4224]{2,1,0:T(8,128)(2,1)} %get-tuple-element.18), channel_id=1, source_target_pairs={{0,8},{4,12},{8,0},{12,4},{1,9},{5,13},{9,1},{13,5},{2,10},{6,14},... | collective-permute-start | bytes 811016 | tf_op jit(solution)/shard_map/ppermute | solution.py:70
  36.5 19.3 %collective-permute-start.5 = (bf16[4,8,4224]{2,1,0:T(8,128)(2,1)}, bf16[4,8,4224]{2,1,0:T(8,128)(2,1)}, u32[]{:S(2)}, u32[]{:S(2)}) collective-permute-start(bf16[4,8,4224]{2,1,0:T(8,128)(2,1)} %get-tuple-element.19), channel_id=1, source_target_pairs={{0,12},{4,0},{8,4},{12,8},{1,13},{5,1},{9,5},{13,9},{2,14},{6,2},{... | collective-permute-start | bytes 811016 | tf_op jit(solution)/shard_map/ppermute | solution.py:70
  38.8 21.7 %copy-start.6 = (bf16[128,1024]{1,0:T(8,128)(2,1)S(1)}, bf16[128,1024]{1,0:T(8,128)(2,1)}, u32[]{:S(2)}) copy-start(bf16[128,1024]{1,0:T(8,128)(2,1)} %param.24) | copy-start | bytes 786436
  38.8 21.7 %copy-start.10 = (f32[1024]{0:T(1024)S(1)}, f32[1024]{0:T(1024)}, u32[]{:S(2)}) copy-start(f32[1024]{0:T(1024)} %param.25) | copy-start | bytes 12292
  73.9 16.3 %all-to-all-start.1 = ((bf16[16,8,576]{2,1,0:T(8,128)(2,1)}), bf16[16,8,576]{2,1,0:T(8,128)(2,1)S(1)}, u32[]{:S(2)}, u32[]{:S(2)}) async-start(bf16[16,8,576]{2,1,0:T(8,128)(2,1)} %bitcast.44), calls=%async_computation.1 | async-start | bytes 327680 | tf_op jit(solution)/shard_map/all_to_all | solution.py:44
  87.3 7.3 %copy-start.4 = (bf16[4,128,64]{2,1,0:T(8,128)(2,1)S(1)}, bf16[4,128,64]{2,1,0:T(8,128)(2,1)}, u32[]{:S(2)}) copy-start(bf16[4,128,64]{2,1,0:T(8,128)(2,1)} %get-tuple-element.9) | copy-start | bytes 196612
  90.2 56.7 %all-to-all-start = ((bf16[16,8,4096]{2,1,0:T(8,128)(2,1)}), bf16[16,8,4096]{2,1,0:T(8,128)(2,1)S(1)}, u32[]{:S(2)}, u32[]{:S(2)}) async-start(bf16[16,8,4096]{2,1,0:T(8,128)(2,1)} %bitcast.106), calls=%async_computation | async-start | bytes 2097152 | tf_op jit(solution)/shard_map/all_to_all | solution.py:44
  95.3 18.7 %collective-permute-start.8 = (bf16[4,8,1024]{2,1,0:T(8,128)(2,1)}, bf16[4,8,1024]{2,1,0:T(8,128)(2,1)}, u32[]{:S(2)}, u32[]{:S(2)}) collective-permute-start(bf16[4,8,1024]{2,1,0:T(8,128)(2,1)} %reshape.351), channel_id=1, source_target_pairs={{0,12},{4,0},{8,4},{12,8},{1,13},{5,1},{9,5},{13,9},{2,14},{6,2},{... | collective-permute-start | bytes 196616 | tf_op jit(solution)/shard_map/ppermute | solution.py:82
  99.1 27.5 %collective-permute-start.7 = (bf16[4,8,1024]{2,1,0:T(8,128)(2,1)}, bf16[4,8,1024]{2,1,0:T(8,128)(2,1)}, u32[]{:S(2)}, u32[]{:S(2)}) collective-permute-start(bf16[4,8,1024]{2,1,0:T(8,128)(2,1)} %reshape.351), channel_id=1, source_target_pairs={{0,8},{4,12},{8,0},{12,4},{1,9},{5,13},{9,1},{13,5},{2,10},{6,14},... | collective-permute-start | bytes 196616 | tf_op jit(solution)/shard_map/ppermute | solution.py:82
  99.1 27.5 %collective-permute-start.6 = (bf16[4,8,1024]{2,1,0:T(8,128)(2,1)}, bf16[4,8,1024]{2,1,0:T(8,128)(2,1)}, u32[]{:S(2)}, u32[]{:S(2)}) collective-permute-start(bf16[4,8,1024]{2,1,0:T(8,128)(2,1)} %reshape.351), channel_id=1, source_target_pairs={{0,4},{4,8},{8,12},{12,0},{1,5},{5,9},{9,13},{13,1},{2,6},{6,10},{... | collective-permute-start | bytes 196616 | tf_op jit(solution)/shard_map/ppermute | solution.py:82
  136.0 3.7 %collective-permute-start.9 = (bf16[4,8,1024]{2,1,0:T(8,128)(2,1)S(1)}, bf16[4,8,1024]{2,1,0:T(8,128)(2,1)S(1)}, u32[]{:S(2)}, u32[]{:S(2)}) collective-permute-start(bf16[4,8,1024]{2,1,0:T(8,128)(2,1)S(1)} %get-tuple-element.23), channel_id=1, source_target_pairs={{0,1},{1,2},{2,3},{3,0},{4,5},{5,6},{6,7},{7,4},{8,9},{9,10},{10,1... | collective-permute-start | bytes 196616 | tf_op jit(solution)/shard_map/ppermute | solution.py:70
  136.1 4.1 %collective-permute-start.11 = (bf16[4,8,1024]{2,1,0:T(8,128)(2,1)S(1)}, bf16[4,8,1024]{2,1,0:T(8,128)(2,1)S(1)}, u32[]{:S(2)}, u32[]{:S(2)}) collective-permute-start(bf16[4,8,1024]{2,1,0:T(8,128)(2,1)S(1)} %get-tuple-element.24), channel_id=1, source_target_pairs={{0,3},{1,0},{2,1},{3,2},{4,7},{5,4},{6,5},{7,6},{8,11},{9,8},{10,9... | collective-permute-start | bytes 196616 | tf_op jit(solution)/shard_map/ppermute | solution.py:70
  137.8 4.6 %collective-permute-start.10 = (bf16[4,8,1024]{2,1,0:T(8,128)(2,1)S(1)}, bf16[4,8,1024]{2,1,0:T(8,128)(2,1)S(1)}, u32[]{:S(2)}, u32[]{:S(2)}) collective-permute-start(bf16[4,8,1024]{2,1,0:T(8,128)(2,1)S(1)} %get-tuple-element.25), channel_id=1, source_target_pairs={{0,2},{1,3},{2,0},{3,1},{4,6},{5,7},{6,4},{7,5},{8,10},{9,11},{10,... | collective-permute-start | bytes 196616 | tf_op jit(solution)/shard_map/ppermute | solution.py:70

commit v9 on v8

--- a/solution.py
+++ b/solution.py
@@ -291,6 +291,7 @@
     mixed = (
         x_float[None] + shifted[None] * (lagging_mixture_weights[1:, None, :] + offsets)
     ).astype(bf16)
+    moved_state, mixed = lax.optimization_barrier((moved_state, mixed))
     main_part = jnp.einsum(
         "inf,ifc->nic", mixed[:4], fourfold_linear_maps, preferred_element_type=f32
     )

time: 155 us -> 153 us (0.987)
  local copies, waits for them, and re-layouts: 33.6 us -> 28.8 us
  waiting for transfers between devices: 50.2 us -> 52.9 us
    all_to_all x2, waiting for transfers between devices: 1.94 us -> 7.72 us  [route_to_slots(): lax.all_to_all(packed, ('batch', 'head'), split_axis=0, concat_axis=0, ti...]
    ppermute x6, waiting for transfers between devices: 20.1 us -> 16.2 us  [exchange_sum(): lax.ppermute(sent, axis_name, [(i, (i + shift) % count) for i in range(co...]
    gather x2, local copies, waits for them, and re-layouts: 3.31 us -> 0.85 us  [per_device(): jnp.take(gathered[STEPS_A:], inverse, axis=1, mode='clip')]
    another operation x2, other arithmetic: 2.7 us -> 1.04 us  [exchange_copies(): return jnp.take(jnp.stack(received), shifts, axis=0, mode='clip')]
  transfers between devices with their start and end apart: 14 -> 14, of which waited for: 9 -> 8; matrix products, arithmetic and copies ran while one was open for 17% -> 10% of each run, Pallas kernels for 0% -> 0%
where the time goes in v9:
time: 153 us; the launch traced here: 152 us
  waiting for transfers between devices  52.9 us (35%)
  starting transfers between devices  29.8 us (19%)
  local copies, waits for them, and re-layouts  28.8 us (19%)
  other arithmetic  16.7 us (11%)
  Pallas kernels  11.4 us (7%)
  matrix products  11.1 us (7%)
    ppermute x6, waiting for transfers between devices, exchange_copies(): lax.ppermute(value, axis_name, [(i, (i + shift) % count) for i in range(c...  29 us
    ppermute x6, waiting for transfers between devices, exchange_sum(): lax.ppermute(sent, axis_name, [(i, (i + shift) % count) for i in range(co...  16.2 us
    ppermute x6, starting transfers between devices, exchange_copies(): lax.ppermute(value, axis_name, [(i, (i + shift) % count) for i in range(c...  11.7 us
    all_to_all x2, starting transfers between devices, route_to_slots(): lax.all_to_all(packed, ('batch', 'head'), split_axis=0, concat_axis=0, ti...  11 us
    all_to_all x2, waiting for transfers between devices, route_to_slots(): lax.all_to_all(packed, ('batch', 'head'), split_axis=0, concat_axis=0, ti...  7.72 us
    ppermute x6, starting transfers between devices, exchange_sum(): lax.ppermute(sent, axis_name, [(i, (i + shift) % count) for i in range(co...  7.06 us
    pallas_call x1, Pallas kernels, run_recurrence(): pl.pallas_call(functools.partial(recurrence_kernel, steps), grid=(rows //...  6.4 us
    dot_general x1, matrix products, per_device(): jnp.einsum('inf,ifc->nic', mixed[:4], fourfold_linear_maps, preferred_ele...  5.17 us
  transfers between devices with their start and end apart: 14, of which 8 were waited for; matrix products, arithmetic and copies ran while one was open for 10% of the time, Pallas kernels for 0%

profile of v9, /device:TPU:0, one launch (start us, length us, event | category | flops | bytes accessed | tf_op | source)
XLA Modules:
  0.0 151.9 jit_solution(13345111482219326883)
XLA Ops:
  0.7 0.8 and_select_fusion.4
  1.5 1.6 %sort.75 = (s32[32]{0:T(128)}, s32[32]{0:T(128)S(1)}) sort(s32[32]{0:T(128)S(1)} %and_select_fusion.4, s32[32]{0:T(128)S(1)} %iota.58), dimensions={0}, to_apply=%region_1.2 | sort | flops 160 | bytes 512 | tf_op jit(solution)/shard_map/jit(argsort)/sort | solution.py:47
  3.2 1.3 gather_fusion.2
  4.5 1.2 and_select_fusion.3
  5.8 1.0 sort.74
  6.8 0.7 gather_fusion
  7.9 1.7 %convert_element_type.101 = bf16[8,16,4096]{2,1,0:T(8,128)(2,1)S(1)} convert(f32[8,16,4096]{2,1,0:T(8,128)} %param.17) | non-fusion elementwise | flops 524288 | bytes 3145728 | tf_op jit(solution)/shard_map/convert_element_type | solution.py:269
  9.6 2.2 %gather_fusion.1 = bf16[128,4096]{1,0:T(8,128)(2,1)} fusion(bf16[128,4096]{1,0:T(8,128)(2,1)S(1)} %bitcast.104, s32[1024]{0:T(1024)S(1)} %pad_clamp_fusion.4), kind=kCustom, calls=%fused_computation.1 | custom fusion | bytes 2097664 | tf_op jit(solution)/shard_map/jit(_take)/gather | solution.py:41
  11.8 7.5 %all-to-all-start = ((bf16[16,8,4096]{2,1,0:T(8,128)(2,1)}), bf16[16,8,4096]{2,1,0:T(8,128)(2,1)S(1)}, u32[]{:S(2)}, u32[]{:S(2)}) async-start(bf16[16,8,4096]{2,1,0:T(8,128)(2,1)} %bitcast.110), calls=%async_computation | async-start | bytes 2097152 | tf_op jit(solution)/shard_map/all_to_all | solution.py:44
  19.7 0.7 copy-done.2
  20.6 0.3 convolution_convert_fusion.1
  20.9 3.8 %collective-permute-start.2 = (bf16[128,320]{0,1:T(8,128)(2,1)S(1)}, bf16[128,320]{0,1:T(8,128)(2,1)S(1)}, u32[]{:S(2)}, u32[]{:S(2)}) collective-permute-start(bf16[128,320]{0,1:T(8,128)(2,1)S(1)} %convolution_convert_fusion.1), channel_id=1, source_target_pairs={{0,12},{4,0},{8,4},{12,8},{1,13},{5,1},{9,5},{13,9},{2,14},{6,2},{... | collective-permute-start | bytes 245768 | tf_op jit(solution)/shard_map/ppermute | solution.py:82
  24.7 1.1 collective-permute-start
  25.8 0.6 slice.52
  26.5 1.0 sort.76
  27.7 0.6 pad_clamp_fusion.1
  28.3 0.6 pad_clamp_fusion.2
  28.9 10.4 %collective-permute-done.2 = bf16[128,320]{0,1:T(8,128)(2,1)S(1)} collective-permute-done((bf16[128,320]{0,1:T(8,128)(2,1)S(1)}, bf16[128,320]{0,1:T(8,128)(2,1)S(1)}, u32[]{:S(2)}, u32[]{:S(2)}) %collective-permute-start.2) | collective-permute-done | bytes 81952 | tf_op jit(solution)/shard_map/ppermute | solution.py:82
  39.3 13.6 %collective-permute-done.1 = bf16[128,320]{0,1:T(8,128)(2,1)S(1)} collective-permute-done((bf16[128,320]{0,1:T(8,128)(2,1)S(1)}, bf16[128,320]{0,1:T(8,128)(2,1)S(1)}, u32[]{:S(2)}, u32[]{:S(2)}) %collective-permute-start.1) | collective-permute-done | bytes 81952 | tf_op jit(solution)/shard_map/ppermute | solution.py:82
  52.9 0.6 copy-done.9
  53.6 1.0 pad_maximum_fusion
  54.6 1.4 gather_fusion.4
  56.0 1.0 convert_reduce_fusion
  57.1 3.0 %add_convert_fusion = bf16[5,128,1024]{2,1,0:T(8,128)(2,1)} fusion(bf16[128,5,64]{0,2,1:T(8,128)(2,1)S(1)} %bitcast.122, bf16[5,64,1024]{2,1,0:T(8,128)(2,1)} %param.21, f32[5,1024]{1,0:T(8,128)} %slice.52, f32[128,1024]{1,0:T(8,128)} %copy-done.3, f32[128,1024]{1,0:T(8,128)} %bitcast.109), kind=kOutput, calls=%fused_computation.9 | convolution fusion | flops 86507520 | bytes 3117056 | tf_op jit(solution)/shard_map/nim,imd->ind/dot_general | solution.py:288
  60.1 2.3 %gather_fusion.3 = bf16[128,4096]{1,0:T(8,128)(2,1)} fusion(bf16[128,4096]{1,0:T(8,128)(2,1)S(1)} %bitcast.105, s32[1024]{0:T(1024)} %pad_clamp_fusion.2), kind=kCustom, calls=%fused_computation.3 | custom fusion | bytes 2097664 | tf_op jit(solution)/shard_map/jit(_take)/gather | solution.py:60
  62.4 5.2 %fusion.2 = bf16[128,4,1024]{2,0,1:T(8,128)(2,1)S(1)} fusion(bf16[5,128,1024]{2,1,0:T(8,128)(2,1)} %add_convert_fusion, bf16[4,1024,1024]{2,1,0:T(8,128)(2,1)} %param.22), kind=kOutput, calls=%fused_computation.17 | convolution fusion | flops 1074266112 | bytes 10747904 | tf_op jit(solution)/shard_map/inf,ifc->nic/dot_general | solution.py:295
  67.6 1.8 %copy.26 = bf16[128,4,1024]{2,1,0:T(4,128)(2,1)} copy(bf16[128,4,1024]{2,0,1:T(8,128)(2,1)S(1)} %fusion.2) | data formatting | bytes 2097152 | tf_op jit(solution)/shard_map/inf,ifc->nic/transpose | solution.py:295
  69.5 1.9 %concatenate.22 = bf16[4,4,8,4096]{3,2,1,0:T(8,128)(2,1)S(1)} reshape(bf16[128,4,1024]{2,1,0:T(4,128)(2,1)} %copy.26) | data formatting | bytes 2097152 | tf_op jit(solution)/shard_map/concatenate | solution.py:300
  71.3 1.2 convolution_convert_fusion.2
  72.5 0.9 fusion.19
  73.4 0.7 collective-permute-start.4
  74.2 3.1 %collective-permute-start.5 = (bf16[4,8,4224]{2,1,0:T(8,128)(2,1)}, bf16[4,8,4224]{2,1,0:T(8,128)(2,1)}, u32[]{:S(2)}, u32[]{:S(2)}) collective-permute-start(bf16[4,8,4224]{2,1,0:T(8,128)(2,1)} %get-tuple-element.23), channel_id=1, source_target_pairs={{0,12},{4,0},{8,4},{12,8},{1,13},{5,1},{9,5},{13,9},{2,14},{6,2},{... | collective-permute-start | bytes 811016 | tf_op jit(solution)/shard_map/ppermute | solution.py:70
  77.3 1.6 %sort.77 = (s32[32]{0:T(128)}, s32[32]{0:T(128)S(1)}) sort(s32[32]{0:T(128)S(1)} %copy-done.1, s32[32]{0:T(128)S(1)} %iota.61), dimensions={0}, to_apply=%region_4.5 | sort | flops 160 | bytes 512 | tf_op jit(solution)/shard_map/jit(argsort)/sort | solution.py:359
  79.1 5.9 %collective-permute-done.3 = bf16[4,8,4224]{2,1,0:T(8,128)(2,1)} collective-permute-done((bf16[4,8,4224]{2,1,0:T(8,128)(2,1)}, bf16[4,8,4224]{2,1,0:T(8,128)(2,1)}, u32[]{:S(2)}, u32[]{:S(2)}) %collective-permute-start.3) | collective-permute-done | bytes 270368 | tf_op jit(solution)/shard_map/ppermute | solution.py:70
  85.0 10.3 %collective-permute-done.4 = bf16[4,8,4224]{2,1,0:T(8,128)(2,1)} collective-permute-done((bf16[4,8,4224]{2,1,0:T(8,128)(2,1)}, bf16[4,8,4224]{2,1,0:T(8,128)(2,1)}, u32[]{:S(2)}, u32[]{:S(2)}) %collective-permute-start.4) | collective-permute-done | bytes 270368 | tf_op jit(solution)/shard_map/ppermute | solution.py:70
  95.3 2.0 %fusion.40 = (bf16[4,8,4224]{2,1,0:T(8,128)(2,1)S(1)}, f32[4,8,4224]{2,1,0:T(8,128)}) fusion(bf16[4,8,4224]{2,1,0:T(8,128)(2,1)} %collective-permute-done.5, bf16[4,8,4224]{2,1,0:T(8,128)(2,1)} %collective-permute-done.4, bf16[4,8,4224]{2,1,0:T(8,128)(2,1)} %collective-permute-done.3, s32[]{:T(128)S(6)} %select_n.157, ...), kind=kLoop, calls=%fused_computation.117 | loop fusion | flops 1622016 | bytes 2703364 | tf_op jit(solution)/shard_map/convert.12
  97.4 0.8 reshape.374.value_ref
  98.2 0.9 divide_multiply_fusion
  99.2 0.8 reshape.358.gate_ref
  100.0 0.9 fusion.11
  100.9 0.8 reshape_reshape.30.decay_ref
  101.7 0.8 reshape.373.key_ref
  102.6 0.8 reshape.372.recept_ref
  103.4 0.7 broadcast_in_dim.25
  104.1 6.4 %shard_map.166 = (bf16[4,128,64]{2,1,0:T(8,128)(2,1)}, bf16[9,128,64]{2,1,0:T(8,128)(2,1)}) custom-call(f32[4,128,64]{2,1,0:T(8,128)} %reshape.372.recept_ref, f32[4,128,64]{2,1,0:T(8,128)} %reshape.373.key_ref, f32[4,128,64]{2,1,0:T(8,128)} %reshape.374.value_ref, f32[4,128,64]{2,1,0:T(8,128)} %reshape_reshape.30.decay_ref, ...), custom_call_target="tpu_custom_call" | custom-call | flops 805306368 | bytes 3063808 | tf_op jit(solution)/shard_map/pallas_call | solution.py:176
  110.5 1.0 reshape.361
  111.5 5.3 %collective-permute-start.8 = (bf16[4,8,1024]{2,1,0:T(8,128)(2,1)S(1)}, bf16[4,8,1024]{2,1,0:T(8,128)(2,1)S(1)}, u32[]{:S(2)}, u32[]{:S(2)}) collective-permute-start(bf16[4,8,1024]{2,1,0:T(8,128)(2,1)S(1)} %reshape.361), channel_id=1, source_target_pairs={{0,12},{4,0},{8,4},{12,8},{1,13},{5,1},{9,5},{13,9},{2,14},{6,2},{... | collective-permute-start | bytes 196616 | tf_op jit(solution)/shard_map/ppermute | solution.py:82
  116.8 1.5 %collective-permute-start.7 = (bf16[4,8,1024]{2,1,0:T(8,128)(2,1)S(1)}, bf16[4,8,1024]{2,1,0:T(8,128)(2,1)S(1)}, u32[]{:S(2)}, u32[]{:S(2)}) collective-permute-start(bf16[4,8,1024]{2,1,0:T(8,128)(2,1)S(1)} %reshape.361), channel_id=1, source_target_pairs={{0,8},{4,12},{8,0},{12,4},{1,9},{5,13},{9,1},{13,5},{2,10},{6,14},... | collective-permute-start | bytes 196616 | tf_op jit(solution)/shard_map/ppermute | solution.py:82
  118.4 1.0 stack_reshape.3
  119.7 3.3 %collective-permute-done.7 = bf16[4,8,1024]{2,1,0:T(8,128)(2,1)S(1)} collective-permute-done((bf16[4,8,1024]{2,1,0:T(8,128)(2,1)S(1)}, bf16[4,8,1024]{2,1,0:T(8,128)(2,1)S(1)}, u32[]{:S(2)}, u32[]{:S(2)}) %collective-permute-start.7) | collective-permute-done | bytes 65568 | tf_op jit(solution)/shard_map/ppermute | solution.py:82
  123.0 1.4 collective-permute-done.6
  124.5 0.7 gather_fusion.5
  125.4 0.8 gather_fusion.6
  126.2 0.4 fusion.6
  126.7 0.7 dynamic-slice_bitcast_fusion.2
  127.4 1.7 %collective-permute-start.11 = (bf16[4,8,1024]{2,1,0:T(8,128)(2,1)}, bf16[4,8,1024]{2,1,0:T(8,128)(2,1)S(1)}, u32[]{:S(2)}, u32[]{:S(2)}) collective-permute-start(bf16[4,8,1024]{2,1,0:T(8,128)(2,1)} %get-tuple-element.28), channel_id=1, source_target_pairs={{0,3},{1,0},{2,1},{3,2},{4,7},{5,4},{6,5},{7,6},{8,11},{9,8},{10,9... | collective-permute-start | bytes 196616 | tf_op jit(solution)/shard_map/ppermute | solution.py:70
  129.1 1.5 collective-permute-start.10
  131.2 1.7 %gather_fusion.7 = bf16[128,576]{1,0:T(8,128)(2,1)} fusion(bf16[128,576]{1,0:T(8,128)(2,1)S(1)} %reshape_reshape.31, s32[1024]{0:T(1024)} %copy-done.13), kind=kCustom, calls=%fused_computation.7 | custom fusion | bytes 295424 | tf_op jit(solution)/shard_map/jit(_take)/gather | solution.py:41
  132.8 3.5 %all-to-all-start.1 = ((bf16[16,8,576]{2,1,0:T(8,128)(2,1)}), bf16[16,8,576]{2,1,0:T(8,128)(2,1)S(1)}, u32[]{:S(2)}, u32[]{:S(2)}) async-start(bf16[16,8,576]{2,1,0:T(8,128)(2,1)} %bitcast.46), calls=%async_computation.1 | async-start | bytes 327680 | tf_op jit(solution)/shard_map/all_to_all | solution.py:44
  136.4 0.6 fusion.43
  137.1 7.7 %all-to-all-done.1 = bf16[16,8,576]{2,1,0:T(8,128)(2,1)S(1)} async-done(((bf16[16,8,576]{2,1,0:T(8,128)(2,1)}), bf16[16,8,576]{2,1,0:T(8,128)(2,1)S(1)}, u32[]{:S(2)}, u32[]{:S(2)}) %all-to-all-start.1) | async-done | bytes 147488 | tf_op jit(solution)/shard_map/all_to_all | solution.py:44
  144.8 1.0 gather_fusion.8
  146.0 0.8 copy.33
  146.9 5.0 %shard_map.167 = f32[128,4096]{1,0:T(8,128)} custom-call(bf16[128,4096]{1,0:T(8,128)(2,1)} %gather_fusion.3, bf16[9,128,64]{2,1,0:T(8,128)(2,1)} %bitcast.115), custom_call_target="tpu_custom_call" | custom-call | flops 603979776 | bytes 3293184 | tf_op jit(solution)/shard_map/pallas_call | solution.py:220
  (95 shorter events, 3.1 us)
Async XLA Ops:
  0.6 125.6 %copy-start = (bf16[1024,1024]{1,0:T(8,128)(2,1)S(1)}, bf16[1024,1024]{1,0:T(8,128)(2,1)}, u32[]{:S(2)}) copy-start(bf16[1024,1024]{1,0:T(8,128)(2,1)} %param.29) | copy-start | bytes 6291460
  7.9 1.7 %copy-start.13 = (s32[1024]{0:T(1024)}, s32[1024]{0:T(1024)S(1)}, u32[]{:S(2)}) copy-start(s32[1024]{0:T(1024)S(1)} %pad_clamp_fusion.4) | copy-start | bytes 12292
  11.8 7.5 %copy-start.4 = (bf16[4,32,1024]{2,1,0:T(8,128)(2,1)S(1)}, bf16[4,32,1024]{2,1,0:T(8,128)(2,1)}, u32[]{:S(2)}) copy-start(bf16[4,32,1024]{2,1,0:T(8,128)(2,1)} %param.15) | copy-start | bytes 786436
  11.8 7.6 %copy-start.11 = (bf16[32,1024]{1,0:T(8,128)(2,1)S(1)}, bf16[32,1024]{1,0:T(8,128)(2,1)}, u32[]{:S(2)}) copy-start(bf16[32,1024]{1,0:T(8,128)(2,1)} %param.16) | copy-start | bytes 196612
  11.8 48.3 %all-to-all-start = ((bf16[16,8,4096]{2,1,0:T(8,128)(2,1)}), bf16[16,8,4096]{2,1,0:T(8,128)(2,1)S(1)}, u32[]{:S(2)}, u32[]{:S(2)}) async-start(bf16[16,8,4096]{2,1,0:T(8,128)(2,1)} %bitcast.110), calls=%async_computation | async-start | bytes 2097152 | tf_op jit(solution)/shard_map/all_to_all | solution.py:44
  19.4 1.1 copy-start.5
  19.4 1.1 slice-start.1
  19.6 6.3 %copy-start.12 = (f32[6,1024]{1,0:T(8,128)S(1)}, f32[6,1024]{1,0:T(8,128)}, u32[]{:S(2)}) copy-start(f32[6,1024]{1,0:T(8,128)} %param.19) | copy-start | bytes 73732
  19.6 6.9 %copy-start.18 = (s32[8]{0:T(128)S(1)}, s32[8]{0:T(128)}, u32[]{:S(2)}) copy-start(s32[8]{0:T(128)} %get-tuple-element.36) | copy-start | bytes 100
  19.6 0.8 copy-start.2
  19.7 1.2 copy-start.3
  20.9 18.4 %collective-permute-start.2 = (bf16[128,320]{0,1:T(8,128)(2,1)S(1)}, bf16[128,320]{0,1:T(8,128)(2,1)S(1)}, u32[]{:S(2)}, u32[]{:S(2)}) collective-permute-start(bf16[128,320]{0,1:T(8,128)(2,1)S(1)} %convolution_convert_fusion.1), channel_id=1, source_target_pairs={{0,12},{4,0},{8,4},{12,8},{1,13},{5,1},{9,5},{13,9},{2,14},{6,2},{... | collective-permute-start | bytes 245768 | tf_op jit(solution)/shard_map/ppermute | solution.py:82
  24.7 28.2 %collective-permute-start.1 = (bf16[128,320]{0,1:T(8,128)(2,1)S(1)}, bf16[128,320]{0,1:T(8,128)(2,1)S(1)}, u32[]{:S(2)}, u32[]{:S(2)}) collective-permute-start(bf16[128,320]{0,1:T(8,128)(2,1)S(1)} %convolution_convert_fusion.1), channel_id=1, source_target_pairs={{0,8},{4,12},{8,0},{12,4},{1,9},{5,13},{9,1},{13,5},{2,10},{6,14},... | collective-permute-start | bytes 245768 | tf_op jit(solution)/shard_map/ppermute | solution.py:82
  24.7 28.2 %collective-permute-start = (bf16[128,320]{0,1:T(8,128)(2,1)S(1)}, bf16[128,320]{0,1:T(8,128)(2,1)S(1)}, u32[]{:S(2)}, u32[]{:S(2)}) collective-permute-start(bf16[128,320]{0,1:T(8,128)(2,1)S(1)} %convolution_convert_fusion.1), channel_id=1, source_target_pairs={{0,4},{4,8},{8,12},{12,0},{1,5},{5,9},{9,13},{13,1},{2,6},{6,10},{... | collective-permute-start | bytes 245768 | tf_op jit(solution)/shard_map/ppermute | solution.py:82
  39.3 13.6 %copy-start.8 = (bf16[128,320]{0,1:T(8,128)(2,1)}, bf16[128,320]{0,1:T(8,128)(2,1)S(1)}, u32[]{:S(2)}) copy-start(bf16[128,320]{0,1:T(8,128)(2,1)S(1)} %collective-permute-done.2) | copy-start | bytes 245764
  52.9 0.6 copy-start.9
  52.9 0.7 copy-start.10
  67.6 3.7 %slice-start = ((bf16[5,128,1024]{2,1,0:T(8,128)(2,1)}), bf16[1,128,1024]{2,1,0:T(8,128)(2,1)S(1)}, s32[]{:S(2)}) async-start(bf16[5,128,1024]{2,1,0:T(8,128)(2,1)} %add_convert_fusion), calls=%async_computation.2 | async-start | bytes 524288 | tf_op jit(solution)/shard_map/slice | solution.py:298
  69.4 7.8 %copy-start.1 = (s32[32]{0:T(128)S(1)}, s32[32]{0:T(128)}, u32[]{:S(2)}) copy-start(s32[32]{0:T(128)} %param.18) | copy-start | bytes 388
  69.4 9.4 %copy-start.15 = (f32[1024]{0:T(1024)S(1)}, f32[1024]{0:T(1024)}, u32[]{:S(2)}) copy-start(f32[1024]{0:T(1024)} %param.26) | copy-start | bytes 12292
  69.4 9.5 %copy-start.16 = (f32[1024]{0:T(1024)S(1)}, f32[1024]{0:T(1024)}, u32[]{:S(2)}) copy-start(f32[1024]{0:T(1024)} %param.27) | copy-start | bytes 12292
  69.4 9.6 %copy-start.17 = (f32[1024]{0:T(1024)S(1)}, f32[1024]{0:T(1024)}, u32[]{:S(2)}) copy-start(f32[1024]{0:T(1024)} %param.28) | copy-start | bytes 12292
  73.4 11.6 %collective-permute-start.3 = (bf16[4,8,4224]{2,1,0:T(8,128)(2,1)}, bf16[4,8,4224]{2,1,0:T(8,128)(2,1)}, u32[]{:S(2)}, u32[]{:S(2)}) collective-permute-start(bf16[4,8,4224]{2,1,0:T(8,128)(2,1)} %get-tuple-element.21), channel_id=1, source_target_pairs={{0,4},{4,8},{8,12},{12,0},{1,5},{5,9},{9,13},{13,1},{2,6},{6,10},{... | collective-permute-start | bytes 811016 | tf_op jit(solution)/shard_map/ppermute | solution.py:70
  73.4 21.9 %collective-permute-start.4 = (bf16[4,8,4224]{2,1,0:T(8,128)(2,1)}, bf16[4,8,4224]{2,1,0:T(8,128)(2,1)}, u32[]{:S(2)}, u32[]{:S(2)}) collective-permute-start(bf16[4,8,4224]{2,1,0:T(8,128)(2,1)} %get-tuple-element.22), channel_id=1, source_target_pairs={{0,8},{4,12},{8,0},{12,4},{1,9},{5,13},{9,1},{13,5},{2,10},{6,14},... | collective-permute-start | bytes 811016 | tf_op jit(solution)/shard_map/ppermute | solution.py:70
  74.2 21.2 %collective-permute-start.5 = (bf16[4,8,4224]{2,1,0:T(8,128)(2,1)}, bf16[4,8,4224]{2,1,0:T(8,128)(2,1)}, u32[]{:S(2)}, u32[]{:S(2)}) collective-permute-start(bf16[4,8,4224]{2,1,0:T(8,128)(2,1)} %get-tuple-element.23), channel_id=1, source_target_pairs={{0,12},{4,0},{8,4},{12,8},{1,13},{5,1},{9,5},{13,9},{2,14},{6,2},{... | collective-permute-start | bytes 811016 | tf_op jit(solution)/shard_map/ppermute | solution.py:70
  79.1 20.9 %copy-start.7 = (bf16[128,1024]{1,0:T(8,128)(2,1)S(1)}, bf16[128,1024]{1,0:T(8,128)(2,1)}, u32[]{:S(2)}) copy-start(bf16[128,1024]{1,0:T(8,128)(2,1)} %param.24) | copy-start | bytes 786436
  79.1 20.9 %copy-start.14 = (f32[1024]{0:T(1024)S(1)}, f32[1024]{0:T(1024)}, u32[]{:S(2)}) copy-start(f32[1024]{0:T(1024)} %param.25) | copy-start | bytes 12292
  111.5 8.2 %collective-permute-start.8 = (bf16[4,8,1024]{2,1,0:T(8,128)(2,1)S(1)}, bf16[4,8,1024]{2,1,0:T(8,128)(2,1)S(1)}, u32[]{:S(2)}, u32[]{:S(2)}) collective-permute-start(bf16[4,8,1024]{2,1,0:T(8,128)(2,1)S(1)} %reshape.361), channel_id=1, source_target_pairs={{0,12},{4,0},{8,4},{12,8},{1,13},{5,1},{9,5},{13,9},{2,14},{6,2},{... | collective-permute-start | bytes 196616 | tf_op jit(solution)/shard_map/ppermute | solution.py:82
  116.8 6.2 %collective-permute-start.7 = (bf16[4,8,1024]{2,1,0:T(8,128)(2,1)S(1)}, bf16[4,8,1024]{2,1,0:T(8,128)(2,1)S(1)}, u32[]{:S(2)}, u32[]{:S(2)}) collective-permute-start(bf16[4,8,1024]{2,1,0:T(8,128)(2,1)S(1)} %reshape.361), channel_id=1, source_target_pairs={{0,8},{4,12},{8,0},{12,4},{1,9},{5,13},{9,1},{13,5},{2,10},{6,14},... | collective-permute-start | bytes 196616 | tf_op jit(solution)/shard_map/ppermute | solution.py:82
  118.4 6.1 %collective-permute-start.6 = (bf16[4,8,1024]{2,1,0:T(8,128)(2,1)S(1)}, bf16[4,8,1024]{2,1,0:T(8,128)(2,1)S(1)}, u32[]{:S(2)}, u32[]{:S(2)}) collective-permute-start(bf16[4,8,1024]{2,1,0:T(8,128)(2,1)S(1)} %reshape.361), channel_id=1, source_target_pairs={{0,4},{4,8},{8,12},{12,0},{1,5},{5,9},{9,13},{13,1},{2,6},{6,10},{... | collective-permute-start | bytes 196616 | tf_op jit(solution)/shard_map/ppermute | solution.py:82
  125.2 5.4 %copy-start.6 = (bf16[9,128,64]{2,1,0:T(8,128)(2,1)S(1)}, bf16[9,128,64]{2,1,0:T(8,128)(2,1)}, u32[]{:S(2)}) copy-start(bf16[9,128,64]{2,1,0:T(8,128)(2,1)} %get-tuple-element.18) | copy-start | bytes 442372
  127.4 9.0 %collective-permute-start.9 = (bf16[4,8,1024]{2,1,0:T(8,128)(2,1)}, bf16[4,8,1024]{2,1,0:T(8,128)(2,1)S(1)}, u32[]{:S(2)}, u32[]{:S(2)}) collective-permute-start(bf16[4,8,1024]{2,1,0:T(8,128)(2,1)} %get-tuple-element.27), channel_id=1, source_target_pairs={{0,1},{1,2},{2,3},{3,0},{4,5},{5,6},{6,7},{7,4},{8,9},{9,10},{10,1... | collective-permute-start | bytes 196616 | tf_op jit(solution)/shard_map/ppermute | solution.py:70
  127.4 9.0 %collective-permute-start.11 = (bf16[4,8,1024]{2,1,0:T(8,128)(2,1)}, bf16[4,8,1024]{2,1,0:T(8,128)(2,1)S(1)}, u32[]{:S(2)}, u32[]{:S(2)}) collective-permute-start(bf16[4,8,1024]{2,1,0:T(8,128)(2,1)} %get-tuple-element.28), channel_id=1, source_target_pairs={{0,3},{1,0},{2,1},{3,2},{4,7},{5,4},{6,5},{7,6},{8,11},{9,8},{10,9... | collective-permute-start | bytes 196616 | tf_op jit(solution)/shard_map/ppermute | solution.py:70
  129.1 7.2 %collective-permute-start.10 = (bf16[4,8,1024]{2,1,0:T(8,128)(2,1)}, bf16[4,8,1024]{2,1,0:T(8,128)(2,1)S(1)}, u32[]{:S(2)}, u32[]{:S(2)}) collective-permute-start(bf16[4,8,1024]{2,1,0:T(8,128)(2,1)} %get-tuple-element.29), channel_id=1, source_target_pairs={{0,2},{1,3},{2,0},{3,1},{4,6},{5,7},{6,4},{7,5},{8,10},{9,11},{10,... | collective-permute-start | bytes 196616 | tf_op jit(solution)/shard_map/ppermute | solution.py:70
  132.8 12.0 %all-to-all-start.1 = ((bf16[16,8,576]{2,1,0:T(8,128)(2,1)}), bf16[16,8,576]{2,1,0:T(8,128)(2,1)S(1)}, u32[]{:S(2)}, u32[]{:S(2)}) async-start(bf16[16,8,576]{2,1,0:T(8,128)(2,1)} %bitcast.46), calls=%async_computation.1 | async-start | bytes 327680 | tf_op jit(solution)/shard_map/all_to_all | solution.py:44

commit v10 on v8

--- a/solution.py
+++ b/solution.py
@@ -265,9 +265,6 @@
     f32 = jnp.float32
     bf16 = jnp.bfloat16
 
-    moved_state = route_to_slots(
-        stream_kept_tableaux.astype(bf16), position_mapping_target, batch_index, head_index
-    )
 
     previous = jnp.concatenate([preceding_feed_each_stream[None], tier_feed_tensor[:-1]], axis=0)
 
@@ -300,6 +297,11 @@
         .astype(bf16)
         .reshape(batch_count, steps, local_rows, -1),
         "batch",
+    )
+
+    kept_for_move, aggregated = lax.optimization_barrier((stream_kept_tableaux, aggregated))
+    moved_state = route_to_slots(
+        kept_for_move.astype(bf16), position_mapping_target, batch_index, head_index
     )
 
     def heads_of(value):
@@ -333,6 +335,7 @@
     mixed_rows, payload = run_recurrence(
         projected, params, stream_kept_tableaux.reshape(rows_here, -1)
     )
+    moved_state, mixed_rows, payload = lax.optimization_barrier((moved_state, mixed_rows, payload))
     combined_response = mixed_rows.reshape(steps, local_rows, width)
     pieces = payload.shape[0]
     moved_terms = route_to_slots(

time: 155 us -> 133 us (0.86)
  waiting for transfers between devices: 50.2 us -> 32.9 us
  local copies, waits for them, and re-layouts: 33.6 us -> 27.9 us
  starting transfers between devices: 30.7 us -> 32.5 us
    ppermute x6, waiting for transfers between devices: 28.2 us -> 6.32 us  [exchange_copies(): lax.ppermute(value, axis_name, [(i, (i + shift) % count) for i in range(c...]
    all_to_all x2, waiting for transfers between devices: 1.94 us -> 9.27 us  [route_to_slots(): lax.all_to_all(packed, ('batch', 'head'), split_axis=0, concat_axis=0, ti...]
    ppermute x6, waiting for transfers between devices: 20.1 us -> 17.3 us  [exchange_sum(): lax.ppermute(sent, axis_name, [(i, (i + shift) % count) for i in range(co...]
    gather x2, local copies, waits for them, and re-layouts: 3.31 us -> 0.85 us  [per_device(): jnp.take(gathered[STEPS_A:], inverse, axis=1, mode='clip')]
    ppermute x6, starting transfers between devices: 11 us -> 13.3 us  [exchange_copies(): lax.ppermute(value, axis_name, [(i, (i + shift) % count) for i in range(c...]
    add x0 -> x1, other arithmetic: none -> 2.07 us  [exchange_sum(): total + lax.ppermute(sent, axis_name, [(i, (i + shift) % count) for i in...]
    another operation x4, local copies, waits for them, and re-layouts: 3.21 us -> 5.06 us  [by_row(): return value.reshape(steps, rows_here, SUBSPACE_EXTENT)]
    another operation x2, other arithmetic: 2.7 us -> 1.08 us  [exchange_copies(): return jnp.take(jnp.stack(received), shifts, axis=0, mode='clip')]
  transfers between devices with their start and end apart: 14 -> 14, of which waited for: 9 -> 6; matrix products, arithmetic and copies ran while one was open for 17% -> 17% of each run, Pallas kernels for 0% -> 5%
where the time goes in v10:
time: 133 us; the launch traced here: 132 us
  waiting for transfers between devices  32.9 us (25%)
  starting transfers between devices  32.5 us (24%)
  local copies, waits for them, and re-layouts  27.9 us (21%)
  other arithmetic  16.4 us (12%)
  Pallas kernels  11.4 us (9%)
  matrix products  10.1 us (8%)
    ppermute x6, waiting for transfers between devices, exchange_sum(): lax.ppermute(sent, axis_name, [(i, (i + shift) % count) for i in range(co...  17.3 us
    ppermute x6, starting transfers between devices, exchange_copies(): lax.ppermute(value, axis_name, [(i, (i + shift) % count) for i in range(c...  13.3 us
    all_to_all x2, starting transfers between devices, route_to_slots(): lax.all_to_all(packed, ('batch', 'head'), split_axis=0, concat_axis=0, ti...  11.5 us
    all_to_all x2, waiting for transfers between devices, route_to_slots(): lax.all_to_all(packed, ('batch', 'head'), split_axis=0, concat_axis=0, ti...  9.27 us
    ppermute x6, starting transfers between devices, exchange_sum(): lax.ppermute(sent, axis_name, [(i, (i + shift) % count) for i in range(co...  7.75 us
    pallas_call x1, Pallas kernels, run_recurrence(): pl.pallas_call(functools.partial(recurrence_kernel, steps), grid=(rows //...  6.39 us
    ppermute x6, waiting for transfers between devices, exchange_copies(): lax.ppermute(value, axis_name, [(i, (i + shift) % count) for i in range(c...  6.32 us
    dot_general x1, matrix products, per_device(): jnp.einsum('inf,ifc->nic', mixed[:4], fourfold_linear_maps, preferred_ele...  5.3 us
  transfers between devices with their start and end apart: 14, of which 6 were waited for; matrix products, arithmetic and copies ran while one was open for 17% of the time, Pallas kernels for 5%

profile of v10, /device:TPU:0, one launch (start us, length us, event | category | flops | bytes accessed | tf_op | source)
XLA Modules:
  0.0 132.4 jit_solution(4971245740769312976)
XLA Ops:
  0.6 1.1 slice_bitcast_fusion
  1.7 1.0 convert_bitcast_fusion
  2.8 0.9 convert_bitcast_fusion.1
  3.9 0.3 convolution_convert_fusion.1
  4.3 5.1 %collective-permute-start.2 = (bf16[128,320]{0,1:T(8,128)(2,1)S(1)}, bf16[128,320]{0,1:T(8,128)(2,1)S(1)}, u32[]{:S(2)}, u32[]{:S(2)}) collective-permute-start(bf16[128,320]{0,1:T(8,128)(2,1)S(1)} %convolution_convert_fusion.1), channel_id=1, source_target_pairs={{0,12},{4,0},{8,4},{12,8},{1,13},{5,1},{9,5},{13,9},{2,14},{6,2},{... | collective-permute-start | bytes 245768 | tf_op jit(solution)/shard_map/ppermute | solution.py:82
  9.4 1.0 collective-permute-start
  10.5 1.6 %sort.75 = (s32[32]{0:T(128)}, s32[32]{0:T(128)S(1)}) sort(s32[32]{0:T(128)S(1)} %and_select_fusion.3, s32[32]{0:T(128)S(1)} %iota.59), dimensions={0}, to_apply=%region_2.3 | sort | flops 160 | bytes 512 | tf_op jit(solution)/shard_map/jit(argsort)/sort | solution.py:47
  12.2 0.6 gather_fusion.3
  13.1 1.0 sort.74
  14.0 0.7 gather_fusion.1
  15.0 1.9 %collective-permute-done.1 = bf16[128,320]{0,1:T(8,128)(2,1)S(1)} collective-permute-done((bf16[128,320]{0,1:T(8,128)(2,1)S(1)}, bf16[128,320]{0,1:T(8,128)(2,1)S(1)}, u32[]{:S(2)}, u32[]{:S(2)}) %collective-permute-start.1) | collective-permute-done | bytes 81952 | tf_op jit(solution)/shard_map/ppermute | solution.py:82
  16.9 0.6 copy-done.9
  17.5 1.0 pad_maximum_fusion
  18.6 1.3 gather_fusion
  19.9 1.0 convert_reduce_fusion
  21.0 1.7 %add_convert_fusion = bf16[5,128,1024]{2,1,0:T(8,128)(2,1)S(1)} fusion(bf16[128,5,64]{0,2,1:T(8,128)(2,1)S(1)} %bitcast.121, bf16[5,64,1024]{2,1,0:T(8,128)(2,1)} %param.21, f32[5,1024]{1,0:T(8,128)S(1)} %slice.52, f32[128,1024]{1,0:T(8,128)S(1)} %bitcast_subtract_fusion, f32[128,1024]{1,0:T(8,128)S(1)} %bitcast.108), kind=kOutput, calls=%fused_computation.9 | convolution fusion | flops 86507520 | bytes 3117056 | tf_op jit(solution)/shard_map/nim,imd->ind/dot_general | solution.py:285
  22.7 5.3 %fusion.2 = bf16[128,4,1024]{2,0,1:T(8,128)(2,1)S(1)} fusion(bf16[5,128,1024]{2,1,0:T(8,128)(2,1)S(1)} %add_convert_fusion, bf16[4,1024,1024]{2,1,0:T(8,128)(2,1)} %param.22), kind=kOutput, calls=%fused_computation.17 | convolution fusion | flops 1074266112 | bytes 10747904 | tf_op jit(solution)/shard_map/inf,ifc->nic/dot_general | solution.py:291
  28.0 1.8 %copy.26 = bf16[128,4,1024]{2,1,0:T(4,128)(2,1)} copy(bf16[128,4,1024]{2,0,1:T(8,128)(2,1)S(1)} %fusion.2) | data formatting | bytes 2097152 | tf_op jit(solution)/shard_map/inf,ifc->nic/transpose | solution.py:291
  29.8 1.9 %concatenate.22 = bf16[4,4,8,4096]{3,2,1,0:T(8,128)(2,1)S(1)} reshape(bf16[128,4,1024]{2,1,0:T(4,128)(2,1)} %copy.26) | data formatting | bytes 2097152 | tf_op jit(solution)/shard_map/concatenate | solution.py:296
  31.7 1.2 convolution_convert_fusion.2
  32.9 0.9 fusion.19
  33.8 0.6 collective-permute-start.3
  34.4 2.1 %collective-permute-start.4 = (bf16[4,8,4224]{2,1,0:T(8,128)(2,1)}, bf16[4,8,4224]{2,1,0:T(8,128)(2,1)}, u32[]{:S(2)}, u32[]{:S(2)}) collective-permute-start(bf16[4,8,4224]{2,1,0:T(8,128)(2,1)} %get-tuple-element.26), channel_id=1, source_target_pairs={{0,8},{4,12},{8,0},{12,4},{1,9},{5,13},{9,1},{13,5},{2,10},{6,14},... | collective-permute-start | bytes 811016 | tf_op jit(solution)/shard_map/ppermute | solution.py:70
  36.5 1.8 %collective-permute-start.5 = (bf16[4,8,4224]{2,1,0:T(8,128)(2,1)}, bf16[4,8,4224]{2,1,0:T(8,128)(2,1)}, u32[]{:S(2)}, u32[]{:S(2)}) collective-permute-start(bf16[4,8,4224]{2,1,0:T(8,128)(2,1)} %get-tuple-element.27), channel_id=1, source_target_pairs={{0,12},{4,0},{8,4},{12,8},{1,13},{5,1},{9,5},{13,9},{2,14},{6,2},{... | collective-permute-start | bytes 811016 | tf_op jit(solution)/shard_map/ppermute | solution.py:70
  38.5 6.9 %collective-permute-done.3 = bf16[4,8,4224]{2,1,0:T(8,128)(2,1)} collective-permute-done((bf16[4,8,4224]{2,1,0:T(8,128)(2,1)}, bf16[4,8,4224]{2,1,0:T(8,128)(2,1)}, u32[]{:S(2)}, u32[]{:S(2)}) %collective-permute-start.3) | collective-permute-done | bytes 270368 | tf_op jit(solution)/shard_map/ppermute | solution.py:70
  45.4 10.4 %collective-permute-done.4 = bf16[4,8,4224]{2,1,0:T(8,128)(2,1)} collective-permute-done((bf16[4,8,4224]{2,1,0:T(8,128)(2,1)}, bf16[4,8,4224]{2,1,0:T(8,128)(2,1)}, u32[]{:S(2)}, u32[]{:S(2)}) %collective-permute-start.4) | collective-permute-done | bytes 270368 | tf_op jit(solution)/shard_map/ppermute | solution.py:70
  55.8 2.1 %fusion.13 = f32[4,8,4224]{2,1,0:T(8,128)} fusion(bf16[4,8,4224]{2,1,0:T(8,128)(2,1)} %collective-permute-done.5, bf16[4,8,4224]{2,1,0:T(8,128)(2,1)} %collective-permute-done.4, bf16[4,8,4224]{2,1,0:T(8,128)(2,1)} %collective-permute-done.3, s32[]{:T(128)S(6)} %select_n.148, bf16[4,4,8,4096]{3,2,1,0:T(8,128)(2,1)S(1)} %concatenate.22, ...), kind=kLoop, calls=%fused_computation.33 | loop fusion | flops 1486848 | bytes 2433028 | tf_op jit(solution)/shard_map/add | solution.py:70
  58.0 2.2 %gather_fusion.2 = bf16[128,4096]{1,0:T(8,128)(2,1)} fusion(bf16[128,4096]{1,0:T(8,128)(2,1)S(1)} %bitcast.103, s32[1024]{0:T(1024)S(1)} %pad_clamp_fusion.3), kind=kCustom, calls=%fused_computation.2 | custom fusion | bytes 2097664 | tf_op jit(solution)/shard_map/jit(_take)/gather | solution.py:41
  60.2 8.0 %all-to-all-start = ((bf16[16,8,4096]{2,1,0:T(8,128)(2,1)}), bf16[16,8,4096]{2,1,0:T(8,128)(2,1)S(1)}, u32[]{:S(2)}, u32[]{:S(2)}) async-start(bf16[16,8,4096]{2,1,0:T(8,128)(2,1)} %bitcast.109), calls=%async_computation | async-start | bytes 2097152 | tf_op jit(solution)/shard_map/all_to_all | solution.py:44
  68.2 1.6 %sort.77 = (s32[32]{0:T(128)}, s32[32]{0:T(128)}) sort(s32[32]{0:T(128)S(1)} %copy-done.1, s32[32]{0:T(128)S(1)} %iota.61), dimensions={0}, to_apply=%region_4.5 | sort | flops 160 | bytes 512 | tf_op jit(solution)/shard_map/jit(argsort)/sort | solution.py:361
  70.0 1.0 sort.76
  71.3 0.6 maximum_bitcast_fusion
  71.9 1.1 convert.25
  73.0 0.9 divide_multiply_fusion
  74.0 0.8 reshape.358.gate_ref
  74.8 0.7 slice_convert_fusion
  75.5 1.7 %reshape.374.value_ref = f32[4,128,64]{2,1,0:T(8,128)} reshape(f32[4,8,1024]{2,1,0:T(8,128)} %get-tuple-element.28) | data formatting | bytes 262144 | tf_op jit(solution)/shard_map/reshape;reshape | solution.py:326
  77.2 1.1 fusion.11
  78.4 0.8 reshape_reshape.30.decay_ref
  79.2 1.7 %reshape.373.key_ref = f32[4,128,64]{2,1,0:T(8,128)} reshape(f32[4,8,1024]{2,1,0:T(8,128)} %get-tuple-element.29) | data formatting | bytes 262144 | tf_op jit(solution)/shard_map/reshape;reshape | solution.py:326
  80.9 0.8 reshape.372.recept_ref
  81.7 1.4 %broadcast_in_dim.25 = f32[3,8,16,64]{3,2,1,0:T(8,128)} broadcast(f32[3,16,64]{2,1,0:T(8,128)} %maximum_bitcast_fusion), dimensions={0,2,3} | broadcast | bytes 110592 | tf_op jit(solution)/shard_map/broadcast_in_dim | solution.py:329
  83.1 6.4 %shard_map.166 = (bf16[4,128,64]{2,1,0:T(8,128)(2,1)}, bf16[9,128,64]{2,1,0:T(8,128)(2,1)}) custom-call(f32[4,128,64]{2,1,0:T(8,128)} %reshape.372.recept_ref, f32[4,128,64]{2,1,0:T(8,128)} %reshape.373.key_ref, f32[4,128,64]{2,1,0:T(8,128)} %reshape.374.value_ref, f32[4,128,64]{2,1,0:T(8,128)} %reshape_reshape.30.decay_ref, ...), custom_call_target="tpu_custom_call" | custom-call | flops 805306368 | bytes 3063808 | tf_op jit(solution)/shard_map/pallas_call | solution.py:176
  89.5 1.6 %all-to-all-done = bf16[16,8,4096]{2,1,0:T(8,128)(2,1)S(1)} async-done(((bf16[16,8,4096]{2,1,0:T(8,128)(2,1)}), bf16[16,8,4096]{2,1,0:T(8,128)(2,1)S(1)}, u32[]{:S(2)}, u32[]{:S(2)}) %all-to-all-start) | async-done | bytes 1048608 | tf_op jit(solution)/shard_map/all_to_all | solution.py:44
  91.1 2.2 %gather_fusion.4 = bf16[128,4096]{1,0:T(8,128)(2,1)} fusion(bf16[128,4096]{1,0:T(8,128)(2,1)S(1)} %bitcast.104, s32[1024]{0:T(1024)S(1)} %pad_clamp_fusion.1), kind=kCustom, calls=%fused_computation.4 | custom fusion | bytes 2097664 | tf_op jit(solution)/shard_map/jit(_take)/gather | solution.py:60
  93.4 3.2 %collective-permute-start.8 = (bf16[4,8,1024]{2,1,0:T(8,128)(2,1)S(1)}, bf16[4,8,1024]{2,1,0:T(8,128)(2,1)S(1)}, u32[]{:S(2)}, u32[]{:S(2)}) collective-permute-start(bf16[4,8,1024]{2,1,0:T(8,128)(2,1)S(1)} %reshape.361), channel_id=1, source_target_pairs={{0,12},{4,0},{8,4},{12,8},{1,13},{5,1},{9,5},{13,9},{2,14},{6,2},{... | collective-permute-start | bytes 196616 | tf_op jit(solution)/shard_map/ppermute | solution.py:82
  96.6 2.0 %collective-permute-start.7 = (bf16[4,8,1024]{2,1,0:T(8,128)(2,1)S(1)}, bf16[4,8,1024]{2,1,0:T(8,128)(2,1)S(1)}, u32[]{:S(2)}, u32[]{:S(2)}) collective-permute-start(bf16[4,8,1024]{2,1,0:T(8,128)(2,1)S(1)} %reshape.361), channel_id=1, source_target_pairs={{0,8},{4,12},{8,0},{12,4},{1,9},{5,13},{9,1},{13,5},{2,10},{6,14},... | collective-permute-start | bytes 196616 | tf_op jit(solution)/shard_map/ppermute | solution.py:82
  98.6 1.9 %collective-permute-start.6 = (bf16[4,8,1024]{2,1,0:T(8,128)(2,1)S(1)}, bf16[4,8,1024]{2,1,0:T(8,128)(2,1)S(1)}, u32[]{:S(2)}, u32[]{:S(2)}) collective-permute-start(bf16[4,8,1024]{2,1,0:T(8,128)(2,1)S(1)} %reshape.361), channel_id=1, source_target_pairs={{0,4},{4,8},{8,12},{12,0},{1,5},{5,9},{9,13},{13,1},{2,6},{6,10},{... | collective-permute-start | bytes 196616 | tf_op jit(solution)/shard_map/ppermute | solution.py:82
  100.7 4.4 %collective-permute-done.7 = bf16[4,8,1024]{2,1,0:T(8,128)(2,1)S(1)} collective-permute-done((bf16[4,8,1024]{2,1,0:T(8,128)(2,1)S(1)}, bf16[4,8,1024]{2,1,0:T(8,128)(2,1)S(1)}, u32[]{:S(2)}, u32[]{:S(2)}) %collective-permute-start.7) | collective-permute-done | bytes 65568 | tf_op jit(solution)/shard_map/ppermute | solution.py:82
  105.1 0.7 gather_fusion.5
  106.0 0.8 gather_fusion.6
  106.9 0.4 fusion.6
  107.4 0.7 dynamic-slice_bitcast_fusion.2
  108.1 1.7 %collective-permute-start.11 = (bf16[4,8,1024]{2,1,0:T(8,128)(2,1)}, bf16[4,8,1024]{2,1,0:T(8,128)(2,1)S(1)}, u32[]{:S(2)}, u32[]{:S(2)}) collective-permute-start(bf16[4,8,1024]{2,1,0:T(8,128)(2,1)} %get-tuple-element.32), channel_id=1, source_target_pairs={{0,3},{1,0},{2,1},{3,2},{4,7},{5,4},{6,5},{7,6},{8,11},{9,8},{10,9... | collective-permute-start | bytes 196616 | tf_op jit(solution)/shard_map/ppermute | solution.py:70
  109.8 1.5 %collective-permute-start.10 = (bf16[4,8,1024]{2,1,0:T(8,128)(2,1)}, bf16[4,8,1024]{2,1,0:T(8,128)(2,1)S(1)}, u32[]{:S(2)}, u32[]{:S(2)}) collective-permute-start(bf16[4,8,1024]{2,1,0:T(8,128)(2,1)} %get-tuple-element.33), channel_id=1, source_target_pairs={{0,2},{1,3},{2,0},{3,1},{4,6},{5,7},{6,4},{7,5},{8,10},{9,11},{10,... | collective-permute-start | bytes 196616 | tf_op jit(solution)/shard_map/ppermute | solution.py:70
  111.5 0.3 reshape_reshape.31
  111.8 1.5 %gather_fusion.7 = bf16[128,576]{1,0:T(8,128)(2,1)} fusion(bf16[128,576]{1,0:T(8,128)(2,1)S(1)} %reshape_reshape.31, s32[1024]{0:T(1024)S(1)} %pad_clamp_fusion.3), kind=kCustom, calls=%fused_computation.7 | custom fusion | bytes 295424 | tf_op jit(solution)/shard_map/jit(_take)/gather | solution.py:41
  113.4 3.5 %all-to-all-start.1 = ((bf16[16,8,576]{2,1,0:T(8,128)(2,1)}), bf16[16,8,576]{2,1,0:T(8,128)(2,1)S(1)}, u32[]{:S(2)}, u32[]{:S(2)}) async-start(bf16[16,8,576]{2,1,0:T(8,128)(2,1)} %bitcast.46), calls=%async_computation.1 | async-start | bytes 327680 | tf_op jit(solution)/shard_map/all_to_all | solution.py:44
  117.0 0.6 fusion.39
  117.6 7.7 %all-to-all-done.1 = bf16[16,8,576]{2,1,0:T(8,128)(2,1)S(1)} async-done(((bf16[16,8,576]{2,1,0:T(8,128)(2,1)}), bf16[16,8,576]{2,1,0:T(8,128)(2,1)S(1)}, u32[]{:S(2)}, u32[]{:S(2)}) %all-to-all-start.1) | async-done | bytes 147488 | tf_op jit(solution)/shard_map/all_to_all | solution.py:44
  125.3 1.0 gather_fusion.8
  126.3 0.2 reshape_reshape.32
  126.6 0.8 copy.33
  127.4 5.0 %shard_map.167 = f32[128,4096]{1,0:T(8,128)} custom-call(bf16[128,4096]{1,0:T(8,128)(2,1)} %gather_fusion.4, bf16[9,128,64]{2,1,0:T(8,128)(2,1)} %bitcast.114), custom_call_target="tpu_custom_call" | custom-call | flops 603979776 | bytes 3293184 | tf_op jit(solution)/shard_map/pallas_call | solution.py:220
  (92 shorter events, 2.4 us)
Async XLA Ops:
  0.6 106.3 %copy-start = (bf16[1024,1024]{1,0:T(8,128)(2,1)S(1)}, bf16[1024,1024]{1,0:T(8,128)(2,1)}, u32[]{:S(2)}) copy-start(bf16[1024,1024]{1,0:T(8,128)(2,1)} %param.29) | copy-start | bytes 6291460
  2.7 1.2 copy-start.4
  2.8 1.2 slice-start.1
  3.8 6.7 %copy-start.10 = (f32[6,1024]{1,0:T(8,128)S(1)}, f32[6,1024]{1,0:T(8,128)}, u32[]{:S(2)}) copy-start(f32[6,1024]{1,0:T(8,128)} %param.19) | copy-start | bytes 73732
  3.8 6.7 %copy-start.1 = (s32[32]{0:T(128)S(1)}, s32[32]{0:T(128)}, u32[]{:S(2)}) copy-start(s32[32]{0:T(128)} %param.18) | copy-start | bytes 388
  4.3 10.5 %copy-start.6 = (bf16[128,320]{0,1:T(8,128)(2,1)}, bf16[128,320]{0,1:T(8,128)(2,1)S(1)}, u32[]{:S(2)}) copy-start(bf16[128,320]{0,1:T(8,128)(2,1)S(1)} %convolution_convert_fusion.1) | copy-start | bytes 245764
  4.3 10.7 %collective-permute-start.2 = (bf16[128,320]{0,1:T(8,128)(2,1)S(1)}, bf16[128,320]{0,1:T(8,128)(2,1)S(1)}, u32[]{:S(2)}, u32[]{:S(2)}) collective-permute-start(bf16[128,320]{0,1:T(8,128)(2,1)S(1)} %convolution_convert_fusion.1), channel_id=1, source_target_pairs={{0,12},{4,0},{8,4},{12,8},{1,13},{5,1},{9,5},{13,9},{2,14},{6,2},{... | collective-permute-start | bytes 245768 | tf_op jit(solution)/shard_map/ppermute | solution.py:82
  9.4 7.5 %collective-permute-start.1 = (bf16[128,320]{0,1:T(8,128)(2,1)S(1)}, bf16[128,320]{0,1:T(8,128)(2,1)S(1)}, u32[]{:S(2)}, u32[]{:S(2)}) collective-permute-start(bf16[128,320]{0,1:T(8,128)(2,1)S(1)} %convolution_convert_fusion.1), channel_id=1, source_target_pairs={{0,8},{4,12},{8,0},{12,4},{1,9},{5,13},{9,1},{13,5},{2,10},{6,14},... | collective-permute-start | bytes 245768 | tf_op jit(solution)/shard_map/ppermute | solution.py:82
  9.4 7.5 %collective-permute-start = (bf16[128,320]{0,1:T(8,128)(2,1)S(1)}, bf16[128,320]{0,1:T(8,128)(2,1)}, u32[]{:S(2)}, u32[]{:S(2)}) collective-permute-start(bf16[128,320]{0,1:T(8,128)(2,1)S(1)} %convolution_convert_fusion.1), channel_id=1, source_target_pairs={{0,4},{4,8},{8,12},{12,0},{1,5},{5,9},{9,13},{13,1},{2,6},{6,10},{... | collective-permute-start | bytes 245768 | tf_op jit(solution)/shard_map/ppermute | solution.py:82
  14.9 7.8 %copy-start.12 = (s32[1024]{0:T(1024)}, s32[1024]{0:T(1024)S(1)}, u32[]{:S(2)}) copy-start(s32[1024]{0:T(1024)S(1)} %pad_clamp_fusion.5) | copy-start | bytes 12292
  14.9 2.0 %copy-start.8 = (bf16[128,320]{0,1:T(8,128)(2,1)}, bf16[128,320]{0,1:T(8,128)(2,1)S(1)}, u32[]{:S(2)}) copy-start(bf16[128,320]{0,1:T(8,128)(2,1)S(1)} %collective-permute-done.2) | copy-start | bytes 245764
  16.9 0.6 copy-start.9
  22.7 5.3 %copy-start.3 = (bf16[5,128,1024]{2,1,0:T(8,128)(2,1)}, bf16[5,128,1024]{2,1,0:T(8,128)(2,1)S(1)}, u32[]{:S(2)}) copy-start(bf16[5,128,1024]{2,1,0:T(8,128)(2,1)S(1)} %add_convert_fusion) | copy-start | bytes 3932164
  29.8 1.9 %slice-start = ((bf16[5,128,1024]{2,1,0:T(8,128)(2,1)}), bf16[1,128,1024]{2,1,0:T(8,128)(2,1)S(1)}, s32[]{:S(2)}) async-start(bf16[5,128,1024]{2,1,0:T(8,128)(2,1)} %copy-done.3), calls=%async_computation.2 | async-start | bytes 524288 | tf_op jit(solution)/shard_map/slice | solution.py:294
  33.8 11.6 %collective-permute-start.3 = (bf16[4,8,4224]{2,1,0:T(8,128)(2,1)}, bf16[4,8,4224]{2,1,0:T(8,128)(2,1)}, u32[]{:S(2)}, u32[]{:S(2)}) collective-permute-start(bf16[4,8,4224]{2,1,0:T(8,128)(2,1)} %get-tuple-element.25), channel_id=1, source_target_pairs={{0,4},{4,8},{8,12},{12,0},{1,5},{5,9},{9,13},{13,1},{2,6},{6,10},{... | collective-permute-start | bytes 811016 | tf_op jit(solution)/shard_map/ppermute | solution.py:70
  34.4 21.4 %collective-permute-start.4 = (bf16[4,8,4224]{2,1,0:T(8,128)(2,1)}, bf16[4,8,4224]{2,1,0:T(8,128)(2,1)}, u32[]{:S(2)}, u32[]{:S(2)}) collective-permute-start(bf16[4,8,4224]{2,1,0:T(8,128)(2,1)} %get-tuple-element.26), channel_id=1, source_target_pairs={{0,8},{4,12},{8,0},{12,4},{1,9},{5,13},{9,1},{13,5},{2,10},{6,14},... | collective-permute-start | bytes 811016 | tf_op jit(solution)/shard_map/ppermute | solution.py:70
  36.5 19.3 %collective-permute-start.5 = (bf16[4,8,4224]{2,1,0:T(8,128)(2,1)}, bf16[4,8,4224]{2,1,0:T(8,128)(2,1)}, u32[]{:S(2)}, u32[]{:S(2)}) collective-permute-start(bf16[4,8,4224]{2,1,0:T(8,128)(2,1)} %get-tuple-element.27), channel_id=1, source_target_pairs={{0,12},{4,0},{8,4},{12,8},{1,13},{5,1},{9,5},{13,9},{2,14},{6,2},{... | collective-permute-start | bytes 811016 | tf_op jit(solution)/shard_map/ppermute | solution.py:70
  38.5 19.4 %copy-start.2 = (f32[8,16,4096]{2,1,0:T(8,128)S(1)}, f32[8,16,4096]{2,1,0:T(8,128)}, u32[]{:S(2)}) copy-start(f32[8,16,4096]{2,1,0:T(8,128)} %param.17) | copy-start | bytes 6291460
  60.2 9.7 %copy-start.13 = (f32[1024]{0:T(1024)S(1)}, f32[1024]{0:T(1024)}, u32[]{:S(2)}) copy-start(f32[1024]{0:T(1024)} %param.26) | copy-start | bytes 12292
  60.2 9.7 %copy-start.14 = (f32[1024]{0:T(1024)S(1)}, f32[1024]{0:T(1024)}, u32[]{:S(2)}) copy-start(f32[1024]{0:T(1024)} %param.27) | copy-start | bytes 12292
  60.2 9.8 %copy-start.15 = (f32[1024]{0:T(1024)S(1)}, f32[1024]{0:T(1024)}, u32[]{:S(2)}) copy-start(f32[1024]{0:T(1024)} %param.28) | copy-start | bytes 12292
  60.2 30.9 %all-to-all-start = ((bf16[16,8,4096]{2,1,0:T(8,128)(2,1)}), bf16[16,8,4096]{2,1,0:T(8,128)(2,1)S(1)}, u32[]{:S(2)}, u32[]{:S(2)}) async-start(bf16[16,8,4096]{2,1,0:T(8,128)(2,1)} %bitcast.109), calls=%async_computation | async-start | bytes 2097152 | tf_op jit(solution)/shard_map/all_to_all | solution.py:44
  71.3 19.8 %copy-start.11 = (s32[1024]{0:T(1024)}, s32[1024]{0:T(1024)S(1)}, u32[]{:S(2)}) copy-start(s32[1024]{0:T(1024)S(1)} %pad_clamp_fusion.1) | copy-start | bytes 12292
  91.1 2.2 %copy-start.5 = (bf16[4,128,64]{2,1,0:T(8,128)(2,1)S(1)}, bf16[4,128,64]{2,1,0:T(8,128)(2,1)}, u32[]{:S(2)}) copy-start(bf16[4,128,64]{2,1,0:T(8,128)(2,1)} %get-tuple-element.21) | copy-start | bytes 196612
  91.1 9.5 %copy-start.16 = (s32[32]{0:T(128)S(1)}, s32[32]{0:T(128)}, u32[]{:S(2)}) copy-start(s32[32]{0:T(128)} %get-tuple-element.22) | copy-start | bytes 388
  93.4 7.3 %collective-permute-start.8 = (bf16[4,8,1024]{2,1,0:T(8,128)(2,1)S(1)}, bf16[4,8,1024]{2,1,0:T(8,128)(2,1)S(1)}, u32[]{:S(2)}, u32[]{:S(2)}) collective-permute-start(bf16[4,8,1024]{2,1,0:T(8,128)(2,1)S(1)} %reshape.361), channel_id=1, source_target_pairs={{0,12},{4,0},{8,4},{12,8},{1,13},{5,1},{9,5},{13,9},{2,14},{6,2},{... | collective-permute-start | bytes 196616 | tf_op jit(solution)/shard_map/ppermute | solution.py:82
  96.6 8.4 %collective-permute-start.7 = (bf16[4,8,1024]{2,1,0:T(8,128)(2,1)S(1)}, bf16[4,8,1024]{2,1,0:T(8,128)(2,1)S(1)}, u32[]{:S(2)}, u32[]{:S(2)}) collective-permute-start(bf16[4,8,1024]{2,1,0:T(8,128)(2,1)S(1)} %reshape.361), channel_id=1, source_target_pairs={{0,8},{4,12},{8,0},{12,4},{1,9},{5,13},{9,1},{13,5},{2,10},{6,14},... | collective-permute-start | bytes 196616 | tf_op jit(solution)/shard_map/ppermute | solution.py:82
  98.6 6.5 %collective-permute-start.6 = (bf16[4,8,1024]{2,1,0:T(8,128)(2,1)S(1)}, bf16[4,8,1024]{2,1,0:T(8,128)(2,1)S(1)}, u32[]{:S(2)}, u32[]{:S(2)}) collective-permute-start(bf16[4,8,1024]{2,1,0:T(8,128)(2,1)S(1)} %reshape.361), channel_id=1, source_target_pairs={{0,4},{4,8},{8,12},{12,0},{1,5},{5,9},{9,13},{13,1},{2,6},{6,10},{... | collective-permute-start | bytes 196616 | tf_op jit(solution)/shard_map/ppermute | solution.py:82
  105.9 5.4 %copy-start.7 = (bf16[9,128,64]{2,1,0:T(8,128)(2,1)S(1)}, bf16[9,128,64]{2,1,0:T(8,128)(2,1)}, u32[]{:S(2)}) copy-start(bf16[9,128,64]{2,1,0:T(8,128)(2,1)} %get-tuple-element.24) | copy-start | bytes 442372
  108.1 8.8 %collective-permute-start.9 = (bf16[4,8,1024]{2,1,0:T(8,128)(2,1)}, bf16[4,8,1024]{2,1,0:T(8,128)(2,1)S(1)}, u32[]{:S(2)}, u32[]{:S(2)}) collective-permute-start(bf16[4,8,1024]{2,1,0:T(8,128)(2,1)} %get-tuple-element.31), channel_id=1, source_target_pairs={{0,1},{1,2},{2,3},{3,0},{4,5},{5,6},{6,7},{7,4},{8,9},{9,10},{10,1... | collective-permute-start | bytes 196616 | tf_op jit(solution)/shard_map/ppermute | solution.py:70
  108.1 8.9 %collective-permute-start.11 = (bf16[4,8,1024]{2,1,0:T(8,128)(2,1)}, bf16[4,8,1024]{2,1,0:T(8,128)(2,1)S(1)}, u32[]{:S(2)}, u32[]{:S(2)}) collective-permute-start(bf16[4,8,1024]{2,1,0:T(8,128)(2,1)} %get-tuple-element.32), channel_id=1, source_target_pairs={{0,3},{1,0},{2,1},{3,2},{4,7},{5,4},{6,5},{7,6},{8,11},{9,8},{10,9... | collective-permute-start | bytes 196616 | tf_op jit(solution)/shard_map/ppermute | solution.py:70
  109.8 7.1 %collective-permute-start.10 = (bf16[4,8,1024]{2,1,0:T(8,128)(2,1)}, bf16[4,8,1024]{2,1,0:T(8,128)(2,1)S(1)}, u32[]{:S(2)}, u32[]{:S(2)}) collective-permute-start(bf16[4,8,1024]{2,1,0:T(8,128)(2,1)} %get-tuple-element.33), channel_id=1, source_target_pairs={{0,2},{1,3},{2,0},{3,1},{4,6},{5,7},{6,4},{7,5},{8,10},{9,11},{10,... | collective-permute-start | bytes 196616 | tf_op jit(solution)/shard_map/ppermute | solution.py:70
  113.4 12.0 %all-to-all-start.1 = ((bf16[16,8,576]{2,1,0:T(8,128)(2,1)}), bf16[16,8,576]{2,1,0:T(8,128)(2,1)S(1)}, u32[]{:S(2)}, u32[]{:S(2)}) async-start(bf16[16,8,576]{2,1,0:T(8,128)(2,1)} %bitcast.46), calls=%async_computation.1 | async-start | bytes 327680 | tf_op jit(solution)/shard_map/all_to_all | solution.py:44

commit v11 on v10

--- a/solution.py
+++ b/solution.py
@@ -11,6 +11,12 @@
 STEPS_A = 2
 MIX_MAPS = 5
 NORMALIZER_GUARD = 0.00064
+
+
+def index_of(values, count):
+    positions = jnp.arange(values.shape[0], dtype=jnp.int32)
+    wanted = jnp.arange(count, dtype=jnp.int32)
+    return jnp.sum(jnp.where(values[None, :] == wanted[:, None], positions[None, :], 0), axis=1)
 
 
 def route_to_slots(value, position_mapping_target, batch_index, head_index):
@@ -24,7 +30,12 @@
     own_map = lax.dynamic_slice_in_dim(
         position_mapping_target, batch_index * local_rows, local_rows
     )
-    send_order = jnp.argsort(own_map // slots_dev, stable=True)
+    dest_key = own_map // slots_dev
+    positions = jnp.arange(local_rows, dtype=jnp.int32)
+    ahead = (dest_key[None, :] < dest_key[:, None]) | (
+        (dest_key[None, :] == dest_key[:, None]) & (positions[None, :] < positions[:, None])
+    )
+    send_order = index_of(jnp.sum(ahead.astype(jnp.int32), axis=1), local_rows)
     dest = jnp.arange(batch_count * head_count, dtype=jnp.int32)
     dest_block = (dest // head_count) * cluster_number + dest % cluster_number
     quad = (dest % head_count) // cluster_number
@@ -43,12 +54,15 @@
     ).reshape(batch_count * head_count, per_pair * quarter, width)
     arrived = lax.all_to_all(packed, ("batch", "head"), split_axis=0, concat_axis=0, tiled=True)
     target = batch_index * cluster_number + head_index % cluster_number
-    arrivals = lax.dynamic_slice_in_dim(
-        jnp.argsort(position_mapping_target // slots_dev, stable=True),
-        target * slots_dev,
-        slots_dev,
-    )
-    placing = jnp.argsort(jnp.take(position_mapping_target, arrivals, mode="clip") % slots_dev)
+    sessions = position_mapping_target.shape[0]
+    chosen = lax.dynamic_slice_in_dim(
+        index_of(position_mapping_target, sessions), target * slots_dev, slots_dev
+    )
+    every = jnp.arange(sessions, dtype=jnp.int32)
+    coming = (position_mapping_target // slots_dev) == target
+    placing = jnp.sum(
+        ((every[None, :] < chosen[:, None]) & coming[None, :]).astype(jnp.int32), axis=1
+    )
     source_head = jnp.arange(head_count, dtype=jnp.int32)
     kept_rows = (
         (
@@ -64,14 +78,20 @@
 def exchange_sum(pieces, axis_name):
     count = lax.axis_size(axis_name)
     index = lax.axis_index(axis_name)
-    total = lax.dynamic_index_in_dim(pieces, index, keepdims=False).astype(jnp.float32)
+
+    def own(shift):
+        return jax.tree.map(
+            lambda value: lax.dynamic_index_in_dim(value, (index + shift) % count, keepdims=False),
+            pieces,
+        )
+
+    total = jax.tree.map(lambda value: value.astype(jnp.float32), own(0))
     for shift in range(1, count):
-        sent = lax.dynamic_index_in_dim(pieces, (index + shift) % count, keepdims=False)
-        total = total + lax.ppermute(
-            sent, axis_name, [(i, (i + shift) % count) for i in range(count)]
-        ).astype(jnp.float32)
+        arrived = lax.ppermute(
+            own(shift), axis_name, [(i, (i + shift) % count) for i in range(count)]
+        )
+        total = jax.tree.map(lambda acc, value: acc + value.astype(jnp.float32), total, arrived)
     return total
-
 
 def exchange_copies(value, axis_name):
     count = lax.axis_size(axis_name)
@@ -289,17 +309,22 @@
         x_float[None] + shifted[None] * (lagging_mixture_weights[1:, None, :] + offsets)
     ).astype(bf16)
     main_part = jnp.einsum(
-        "inf,ifc->nic", mixed[:4], fourfold_linear_maps, preferred_element_type=f32
+        "inf,ifc->inc", mixed[:4], fourfold_linear_maps, preferred_element_type=f32
     )
     decay_part = jnp.dot(mixed[4], attenuation_narrow_lowering, preferred_element_type=f32)
-    aggregated = exchange_sum(
-        jnp.concatenate([main_part.reshape(rows, -1), decay_part], axis=1)
-        .astype(bf16)
-        .reshape(batch_count, steps, local_rows, -1),
+    main_sum, decay_sum = exchange_sum(
+        (
+            main_part.astype(bf16)
+            .reshape(4, batch_count, steps * local_rows, width)
+            .transpose(1, 0, 2, 3),
+            decay_part.astype(bf16).reshape(batch_count, steps * local_rows, -1),
+        ),
         "batch",
     )
 
-    kept_for_move, aggregated = lax.optimization_barrier((stream_kept_tableaux, aggregated))
+    kept_for_move, main_sum, decay_sum = lax.optimization_barrier(
+        (stream_kept_tableaux, main_sum, decay_sum)
+    )
     moved_state = route_to_slots(
         kept_for_move.astype(bf16), position_mapping_target, batch_index, head_index
     )
@@ -307,11 +332,12 @@
     def heads_of(value):
         return value.reshape(steps, local_rows, heads_here, SUBSPACE_EXTENT)
 
-    recept = heads_of(widen(aggregated[..., :width]))
-    key_vec = heads_of(widen(aggregated[..., width : 2 * width]))
-    valued = heads_of(widen(aggregated[..., 2 * width : 3 * width]))
-    gate_act = jax.nn.silu(aggregated[..., 3 * width : 4 * width])
-    low_rank = jnp.tanh(aggregated[..., 4 * width :]).astype(bf16)
+    main_sum = main_sum.reshape(4, steps, local_rows, width)
+    recept = heads_of(widen(main_sum[0]))
+    key_vec = heads_of(widen(main_sum[1]))
+    valued = heads_of(widen(main_sum[2]))
+    gate_act = jax.nn.silu(main_sum[3])
+    low_rank = jnp.tanh(decay_sum.reshape(steps, local_rows, -1)).astype(bf16)
     decay_rate = heads_of(
         jnp.exp(
             -jnp.exp(
@@ -358,7 +384,7 @@
 
     gathered = exchange_copies(combined_response, "batch").transpose(1, 0, 2, 3)
     gathered = gathered.reshape(steps, sessions, width)
-    inverse = jnp.argsort(position_mapping_target)
+    inverse = index_of(position_mapping_target, sessions)
     arranged = jnp.concatenate(
         [gathered[:STEPS_A], jnp.take(gathered[STEPS_A:], inverse, axis=1, mode="clip")], axis=0
     )

time: 133 us -> 134 us (level)
  waiting for transfers between devices: 32.9 us -> 39 us
  local copies, waits for them, and re-layouts: 27.9 us -> 25 us
  matrix products: 10.1 us -> 8.64 us
  other arithmetic: 16.4 us -> 15 us
    sort x4 -> x0, other arithmetic: 5.16 us -> none  [the longest x1 1.63 us: per_device(): inverse = jnp.argsort(position_mapping_target)]
    ppermute x6 -> x9, starting transfers between devices: 7.75 us -> 12.1 us  [exchange_sum(): lax.ppermute(own(shift), axis_name, [(i, (i + shift) % count) for i in ra...]
    another operation x4 -> x1, local copies, waits for them, and re-layouts: 5.06 us -> 0.8 us  [by_row(): return value.reshape(steps, rows_here, SUBSPACE_EXTENT)]
    convert_element_type x0 -> x3, local copies, waits for them, and re-layouts: none -> 4.23 us  [widen(): return value.astype(jnp.bfloat16).astype(jnp.float32)]
    ppermute x6 -> x9, waiting for transfers between devices: 17.3 us -> 21.3 us  [exchange_sum(): lax.ppermute(own(shift), axis_name, [(i, (i + shift) % count) for i in ra...]
    all_to_all x2, starting transfers between devices: 11.5 us -> 7.74 us  [route_to_slots(): lax.all_to_all(packed, ('batch', 'head'), split_axis=0, concat_axis=0, ti...]
    all_to_all x2, waiting for transfers between devices: 9.27 us -> 11.2 us  [route_to_slots(): lax.all_to_all(packed, ('batch', 'head'), split_axis=0, concat_axis=0, ti...]
    concatenate x1 -> x0, local copies, waits for them, and re-layouts: 1.86 us -> none  [per_device(): jnp.concatenate([main_part.reshape(rows, -1), decay_part], axis=1)]
  transfers between devices with their start and end apart: 14 -> 17, of which waited for: 6 -> 7; matrix products, arithmetic and copies ran while one was open for 17% -> 16% of each run, Pallas kernels for 5% -> 5%
where the time goes in v11:
time: 134 us; the launch traced here: 133 us
  waiting for transfers between devices  39 us (29%)
  starting transfers between devices  33.1 us (25%)
  local copies, waits for them, and re-layouts  25 us (19%)
  other arithmetic  15 us (11%)
  Pallas kernels  11.4 us (9%)
  matrix products  8.64 us (6%)
    ppermute x9, waiting for transfers between devices, exchange_sum(): lax.ppermute(own(shift), axis_name, [(i, (i + shift) % count) for i in ra...  21.3 us
    ppermute x6, starting transfers between devices, exchange_copies(): lax.ppermute(value, axis_name, [(i, (i + shift) % count) for i in range(c...  13.3 us
    ppermute x9, starting transfers between devices, exchange_sum(): lax.ppermute(own(shift), axis_name, [(i, (i + shift) % count) for i in ra...  12.1 us
    all_to_all x2, waiting for transfers between devices, route_to_slots(): lax.all_to_all(packed, ('batch', 'head'), split_axis=0, concat_axis=0, ti...  11.2 us
    all_to_all x2, starting transfers between devices, route_to_slots(): lax.all_to_all(packed, ('batch', 'head'), split_axis=0, concat_axis=0, ti...  7.74 us
    ppermute x6, waiting for transfers between devices, exchange_copies(): lax.ppermute(value, axis_name, [(i, (i + shift) % count) for i in range(c...  6.56 us
    pallas_call x1, Pallas kernels, run_recurrence(): pl.pallas_call(functools.partial(recurrence_kernel, steps), grid=(rows //...  6.39 us
    pallas_call x1, Pallas kernels, rebuild_state(): pl.pallas_call(functools.partial(rebuild_kernel, steps), grid=(rows // bl...  4.98 us
  transfers between devices with their start and end apart: 17, of which 7 were waited for; matrix products, arithmetic and copies ran while one was open for 16% of the time, Pallas kernels for 5%

profile of v11, /device:TPU:0, one launch (start us, length us, event | category | flops | bytes accessed | tf_op | source)
XLA Modules:
  0.0 133.3 jit_solution(7836516697840991535)
XLA Ops:
  0.6 1.1 slice_bitcast_fusion.2
  1.7 1.0 convert_bitcast_fusion
  2.8 0.9 convert_bitcast_fusion.1
  3.9 0.4 convolution_convert_fusion.1
  4.3 5.1 %collective-permute-start.2 = (bf16[128,320]{0,1:T(8,128)(2,1)S(1)}, bf16[128,320]{0,1:T(8,128)(2,1)S(1)}, u32[]{:S(2)}, u32[]{:S(2)}) collective-permute-start(bf16[128,320]{0,1:T(8,128)(2,1)S(1)} %convolution_convert_fusion.1), channel_id=1, source_target_pairs={{0,12},{4,0},{8,4},{12,8},{1,13},{5,1},{9,5},{13,9},{2,14},{6,2},{... | collective-permute-start | bytes 245768 | tf_op jit(solution)/shard_map/ppermute | solution.py:102
  9.4 1.0 collective-permute-start
  10.6 0.6 slice.53
  11.4 0.5 fusion.33
  12.5 0.7 gather_fusion.1
  13.4 0.7 reshape.463
  14.1 0.6 pad_clamp_fusion.4
  14.7 2.2 %collective-permute-done.1 = bf16[128,320]{0,1:T(8,128)(2,1)S(1)} collective-permute-done((bf16[128,320]{0,1:T(8,128)(2,1)S(1)}, bf16[128,320]{0,1:T(8,128)(2,1)S(1)}, u32[]{:S(2)}, u32[]{:S(2)}) %collective-permute-start.1) | collective-permute-done | bytes 81952 | tf_op jit(solution)/shard_map/ppermute | solution.py:102
  16.9 0.6 copy-done.6
  17.6 1.0 pad_maximum_fusion
  18.6 1.4 %gather_fusion = bf16[4,128,320]{1,2,0:T(8,128)(2,1)} fusion(bf16[4,128,320]{1,2,0:T(8,128)(2,1)S(1)} %pad_maximum_fusion, s32[1024]{0:T(1024)} %pad_clamp_fusion.4), kind=kCustom, calls=%fused_computation | custom fusion | bytes 655376 | tf_op jit(solution)/shard_map/jit(_take)/gather | solution.py:105
  20.0 1.1 convert_reduce_fusion
  21.1 1.7 %add_convert_fusion = bf16[5,128,1024]{2,1,0:T(8,128)(2,1)S(1)} fusion(bf16[128,5,64]{0,2,1:T(8,128)(2,1)S(1)} %bitcast.131, bf16[5,64,1024]{2,1,0:T(8,128)(2,1)} %param.21, f32[5,1024]{1,0:T(8,128)} %slice.53, f32[128,1024]{1,0:T(8,128)S(1)} %bitcast_subtract_fusion, f32[128,1024]{1,0:T(8,128)S(1)} %bitcast.117), kind=kOutput, calls=%fused_computation.8 | convolution fusion | flops 86507520 | bytes 3117056 | tf_op jit(solution)/shard_map/nim,imd->ind/dot_general | solution.py:305
  23.0 4.8 %convolution_convert_fusion = bf16[4,128,1024]{2,1,0:T(8,128)(2,1)S(1)} fusion(bf16[5,128,1024]{2,1,0:T(8,128)(2,1)S(1)} %add_convert_fusion, bf16[4,1024,1024]{2,1,0:T(8,128)(2,1)} %param.22), kind=kOutput, calls=%fused_computation.11 | convolution fusion | flops 1074266112 | bytes 10747904 | tf_op jit(solution)/shard_map/inf,ifc->inc/dot_general | solution.py:311
  27.9 0.4 collective-permute-start.6
  28.3 3.5 %collective-permute-start.8 = (bf16[32,128]{1,0:T(8,128)(2,1)S(1)}, bf16[32,128]{1,0:T(8,128)(2,1)S(1)}, u32[]{:S(2)}, u32[]{:S(2)}) collective-permute-start(bf16[32,128]{1,0:T(8,128)(2,1)S(1)} %get-tuple-element.33), channel_id=1, source_target_pairs={{0,12},{4,0},{8,4},{12,8},{1,13},{5,1},{9,5},{13,9},{2,14},{6,2},{... | collective-permute-start | bytes 24584 | tf_op jit(solution)/shard_map/ppermute | solution.py:90
  31.8 0.3 collective-permute-start.7
  32.0 0.9 dynamic-slice_bitcast_fusion.2
  32.9 0.6 collective-permute-start.3
  33.5 3.2 %collective-permute-start.5 = (bf16[4,32,1024]{2,1,0:T(8,128)(2,1)}, bf16[4,32,1024]{2,1,0:T(8,128)(2,1)}, u32[]{:S(2)}, u32[]{:S(2)}) collective-permute-start(bf16[4,32,1024]{2,1,0:T(8,128)(2,1)} %get-tuple-element.20), channel_id=1, source_target_pairs={{0,12},{4,0},{8,4},{12,8},{1,13},{5,1},{9,5},{13,9},{2,14},{6,2},{... | collective-permute-start | bytes 786440 | tf_op jit(solution)/shard_map/ppermute | solution.py:90
  36.7 0.9 collective-permute-start.4
  37.7 6.6 %collective-permute-done.3 = bf16[4,32,1024]{2,1,0:T(8,128)(2,1)} collective-permute-done((bf16[4,32,1024]{2,1,0:T(8,128)(2,1)}, bf16[4,32,1024]{2,1,0:T(8,128)(2,1)}, u32[]{:S(2)}, u32[]{:S(2)}) %collective-permute-start.3) | collective-permute-done | bytes 262176 | tf_op jit(solution)/shard_map/ppermute | solution.py:90
  44.3 2.9 %collective-permute-done.5 = bf16[4,32,1024]{2,1,0:T(8,128)(2,1)} collective-permute-done((bf16[4,32,1024]{2,1,0:T(8,128)(2,1)}, bf16[4,32,1024]{2,1,0:T(8,128)(2,1)}, u32[]{:S(2)}, u32[]{:S(2)}) %collective-permute-start.5) | collective-permute-done | bytes 262176 | tf_op jit(solution)/shard_map/ppermute | solution.py:90
  47.2 11.8 %collective-permute-done.4 = bf16[4,32,1024]{2,1,0:T(8,128)(2,1)} collective-permute-done((bf16[4,32,1024]{2,1,0:T(8,128)(2,1)S(1)}, bf16[4,32,1024]{2,1,0:T(8,128)(2,1)}, u32[]{:S(2)}, u32[]{:S(2)}) %collective-permute-start.4) | collective-permute-done | bytes 262176 | tf_op jit(solution)/shard_map/ppermute | solution.py:90
  59.0 2.1 %fusion.12 = f32[4,32,1024]{2,1,0:T(8,128)} fusion(bf16[4,32,1024]{2,1,0:T(8,128)(2,1)} %collective-permute-done.5, bf16[4,32,1024]{2,1,0:T(8,128)(2,1)} %collective-permute-done.4, bf16[4,32,1024]{2,1,0:T(8,128)(2,1)} %collective-permute-done.3, bf16[4,4,32,1024]{3,2,1,0:T(8,128)(2,1)S(1)} %bitcast.125, s32[]{:T(128)S(6)} %select_n.181), kind=kLoop, calls=%fused_computation.23 | loop fusion | flops 917504 | bytes 1572868 | tf_op jit(solution)/shard_map/add | solution.py:93
  61.0 1.7 %convert_element_type.180 = bf16[8,16,4096]{2,1,0:T(8,128)(2,1)S(1)} convert(f32[8,16,4096]{2,1,0:T(8,128)} %param.17) | non-fusion elementwise | flops 524288 | bytes 3145728 | tf_op jit(solution)/shard_map/convert_element_type | solution.py:329
  62.7 2.2 %gather_fusion.2 = bf16[128,4096]{1,0:T(8,128)(2,1)} fusion(bf16[128,4096]{1,0:T(8,128)(2,1)S(1)} %bitcast.112, s32[1024]{0:T(1024)S(1)} %pad_clamp_fusion.2), kind=kCustom, calls=%fused_computation.2 | custom fusion | bytes 2097664 | tf_op jit(solution)/shard_map/jit(_take)/gather | solution.py:52
  65.0 4.2 %all-to-all-start = ((bf16[16,8,4096]{2,1,0:T(8,128)(2,1)}), bf16[16,8,4096]{2,1,0:T(8,128)(2,1)S(1)}, u32[]{:S(2)}, u32[]{:S(2)}) async-start(bf16[16,8,4096]{2,1,0:T(8,128)(2,1)} %bitcast.118), calls=%async_computation | async-start | bytes 2097152 | tf_op jit(solution)/shard_map/all_to_all | solution.py:55
  69.7 0.6 maximum_bitcast_fusion
  70.4 1.8 %convert.16 = bf16[4,32,1024]{2,1,0:T(8,128)(2,1)} convert(f32[4,32,1024]{2,1,0:T(8,128)} %fusion.12) | non-fusion elementwise | flops 131072 | bytes 786432 | tf_op jit(solution)/shard_map/convert.13
  72.2 1.1 fusion.10
  73.3 0.8 reshape_reshape.12.decay_ref
  74.2 1.6 %slice_convert_fusion = (f32[1,32,1024]{2,1,0:T(8,128)}, f32[1,32,1024]{2,1,0:T(8,128)}, f32[1,32,1024]{2,1,0:T(8,128)S(1)}) fusion(bf16[4,32,1024]{2,1,0:T(8,128)(2,1)} %convert.16), kind=kLoop, calls=%fused_computation.50 | loop fusion | flops 98304 | bytes 589824 | tf_op jit(solution)/shard_map/convert_element_type | solution.py:108
  75.8 1.7 %reshape.442.value_ref = f32[4,128,64]{2,1,0:T(8,128)} reshape(f32[1,32,1024]{2,1,0:T(8,128)} %get-tuple-element.27) | data formatting | bytes 262144 | tf_op jit(solution)/shard_map/convert_element_type | solution.py:108
  77.6 1.7 %reshape.441.key_ref = f32[4,128,64]{2,1,0:T(8,128)} reshape(f32[1,32,1024]{2,1,0:T(8,128)} %get-tuple-element.28) | data formatting | bytes 262144 | tf_op jit(solution)/shard_map/convert_element_type | solution.py:108
  79.3 0.8 reshape.440.recept_ref
  80.1 0.8 divide_multiply_fusion.gate_ref
  80.9 1.4 %broadcast_in_dim.56 = f32[3,8,16,64]{3,2,1,0:T(8,128)} broadcast(f32[3,16,64]{2,1,0:T(8,128)} %maximum_bitcast_fusion), dimensions={0,2,3} | broadcast | bytes 110592 | tf_op jit(solution)/shard_map/broadcast_in_dim | solution.py:355
  82.3 6.4 %shard_map.166 = (bf16[4,128,64]{2,1,0:T(8,128)(2,1)}, bf16[9,128,64]{2,1,0:T(8,128)(2,1)}) custom-call(f32[4,128,64]{2,1,0:T(8,128)} %reshape.440.recept_ref, f32[4,128,64]{2,1,0:T(8,128)} %reshape.441.key_ref, f32[4,128,64]{2,1,0:T(8,128)} %reshape.442.value_ref, f32[4,128,64]{2,1,0:T(8,128)} %reshape_reshape.12.decay_ref, ...), custom_call_target="tpu_custom_call" | custom-call | flops 805306368 | bytes 3063808 | tf_op jit(solution)/shard_map/pallas_call | solution.py:196
  88.7 3.5 %all-to-all-done = bf16[16,8,4096]{2,1,0:T(8,128)(2,1)S(1)} async-done(((bf16[16,8,4096]{2,1,0:T(8,128)(2,1)}), bf16[16,8,4096]{2,1,0:T(8,128)(2,1)S(1)}, u32[]{:S(2)}, u32[]{:S(2)}) %all-to-all-start) | async-done | bytes 1048608 | tf_op jit(solution)/shard_map/all_to_all | solution.py:55
  92.1 2.2 %gather_fusion.3 = bf16[128,4096]{1,0:T(8,128)(2,1)} fusion(bf16[128,4096]{1,0:T(8,128)(2,1)S(1)} %bitcast.113, s32[1024]{0:T(1024)S(1)} %pad_clamp_fusion.1), kind=kCustom, calls=%fused_computation.3 | custom fusion | bytes 2097664 | tf_op jit(solution)/shard_map/jit(_take)/gather | solution.py:74
  94.4 3.2 %collective-permute-start.11 = (bf16[4,8,1024]{2,1,0:T(8,128)(2,1)S(1)}, bf16[4,8,1024]{2,1,0:T(8,128)(2,1)S(1)}, u32[]{:S(2)}, u32[]{:S(2)}) collective-permute-start(bf16[4,8,1024]{2,1,0:T(8,128)(2,1)S(1)} %reshape.428), channel_id=1, source_target_pairs={{0,12},{4,0},{8,4},{12,8},{1,13},{5,1},{9,5},{13,9},{2,14},{6,2},{... | collective-permute-start | bytes 196616 | tf_op jit(solution)/shard_map/ppermute | solution.py:102
  97.7 2.0 %collective-permute-start.10 = (bf16[4,8,1024]{2,1,0:T(8,128)(2,1)S(1)}, bf16[4,8,1024]{2,1,0:T(8,128)(2,1)S(1)}, u32[]{:S(2)}, u32[]{:S(2)}) collective-permute-start(bf16[4,8,1024]{2,1,0:T(8,128)(2,1)S(1)} %reshape.428), channel_id=1, source_target_pairs={{0,8},{4,12},{8,0},{12,4},{1,9},{5,13},{9,1},{13,5},{2,10},{6,14},... | collective-permute-start | bytes 196616 | tf_op jit(solution)/shard_map/ppermute | solution.py:102
  99.6 1.9 %collective-permute-start.9 = (bf16[4,8,1024]{2,1,0:T(8,128)(2,1)S(1)}, bf16[4,8,1024]{2,1,0:T(8,128)(2,1)S(1)}, u32[]{:S(2)}, u32[]{:S(2)}) collective-permute-start(bf16[4,8,1024]{2,1,0:T(8,128)(2,1)S(1)} %reshape.428), channel_id=1, source_target_pairs={{0,4},{4,8},{8,12},{12,0},{1,5},{5,9},{9,13},{13,1},{2,6},{6,10},{... | collective-permute-start | bytes 196616 | tf_op jit(solution)/shard_map/ppermute | solution.py:102
  101.7 4.4 %collective-permute-done.10 = bf16[4,8,1024]{2,1,0:T(8,128)(2,1)S(1)} collective-permute-done((bf16[4,8,1024]{2,1,0:T(8,128)(2,1)S(1)}, bf16[4,8,1024]{2,1,0:T(8,128)(2,1)S(1)}, u32[]{:S(2)}, u32[]{:S(2)}) %collective-permute-start.10) | collective-permute-done | bytes 65568 | tf_op jit(solution)/shard_map/ppermute | solution.py:102
  106.2 0.7 gather_fusion.4
  107.1 0.8 gather_fusion.5
  107.9 0.4 fusion.5
  108.4 0.7 dynamic-slice_bitcast_fusion.5
  109.1 1.7 %collective-permute-start.14 = (bf16[4,8,1024]{2,1,0:T(8,128)(2,1)}, bf16[4,8,1024]{2,1,0:T(8,128)(2,1)S(1)}, u32[]{:S(2)}, u32[]{:S(2)}) collective-permute-start(bf16[4,8,1024]{2,1,0:T(8,128)(2,1)} %get-tuple-element.23), channel_id=1, source_target_pairs={{0,3},{1,0},{2,1},{3,2},{4,7},{5,4},{6,5},{7,6},{8,11},{9,8},{10,9... | collective-permute-start | bytes 196616 | tf_op jit(solution)/shard_map/ppermute | solution.py:90
  110.8 1.5 %collective-permute-start.13 = (bf16[4,8,1024]{2,1,0:T(8,128)(2,1)}, bf16[4,8,1024]{2,1,0:T(8,128)(2,1)S(1)}, u32[]{:S(2)}, u32[]{:S(2)}) collective-permute-start(bf16[4,8,1024]{2,1,0:T(8,128)(2,1)} %get-tuple-element.24), channel_id=1, source_target_pairs={{0,2},{1,3},{2,0},{3,1},{4,6},{5,7},{6,4},{7,5},{8,10},{9,11},{10,... | collective-permute-start | bytes 196616 | tf_op jit(solution)/shard_map/ppermute | solution.py:90
  112.6 0.3 reshape_reshape.13
  112.9 1.5 %gather_fusion.6 = bf16[128,576]{1,0:T(8,128)(2,1)} fusion(bf16[128,576]{1,0:T(8,128)(2,1)S(1)} %reshape_reshape.13, s32[1024]{0:T(1024)S(1)} %pad_clamp_fusion.2), kind=kCustom, calls=%fused_computation.6 | custom fusion | bytes 295424 | tf_op jit(solution)/shard_map/jit(_take)/gather | solution.py:52
  114.4 3.5 %all-to-all-start.1 = ((bf16[16,8,576]{2,1,0:T(8,128)(2,1)}), bf16[16,8,576]{2,1,0:T(8,128)(2,1)S(1)}, u32[]{:S(2)}, u32[]{:S(2)}) async-start(bf16[16,8,576]{2,1,0:T(8,128)(2,1)} %bitcast.50), calls=%async_computation.1 | async-start | bytes 327680 | tf_op jit(solution)/shard_map/all_to_all | solution.py:55
  118.0 0.6 fusion.36
  118.7 7.7 %all-to-all-done.1 = bf16[16,8,576]{2,1,0:T(8,128)(2,1)S(1)} async-done(((bf16[16,8,576]{2,1,0:T(8,128)(2,1)}), bf16[16,8,576]{2,1,0:T(8,128)(2,1)S(1)}, u32[]{:S(2)}, u32[]{:S(2)}) %all-to-all-start.1) | async-done | bytes 147488 | tf_op jit(solution)/shard_map/all_to_all | solution.py:55
  126.4 0.9 gather_fusion.7
  127.2 0.2 reshape_reshape.14
  127.5 0.8 copy.44
  128.3 5.0 %shard_map.167 = f32[128,4096]{1,0:T(8,128)} custom-call(bf16[128,4096]{1,0:T(8,128)(2,1)} %gather_fusion.3, bf16[9,128,64]{2,1,0:T(8,128)(2,1)} %bitcast.122), custom_call_target="tpu_custom_call" | custom-call | flops 603979776 | bytes 3293184 | tf_op jit(solution)/shard_map/pallas_call | solution.py:240
  (95 shorter events, 3.1 us)
Async XLA Ops:
  0.6 107.3 %copy-start = (bf16[1024,1024]{1,0:T(8,128)(2,1)S(1)}, bf16[1024,1024]{1,0:T(8,128)(2,1)}, u32[]{:S(2)}) copy-start(bf16[1024,1024]{1,0:T(8,128)(2,1)} %param.29) | copy-start | bytes 6291460
  2.7 1.2 copy-start.1
  2.8 1.2 slice-start.1
  3.8 6.6 %copy-start.18 = (s32[32]{0:T(128)S(1)}, s32[32]{0:T(128)}, u32[]{:S(2)}) copy-start(s32[32]{0:T(128)} %param.18) | copy-start | bytes 388
  3.8 6.8 %copy-start.8 = (f32[6,1024]{1,0:T(8,128)S(1)}, f32[6,1024]{1,0:T(8,128)}, u32[]{:S(2)}) copy-start(f32[6,1024]{1,0:T(8,128)} %param.19) | copy-start | bytes 73732
  4.3 10.4 %collective-permute-start.2 = (bf16[128,320]{0,1:T(8,128)(2,1)S(1)}, bf16[128,320]{0,1:T(8,128)(2,1)S(1)}, u32[]{:S(2)}, u32[]{:S(2)}) collective-permute-start(bf16[128,320]{0,1:T(8,128)(2,1)S(1)} %convolution_convert_fusion.1), channel_id=1, source_target_pairs={{0,12},{4,0},{8,4},{12,8},{1,13},{5,1},{9,5},{13,9},{2,14},{6,2},{... | collective-permute-start | bytes 245768 | tf_op jit(solution)/shard_map/ppermute | solution.py:102
  9.4 7.5 %collective-permute-start.1 = (bf16[128,320]{0,1:T(8,128)(2,1)S(1)}, bf16[128,320]{0,1:T(8,128)(2,1)S(1)}, u32[]{:S(2)}, u32[]{:S(2)}) collective-permute-start(bf16[128,320]{0,1:T(8,128)(2,1)S(1)} %convolution_convert_fusion.1), channel_id=1, source_target_pairs={{0,8},{4,12},{8,0},{12,4},{1,9},{5,13},{9,1},{13,5},{2,10},{6,14},... | collective-permute-start | bytes 245768 | tf_op jit(solution)/shard_map/ppermute | solution.py:102
  9.4 7.5 %collective-permute-start = (bf16[128,320]{0,1:T(8,128)(2,1)S(1)}, bf16[128,320]{0,1:T(8,128)(2,1)S(1)}, u32[]{:S(2)}, u32[]{:S(2)}) collective-permute-start(bf16[128,320]{0,1:T(8,128)(2,1)S(1)} %convolution_convert_fusion.1), channel_id=1, source_target_pairs={{0,4},{4,8},{8,12},{12,0},{1,5},{5,9},{9,13},{13,1},{2,6},{6,10},{... | collective-permute-start | bytes 245768 | tf_op jit(solution)/shard_map/ppermute | solution.py:102
  10.5 1.5 %copy-start.16 = (s32[32]{0:T(128)}, s32[32]{0:T(128)S(1)}, u32[]{:S(2)}) copy-start(s32[32]{0:T(128)S(1)} %select_reduce_fusion) | copy-start | bytes 388
  14.7 2.2 %copy-start.5 = (bf16[128,320]{0,1:T(8,128)(2,1)}, bf16[128,320]{0,1:T(8,128)(2,1)S(1)}, u32[]{:S(2)}) copy-start(bf16[128,320]{0,1:T(8,128)(2,1)S(1)} %collective-permute-done.2) | copy-start | bytes 245764
  16.9 0.6 copy-start.6
  16.9 0.7 copy-start.7
  20.0 2.8 %copy-start.4 = (bf16[1024,128]{1,0:T(8,128)(2,1)S(1)}, bf16[1024,128]{1,0:T(8,128)(2,1)}, u32[]{:S(2)}) copy-start(bf16[1024,128]{1,0:T(8,128)(2,1)} %param.23) | copy-start | bytes 786436
  23.0 14.6 %copy-start.13 = (s32[128]{0:T(128)S(1)}, s32[128]{0:T(128)}, u32[]{:S(2)}) copy-start(s32[128]{0:T(128)} %reshape.463) | copy-start | bytes 1540
  27.9 8.8 %collective-permute-start.6 = (bf16[32,128]{1,0:T(8,128)(2,1)S(1)}, bf16[32,128]{1,0:T(8,128)(2,1)S(1)}, u32[]{:S(2)}, u32[]{:S(2)}) collective-permute-start(bf16[32,128]{1,0:T(8,128)(2,1)S(1)} %get-tuple-element.32), channel_id=1, source_target_pairs={{0,4},{4,8},{8,12},{12,0},{1,5},{5,9},{9,13},{13,1},{2,6},{6,10},{... | collective-permute-start | bytes 24584 | tf_op jit(solution)/shard_map/ppermute | solution.py:90
  28.3 9.4 %collective-permute-start.8 = (bf16[32,128]{1,0:T(8,128)(2,1)S(1)}, bf16[32,128]{1,0:T(8,128)(2,1)S(1)}, u32[]{:S(2)}, u32[]{:S(2)}) collective-permute-start(bf16[32,128]{1,0:T(8,128)(2,1)S(1)} %get-tuple-element.33), channel_id=1, source_target_pairs={{0,12},{4,0},{8,4},{12,8},{1,13},{5,1},{9,5},{13,9},{2,14},{6,2},{... | collective-permute-start | bytes 24584 | tf_op jit(solution)/shard_map/ppermute | solution.py:90
  31.8 5.8 %collective-permute-start.7 = (bf16[32,128]{1,0:T(8,128)(2,1)S(1)}, bf16[32,128]{1,0:T(8,128)(2,1)S(1)}, u32[]{:S(2)}, u32[]{:S(2)}) collective-permute-start(bf16[32,128]{1,0:T(8,128)(2,1)S(1)} %get-tuple-element.34), channel_id=1, source_target_pairs={{0,8},{4,12},{8,0},{12,4},{1,9},{5,13},{9,1},{13,5},{2,10},{6,14},... | collective-permute-start | bytes 24584 | tf_op jit(solution)/shard_map/ppermute | solution.py:90
  32.9 11.4 %collective-permute-start.3 = (bf16[4,32,1024]{2,1,0:T(8,128)(2,1)}, bf16[4,32,1024]{2,1,0:T(8,128)(2,1)}, u32[]{:S(2)}, u32[]{:S(2)}) collective-permute-start(bf16[4,32,1024]{2,1,0:T(8,128)(2,1)} %get-tuple-element.19), channel_id=1, source_target_pairs={{0,4},{4,8},{8,12},{12,0},{1,5},{5,9},{9,13},{13,1},{2,6},{6,10},{... | collective-permute-start | bytes 786440 | tf_op jit(solution)/shard_map/ppermute | solution.py:90
  33.5 13.7 %collective-permute-start.5 = (bf16[4,32,1024]{2,1,0:T(8,128)(2,1)}, bf16[4,32,1024]{2,1,0:T(8,128)(2,1)}, u32[]{:S(2)}, u32[]{:S(2)}) collective-permute-start(bf16[4,32,1024]{2,1,0:T(8,128)(2,1)} %get-tuple-element.20), channel_id=1, source_target_pairs={{0,12},{4,0},{8,4},{12,8},{1,13},{5,1},{9,5},{13,9},{2,14},{6,2},{... | collective-permute-start | bytes 786440 | tf_op jit(solution)/shard_map/ppermute | solution.py:90
  36.7 22.2 %collective-permute-start.4 = (bf16[4,32,1024]{2,1,0:T(8,128)(2,1)S(1)}, bf16[4,32,1024]{2,1,0:T(8,128)(2,1)}, u32[]{:S(2)}, u32[]{:S(2)}) collective-permute-start(bf16[4,32,1024]{2,1,0:T(8,128)(2,1)S(1)} %get-tuple-element.21), channel_id=1, source_target_pairs={{0,8},{4,12},{8,0},{12,4},{1,9},{5,13},{9,1},{13,5},{2,10},{6,14},... | collective-permute-start | bytes 786440 | tf_op jit(solution)/shard_map/ppermute | solution.py:90
  64.9 4.3 %copy-start.10 = (f32[1024]{0:T(1024)S(1)}, f32[1024]{0:T(1024)}, u32[]{:S(2)}) copy-start(f32[1024]{0:T(1024)} %param.26) | copy-start | bytes 12292
  64.9 4.4 %copy-start.11 = (f32[1024]{0:T(1024)S(1)}, f32[1024]{0:T(1024)}, u32[]{:S(2)}) copy-start(f32[1024]{0:T(1024)} %param.27) | copy-start | bytes 12292
  64.9 4.5 %copy-start.12 = (f32[1024]{0:T(1024)S(1)}, f32[1024]{0:T(1024)}, u32[]{:S(2)}) copy-start(f32[1024]{0:T(1024)} %param.28) | copy-start | bytes 12292
  64.9 4.5 %copy-start.14 = (s32[8]{0:T(128)S(1)}, s32[8]{0:T(128)}, u32[]{:S(2)}) copy-start(s32[8]{0:T(128)} %get-tuple-element.35) | copy-start | bytes 100
  64.9 4.5 %copy-start.15 = (s32[8]{0:T(128)S(1)}, s32[8]{0:T(128)}, u32[]{:S(2)}) copy-start(s32[8]{0:T(128)} %get-tuple-element.36) | copy-start | bytes 100
  64.9 7.2 %copy-start.9 = (f32[1024]{0:T(1024)S(1)}, f32[1024]{0:T(1024)}, u32[]{:S(2)}) copy-start(f32[1024]{0:T(1024)} %param.25) | copy-start | bytes 12292
  64.9 9.2 %slice-start = ((f32[4,32,1024]{2,1,0:T(8,128)}), f32[1,32,1024]{2,1,0:T(8,128)S(1)}, s32[]{:S(2)}) async-start(f32[4,32,1024]{2,1,0:T(8,128)} %fusion.12), calls=%async_computation.2 | async-start | bytes 262144 | tf_op jit(solution)/shard_map/slice | solution.py:339
  65.0 27.2 %all-to-all-start = ((bf16[16,8,4096]{2,1,0:T(8,128)(2,1)}), bf16[16,8,4096]{2,1,0:T(8,128)(2,1)S(1)}, u32[]{:S(2)}, u32[]{:S(2)}) async-start(bf16[16,8,4096]{2,1,0:T(8,128)(2,1)} %bitcast.118), calls=%async_computation | async-start | bytes 2097152 | tf_op jit(solution)/shard_map/all_to_all | solution.py:55
  92.1 2.2 %copy-start.2 = (bf16[4,128,64]{2,1,0:T(8,128)(2,1)S(1)}, bf16[4,128,64]{2,1,0:T(8,128)(2,1)}, u32[]{:S(2)}) copy-start(bf16[4,128,64]{2,1,0:T(8,128)(2,1)} %get-tuple-element.16) | copy-start | bytes 196612
  92.1 9.5 %copy-start.17 = (s32[32]{0:T(128)S(1)}, s32[32]{0:T(128)}, u32[]{:S(2)}) copy-start(s32[32]{0:T(128)} %copy-done.16) | copy-start | bytes 388
  94.4 7.3 %collective-permute-start.11 = (bf16[4,8,1024]{2,1,0:T(8,128)(2,1)S(1)}, bf16[4,8,1024]{2,1,0:T(8,128)(2,1)S(1)}, u32[]{:S(2)}, u32[]{:S(2)}) collective-permute-start(bf16[4,8,1024]{2,1,0:T(8,128)(2,1)S(1)} %reshape.428), channel_id=1, source_target_pairs={{0,12},{4,0},{8,4},{12,8},{1,13},{5,1},{9,5},{13,9},{2,14},{6,2},{... | collective-permute-start | bytes 196616 | tf_op jit(solution)/shard_map/ppermute | solution.py:102
  97.7 8.4 %collective-permute-start.10 = (bf16[4,8,1024]{2,1,0:T(8,128)(2,1)S(1)}, bf16[4,8,1024]{2,1,0:T(8,128)(2,1)S(1)}, u32[]{:S(2)}, u32[]{:S(2)}) collective-permute-start(bf16[4,8,1024]{2,1,0:T(8,128)(2,1)S(1)} %reshape.428), channel_id=1, source_target_pairs={{0,8},{4,12},{8,0},{12,4},{1,9},{5,13},{9,1},{13,5},{2,10},{6,14},... | collective-permute-start | bytes 196616 | tf_op jit(solution)/shard_map/ppermute | solution.py:102
  99.6 6.5 %collective-permute-start.9 = (bf16[4,8,1024]{2,1,0:T(8,128)(2,1)S(1)}, bf16[4,8,1024]{2,1,0:T(8,128)(2,1)S(1)}, u32[]{:S(2)}, u32[]{:S(2)}) collective-permute-start(bf16[4,8,1024]{2,1,0:T(8,128)(2,1)S(1)} %reshape.428), channel_id=1, source_target_pairs={{0,4},{4,8},{8,12},{12,0},{1,5},{5,9},{9,13},{13,1},{2,6},{6,10},{... | collective-permute-start | bytes 196616 | tf_op jit(solution)/shard_map/ppermute | solution.py:102
  106.9 5.4 %copy-start.3 = (bf16[9,128,64]{2,1,0:T(8,128)(2,1)S(1)}, bf16[9,128,64]{2,1,0:T(8,128)(2,1)}, u32[]{:S(2)}) copy-start(bf16[9,128,64]{2,1,0:T(8,128)(2,1)} %get-tuple-element.18) | copy-start | bytes 442372
  109.1 8.8 %collective-permute-start.12 = (bf16[4,8,1024]{2,1,0:T(8,128)(2,1)}, bf16[4,8,1024]{2,1,0:T(8,128)(2,1)S(1)}, u32[]{:S(2)}, u32[]{:S(2)}) collective-permute-start(bf16[4,8,1024]{2,1,0:T(8,128)(2,1)} %get-tuple-element.22), channel_id=1, source_target_pairs={{0,1},{1,2},{2,3},{3,0},{4,5},{5,6},{6,7},{7,4},{8,9},{9,10},{10,1... | collective-permute-start | bytes 196616 | tf_op jit(solution)/shard_map/ppermute | solution.py:90
  109.1 8.9 %collective-permute-start.14 = (bf16[4,8,1024]{2,1,0:T(8,128)(2,1)}, bf16[4,8,1024]{2,1,0:T(8,128)(2,1)S(1)}, u32[]{:S(2)}, u32[]{:S(2)}) collective-permute-start(bf16[4,8,1024]{2,1,0:T(8,128)(2,1)} %get-tuple-element.23), channel_id=1, source_target_pairs={{0,3},{1,0},{2,1},{3,2},{4,7},{5,4},{6,5},{7,6},{8,11},{9,8},{10,9... | collective-permute-start | bytes 196616 | tf_op jit(solution)/shard_map/ppermute | solution.py:90
  110.8 7.1 %collective-permute-start.13 = (bf16[4,8,1024]{2,1,0:T(8,128)(2,1)}, bf16[4,8,1024]{2,1,0:T(8,128)(2,1)S(1)}, u32[]{:S(2)}, u32[]{:S(2)}) collective-permute-start(bf16[4,8,1024]{2,1,0:T(8,128)(2,1)} %get-tuple-element.24), channel_id=1, source_target_pairs={{0,2},{1,3},{2,0},{3,1},{4,6},{5,7},{6,4},{7,5},{8,10},{9,11},{10,... | collective-permute-start | bytes 196616 | tf_op jit(solution)/shard_map/ppermute | solution.py:90
  114.4 12.0 %all-to-all-start.1 = ((bf16[16,8,576]{2,1,0:T(8,128)(2,1)}), bf16[16,8,576]{2,1,0:T(8,128)(2,1)S(1)}, u32[]{:S(2)}, u32[]{:S(2)}) async-start(bf16[16,8,576]{2,1,0:T(8,128)(2,1)} %bitcast.50), calls=%async_computation.1 | async-start | bytes 327680 | tf_op jit(solution)/shard_map/all_to_all | solution.py:55

commit v12 on v11

--- a/solution.py
+++ b/solution.py
@@ -103,6 +103,46 @@
         )
     shifts = (index - jnp.arange(count, dtype=jnp.int32)) % count
     return jnp.take(jnp.stack(received), shifts, axis=0, mode="clip")
+
+def by_source(received, index, count):
+    shifts = (index - jnp.arange(count, dtype=jnp.int32)) % count
+    return jnp.take(jnp.stack(received), shifts, axis=0, mode="clip")
+
+
+def gather_with_parts(value, parts, axis_name):
+    count = lax.axis_size(axis_name)
+    index = lax.axis_index(axis_name)
+    copies = [value]
+    moved = [lax.dynamic_index_in_dim(parts, index, keepdims=False)]
+    for shift in range(1, count):
+        sent = lax.dynamic_index_in_dim(parts, (index + shift) % count, keepdims=False)
+        copy, part = lax.ppermute(
+            (value, sent), axis_name, [(i, (i + shift) % count) for i in range(count)]
+        )
+        copies.append(copy)
+        moved.append(part)
+    return by_source(copies, index, count), by_source(moved, index, count)
+
+
+def sum_with_parts(pieces, parts, axis_name):
+    count = lax.axis_size(axis_name)
+    index = lax.axis_index(axis_name)
+    total = lax.dynamic_index_in_dim(pieces, index, keepdims=False).astype(jnp.float32)
+    moved = [lax.dynamic_index_in_dim(parts, index, keepdims=False)]
+    for shift in range(1, count):
+        target = (index + shift) % count
+        piece, part = lax.ppermute(
+            (
+                lax.dynamic_index_in_dim(pieces, target, keepdims=False),
+                lax.dynamic_index_in_dim(parts, target, keepdims=False),
+            ),
+            axis_name,
+            [(i, (i + shift) % count) for i in range(count)],
+        )
+        total = total + piece.astype(jnp.float32)
+        moved.append(part)
+    return total, by_source(moved, index, count)
+
 
 def widen(value):
     return value.astype(jnp.bfloat16).astype(jnp.float32)
@@ -364,38 +404,66 @@
     moved_state, mixed_rows, payload = lax.optimization_barrier((moved_state, mixed_rows, payload))
     combined_response = mixed_rows.reshape(steps, local_rows, width)
     pieces = payload.shape[0]
-    moved_terms = route_to_slots(
-        payload.reshape(pieces, local_rows, heads_here, SUBSPACE_EXTENT)
-        .transpose(1, 2, 0, 3)
-        .reshape(local_rows, heads_here, pieces * SUBSPACE_EXTENT),
-        position_mapping_target,
-        batch_index,
-        head_index,
-    )
-    slots_dev, columns, _ = moved_terms.shape
-    moved_terms = (
-        moved_terms.reshape(slots_dev, columns, pieces, SUBSPACE_EXTENT)
-        .transpose(2, 0, 1, 3)
-        .reshape(pieces, slots_dev * columns, SUBSPACE_EXTENT)
-    )
+    head_count = lax.axis_size("head")
+    cluster_number = head_count // 4
+    slots_dev = local_rows // cluster_number
+    per_pair = slots_dev // batch_count
+    quarter = heads_here // 4
+    own_map = lax.dynamic_slice_in_dim(
+        position_mapping_target, batch_index * local_rows, local_rows
+    )
+    dest_key = own_map // slots_dev
+    positions = jnp.arange(local_rows, dtype=jnp.int32)
+    ahead = (dest_key[None, :] < dest_key[:, None]) | (
+        (dest_key[None, :] == dest_key[:, None]) & (positions[None, :] < positions[:, None])
+    )
+    send_order = index_of(jnp.sum(ahead.astype(jnp.int32), axis=1), local_rows)
+    factors = jnp.take(
+        payload.reshape(pieces, local_rows, heads_here, SUBSPACE_EXTENT),
+        send_order,
+        axis=1,
+        mode="clip",
+    ).reshape(pieces, batch_count, cluster_number * per_pair, heads_here, SUBSPACE_EXTENT)
+    gathered, factors = gather_with_parts(
+        combined_response, factors.transpose(1, 0, 2, 3, 4), "batch"
+    )
+    gathered = gathered.transpose(1, 0, 2, 3).reshape(steps, sessions, width)
+    factors = factors.reshape(
+        batch_count, pieces, cluster_number, per_pair, 4, quarter, SUBSPACE_EXTENT
+    ).transpose(4, 2, 0, 1, 3, 5, 6)
+    factors = factors.reshape(
+        head_count, batch_count, pieces, per_pair, quarter, SUBSPACE_EXTENT
+    )
+    inverse = index_of(position_mapping_target, sessions)
+    arranged = jnp.concatenate(
+        [gathered[:STEPS_A], jnp.take(gathered[STEPS_A:], inverse, axis=1, mode="clip")], axis=0
+    )
+    partial_y = jnp.einsum(
+        "tnf,fo->tno", arranged, outgoing_linear_map, preferred_element_type=f32
+    ).astype(bf16)
+    produced, factors = sum_with_parts(
+        partial_y.reshape(steps, head_count, sessions // head_count, -1).transpose(1, 0, 2, 3),
+        factors,
+        "head",
+    )
+    produced = produced.astype(bf16)
+    factors = factors.transpose(2, 1, 3, 0, 4, 5).reshape(
+        pieces, batch_count * per_pair, head_count * quarter, SUBSPACE_EXTENT
+    )
+    target = batch_index * cluster_number + head_index % cluster_number
+    chosen = lax.dynamic_slice_in_dim(inverse, target * slots_dev, slots_dev)
+    every = jnp.arange(sessions, dtype=jnp.int32)
+    coming = (position_mapping_target // slots_dev) == target
+    placing = jnp.sum(
+        ((every[None, :] < chosen[:, None]) & coming[None, :]).astype(jnp.int32), axis=1
+    )
+    moved_terms = jnp.take(factors, placing, axis=1, mode="clip").reshape(
+        pieces, slots_dev * head_count * quarter, SUBSPACE_EXTENT
+    )
+    columns = head_count * quarter
     final_state = rebuild_state(
         moved_state.reshape(slots_dev * columns, -1), moved_terms, steps
     ).reshape(slots_dev, columns, -1)
-
-    gathered = exchange_copies(combined_response, "batch").transpose(1, 0, 2, 3)
-    gathered = gathered.reshape(steps, sessions, width)
-    inverse = index_of(position_mapping_target, sessions)
-    arranged = jnp.concatenate(
-        [gathered[:STEPS_A], jnp.take(gathered[STEPS_A:], inverse, axis=1, mode="clip")], axis=0
-    )
-    partial_y = jnp.einsum(
-        "tnf,fo->tno", arranged, outgoing_linear_map, preferred_element_type=f32
-    ).astype(bf16)
-    head_count = lax.axis_size("head")
-    produced = exchange_sum(
-        partial_y.reshape(steps, head_count, sessions // head_count, -1).transpose(1, 0, 2, 3),
-        "head",
-    ).astype(bf16)
     return (produced[:STEPS_A], produced[STEPS_A:], final_state)
 
 

time: 134 us -> 131 us (0.978)
  waiting for transfers between devices: 39 us -> 30.1 us
  starting transfers between devices: 33.1 us -> 37.2 us
  other arithmetic: 15 us -> 16.9 us
    ppermute x0 -> x12, starting transfers between devices: none -> 18.1 us  [the longest x6 9.28 us: gather_with_parts(): lax.ppermute((value, sent), axis_name, [(i, (i + shift) % count) for i in...]
    all_to_all x2 -> x1, waiting for transfers between devices: 11.2 us -> 1.8 us  [route_to_slots(): lax.all_to_all(packed, ('batch', 'head'), split_axis=0, concat_axis=0, ti...]
    ppermute x6 -> x3, starting transfers between devices: 13.3 us -> 6.12 us  [exchange_copies(): lax.ppermute(value, axis_name, [(i, (i + shift) % count) for i in range(c...]
    gather x0 -> x6, local copies, waits for them, and re-layouts: none -> 5.14 us  [the longest x3 1.97 us: by_source(): return jnp.take(jnp.stack(received), shifts, axis=0, mode='clip')]
    all_to_all x2 -> x1, starting transfers between devices: 7.74 us -> 4.22 us  [route_to_slots(): lax.all_to_all(packed, ('batch', 'head'), split_axis=0, concat_axis=0, ti...]
    ppermute x9 -> x6, starting transfers between devices: 12.1 us -> 8.82 us  [exchange_sum(): lax.ppermute(own(shift), axis_name, [(i, (i + shift) % count) for i in ra...]
    ppermute x0 -> x12, waiting for transfers between devices: none -> 2.58 us  [the longest x6 2.56 us: gather_with_parts(): lax.ppermute((value, sent), axis_name, [(i, (i + shift) % count) for i in...]
    ppermute x6 -> x3, waiting for transfers between devices: 6.56 us -> 4.34 us  [exchange_copies(): lax.ppermute(value, axis_name, [(i, (i + shift) % count) for i in range(c...]
  transfers between devices with their start and end apart: 17 -> 22, of which waited for: 7 -> 7; matrix products, arithmetic and copies ran while one was open for 16% -> 19% of each run, Pallas kernels for 5% -> 9%
where the time goes in v12:
time: 131 us; the launch traced here: 130 us
  starting transfers between devices  37.2 us (28%)
  waiting for transfers between devices  30.1 us (23%)
  local copies, waits for them, and re-layouts  24.3 us (19%)
  other arithmetic  16.9 us (13%)
  Pallas kernels  11.4 us (9%)
  matrix products  8.65 us (7%)
    ppermute x6, waiting for transfers between devices, exchange_sum(): lax.ppermute(own(shift), axis_name, [(i, (i + shift) % count) for i in ra...  21.3 us
    ppermute x6, starting transfers between devices, gather_with_parts(): lax.ppermute((value, sent), axis_name, [(i, (i + shift) % count) for i in...  9.28 us
    ppermute x6, starting transfers between devices, exchange_sum(): lax.ppermute(own(shift), axis_name, [(i, (i + shift) % count) for i in ra...  8.82 us
    ppermute x6, starting transfers between devices, sum_with_parts(): lax.ppermute((lax.dynamic_index_in_dim(pieces, target, keepdims=False), l...  8.78 us
    pallas_call x1, Pallas kernels, run_recurrence(): pl.pallas_call(functools.partial(recurrence_kernel, steps), grid=(rows //...  6.43 us
    ppermute x3, starting transfers between devices, exchange_copies(): lax.ppermute(value, axis_name, [(i, (i + shift) % count) for i in range(c...  6.12 us
    pallas_call x1, Pallas kernels, rebuild_state(): pl.pallas_call(functools.partial(rebuild_kernel, steps), grid=(rows // bl...  4.99 us
    dot_general x1, matrix products, per_device(): jnp.einsum('inf,ifc->inc', mixed[:4], fourfold_linear_maps, preferred_ele...  4.83 us
  transfers between devices with their start and end apart: 22, of which 7 were waited for; matrix products, arithmetic and copies ran while one was open for 19% of the time, Pallas kernels for 9%

profile of v12, /device:TPU:0, one launch (start us, length us, event | category | flops | bytes accessed | tf_op | source)
XLA Modules:
  0.0 129.8 jit_solution(3833731994498239153)
XLA Ops:
  0.6 1.1 slice_bitcast_fusion.2
  1.7 1.0 convert_bitcast_fusion
  2.8 0.9 convert_bitcast_fusion.1
  3.9 0.4 convolution_convert_fusion.1
  4.3 5.1 %collective-permute-start.2 = (bf16[128,320]{0,1:T(8,128)(2,1)S(1)}, bf16[128,320]{0,1:T(8,128)(2,1)S(1)}, u32[]{:S(2)}, u32[]{:S(2)}) collective-permute-start(bf16[128,320]{0,1:T(8,128)(2,1)S(1)} %convolution_convert_fusion.1), channel_id=1, source_target_pairs={{0,12},{4,0},{8,4},{12,8},{1,13},{5,1},{9,5},{13,9},{2,14},{6,2},{... | collective-permute-start | bytes 245768 | tf_op jit(solution)/shard_map/ppermute | solution.py:102
  9.4 1.0 collective-permute-start
  11.4 0.7 gather_fusion.1
  12.6 4.3 %collective-permute-done.1 = bf16[128,320]{0,1:T(8,128)(2,1)S(1)} collective-permute-done((bf16[128,320]{0,1:T(8,128)(2,1)S(1)}, bf16[128,320]{0,1:T(8,128)(2,1)S(1)}, u32[]{:S(2)}, u32[]{:S(2)}) %collective-permute-start.1) | collective-permute-done | bytes 81952 | tf_op jit(solution)/shard_map/ppermute | solution.py:102
  16.9 0.6 copy-done.6
  17.5 1.0 pad_maximum_fusion
  18.6 1.3 %gather_fusion = bf16[4,128,320]{1,2,0:T(8,128)(2,1)} fusion(bf16[4,128,320]{1,2,0:T(8,128)(2,1)S(1)} %pad_maximum_fusion, s32[1024]{0:T(1024)S(1)} %pad_clamp_fusion.7), kind=kCustom, calls=%fused_computation | custom fusion | bytes 655376 | tf_op jit(solution)/shard_map/jit(_take)/gather | solution.py:105
  19.9 1.1 convert_reduce_fusion
  21.0 1.7 %add_convert_fusion = bf16[5,128,1024]{2,1,0:T(8,128)(2,1)S(1)} fusion(bf16[128,5,64]{0,2,1:T(8,128)(2,1)S(1)} %bitcast.162, bf16[5,64,1024]{2,1,0:T(8,128)(2,1)} %param.21, f32[5,1024]{1,0:T(8,128)S(1)} %slice.53, f32[128,1024]{1,0:T(8,128)S(1)} %bitcast_subtract_fusion, f32[128,1024]{1,0:T(8,128)S(1)} %bitcast.145), kind=kOutput, calls=%fused_computation.10 | convolution fusion | flops 86507520 | bytes 3117056 | tf_op jit(solution)/shard_map/nim,imd->ind/dot_general | solution.py:345
  22.9 4.8 %convolution_convert_fusion = bf16[4,128,1024]{2,1,0:T(8,128)(2,1)S(1)} fusion(bf16[5,128,1024]{2,1,0:T(8,128)(2,1)S(1)} %add_convert_fusion, bf16[4,1024,1024]{2,1,0:T(8,128)(2,1)} %param.22), kind=kOutput, calls=%fused_computation.13 | convolution fusion | flops 1074266112 | bytes 10747904 | tf_op jit(solution)/shard_map/inf,ifc->inc/dot_general | solution.py:351
  27.8 3.8 %collective-permute-start.8 = (bf16[32,128]{1,0:T(8,128)(2,1)S(1)}, bf16[32,128]{1,0:T(8,128)(2,1)S(1)}, u32[]{:S(2)}, u32[]{:S(2)}) collective-permute-start(bf16[32,128]{1,0:T(8,128)(2,1)S(1)} %get-tuple-element.41), channel_id=1, source_target_pairs={{0,12},{4,0},{8,4},{12,8},{1,13},{5,1},{9,5},{13,9},{2,14},{6,2},{... | collective-permute-start | bytes 24584 | tf_op jit(solution)/shard_map/ppermute | solution.py:90
  31.7 0.8 dynamic-slice_bitcast_fusion.2
  32.5 0.9 collective-permute-start.3
  33.4 2.9 %collective-permute-start.5 = (bf16[4,32,1024]{2,1,0:T(8,128)(2,1)}, bf16[4,32,1024]{2,1,0:T(8,128)(2,1)}, u32[]{:S(2)}, u32[]{:S(2)}) collective-permute-start(bf16[4,32,1024]{2,1,0:T(8,128)(2,1)} %get-tuple-element.20), channel_id=1, source_target_pairs={{0,12},{4,0},{8,4},{12,8},{1,13},{5,1},{9,5},{13,9},{2,14},{6,2},{... | collective-permute-start | bytes 786440 | tf_op jit(solution)/shard_map/ppermute | solution.py:90
  36.3 1.1 collective-permute-start.4
  37.5 6.4 %collective-permute-done.3 = bf16[4,32,1024]{2,1,0:T(8,128)(2,1)} collective-permute-done((bf16[4,32,1024]{2,1,0:T(8,128)(2,1)}, bf16[4,32,1024]{2,1,0:T(8,128)(2,1)}, u32[]{:S(2)}, u32[]{:S(2)}) %collective-permute-start.3) | collective-permute-done | bytes 262176 | tf_op jit(solution)/shard_map/ppermute | solution.py:90
  43.9 3.2 %collective-permute-done.5 = bf16[4,32,1024]{2,1,0:T(8,128)(2,1)} collective-permute-done((bf16[4,32,1024]{2,1,0:T(8,128)(2,1)}, bf16[4,32,1024]{2,1,0:T(8,128)(2,1)}, u32[]{:S(2)}, u32[]{:S(2)}) %collective-permute-start.5) | collective-permute-done | bytes 262176 | tf_op jit(solution)/shard_map/ppermute | solution.py:90
  47.1 11.8 %collective-permute-done.4 = bf16[4,32,1024]{2,1,0:T(8,128)(2,1)} collective-permute-done((bf16[4,32,1024]{2,1,0:T(8,128)(2,1)S(1)}, bf16[4,32,1024]{2,1,0:T(8,128)(2,1)}, u32[]{:S(2)}, u32[]{:S(2)}) %collective-permute-start.4) | collective-permute-done | bytes 262176 | tf_op jit(solution)/shard_map/ppermute | solution.py:90
  58.8 2.1 %fusion.12 = f32[4,32,1024]{2,1,0:T(8,128)} fusion(bf16[4,32,1024]{2,1,0:T(8,128)(2,1)} %collective-permute-done.5, bf16[4,32,1024]{2,1,0:T(8,128)(2,1)} %collective-permute-done.4, bf16[4,32,1024]{2,1,0:T(8,128)(2,1)} %collective-permute-done.3, bf16[4,4,32,1024]{3,2,1,0:T(8,128)(2,1)S(1)} %bitcast.156, s32[]{:T(128)S(6)} %select_n.198), kind=kLoop, calls=%fused_computation.25 | loop fusion | flops 917504 | bytes 1572868 | tf_op jit(solution)/shard_map/add | solution.py:93
  60.9 1.7 %convert_element_type.180 = bf16[8,16,4096]{2,1,0:T(8,128)(2,1)S(1)} convert(f32[8,16,4096]{2,1,0:T(8,128)} %param.17) | non-fusion elementwise | flops 524288 | bytes 3145728 | tf_op jit(solution)/shard_map/convert_element_type | solution.py:369
  62.6 2.2 %gather_fusion.2 = bf16[128,4096]{1,0:T(8,128)(2,1)} fusion(bf16[128,4096]{1,0:T(8,128)(2,1)S(1)} %bitcast.141, s32[1024]{0:T(1024)S(1)} %pad_clamp_fusion.5), kind=kCustom, calls=%fused_computation.2 | custom fusion | bytes 2097664 | tf_op jit(solution)/shard_map/jit(_take)/gather | solution.py:52
  64.8 4.2 %all-to-all-start = ((bf16[16,8,4096]{2,1,0:T(8,128)(2,1)}), bf16[16,8,4096]{2,1,0:T(8,128)(2,1)S(1)}, u32[]{:S(2)}, u32[]{:S(2)}) async-start(bf16[16,8,4096]{2,1,0:T(8,128)(2,1)} %bitcast.146), calls=%async_computation | async-start | bytes 2097152 | tf_op jit(solution)/shard_map/all_to_all | solution.py:55
  69.5 0.5 fusion.31
  70.1 0.6 pad_clamp_fusion
  70.6 0.6 pad_clamp_fusion.2
  71.3 0.6 maximum_bitcast_fusion
  71.9 1.8 %convert.16 = bf16[4,32,1024]{2,1,0:T(8,128)(2,1)} convert(f32[4,32,1024]{2,1,0:T(8,128)} %fusion.12) | non-fusion elementwise | flops 131072 | bytes 786432 | tf_op jit(solution)/shard_map/convert.13
  73.6 1.1 fusion.10
  74.8 0.8 reshape_reshape.2.decay_ref
  75.7 1.6 %slice_convert_fusion = (f32[1,32,1024]{2,1,0:T(8,128)}, f32[1,32,1024]{2,1,0:T(8,128)}, f32[1,32,1024]{2,1,0:T(8,128)S(1)}) fusion(bf16[4,32,1024]{2,1,0:T(8,128)(2,1)} %convert.16), kind=kLoop, calls=%fused_computation.61 | loop fusion | flops 98304 | bytes 589824 | tf_op jit(solution)/shard_map/convert_element_type | solution.py:148
  77.3 1.7 %reshape.507.value_ref = f32[4,128,64]{2,1,0:T(8,128)} reshape(f32[1,32,1024]{2,1,0:T(8,128)} %get-tuple-element.35) | data formatting | bytes 262144 | tf_op jit(solution)/shard_map/convert_element_type | solution.py:148
  79.0 1.7 %reshape.506.key_ref = f32[4,128,64]{2,1,0:T(8,128)} reshape(f32[1,32,1024]{2,1,0:T(8,128)} %get-tuple-element.36) | data formatting | bytes 262144 | tf_op jit(solution)/shard_map/convert_element_type | solution.py:148
  80.7 0.8 reshape.505.recept_ref
  81.5 0.8 divide_multiply_fusion.gate_ref
  82.3 1.4 %broadcast_in_dim.57 = f32[3,8,16,64]{3,2,1,0:T(8,128)} broadcast(f32[3,16,64]{2,1,0:T(8,128)} %maximum_bitcast_fusion), dimensions={0,2,3} | broadcast | bytes 110592 | tf_op jit(solution)/shard_map/broadcast_in_dim | solution.py:395
  83.7 6.4 %shard_map.166 = (bf16[4,128,64]{2,1,0:T(8,128)(2,1)}, bf16[9,128,64]{2,1,0:T(8,128)(2,1)}) custom-call(f32[4,128,64]{2,1,0:T(8,128)} %reshape.505.recept_ref, f32[4,128,64]{2,1,0:T(8,128)} %reshape.506.key_ref, f32[4,128,64]{2,1,0:T(8,128)} %reshape.507.value_ref, f32[4,128,64]{2,1,0:T(8,128)} %reshape_reshape.2.decay_ref, ...), custom_call_target="tpu_custom_call" | custom-call | flops 805306368 | bytes 3063808 | tf_op jit(solution)/shard_map/pallas_call | solution.py:236
  90.2 1.8 %all-to-all-done = bf16[16,8,4096]{2,1,0:T(8,128)(2,1)S(1)} async-done(((bf16[16,8,4096]{2,1,0:T(8,128)(2,1)}), bf16[16,8,4096]{2,1,0:T(8,128)(2,1)S(1)}, u32[]{:S(2)}, u32[]{:S(2)}) %all-to-all-start) | async-done | bytes 1048608 | tf_op jit(solution)/shard_map/all_to_all | solution.py:55
  92.0 2.2 %gather_fusion.3 = bf16[128,4096]{1,0:T(8,128)(2,1)} fusion(bf16[128,4096]{1,0:T(8,128)(2,1)S(1)} %bitcast.142, s32[1024]{0:T(1024)S(1)} %pad_clamp_fusion.4), kind=kCustom, calls=%fused_computation.3 | custom fusion | bytes 2097664 | tf_op jit(solution)/shard_map/jit(_take)/gather | solution.py:74
  94.1 1.7 %gather_fusion.6 = bf16[8,9,16,64]{3,2,1,0:T(8,128)(2,1)S(1)} fusion(bf16[9,8,16,64]{3,2,1,0:T(8,128)(2,1)} %bitcast.164, s32[1024]{0:T(1024)} %pad_clamp_fusion.2), kind=kCustom, calls=%fused_computation.6 | custom fusion | bytes 294944 | tf_op jit(solution)/shard_map/jit(_take)/gather | solution.py:421
  95.9 3.2 %collective-permute-start.17 = (bf16[9,2,16,64]{3,2,1,0:T(8,128)(2,1)S(1)}, bf16[9,2,16,64]{3,2,1,0:T(8,128)(2,1)S(1)}, u32[]{:S(2)}, u32[]{:S(2)}) collective-permute-start(bf16[9,2,16,64]{3,2,1,0:T(8,128)(2,1)S(1)} %bitcast.177), channel_id=1, source_target_pairs={{0,12},{4,0},{8,4},{12,8},{1,13},{5,1},{9,5},{13,9},{2,14},{6,2},{... | collective-permute-start | bytes 110600 | tf_op jit(solution)/shard_map/ppermute | solution.py:119
  99.3 3.8 %collective-permute-start.16 = (bf16[9,2,16,64]{3,2,1,0:T(8,128)(2,1)S(1)}, bf16[9,2,16,64]{3,2,1,0:T(8,128)(2,1)S(1)}, u32[]{:S(2)}, u32[]{:S(2)}) collective-permute-start(bf16[9,2,16,64]{3,2,1,0:T(8,128)(2,1)S(1)} %bitcast.175), channel_id=1, source_target_pairs={{0,8},{4,12},{8,0},{12,4},{1,9},{5,13},{9,1},{13,5},{2,10},{6,14},... | collective-permute-start | bytes 110600 | tf_op jit(solution)/shard_map/ppermute | solution.py:119
  103.4 1.0 collective-permute-start.11
  104.4 1.0 collective-permute-start.10
  105.6 1.7 %collective-permute-done.15 = bf16[9,2,16,64]{3,2,1,0:T(8,128)(2,1)S(1)} collective-permute-done((bf16[9,2,16,64]{3,2,1,0:T(8,128)(2,1)S(1)}, bf16[9,2,16,64]{3,2,1,0:T(8,128)(2,1)S(1)}, u32[]{:S(2)}, u32[]{:S(2)}) %collective-permute-start.15) | collective-permute-done | bytes 36896 | tf_op jit(solution)/shard_map/ppermute | solution.py:119
  107.3 0.8 collective-permute-done.16
  108.2 0.6 gather_fusion.7
  109.0 5.1 %collective-permute-start.19 = (bf16[4,9,2,4,64]{4,3,2,1,0:T(4,128)(2,1)S(1)}, bf16[4,9,2,4,64]{4,3,2,1,0:T(4,128)(2,1)S(1)}, u32[]{:S(2)}, u32[]{:S(2)}) collective-permute-start(bf16[4,9,2,4,64]{4,3,2,1,0:T(4,128)(2,1)S(1)} %get-tuple-element.24), channel_id=1, source_target_pairs={{0,2},{1,3},{2,0},{3,1},{4,6},{5,7},{6,4},{7,5},{8,10},{9,11},{10,... | collective-permute-start | bytes 110600 | tf_op jit(solution)/shard_map/ppermute | solution.py:134
  114.4 0.6 gather_fusion.4
  115.1 0.8 gather_fusion.5
  116.0 0.4 fusion.5
  116.5 0.7 dynamic-slice_bitcast_fusion.9
  117.2 1.7 %collective-permute-start.14 = (bf16[4,8,1024]{2,1,0:T(8,128)(2,1)}, bf16[4,8,1024]{2,1,0:T(8,128)(2,1)}, u32[]{:S(2)}, u32[]{:S(2)}) collective-permute-start(bf16[4,8,1024]{2,1,0:T(8,128)(2,1)} %get-tuple-element.31), channel_id=1, source_target_pairs={{0,3},{1,0},{2,1},{3,2},{4,7},{5,4},{6,5},{7,6},{8,11},{9,8},{10,9... | collective-permute-start | bytes 196616 | tf_op jit(solution)/shard_map/ppermute | solution.py:134
  118.9 1.7 %collective-permute-start.13 = (bf16[4,8,1024]{2,1,0:T(8,128)(2,1)}, bf16[4,8,1024]{2,1,0:T(8,128)(2,1)S(1)}, u32[]{:S(2)}, u32[]{:S(2)}) collective-permute-start(bf16[4,8,1024]{2,1,0:T(8,128)(2,1)} %get-tuple-element.32), channel_id=1, source_target_pairs={{0,2},{1,3},{2,0},{3,1},{4,6},{5,7},{6,4},{7,5},{8,10},{9,11},{10,... | collective-permute-start | bytes 196616 | tf_op jit(solution)/shard_map/ppermute | solution.py:134
  120.6 0.3 pad_maximum_fusion.2
  120.9 0.8 gather_fusion.8
  121.8 0.7 gather_fusion.9
  122.6 0.7 copy.79
  123.3 5.0 %shard_map.167 = f32[128,4096]{1,0:T(8,128)} custom-call(bf16[128,4096]{1,0:T(8,128)(2,1)} %gather_fusion.3, bf16[9,128,64]{2,1,0:T(8,128)(2,1)} %bitcast.153), custom_call_target="tpu_custom_call" | custom-call | flops 603979776 | bytes 3293184 | tf_op jit(solution)/shard_map/pallas_call | solution.py:280
  128.3 0.9 fusion.20
  129.2 0.6 fusion.38
  (107 shorter events, 3.9 us)
Async XLA Ops:
  0.6 115.4 %copy-start = (bf16[1024,1024]{1,0:T(8,128)(2,1)S(1)}, bf16[1024,1024]{1,0:T(8,128)(2,1)}, u32[]{:S(2)}) copy-start(bf16[1024,1024]{1,0:T(8,128)(2,1)} %param.29) | copy-start | bytes 6291460
  2.7 1.2 copy-start.1
  2.8 1.2 slice-start.1
  3.8 6.6 %copy-start.13 = (s32[32]{0:T(128)S(1)}, s32[32]{0:T(128)}, u32[]{:S(2)}) copy-start(s32[32]{0:T(128)} %param.18) | copy-start | bytes 388
  3.8 6.8 %copy-start.7 = (f32[6,1024]{1,0:T(8,128)S(1)}, f32[6,1024]{1,0:T(8,128)}, u32[]{:S(2)}) copy-start(f32[6,1024]{1,0:T(8,128)} %param.19) | copy-start | bytes 73732
  4.3 7.8 %copy-start.3 = (bf16[128,320]{0,1:T(8,128)(2,1)}, bf16[128,320]{0,1:T(8,128)(2,1)S(1)}, u32[]{:S(2)}) copy-start(bf16[128,320]{0,1:T(8,128)(2,1)S(1)} %convolution_convert_fusion.1) | copy-start | bytes 245764
  4.3 8.3 %collective-permute-start.2 = (bf16[128,320]{0,1:T(8,128)(2,1)S(1)}, bf16[128,320]{0,1:T(8,128)(2,1)S(1)}, u32[]{:S(2)}, u32[]{:S(2)}) collective-permute-start(bf16[128,320]{0,1:T(8,128)(2,1)S(1)} %convolution_convert_fusion.1), channel_id=1, source_target_pairs={{0,12},{4,0},{8,4},{12,8},{1,13},{5,1},{9,5},{13,9},{2,14},{6,2},{... | collective-permute-start | bytes 245768 | tf_op jit(solution)/shard_map/ppermute | solution.py:102
  9.4 7.5 %collective-permute-start.1 = (bf16[128,320]{0,1:T(8,128)(2,1)S(1)}, bf16[128,320]{0,1:T(8,128)(2,1)S(1)}, u32[]{:S(2)}, u32[]{:S(2)}) collective-permute-start(bf16[128,320]{0,1:T(8,128)(2,1)S(1)} %convolution_convert_fusion.1), channel_id=1, source_target_pairs={{0,8},{4,12},{8,0},{12,4},{1,9},{5,13},{9,1},{13,5},{2,10},{6,14},... | collective-permute-start | bytes 245768 | tf_op jit(solution)/shard_map/ppermute | solution.py:102
  9.4 7.5 %collective-permute-start = (bf16[128,320]{0,1:T(8,128)(2,1)S(1)}, bf16[128,320]{0,1:T(8,128)(2,1)}, u32[]{:S(2)}, u32[]{:S(2)}) collective-permute-start(bf16[128,320]{0,1:T(8,128)(2,1)S(1)} %convolution_convert_fusion.1), channel_id=1, source_target_pairs={{0,4},{4,8},{8,12},{12,0},{1,5},{5,9},{9,13},{13,1},{2,6},{6,10},{... | collective-permute-start | bytes 245768 | tf_op jit(solution)/shard_map/ppermute | solution.py:102
  12.5 4.4 %copy-start.5 = (bf16[128,320]{0,1:T(8,128)(2,1)}, bf16[128,320]{0,1:T(8,128)(2,1)S(1)}, u32[]{:S(2)}) copy-start(bf16[128,320]{0,1:T(8,128)(2,1)S(1)} %collective-permute-done.2) | copy-start | bytes 245764
  16.9 0.6 copy-start.6
  19.9 2.8 %copy-start.4 = (bf16[1024,128]{1,0:T(8,128)(2,1)S(1)}, bf16[1024,128]{1,0:T(8,128)(2,1)}, u32[]{:S(2)}) copy-start(bf16[1024,128]{1,0:T(8,128)(2,1)} %param.23) | copy-start | bytes 786436
  27.8 8.6 %collective-permute-start.6 = (bf16[32,128]{1,0:T(8,128)(2,1)S(1)}, bf16[32,128]{1,0:T(8,128)(2,1)S(1)}, u32[]{:S(2)}, u32[]{:S(2)}) collective-permute-start(bf16[32,128]{1,0:T(8,128)(2,1)S(1)} %get-tuple-element.40), channel_id=1, source_target_pairs={{0,4},{4,8},{8,12},{12,0},{1,5},{5,9},{9,13},{13,1},{2,6},{6,10},{... | collective-permute-start | bytes 24584 | tf_op jit(solution)/shard_map/ppermute | solution.py:90
  27.8 9.6 %collective-permute-start.8 = (bf16[32,128]{1,0:T(8,128)(2,1)S(1)}, bf16[32,128]{1,0:T(8,128)(2,1)S(1)}, u32[]{:S(2)}, u32[]{:S(2)}) collective-permute-start(bf16[32,128]{1,0:T(8,128)(2,1)S(1)} %get-tuple-element.41), channel_id=1, source_target_pairs={{0,12},{4,0},{8,4},{12,8},{1,13},{5,1},{9,5},{13,9},{2,14},{6,2},{... | collective-permute-start | bytes 24584 | tf_op jit(solution)/shard_map/ppermute | solution.py:90
  31.7 5.8 %collective-permute-start.7 = (bf16[32,128]{1,0:T(8,128)(2,1)S(1)}, bf16[32,128]{1,0:T(8,128)(2,1)S(1)}, u32[]{:S(2)}, u32[]{:S(2)}) collective-permute-start(bf16[32,128]{1,0:T(8,128)(2,1)S(1)} %get-tuple-element.42), channel_id=1, source_target_pairs={{0,8},{4,12},{8,0},{12,4},{1,9},{5,13},{9,1},{13,5},{2,10},{6,14},... | collective-permute-start | bytes 24584 | tf_op jit(solution)/shard_map/ppermute | solution.py:90
  32.5 11.4 %collective-permute-start.3 = (bf16[4,32,1024]{2,1,0:T(8,128)(2,1)}, bf16[4,32,1024]{2,1,0:T(8,128)(2,1)}, u32[]{:S(2)}, u32[]{:S(2)}) collective-permute-start(bf16[4,32,1024]{2,1,0:T(8,128)(2,1)} %get-tuple-element.19), channel_id=1, source_target_pairs={{0,4},{4,8},{8,12},{12,0},{1,5},{5,9},{9,13},{13,1},{2,6},{6,10},{... | collective-permute-start | bytes 786440 | tf_op jit(solution)/shard_map/ppermute | solution.py:90
  33.4 13.7 %collective-permute-start.5 = (bf16[4,32,1024]{2,1,0:T(8,128)(2,1)}, bf16[4,32,1024]{2,1,0:T(8,128)(2,1)}, u32[]{:S(2)}, u32[]{:S(2)}) collective-permute-start(bf16[4,32,1024]{2,1,0:T(8,128)(2,1)} %get-tuple-element.20), channel_id=1, source_target_pairs={{0,12},{4,0},{8,4},{12,8},{1,13},{5,1},{9,5},{13,9},{2,14},{6,2},{... | collective-permute-start | bytes 786440 | tf_op jit(solution)/shard_map/ppermute | solution.py:90
  36.3 22.5 %collective-permute-start.4 = (bf16[4,32,1024]{2,1,0:T(8,128)(2,1)S(1)}, bf16[4,32,1024]{2,1,0:T(8,128)(2,1)}, u32[]{:S(2)}, u32[]{:S(2)}) collective-permute-start(bf16[4,32,1024]{2,1,0:T(8,128)(2,1)S(1)} %get-tuple-element.21), channel_id=1, source_target_pairs={{0,8},{4,12},{8,0},{12,4},{1,9},{5,13},{9,1},{13,5},{2,10},{6,14},... | collective-permute-start | bytes 786440 | tf_op jit(solution)/shard_map/ppermute | solution.py:90
  64.8 4.3 %copy-start.9 = (f32[1024]{0:T(1024)S(1)}, f32[1024]{0:T(1024)}, u32[]{:S(2)}) copy-start(f32[1024]{0:T(1024)} %param.26) | copy-start | bytes 12292
  64.8 4.3 %copy-start.10 = (f32[1024]{0:T(1024)S(1)}, f32[1024]{0:T(1024)}, u32[]{:S(2)}) copy-start(f32[1024]{0:T(1024)} %param.27) | copy-start | bytes 12292
  64.8 4.4 %copy-start.11 = (f32[1024]{0:T(1024)S(1)}, f32[1024]{0:T(1024)}, u32[]{:S(2)}) copy-start(f32[1024]{0:T(1024)} %param.28) | copy-start | bytes 12292
  64.8 8.9 %copy-start.8 = (f32[1024]{0:T(1024)S(1)}, f32[1024]{0:T(1024)}, u32[]{:S(2)}) copy-start(f32[1024]{0:T(1024)} %param.25) | copy-start | bytes 12292
  64.8 10.8 %slice-start = ((f32[4,32,1024]{2,1,0:T(8,128)}), f32[1,32,1024]{2,1,0:T(8,128)S(1)}, s32[]{:S(2)}) async-start(f32[4,32,1024]{2,1,0:T(8,128)} %fusion.12), calls=%async_computation.1 | async-start | bytes 262144 | tf_op jit(solution)/shard_map/slice | solution.py:379
  64.8 27.2 %all-to-all-start = ((bf16[16,8,4096]{2,1,0:T(8,128)(2,1)}), bf16[16,8,4096]{2,1,0:T(8,128)(2,1)S(1)}, u32[]{:S(2)}, u32[]{:S(2)}) async-start(bf16[16,8,4096]{2,1,0:T(8,128)(2,1)} %bitcast.146), calls=%async_computation | async-start | bytes 2097152 | tf_op jit(solution)/shard_map/all_to_all | solution.py:55
  92.0 11.1 %copy-start.12 = (s32[4]{0:T(128)S(1)}, s32[4]{0:T(128)}, u32[]{:S(2)}) copy-start(s32[4]{0:T(128)} %fusion.31) | copy-start | bytes 52
  92.0 11.2 %copy-start.2 = (bf16[4,128,64]{2,1,0:T(8,128)(2,1)S(1)}, bf16[4,128,64]{2,1,0:T(8,128)(2,1)}, u32[]{:S(2)}) copy-start(bf16[4,128,64]{2,1,0:T(8,128)(2,1)} %get-tuple-element.16) | copy-start | bytes 196612
  95.9 9.5 %collective-permute-start.17 = (bf16[9,2,16,64]{3,2,1,0:T(8,128)(2,1)S(1)}, bf16[9,2,16,64]{3,2,1,0:T(8,128)(2,1)S(1)}, u32[]{:S(2)}, u32[]{:S(2)}) collective-permute-start(bf16[9,2,16,64]{3,2,1,0:T(8,128)(2,1)S(1)} %bitcast.177), channel_id=1, source_target_pairs={{0,12},{4,0},{8,4},{12,8},{1,13},{5,1},{9,5},{13,9},{2,14},{6,2},{... | collective-permute-start | bytes 110600 | tf_op jit(solution)/shard_map/ppermute | solution.py:119
  99.2 8.1 %collective-permute-start.15 = (bf16[9,2,16,64]{3,2,1,0:T(8,128)(2,1)S(1)}, bf16[9,2,16,64]{3,2,1,0:T(8,128)(2,1)S(1)}, u32[]{:S(2)}, u32[]{:S(2)}) collective-permute-start(bf16[9,2,16,64]{3,2,1,0:T(8,128)(2,1)S(1)} %bitcast.176), channel_id=1, source_target_pairs={{0,4},{4,8},{8,12},{12,0},{1,5},{5,9},{9,13},{13,1},{2,6},{6,10},{... | collective-permute-start | bytes 110600 | tf_op jit(solution)/shard_map/ppermute | solution.py:119
  99.3 8.9 %collective-permute-start.16 = (bf16[9,2,16,64]{3,2,1,0:T(8,128)(2,1)S(1)}, bf16[9,2,16,64]{3,2,1,0:T(8,128)(2,1)S(1)}, u32[]{:S(2)}, u32[]{:S(2)}) collective-permute-start(bf16[9,2,16,64]{3,2,1,0:T(8,128)(2,1)S(1)} %bitcast.175), channel_id=1, source_target_pairs={{0,8},{4,12},{8,0},{12,4},{1,9},{5,13},{9,1},{13,5},{2,10},{6,14},... | collective-permute-start | bytes 110600 | tf_op jit(solution)/shard_map/ppermute | solution.py:119
  103.4 10.7 %collective-permute-start.11 = (bf16[4,8,1024]{2,1,0:T(8,128)(2,1)S(1)}, bf16[4,8,1024]{2,1,0:T(8,128)(2,1)S(1)}, u32[]{:S(2)}, u32[]{:S(2)}) collective-permute-start(bf16[4,8,1024]{2,1,0:T(8,128)(2,1)S(1)} %reshape.492), channel_id=1, source_target_pairs={{0,12},{4,0},{8,4},{12,8},{1,13},{5,1},{9,5},{13,9},{2,14},{6,2},{... | collective-permute-start | bytes 196616 | tf_op jit(solution)/shard_map/ppermute | solution.py:119
  104.4 9.9 %collective-permute-start.10 = (bf16[4,8,1024]{2,1,0:T(8,128)(2,1)S(1)}, bf16[4,8,1024]{2,1,0:T(8,128)(2,1)S(1)}, u32[]{:S(2)}, u32[]{:S(2)}) collective-permute-start(bf16[4,8,1024]{2,1,0:T(8,128)(2,1)S(1)} %reshape.492), channel_id=1, source_target_pairs={{0,8},{4,12},{8,0},{12,4},{1,9},{5,13},{9,1},{13,5},{2,10},{6,14},... | collective-permute-start | bytes 196616 | tf_op jit(solution)/shard_map/ppermute | solution.py:119
  105.4 8.9 %collective-permute-start.9 = (bf16[4,8,1024]{2,1,0:T(8,128)(2,1)S(1)}, bf16[4,8,1024]{2,1,0:T(8,128)(2,1)S(1)}, u32[]{:S(2)}, u32[]{:S(2)}) collective-permute-start(bf16[4,8,1024]{2,1,0:T(8,128)(2,1)S(1)} %reshape.492), channel_id=1, source_target_pairs={{0,4},{4,8},{8,12},{12,0},{1,5},{5,9},{9,13},{13,1},{2,6},{6,10},{... | collective-permute-start | bytes 196616 | tf_op jit(solution)/shard_map/ppermute | solution.py:119
  109.0 9.9 %collective-permute-start.20 = (bf16[4,9,2,4,64]{4,3,2,1,0:T(4,128)(2,1)S(1)}, bf16[4,9,2,4,64]{4,3,2,1,0:T(4,128)(2,1)S(1)}, u32[]{:S(2)}, u32[]{:S(2)}) collective-permute-start(bf16[4,9,2,4,64]{4,3,2,1,0:T(4,128)(2,1)S(1)} %get-tuple-element.23), channel_id=1, source_target_pairs={{0,3},{1,0},{2,1},{3,2},{4,7},{5,4},{6,5},{7,6},{8,11},{9,8},{10,9... | collective-permute-start | bytes 110600 | tf_op jit(solution)/shard_map/ppermute | solution.py:134
  109.0 11.6 %collective-permute-start.19 = (bf16[4,9,2,4,64]{4,3,2,1,0:T(4,128)(2,1)S(1)}, bf16[4,9,2,4,64]{4,3,2,1,0:T(4,128)(2,1)S(1)}, u32[]{:S(2)}, u32[]{:S(2)}) collective-permute-start(bf16[4,9,2,4,64]{4,3,2,1,0:T(4,128)(2,1)S(1)} %get-tuple-element.24), channel_id=1, source_target_pairs={{0,2},{1,3},{2,0},{3,1},{4,6},{5,7},{6,4},{7,5},{8,10},{9,11},{10,... | collective-permute-start | bytes 110600 | tf_op jit(solution)/shard_map/ppermute | solution.py:134
  114.1 6.4 %collective-permute-start.18 = (bf16[4,9,2,4,64]{4,3,2,1,0:T(4,128)(2,1)S(1)}, bf16[4,9,2,4,64]{4,3,2,1,0:T(4,128)(2,1)S(1)}, u32[]{:S(2)}, u32[]{:S(2)}) collective-permute-start(bf16[4,9,2,4,64]{4,3,2,1,0:T(4,128)(2,1)S(1)} %get-tuple-element.25), channel_id=1, source_target_pairs={{0,1},{1,2},{2,3},{3,0},{4,5},{5,6},{6,7},{7,4},{8,9},{9,10},{10,1... | collective-permute-start | bytes 110600 | tf_op jit(solution)/shard_map/ppermute | solution.py:134
  117.1 11.1 %collective-permute-start.12 = (bf16[4,8,1024]{2,1,0:T(8,128)(2,1)}, bf16[4,8,1024]{2,1,0:T(8,128)(2,1)S(1)}, u32[]{:S(2)}, u32[]{:S(2)}) collective-permute-start(bf16[4,8,1024]{2,1,0:T(8,128)(2,1)} %get-tuple-element.30), channel_id=1, source_target_pairs={{0,1},{1,2},{2,3},{3,0},{4,5},{5,6},{6,7},{7,4},{8,9},{9,10},{10,1... | collective-permute-start | bytes 196616 | tf_op jit(solution)/shard_map/ppermute | solution.py:134
  117.2 11.1 %collective-permute-start.14 = (bf16[4,8,1024]{2,1,0:T(8,128)(2,1)}, bf16[4,8,1024]{2,1,0:T(8,128)(2,1)}, u32[]{:S(2)}, u32[]{:S(2)}) collective-permute-start(bf16[4,8,1024]{2,1,0:T(8,128)(2,1)} %get-tuple-element.31), channel_id=1, source_target_pairs={{0,3},{1,0},{2,1},{3,2},{4,7},{5,4},{6,5},{7,6},{8,11},{9,8},{10,9... | collective-permute-start | bytes 196616 | tf_op jit(solution)/shard_map/ppermute | solution.py:134
  118.9 9.4 %collective-permute-start.13 = (bf16[4,8,1024]{2,1,0:T(8,128)(2,1)}, bf16[4,8,1024]{2,1,0:T(8,128)(2,1)S(1)}, u32[]{:S(2)}, u32[]{:S(2)}) collective-permute-start(bf16[4,8,1024]{2,1,0:T(8,128)(2,1)} %get-tuple-element.32), channel_id=1, source_target_pairs={{0,2},{1,3},{2,0},{3,1},{4,6},{5,7},{6,4},{7,5},{8,10},{9,11},{10,... | collective-permute-start | bytes 196616 | tf_op jit(solution)/shard_map/ppermute | solution.py:134

commit v13 on v12

--- a/solution.py
+++ b/solution.py
@@ -19,7 +19,7 @@
     return jnp.sum(jnp.where(values[None, :] == wanted[:, None], positions[None, :], 0), axis=1)
 
 
-def route_to_slots(value, position_mapping_target, batch_index, head_index):
+def route_to_slots(value, position_mapping_target, batch_index, head_index, after=None):
     batch_count = lax.axis_size("batch")
     head_count = lax.axis_size("head")
     local_rows, heads_here, width = value.shape
@@ -52,6 +52,8 @@
     packed = jnp.take(
         value.reshape(local_rows * heads_here, width), sent_rows.reshape(-1), axis=0, mode="clip"
     ).reshape(batch_count * head_count, per_pair * quarter, width)
+    if after is not None:
+        packed, after = lax.optimization_barrier((packed, after))
     arrived = lax.all_to_all(packed, ("batch", "head"), split_axis=0, concat_axis=0, tiled=True)
     target = batch_index * cluster_number + head_index % cluster_number
     sessions = position_mapping_target.shape[0]
@@ -362,11 +364,12 @@
         "batch",
     )
 
-    kept_for_move, main_sum, decay_sum = lax.optimization_barrier(
-        (stream_kept_tableaux, main_sum, decay_sum)
-    )
     moved_state = route_to_slots(
-        kept_for_move.astype(bf16), position_mapping_target, batch_index, head_index
+        stream_kept_tableaux.astype(bf16),
+        position_mapping_target,
+        batch_index,
+        head_index,
+        after=(main_sum, decay_sum),
     )
 
     def heads_of(value):

time: 131 us -> 128 us (0.977)
  waiting for transfers between devices: 30.1 us -> 25.7 us
  local copies, waits for them, and re-layouts: 24.3 us -> 28.4 us
  starting transfers between devices: 37.2 us -> 33.6 us
    ppermute x6, waiting for transfers between devices: 21.3 us -> 17.5 us  [exchange_sum(): lax.ppermute(own(shift), axis_name, [(i, (i + shift) % count) for i in ra...]
    ppermute x6, starting transfers between devices: 8.78 us -> 4.9 us  [sum_with_parts(): lax.ppermute((lax.dynamic_index_in_dim(pieces, target, keepdims=False), l...]
    ppermute x6, waiting for transfers between devices: 2.56 us -> 4.83 us  [gather_with_parts(): lax.ppermute((value, sent), axis_name, [(i, (i + shift) % count) for i in...]
    add x2 -> x1, other arithmetic: 2.07 us -> 0.01 us  [exchange_sum(): acc + value.astype(jnp.float32)]
    another operation x3, local copies, waits for them, and re-layouts: 0.21 us -> 2.27 us  [per_device(): jnp.stack([instant_premium, norming_multiplier, norming_intercept])]
    all_to_all x1, waiting for transfers between devices: 1.8 us -> 0.01 us  [route_to_slots(): lax.all_to_all(packed, ('batch', 'head'), split_axis=0, concat_axis=0, ti...]
  transfers between devices with their start and end apart: 22 -> 22, of which waited for: 7 -> 7; matrix products, arithmetic and copies ran while one was open for 19% -> 26% of each run, Pallas kernels for 9% -> 9%
where the time goes in v13:
time: 128 us; the launch traced here: 127 us
  starting transfers between devices  33.6 us (26%)
  local copies, waits for them, and re-layouts  28.4 us (22%)
  waiting for transfers between devices  25.7 us (20%)
  other arithmetic  18.1 us (14%)
  Pallas kernels  11.4 us (9%)
  matrix products  8.39 us (7%)
  between operations  1.29 us (1%)
    ppermute x6, waiting for transfers between devices, exchange_sum(): lax.ppermute(own(shift), axis_name, [(i, (i + shift) % count) for i in ra...  17.5 us
    ppermute x6, starting transfers between devices, gather_with_parts(): lax.ppermute((value, sent), axis_name, [(i, (i + shift) % count) for i in...  9.73 us
    ppermute x6, starting transfers between devices, exchange_sum(): lax.ppermute(own(shift), axis_name, [(i, (i + shift) % count) for i in ra...  8.82 us
    pallas_call x1, Pallas kernels, run_recurrence(): pl.pallas_call(functools.partial(recurrence_kernel, steps), grid=(rows //...  6.41 us
    ppermute x3, starting transfers between devices, exchange_copies(): lax.ppermute(value, axis_name, [(i, (i + shift) % count) for i in range(c...  6.12 us
    pallas_call x1, Pallas kernels, rebuild_state(): pl.pallas_call(functools.partial(rebuild_kernel, steps), grid=(rows // bl...  4.98 us
    ppermute x6, starting transfers between devices, sum_with_parts(): lax.ppermute((lax.dynamic_index_in_dim(pieces, target, keepdims=False), l...  4.9 us
    dot_general x1, matrix products, per_device(): jnp.einsum('inf,ifc->inc', mixed[:4], fourfold_linear_maps, preferred_ele...  4.83 us
  transfers between devices with their start and end apart: 22, of which 7 were waited for; matrix products, arithmetic and copies ran while one was open for 26% of the time, Pallas kernels for 9%

profile of v13, /device:TPU:0, one launch (start us, length us, event | category | flops | bytes accessed | tf_op | source)
XLA Modules:
  0.0 126.9 jit_solution(9321900413786204007)
XLA Ops:
  0.6 1.1 slice_bitcast_fusion.2
  1.7 1.0 convert_bitcast_fusion
  2.8 0.9 convert_bitcast_fusion.1
  4.3 5.1 %collective-permute-start.2 = (bf16[128,320]{0,1:T(8,128)(2,1)S(1)}, bf16[128,320]{0,1:T(8,128)(2,1)S(1)}, u32[]{:S(2)}, u32[]{:S(2)}) collective-permute-start(bf16[128,320]{0,1:T(8,128)(2,1)S(1)} %convolution_convert_fusion.1), channel_id=1, source_target_pairs={{0,12},{4,0},{8,4},{12,8},{1,13},{5,1},{9,5},{13,9},{2,14},{6,2},{... | collective-permute-start | bytes 245768 | tf_op jit(solution)/shard_map/ppermute | solution.py:104
  9.4 1.0 collective-permute-start
  11.3 0.6 fusion.35
  12.4 0.7 gather_fusion
  13.5 3.4 %collective-permute-done.1 = bf16[128,320]{0,1:T(8,128)(2,1)S(1)} collective-permute-done((bf16[128,320]{0,1:T(8,128)(2,1)S(1)}, bf16[128,320]{0,1:T(8,128)(2,1)S(1)}, u32[]{:S(2)}, u32[]{:S(2)}) %collective-permute-start.1) | collective-permute-done | bytes 81952 | tf_op jit(solution)/shard_map/ppermute | solution.py:104
  16.9 0.6 copy-done.8
  17.5 1.0 pad_maximum_fusion
  18.6 1.3 %gather_fusion.2 = bf16[4,128,320]{1,2,0:T(8,128)(2,1)} fusion(bf16[4,128,320]{1,2,0:T(8,128)(2,1)S(1)} %pad_maximum_fusion, s32[1024]{0:T(1024)S(1)} %pad_clamp_fusion.5), kind=kCustom, calls=%fused_computation.2 | custom fusion | bytes 655376 | tf_op jit(solution)/shard_map/jit(_take)/gather | solution.py:107
  19.9 1.1 convert_reduce_fusion
  21.0 1.7 %add_convert_fusion = bf16[5,128,1024]{2,1,0:T(8,128)(2,1)S(1)} fusion(bf16[128,5,64]{0,2,1:T(8,128)(2,1)S(1)} %bitcast.163, bf16[5,64,1024]{2,1,0:T(8,128)(2,1)} %param.21, f32[5,1024]{1,0:T(8,128)S(1)} %slice.53, f32[128,1024]{1,0:T(8,128)S(1)} %bitcast_subtract_fusion, f32[128,1024]{1,0:T(8,128)S(1)} %bitcast.146), kind=kOutput, calls=%fused_computation.10 | convolution fusion | flops 86507520 | bytes 3117056 | tf_op jit(solution)/shard_map/nim,imd->ind/dot_general | solution.py:347
  22.9 4.8 %convolution_convert_fusion = bf16[4,128,1024]{2,1,0:T(8,128)(2,1)S(1)} fusion(bf16[5,128,1024]{2,1,0:T(8,128)(2,1)S(1)} %add_convert_fusion, bf16[4,1024,1024]{2,1,0:T(8,128)(2,1)} %param.22), kind=kOutput, calls=%fused_computation.13 | convolution fusion | flops 1074266112 | bytes 10747904 | tf_op jit(solution)/shard_map/inf,ifc->inc/dot_general | solution.py:353
  27.9 3.8 %collective-permute-start.8 = (bf16[32,128]{1,0:T(8,128)(2,1)S(1)}, bf16[32,128]{1,0:T(8,128)(2,1)S(1)}, u32[]{:S(2)}, u32[]{:S(2)}) collective-permute-start(bf16[32,128]{1,0:T(8,128)(2,1)S(1)} %get-tuple-element.39), channel_id=1, source_target_pairs={{0,12},{4,0},{8,4},{12,8},{1,13},{5,1},{9,5},{13,9},{2,14},{6,2},{... | collective-permute-start | bytes 24584 | tf_op jit(solution)/shard_map/ppermute | solution.py:92
  31.7 0.9 dynamic-slice_bitcast_fusion.2
  32.5 0.9 collective-permute-start.3
  33.4 2.9 %collective-permute-start.5 = (bf16[4,32,1024]{2,1,0:T(8,128)(2,1)}, bf16[4,32,1024]{2,1,0:T(8,128)(2,1)}, u32[]{:S(2)}, u32[]{:S(2)}) collective-permute-start(bf16[4,32,1024]{2,1,0:T(8,128)(2,1)} %get-tuple-element.18), channel_id=1, source_target_pairs={{0,12},{4,0},{8,4},{12,8},{1,13},{5,1},{9,5},{13,9},{2,14},{6,2},{... | collective-permute-start | bytes 786440 | tf_op jit(solution)/shard_map/ppermute | solution.py:92
  36.4 1.1 collective-permute-start.4
  37.5 1.7 %convert_element_type.155 = bf16[8,16,4096]{2,1,0:T(8,128)(2,1)S(1)} convert(f32[8,16,4096]{2,1,0:T(8,128)} %param.17) | non-fusion elementwise | flops 524288 | bytes 3145728 | tf_op jit(solution)/shard_map/convert_element_type | solution.py:368
  39.2 2.2 %gather_fusion.1 = bf16[128,4096]{1,0:T(8,128)(2,1)} fusion(bf16[128,4096]{1,0:T(8,128)(2,1)S(1)} %bitcast.142, s32[1024]{0:T(1024)S(1)} %pad_clamp_fusion.6), kind=kCustom, calls=%fused_computation.1 | custom fusion | bytes 2097664 | tf_op jit(solution)/shard_map/jit(_take)/gather | solution.py:52
  41.4 2.5 %collective-permute-done.3 = bf16[4,32,1024]{2,1,0:T(8,128)(2,1)} collective-permute-done((bf16[4,32,1024]{2,1,0:T(8,128)(2,1)}, bf16[4,32,1024]{2,1,0:T(8,128)(2,1)}, u32[]{:S(2)}, u32[]{:S(2)}) %collective-permute-start.3) | collective-permute-done | bytes 262176 | tf_op jit(solution)/shard_map/ppermute | solution.py:92
  44.0 3.2 %collective-permute-done.5 = bf16[4,32,1024]{2,1,0:T(8,128)(2,1)} collective-permute-done((bf16[4,32,1024]{2,1,0:T(8,128)(2,1)}, bf16[4,32,1024]{2,1,0:T(8,128)(2,1)}, u32[]{:S(2)}, u32[]{:S(2)}) %collective-permute-start.5) | collective-permute-done | bytes 262176 | tf_op jit(solution)/shard_map/ppermute | solution.py:92
  47.1 11.8 %collective-permute-done.4 = bf16[4,32,1024]{2,1,0:T(8,128)(2,1)} collective-permute-done((bf16[4,32,1024]{2,1,0:T(8,128)(2,1)S(1)}, bf16[4,32,1024]{2,1,0:T(8,128)(2,1)}, u32[]{:S(2)}, u32[]{:S(2)}) %collective-permute-start.4) | collective-permute-done | bytes 262176 | tf_op jit(solution)/shard_map/ppermute | solution.py:92
  58.9 2.3 %fusion.37 = (bf16[4,32,1024]{2,1,0:T(8,128)(2,1)}, f32[4,32,1024]{2,1,0:T(8,128)}) fusion(bf16[4,32,1024]{2,1,0:T(8,128)(2,1)} %collective-permute-done.5, bf16[4,32,1024]{2,1,0:T(8,128)(2,1)} %collective-permute-done.4, bf16[4,32,1024]{2,1,0:T(8,128)(2,1)} %collective-permute-done.3, bf16[4,4,32,1024]{3,2,1,0:T(8,128)(2,1)} %bitcast.157, s32[]{:T(128)S(6)} %select_n.203), kind=kLoop, calls=%fused_computation.138 | loop fusion | flops 1048576 | bytes 1835012 | tf_op jit(solution)/shard_map/convert.13
  61.2 4.1 %all-to-all-start = ((bf16[16,8,4096]{2,1,0:T(8,128)(2,1)}), bf16[16,8,4096]{2,1,0:T(8,128)(2,1)S(1)}, u32[]{:S(2)}, u32[]{:S(2)}) async-start(bf16[16,8,4096]{2,1,0:T(8,128)(2,1)} %bitcast.147), calls=%async_computation | async-start | bytes 2097152 | tf_op jit(solution)/shard_map/all_to_all | solution.py:57
  65.3 0.8 stack.70
  66.0 0.8 stack.71
  66.8 0.8 stack.72
  67.5 0.7 add_multiply_fusion
  69.0 1.2 pad_clamp_fusion
  70.2 1.3 pad_clamp_fusion.3
  72.1 0.6 pad_clamp_fusion.4
  72.6 0.6 maximum_bitcast_fusion
  73.3 0.9 fusion.10
  74.1 0.8 reshape_reshape.2.decay_ref
  74.9 0.9 slice.91
  76.0 1.6 %slice_convert_fusion = (f32[1,32,1024]{2,1,0:T(8,128)}, f32[1,32,1024]{2,1,0:T(8,128)}, f32[1,32,1024]{2,1,0:T(8,128)S(1)}) fusion(bf16[4,32,1024]{2,1,0:T(8,128)(2,1)} %get-tuple-element.15), kind=kLoop, calls=%fused_computation.61 | loop fusion | flops 98304 | bytes 589824 | tf_op jit(solution)/shard_map/convert_element_type | solution.py:150
  77.6 1.7 %reshape.507.value_ref = f32[4,128,64]{2,1,0:T(8,128)} reshape(f32[1,32,1024]{2,1,0:T(8,128)} %get-tuple-element.33) | data formatting | bytes 262144 | tf_op jit(solution)/shard_map/convert_element_type | solution.py:150
  79.3 1.7 %reshape.506.key_ref = f32[4,128,64]{2,1,0:T(8,128)} reshape(f32[1,32,1024]{2,1,0:T(8,128)} %get-tuple-element.34) | data formatting | bytes 262144 | tf_op jit(solution)/shard_map/convert_element_type | solution.py:150
  81.0 0.8 reshape.505.recept_ref
  81.8 0.8 divide_multiply_fusion.gate_ref
  82.6 1.4 %broadcast_in_dim.57 = f32[3,8,16,64]{3,2,1,0:T(8,128)} broadcast(f32[3,16,64]{2,1,0:T(8,128)} %maximum_bitcast_fusion), dimensions={0,2,3} | broadcast | bytes 110592 | tf_op jit(solution)/shard_map/broadcast_in_dim | solution.py:398
  84.0 6.4 %shard_map.166 = (bf16[4,128,64]{2,1,0:T(8,128)(2,1)}, bf16[9,128,64]{2,1,0:T(8,128)(2,1)}) custom-call(f32[4,128,64]{2,1,0:T(8,128)} %reshape.505.recept_ref, f32[4,128,64]{2,1,0:T(8,128)} %reshape.506.key_ref, f32[4,128,64]{2,1,0:T(8,128)} %reshape.507.value_ref, f32[4,128,64]{2,1,0:T(8,128)} %reshape_reshape.2.decay_ref, ...), custom_call_target="tpu_custom_call" | custom-call | flops 805306368 | bytes 3063808 | tf_op jit(solution)/shard_map/pallas_call | solution.py:238
  90.5 2.4 %gather_fusion.3 = bf16[128,4096]{1,0:T(8,128)(2,1)} fusion(bf16[128,4096]{1,0:T(8,128)(2,1)S(1)} %bitcast.143, s32[1024]{0:T(1024)} %pad_clamp_fusion.4), kind=kCustom, calls=%fused_computation.3 | custom fusion | bytes 2097664 | tf_op jit(solution)/shard_map/jit(_take)/gather | solution.py:76
  92.9 1.7 %gather_fusion.6 = bf16[8,9,16,64]{3,2,1,0:T(8,128)(2,1)S(1)} fusion(bf16[9,8,16,64]{3,2,1,0:T(8,128)(2,1)} %bitcast.165, s32[1024]{0:T(1024)} %pad_clamp_fusion.2), kind=kCustom, calls=%fused_computation.6 | custom fusion | bytes 294944 | tf_op jit(solution)/shard_map/jit(_take)/gather | solution.py:424
  94.7 3.8 %collective-permute-start.17 = (bf16[9,2,16,64]{3,2,1,0:T(8,128)(2,1)S(1)}, bf16[9,2,16,64]{3,2,1,0:T(8,128)(2,1)S(1)}, u32[]{:S(2)}, u32[]{:S(2)}) collective-permute-start(bf16[9,2,16,64]{3,2,1,0:T(8,128)(2,1)S(1)} %bitcast.178), channel_id=1, source_target_pairs={{0,12},{4,0},{8,4},{12,8},{1,13},{5,1},{9,5},{13,9},{2,14},{6,2},{... | collective-permute-start | bytes 110600 | tf_op jit(solution)/shard_map/ppermute | solution.py:121
  98.4 1.1 collective-permute-start.16
  99.9 2.8 %collective-permute-start.11 = (bf16[4,8,1024]{2,1,0:T(8,128)(2,1)S(1)}, bf16[4,8,1024]{2,1,0:T(8,128)(2,1)S(1)}, u32[]{:S(2)}, u32[]{:S(2)}) collective-permute-start(bf16[4,8,1024]{2,1,0:T(8,128)(2,1)S(1)} %reshape.492), channel_id=1, source_target_pairs={{0,12},{4,0},{8,4},{12,8},{1,13},{5,1},{9,5},{13,9},{2,14},{6,2},{... | collective-permute-start | bytes 196616 | tf_op jit(solution)/shard_map/ppermute | solution.py:121
  102.7 2.0 %collective-permute-start.10 = (bf16[4,8,1024]{2,1,0:T(8,128)(2,1)S(1)}, bf16[4,8,1024]{2,1,0:T(8,128)(2,1)S(1)}, u32[]{:S(2)}, u32[]{:S(2)}) collective-permute-start(bf16[4,8,1024]{2,1,0:T(8,128)(2,1)S(1)} %reshape.492), channel_id=1, source_target_pairs={{0,8},{4,12},{8,0},{12,4},{1,9},{5,13},{9,1},{13,5},{2,10},{6,14},... | collective-permute-start | bytes 196616 | tf_op jit(solution)/shard_map/ppermute | solution.py:121
  104.8 0.7 collective-permute-done.15
  105.4 4.0 %collective-permute-done.16 = bf16[9,2,16,64]{3,2,1,0:T(8,128)(2,1)S(1)} collective-permute-done((bf16[9,2,16,64]{3,2,1,0:T(8,128)(2,1)S(1)}, bf16[9,2,16,64]{3,2,1,0:T(8,128)(2,1)S(1)}, u32[]{:S(2)}, u32[]{:S(2)}) %collective-permute-start.16) | collective-permute-done | bytes 36896 | tf_op jit(solution)/shard_map/ppermute | solution.py:121
  109.6 0.7 gather_fusion.7
  110.5 1.5 %collective-permute-start.19 = (bf16[4,9,2,4,64]{4,3,2,1,0:T(4,128)(2,1)S(1)}, bf16[4,9,2,4,64]{4,3,2,1,0:T(4,128)(2,1)S(1)}, u32[]{:S(2)}, u32[]{:S(2)}) collective-permute-start(bf16[4,9,2,4,64]{4,3,2,1,0:T(4,128)(2,1)S(1)} %get-tuple-element.22), channel_id=1, source_target_pairs={{0,2},{1,3},{2,0},{3,1},{4,6},{5,7},{6,4},{7,5},{8,10},{9,11},{10,... | collective-permute-start | bytes 110600 | tf_op jit(solution)/shard_map/ppermute | solution.py:136
  112.3 0.7 gather_fusion.4
  113.2 0.9 gather_fusion.5
  114.7 0.7 dynamic-slice_bitcast_fusion.9
  115.8 1.3 %collective-permute-start.14 = (bf16[4,8,1024]{2,1,0:T(8,128)(2,1)}, bf16[4,8,1024]{2,1,0:T(8,128)(2,1)S(1)}, u32[]{:S(2)}, u32[]{:S(2)}) collective-permute-start(bf16[4,8,1024]{2,1,0:T(8,128)(2,1)} %get-tuple-element.29), channel_id=1, source_target_pairs={{0,3},{1,0},{2,1},{3,2},{4,7},{5,4},{6,5},{7,6},{8,11},{9,8},{10,9... | collective-permute-start | bytes 196616 | tf_op jit(solution)/shard_map/ppermute | solution.py:136
  117.1 1.4 %collective-permute-start.13 = (bf16[4,8,1024]{2,1,0:T(8,128)(2,1)S(1)}, bf16[4,8,1024]{2,1,0:T(8,128)(2,1)S(1)}, u32[]{:S(2)}, u32[]{:S(2)}) collective-permute-start(bf16[4,8,1024]{2,1,0:T(8,128)(2,1)S(1)} %get-tuple-element.30), channel_id=1, source_target_pairs={{0,2},{1,3},{2,0},{3,1},{4,6},{5,7},{6,4},{7,5},{8,10},{9,11},{10,... | collective-permute-start | bytes 196616 | tf_op jit(solution)/shard_map/ppermute | solution.py:136
  118.8 0.8 gather_fusion.8
  119.8 0.7 gather_fusion.9
  120.5 0.7 copy.79
  121.2 5.0 %shard_map.167 = f32[128,4096]{1,0:T(8,128)} custom-call(bf16[128,4096]{1,0:T(8,128)(2,1)} %gather_fusion.3, bf16[9,128,64]{2,1,0:T(8,128)(2,1)} %bitcast.154), custom_call_target="tpu_custom_call" | custom-call | flops 603979776 | bytes 3293184 | tf_op jit(solution)/shard_map/pallas_call | solution.py:282
  126.3 0.6 fusion.40
  (107 shorter events, 6.6 us)
Async XLA Ops:
  0.6 113.6 %copy-start = (bf16[1024,1024]{1,0:T(8,128)(2,1)S(1)}, bf16[1024,1024]{1,0:T(8,128)(2,1)}, u32[]{:S(2)}) copy-start(bf16[1024,1024]{1,0:T(8,128)(2,1)} %param.29) | copy-start | bytes 6291460
  2.7 1.2 copy-start.2
  2.8 1.2 slice-start
  3.8 6.6 %copy-start.14 = (s32[32]{0:T(128)S(1)}, s32[32]{0:T(128)}, u32[]{:S(2)}) copy-start(s32[32]{0:T(128)} %param.18) | copy-start | bytes 388
  3.8 6.8 %copy-start.9 = (f32[6,1024]{1,0:T(8,128)S(1)}, f32[6,1024]{1,0:T(8,128)}, u32[]{:S(2)}) copy-start(f32[6,1024]{1,0:T(8,128)} %param.19) | copy-start | bytes 73732
  4.3 8.8 %copy-start.4 = (bf16[128,320]{0,1:T(8,128)(2,1)}, bf16[128,320]{0,1:T(8,128)(2,1)S(1)}, u32[]{:S(2)}) copy-start(bf16[128,320]{0,1:T(8,128)(2,1)S(1)} %convolution_convert_fusion.1) | copy-start | bytes 245764
  4.3 9.2 %collective-permute-start.2 = (bf16[128,320]{0,1:T(8,128)(2,1)S(1)}, bf16[128,320]{0,1:T(8,128)(2,1)S(1)}, u32[]{:S(2)}, u32[]{:S(2)}) collective-permute-start(bf16[128,320]{0,1:T(8,128)(2,1)S(1)} %convolution_convert_fusion.1), channel_id=1, source_target_pairs={{0,12},{4,0},{8,4},{12,8},{1,13},{5,1},{9,5},{13,9},{2,14},{6,2},{... | collective-permute-start | bytes 245768 | tf_op jit(solution)/shard_map/ppermute | solution.py:104
  9.4 7.5 %collective-permute-start.1 = (bf16[128,320]{0,1:T(8,128)(2,1)S(1)}, bf16[128,320]{0,1:T(8,128)(2,1)S(1)}, u32[]{:S(2)}, u32[]{:S(2)}) collective-permute-start(bf16[128,320]{0,1:T(8,128)(2,1)S(1)} %convolution_convert_fusion.1), channel_id=1, source_target_pairs={{0,8},{4,12},{8,0},{12,4},{1,9},{5,13},{9,1},{13,5},{2,10},{6,14},... | collective-permute-start | bytes 245768 | tf_op jit(solution)/shard_map/ppermute | solution.py:104
  9.4 7.5 %collective-permute-start = (bf16[128,320]{0,1:T(8,128)(2,1)S(1)}, bf16[128,320]{0,1:T(8,128)(2,1)}, u32[]{:S(2)}, u32[]{:S(2)}) collective-permute-start(bf16[128,320]{0,1:T(8,128)(2,1)S(1)} %convolution_convert_fusion.1), channel_id=1, source_target_pairs={{0,4},{4,8},{8,12},{12,0},{1,5},{5,9},{9,13},{13,1},{2,6},{6,10},{... | collective-permute-start | bytes 245768 | tf_op jit(solution)/shard_map/ppermute | solution.py:104
  10.5 0.5 copy-start.12
  11.3 0.6 copy-start.11
  13.5 9.2 %copy-start.10 = (s32[1024]{0:T(1024)}, s32[1024]{0:T(1024)S(1)}, u32[]{:S(2)}) copy-start(s32[1024]{0:T(1024)S(1)} %pad_clamp_fusion.5) | copy-start | bytes 12292
  13.5 3.4 %copy-start.7 = (bf16[128,320]{0,1:T(8,128)(2,1)}, bf16[128,320]{0,1:T(8,128)(2,1)S(1)}, u32[]{:S(2)}) copy-start(bf16[128,320]{0,1:T(8,128)(2,1)S(1)} %collective-permute-done.2) | copy-start | bytes 245764
  16.9 0.6 copy-start.8
  19.9 2.8 %copy-start.5 = (bf16[1024,128]{1,0:T(8,128)(2,1)S(1)}, bf16[1024,128]{1,0:T(8,128)(2,1)}, u32[]{:S(2)}) copy-start(bf16[1024,128]{1,0:T(8,128)(2,1)} %param.23) | copy-start | bytes 786436
  27.8 3.9 %copy-start.1 = (bf16[4,128,1024]{2,1,0:T(8,128)(2,1)}, bf16[4,128,1024]{2,1,0:T(8,128)(2,1)S(1)}, u32[]{:S(2)}) copy-start(bf16[4,128,1024]{2,1,0:T(8,128)(2,1)S(1)} %convolution_convert_fusion) | copy-start | bytes 3145732
  27.8 8.6 %collective-permute-start.6 = (bf16[32,128]{1,0:T(8,128)(2,1)S(1)}, bf16[32,128]{1,0:T(8,128)(2,1)S(1)}, u32[]{:S(2)}, u32[]{:S(2)}) collective-permute-start(bf16[32,128]{1,0:T(8,128)(2,1)S(1)} %get-tuple-element.38), channel_id=1, source_target_pairs={{0,4},{4,8},{8,12},{12,0},{1,5},{5,9},{9,13},{13,1},{2,6},{6,10},{... | collective-permute-start | bytes 24584 | tf_op jit(solution)/shard_map/ppermute | solution.py:92
  27.9 13.5 %collective-permute-start.8 = (bf16[32,128]{1,0:T(8,128)(2,1)S(1)}, bf16[32,128]{1,0:T(8,128)(2,1)S(1)}, u32[]{:S(2)}, u32[]{:S(2)}) collective-permute-start(bf16[32,128]{1,0:T(8,128)(2,1)S(1)} %get-tuple-element.39), channel_id=1, source_target_pairs={{0,12},{4,0},{8,4},{12,8},{1,13},{5,1},{9,5},{13,9},{2,14},{6,2},{... | collective-permute-start | bytes 24584 | tf_op jit(solution)/shard_map/ppermute | solution.py:92
  31.7 9.7 %collective-permute-start.7 = (bf16[32,128]{1,0:T(8,128)(2,1)S(1)}, bf16[32,128]{1,0:T(8,128)(2,1)S(1)}, u32[]{:S(2)}, u32[]{:S(2)}) collective-permute-start(bf16[32,128]{1,0:T(8,128)(2,1)S(1)} %get-tuple-element.40), channel_id=1, source_target_pairs={{0,8},{4,12},{8,0},{12,4},{1,9},{5,13},{9,1},{13,5},{2,10},{6,14},... | collective-permute-start | bytes 24584 | tf_op jit(solution)/shard_map/ppermute | solution.py:92
  32.5 11.4 %collective-permute-start.3 = (bf16[4,32,1024]{2,1,0:T(8,128)(2,1)}, bf16[4,32,1024]{2,1,0:T(8,128)(2,1)}, u32[]{:S(2)}, u32[]{:S(2)}) collective-permute-start(bf16[4,32,1024]{2,1,0:T(8,128)(2,1)} %get-tuple-element.17), channel_id=1, source_target_pairs={{0,4},{4,8},{8,12},{12,0},{1,5},{5,9},{9,13},{13,1},{2,6},{6,10},{... | collective-permute-start | bytes 786440 | tf_op jit(solution)/shard_map/ppermute | solution.py:92
  33.4 13.7 %collective-permute-start.5 = (bf16[4,32,1024]{2,1,0:T(8,128)(2,1)}, bf16[4,32,1024]{2,1,0:T(8,128)(2,1)}, u32[]{:S(2)}, u32[]{:S(2)}) collective-permute-start(bf16[4,32,1024]{2,1,0:T(8,128)(2,1)} %get-tuple-element.18), channel_id=1, source_target_pairs={{0,12},{4,0},{8,4},{12,8},{1,13},{5,1},{9,5},{13,9},{2,14},{6,2},{... | collective-permute-start | bytes 786440 | tf_op jit(solution)/shard_map/ppermute | solution.py:92
  36.4 22.5 %collective-permute-start.4 = (bf16[4,32,1024]{2,1,0:T(8,128)(2,1)S(1)}, bf16[4,32,1024]{2,1,0:T(8,128)(2,1)}, u32[]{:S(2)}, u32[]{:S(2)}) collective-permute-start(bf16[4,32,1024]{2,1,0:T(8,128)(2,1)S(1)} %get-tuple-element.19), channel_id=1, source_target_pairs={{0,8},{4,12},{8,0},{12,4},{1,9},{5,13},{9,1},{13,5},{2,10},{6,14},... | collective-permute-start | bytes 786440 | tf_op jit(solution)/shard_map/ppermute | solution.py:92
  58.9 14.4 %copy-start.6 = (bf16[128,1024]{1,0:T(8,128)(2,1)S(1)}, bf16[128,1024]{1,0:T(8,128)(2,1)}, u32[]{:S(2)}) copy-start(bf16[128,1024]{1,0:T(8,128)(2,1)} %param.24) | copy-start | bytes 786436
  61.2 29.2 %all-to-all-start = ((bf16[16,8,4096]{2,1,0:T(8,128)(2,1)}), bf16[16,8,4096]{2,1,0:T(8,128)(2,1)S(1)}, u32[]{:S(2)}, u32[]{:S(2)}) async-start(bf16[16,8,4096]{2,1,0:T(8,128)(2,1)} %bitcast.147), calls=%async_computation | async-start | bytes 2097152 | tf_op jit(solution)/shard_map/all_to_all | solution.py:57
  90.4 9.1 %copy-start.13 = (s32[4]{0:T(128)S(1)}, s32[4]{0:T(128)}, u32[]{:S(2)}) copy-start(s32[4]{0:T(128)} %fusion.31) | copy-start | bytes 52
  90.4 9.2 %copy-start.3 = (bf16[4,128,64]{2,1,0:T(8,128)(2,1)S(1)}, bf16[4,128,64]{2,1,0:T(8,128)(2,1)}, u32[]{:S(2)}) copy-start(bf16[4,128,64]{2,1,0:T(8,128)(2,1)} %get-tuple-element.12) | copy-start | bytes 196612
  94.7 10.0 %collective-permute-start.17 = (bf16[9,2,16,64]{3,2,1,0:T(8,128)(2,1)S(1)}, bf16[9,2,16,64]{3,2,1,0:T(8,128)(2,1)S(1)}, u32[]{:S(2)}, u32[]{:S(2)}) collective-permute-start(bf16[9,2,16,64]{3,2,1,0:T(8,128)(2,1)S(1)} %bitcast.178), channel_id=1, source_target_pairs={{0,12},{4,0},{8,4},{12,8},{1,13},{5,1},{9,5},{13,9},{2,14},{6,2},{... | collective-permute-start | bytes 110600 | tf_op jit(solution)/shard_map/ppermute | solution.py:121
  98.4 7.0 %collective-permute-start.15 = (bf16[9,2,16,64]{3,2,1,0:T(8,128)(2,1)S(1)}, bf16[9,2,16,64]{3,2,1,0:T(8,128)(2,1)S(1)}, u32[]{:S(2)}, u32[]{:S(2)}) collective-permute-start(bf16[9,2,16,64]{3,2,1,0:T(8,128)(2,1)S(1)} %bitcast.177), channel_id=1, source_target_pairs={{0,4},{4,8},{8,12},{12,0},{1,5},{5,9},{9,13},{13,1},{2,6},{6,10},{... | collective-permute-start | bytes 110600 | tf_op jit(solution)/shard_map/ppermute | solution.py:121
  98.4 11.0 %collective-permute-start.16 = (bf16[9,2,16,64]{3,2,1,0:T(8,128)(2,1)S(1)}, bf16[9,2,16,64]{3,2,1,0:T(8,128)(2,1)S(1)}, u32[]{:S(2)}, u32[]{:S(2)}) collective-permute-start(bf16[9,2,16,64]{3,2,1,0:T(8,128)(2,1)S(1)} %bitcast.176), channel_id=1, source_target_pairs={{0,8},{4,12},{8,0},{12,4},{1,9},{5,13},{9,1},{13,5},{2,10},{6,14},... | collective-permute-start | bytes 110600 | tf_op jit(solution)/shard_map/ppermute | solution.py:121
  99.9 12.1 %collective-permute-start.11 = (bf16[4,8,1024]{2,1,0:T(8,128)(2,1)S(1)}, bf16[4,8,1024]{2,1,0:T(8,128)(2,1)S(1)}, u32[]{:S(2)}, u32[]{:S(2)}) collective-permute-start(bf16[4,8,1024]{2,1,0:T(8,128)(2,1)S(1)} %reshape.492), channel_id=1, source_target_pairs={{0,12},{4,0},{8,4},{12,8},{1,13},{5,1},{9,5},{13,9},{2,14},{6,2},{... | collective-permute-start | bytes 196616 | tf_op jit(solution)/shard_map/ppermute | solution.py:121
  102.7 9.6 %collective-permute-start.10 = (bf16[4,8,1024]{2,1,0:T(8,128)(2,1)S(1)}, bf16[4,8,1024]{2,1,0:T(8,128)(2,1)S(1)}, u32[]{:S(2)}, u32[]{:S(2)}) collective-permute-start(bf16[4,8,1024]{2,1,0:T(8,128)(2,1)S(1)} %reshape.492), channel_id=1, source_target_pairs={{0,8},{4,12},{8,0},{12,4},{1,9},{5,13},{9,1},{13,5},{2,10},{6,14},... | collective-permute-start | bytes 196616 | tf_op jit(solution)/shard_map/ppermute | solution.py:121
  104.7 7.6 %collective-permute-start.9 = (bf16[4,8,1024]{2,1,0:T(8,128)(2,1)S(1)}, bf16[4,8,1024]{2,1,0:T(8,128)(2,1)S(1)}, u32[]{:S(2)}, u32[]{:S(2)}) collective-permute-start(bf16[4,8,1024]{2,1,0:T(8,128)(2,1)S(1)} %reshape.492), channel_id=1, source_target_pairs={{0,4},{4,8},{8,12},{12,0},{1,5},{5,9},{9,13},{13,1},{2,6},{6,10},{... | collective-permute-start | bytes 196616 | tf_op jit(solution)/shard_map/ppermute | solution.py:121
  110.4 6.7 %collective-permute-start.20 = (bf16[4,9,2,4,64]{4,3,2,1,0:T(4,128)(2,1)S(1)}, bf16[4,9,2,4,64]{4,3,2,1,0:T(4,128)(2,1)S(1)}, u32[]{:S(2)}, u32[]{:S(2)}) collective-permute-start(bf16[4,9,2,4,64]{4,3,2,1,0:T(4,128)(2,1)S(1)} %get-tuple-element.21), channel_id=1, source_target_pairs={{0,3},{1,0},{2,1},{3,2},{4,7},{5,4},{6,5},{7,6},{8,11},{9,8},{10,9... | collective-permute-start | bytes 110600 | tf_op jit(solution)/shard_map/ppermute | solution.py:136
  110.5 8.1 %collective-permute-start.19 = (bf16[4,9,2,4,64]{4,3,2,1,0:T(4,128)(2,1)S(1)}, bf16[4,9,2,4,64]{4,3,2,1,0:T(4,128)(2,1)S(1)}, u32[]{:S(2)}, u32[]{:S(2)}) collective-permute-start(bf16[4,9,2,4,64]{4,3,2,1,0:T(4,128)(2,1)S(1)} %get-tuple-element.22), channel_id=1, source_target_pairs={{0,2},{1,3},{2,0},{3,1},{4,6},{5,7},{6,4},{7,5},{8,10},{9,11},{10,... | collective-permute-start | bytes 110600 | tf_op jit(solution)/shard_map/ppermute | solution.py:136
  112.0 6.6 %collective-permute-start.18 = (bf16[4,9,2,4,64]{4,3,2,1,0:T(4,128)(2,1)S(1)}, bf16[4,9,2,4,64]{4,3,2,1,0:T(4,128)(2,1)S(1)}, u32[]{:S(2)}, u32[]{:S(2)}) collective-permute-start(bf16[4,9,2,4,64]{4,3,2,1,0:T(4,128)(2,1)S(1)} %get-tuple-element.23), channel_id=1, source_target_pairs={{0,1},{1,2},{2,3},{3,0},{4,5},{5,6},{6,7},{7,4},{8,9},{9,10},{10,1... | collective-permute-start | bytes 110600 | tf_op jit(solution)/shard_map/ppermute | solution.py:136
  115.4 10.9 %collective-permute-start.12 = (bf16[4,8,1024]{2,1,0:T(8,128)(2,1)}, bf16[4,8,1024]{2,1,0:T(8,128)(2,1)S(1)}, u32[]{:S(2)}, u32[]{:S(2)}) collective-permute-start(bf16[4,8,1024]{2,1,0:T(8,128)(2,1)} %get-tuple-element.28), channel_id=1, source_target_pairs={{0,1},{1,2},{2,3},{3,0},{4,5},{5,6},{6,7},{7,4},{8,9},{9,10},{10,1... | collective-permute-start | bytes 196616 | tf_op jit(solution)/shard_map/ppermute | solution.py:136
  115.8 10.5 %collective-permute-start.14 = (bf16[4,8,1024]{2,1,0:T(8,128)(2,1)}, bf16[4,8,1024]{2,1,0:T(8,128)(2,1)S(1)}, u32[]{:S(2)}, u32[]{:S(2)}) collective-permute-start(bf16[4,8,1024]{2,1,0:T(8,128)(2,1)} %get-tuple-element.29), channel_id=1, source_target_pairs={{0,3},{1,0},{2,1},{3,2},{4,7},{5,4},{6,5},{7,6},{8,11},{9,8},{10,9... | collective-permute-start | bytes 196616 | tf_op jit(solution)/shard_map/ppermute | solution.py:136
  117.1 9.1 %collective-permute-start.13 = (bf16[4,8,1024]{2,1,0:T(8,128)(2,1)S(1)}, bf16[4,8,1024]{2,1,0:T(8,128)(2,1)S(1)}, u32[]{:S(2)}, u32[]{:S(2)}) collective-permute-start(bf16[4,8,1024]{2,1,0:T(8,128)(2,1)S(1)} %get-tuple-element.30), channel_id=1, source_target_pairs={{0,2},{1,3},{2,0},{3,1},{4,6},{5,7},{6,4},{7,5},{8,10},{9,11},{10,... | collective-permute-start | bytes 196616 | tf_op jit(solution)/shard_map/ppermute | solution.py:136

commit v14 on v12

--- a/solution.py
+++ b/solution.py
@@ -19,10 +19,10 @@
     return jnp.sum(jnp.where(values[None, :] == wanted[:, None], positions[None, :], 0), axis=1)
 
 
-def route_to_slots(value, position_mapping_target, batch_index, head_index):
+def slot_routes(position_mapping_target, local_rows, heads_here, batch_index, head_index):
     batch_count = lax.axis_size("batch")
     head_count = lax.axis_size("head")
-    local_rows, heads_here, width = value.shape
+    sessions = position_mapping_target.shape[0]
     cluster_number = head_count // 4
     slots_dev = local_rows // cluster_number
     per_pair = slots_dev // batch_count
@@ -48,16 +48,10 @@
         sent_sessions[:, :, None] * heads_here
         + (quad * quarter)[:, None, None]
         + within[None, None, :]
-    )
-    packed = jnp.take(
-        value.reshape(local_rows * heads_here, width), sent_rows.reshape(-1), axis=0, mode="clip"
-    ).reshape(batch_count * head_count, per_pair * quarter, width)
-    arrived = lax.all_to_all(packed, ("batch", "head"), split_axis=0, concat_axis=0, tiled=True)
+    ).reshape(-1)
+    inverse = index_of(position_mapping_target, sessions)
     target = batch_index * cluster_number + head_index % cluster_number
-    sessions = position_mapping_target.shape[0]
-    chosen = lax.dynamic_slice_in_dim(
-        index_of(position_mapping_target, sessions), target * slots_dev, slots_dev
-    )
+    chosen = lax.dynamic_slice_in_dim(inverse, target * slots_dev, slots_dev)
     every = jnp.arange(sessions, dtype=jnp.int32)
     coming = (position_mapping_target // slots_dev) == target
     placing = jnp.sum(
@@ -71,8 +65,30 @@
         * per_pair
         + placing[:, None, None] % per_pair
     ) * quarter + within[None, None, :]
+    return {
+        "send_order": send_order,
+        "sent_rows": sent_rows,
+        "inverse": inverse,
+        "placing": placing,
+        "kept_rows": kept_rows.reshape(-1),
+    }
+
+
+def route_to_slots(value, routes, after=None):
+    batch_count = lax.axis_size("batch")
+    head_count = lax.axis_size("head")
+    local_rows, heads_here, width = value.shape
+    cluster_number = head_count // 4
+    slots_dev = local_rows // cluster_number
+    quarter = heads_here // 4
+    packed = jnp.take(
+        value.reshape(local_rows * heads_here, width), routes["sent_rows"], axis=0, mode="clip"
+    ).reshape(batch_count * head_count, -1, width)
+    if after is not None:
+        packed, after = lax.optimization_barrier((packed, after))
+    arrived = lax.all_to_all(packed, ("batch", "head"), split_axis=0, concat_axis=0, tiled=True)
     return jnp.take(
-        arrived.reshape(-1, width), kept_rows.reshape(-1), axis=0, mode="clip"
+        arrived.reshape(-1, width), routes["kept_rows"], axis=0, mode="clip"
     ).reshape(slots_dev, head_count * quarter, width)
 
 def exchange_sum(pieces, axis_name):
@@ -341,6 +357,10 @@
     hidden = jnp.tanh(
         jnp.sum(exchange_copies(partial_value.astype(bf16), "batch").astype(f32), axis=0)
     ).astype(bf16)
+    routes = slot_routes(
+        position_mapping_target, local_rows, heads_here, batch_index, head_index
+    )
+    routes, hidden = lax.optimization_barrier((routes, hidden))
     hidden = hidden.reshape(rows, MIX_MAPS, lagging_narrow_raising.shape[1])
     offsets = jnp.einsum(
         "nim,imd->ind", hidden, lagging_narrow_raising, preferred_element_type=f32
@@ -362,11 +382,8 @@
         "batch",
     )
 
-    kept_for_move, main_sum, decay_sum = lax.optimization_barrier(
-        (stream_kept_tableaux, main_sum, decay_sum)
-    )
     moved_state = route_to_slots(
-        kept_for_move.astype(bf16), position_mapping_target, batch_index, head_index
+        stream_kept_tableaux.astype(bf16), routes, after=(main_sum, decay_sum)
     )
 
     def heads_of(value):
@@ -409,15 +426,7 @@
     slots_dev = local_rows // cluster_number
     per_pair = slots_dev // batch_count
     quarter = heads_here // 4
-    own_map = lax.dynamic_slice_in_dim(
-        position_mapping_target, batch_index * local_rows, local_rows
-    )
-    dest_key = own_map // slots_dev
-    positions = jnp.arange(local_rows, dtype=jnp.int32)
-    ahead = (dest_key[None, :] < dest_key[:, None]) | (
-        (dest_key[None, :] == dest_key[:, None]) & (positions[None, :] < positions[:, None])
-    )
-    send_order = index_of(jnp.sum(ahead.astype(jnp.int32), axis=1), local_rows)
+    send_order = routes["send_order"]
     factors = jnp.take(
         payload.reshape(pieces, local_rows, heads_here, SUBSPACE_EXTENT),
         send_order,
@@ -434,7 +443,7 @@
     factors = factors.reshape(
         head_count, batch_count, pieces, per_pair, quarter, SUBSPACE_EXTENT
     )
-    inverse = index_of(position_mapping_target, sessions)
+    inverse = routes["inverse"]
     arranged = jnp.concatenate(
         [gathered[:STEPS_A], jnp.take(gathered[STEPS_A:], inverse, axis=1, mode="clip")], axis=0
     )
@@ -450,13 +459,7 @@
     factors = factors.transpose(2, 1, 3, 0, 4, 5).reshape(
         pieces, batch_count * per_pair, head_count * quarter, SUBSPACE_EXTENT
     )
-    target = batch_index * cluster_number + head_index % cluster_number
-    chosen = lax.dynamic_slice_in_dim(inverse, target * slots_dev, slots_dev)
-    every = jnp.arange(sessions, dtype=jnp.int32)
-    coming = (position_mapping_target // slots_dev) == target
-    placing = jnp.sum(
-        ((every[None, :] < chosen[:, None]) & coming[None, :]).astype(jnp.int32), axis=1
-    )
+    placing = routes["placing"]
     moved_terms = jnp.take(factors, placing, axis=1, mode="clip").reshape(
         pieces, slots_dev * head_count * quarter, SUBSPACE_EXTENT
     )

time: 131 us -> 128 us (0.977)
  waiting for transfers between devices: 30.1 us -> 24.1 us
  local copies, waits for them, and re-layouts: 24.3 us -> 28 us
    ppermute x3, waiting for transfers between devices: 4.34 us -> 1.2 us  [exchange_copies(): lax.ppermute(value, axis_name, [(i, (i + shift) % count) for i in range(c...]
    ppermute x6, waiting for transfers between devices: 21.3 us -> 18.6 us  [exchange_sum(): lax.ppermute(own(shift), axis_name, [(i, (i + shift) % count) for i in ra...]
    add x2 -> x1, other arithmetic: 2.07 us -> 0.62 us  [exchange_sum(): acc + value.astype(jnp.float32)]
    unnamed x32 -> x40, local copies, waits for them, and re-layouts: 0.71 us -> 2.07 us
  transfers between devices with their start and end apart: 22 -> 22, of which waited for: 7 -> 7; matrix products, arithmetic and copies ran while one was open for 19% -> 23% of each run, Pallas kernels for 9% -> 9%
where the time goes in v14:
time: 128 us; the launch traced here: 127 us
  starting transfers between devices  37 us (29%)
  local copies, waits for them, and re-layouts  28 us (22%)
  waiting for transfers between devices  24.1 us (19%)
  other arithmetic  16.7 us (13%)
  Pallas kernels  11.4 us (9%)
  matrix products  8.72 us (7%)
    ppermute x6, waiting for transfers between devices, exchange_sum(): lax.ppermute(own(shift), axis_name, [(i, (i + shift) % count) for i in ra...  18.6 us
    ppermute x6, starting transfers between devices, gather_with_parts(): lax.ppermute((value, sent), axis_name, [(i, (i + shift) % count) for i in...  9.28 us
    ppermute x6, starting transfers between devices, exchange_sum(): lax.ppermute(own(shift), axis_name, [(i, (i + shift) % count) for i in ra...  8.83 us
    ppermute x6, starting transfers between devices, sum_with_parts(): lax.ppermute((lax.dynamic_index_in_dim(pieces, target, keepdims=False), l...  8.76 us
    pallas_call x1, Pallas kernels, run_recurrence(): pl.pallas_call(functools.partial(recurrence_kernel, steps), grid=(rows //...  6.4 us
    ppermute x3, starting transfers between devices, exchange_copies(): lax.ppermute(value, axis_name, [(i, (i + shift) % count) for i in range(c...  6.11 us
    pallas_call x1, Pallas kernels, rebuild_state(): pl.pallas_call(functools.partial(rebuild_kernel, steps), grid=(rows // bl...  4.99 us
    dot_general x1, matrix products, per_device(): jnp.einsum('inf,ifc->inc', mixed[:4], fourfold_linear_maps, preferred_ele...  4.83 us
  transfers between devices with their start and end apart: 22, of which 7 were waited for; matrix products, arithmetic and copies ran while one was open for 23% of the time, Pallas kernels for 9%

profile of v14, /device:TPU:0, one launch (start us, length us, event | category | flops | bytes accessed | tf_op | source)
XLA Modules:
  0.0 127.1 jit_solution(14051596919637635277)
XLA Ops:
  0.6 1.1 slice_bitcast_fusion.2
  1.7 1.0 convert_bitcast_fusion
  2.8 0.9 convert_bitcast_fusion.1
  3.9 0.7 copy-done.1
  5.0 5.1 %collective-permute-start.2 = (bf16[128,320]{0,1:T(8,128)(2,1)S(1)}, bf16[128,320]{0,1:T(8,128)(2,1)S(1)}, u32[]{:S(2)}, u32[]{:S(2)}) collective-permute-start(bf16[128,320]{0,1:T(8,128)(2,1)S(1)} %convolution_convert_fusion.1), channel_id=1, source_target_pairs={{0,12},{4,0},{8,4},{12,8},{1,13},{5,1},{9,5},{13,9},{2,14},{6,2},{... | collective-permute-start | bytes 245768 | tf_op jit(solution)/shard_map/ppermute | solution.py:118
  10.1 1.0 collective-permute-start
  12.8 0.7 gather_fusion
  14.0 0.7 add.337
  14.7 1.7 %convert_element_type.149 = bf16[8,16,4096]{2,1,0:T(8,128)(2,1)S(1)} convert(f32[8,16,4096]{2,1,0:T(8,128)} %param.17) | non-fusion elementwise | flops 524288 | bytes 3145728 | tf_op jit(solution)/shard_map/convert_element_type | solution.py:386
  16.4 1.2 collective-permute-done.1
  17.6 0.6 copy-done.10
  18.3 1.0 pad_maximum_fusion
  19.3 1.3 %gather_fusion.1 = bf16[4,128,320]{1,2,0:T(8,128)(2,1)} fusion(bf16[4,128,320]{1,2,0:T(8,128)(2,1)S(1)} %pad_maximum_fusion, s32[1024]{0:T(1024)S(1)} %pad_clamp_fusion.6), kind=kCustom, calls=%fused_computation.1 | custom fusion | bytes 655376 | tf_op jit(solution)/shard_map/jit(_take)/gather | solution.py:121
  20.7 1.1 convert_reduce_fusion
  21.8 2.0 %add_convert_fusion = bf16[5,128,1024]{2,1,0:T(8,128)(2,1)S(1)} fusion(bf16[128,5,64]{0,2,1:T(8,128)(2,1)S(1)} %bitcast.163, bf16[5,64,1024]{2,1,0:T(8,128)(2,1)} %param.21, f32[5,1024]{1,0:T(8,128)S(1)} %slice.54, f32[128,1024]{1,0:T(8,128)} %copy-done.2, f32[128,1024]{1,0:T(8,128)} %bitcast.146), kind=kOutput, calls=%fused_computation.10 | convolution fusion | flops 86507520 | bytes 3117056 | tf_op jit(solution)/shard_map/nim,imd->ind/dot_general | solution.py:365
  24.0 4.8 %convolution_convert_fusion = bf16[4,128,1024]{2,1,0:T(8,128)(2,1)S(1)} fusion(bf16[5,128,1024]{2,1,0:T(8,128)(2,1)S(1)} %add_convert_fusion, bf16[4,1024,1024]{2,1,0:T(8,128)(2,1)} %param.22), kind=kOutput, calls=%fused_computation.13 | convolution fusion | flops 1074266112 | bytes 10747904 | tf_op jit(solution)/shard_map/inf,ifc->inc/dot_general | solution.py:371
  28.9 1.4 %collective-permute-start.6 = (bf16[32,128]{1,0:T(8,128)(2,1)S(1)}, bf16[32,128]{1,0:T(8,128)(2,1)S(1)}, u32[]{:S(2)}, u32[]{:S(2)}) collective-permute-start(bf16[32,128]{1,0:T(8,128)(2,1)S(1)} %get-tuple-element.50), channel_id=1, source_target_pairs={{0,4},{4,8},{8,12},{12,0},{1,5},{5,9},{9,13},{13,1},{2,6},{6,10},{... | collective-permute-start | bytes 24584 | tf_op jit(solution)/shard_map/ppermute | solution.py:106
  30.2 2.5 %collective-permute-start.8 = (bf16[32,128]{1,0:T(8,128)(2,1)S(1)}, bf16[32,128]{1,0:T(8,128)(2,1)S(1)}, u32[]{:S(2)}, u32[]{:S(2)}) collective-permute-start(bf16[32,128]{1,0:T(8,128)(2,1)S(1)} %get-tuple-element.51), channel_id=1, source_target_pairs={{0,12},{4,0},{8,4},{12,8},{1,13},{5,1},{9,5},{13,9},{2,14},{6,2},{... | collective-permute-start | bytes 24584 | tf_op jit(solution)/shard_map/ppermute | solution.py:106
  32.7 0.9 dynamic-slice_bitcast_fusion.2
  33.6 0.9 collective-permute-start.3
  34.5 2.9 %collective-permute-start.5 = (bf16[4,32,1024]{2,1,0:T(8,128)(2,1)}, bf16[4,32,1024]{2,1,0:T(8,128)(2,1)}, u32[]{:S(2)}, u32[]{:S(2)}) collective-permute-start(bf16[4,32,1024]{2,1,0:T(8,128)(2,1)} %get-tuple-element.30), channel_id=1, source_target_pairs={{0,12},{4,0},{8,4},{12,8},{1,13},{5,1},{9,5},{13,9},{2,14},{6,2},{... | collective-permute-start | bytes 786440 | tf_op jit(solution)/shard_map/ppermute | solution.py:106
  37.4 1.1 collective-permute-start.4
  38.6 2.2 %gather_fusion.2 = bf16[128,4096]{1,0:T(8,128)(2,1)} fusion(bf16[128,4096]{1,0:T(8,128)(2,1)S(1)} %bitcast.142, s32[1024]{0:T(1024)S(1)} %pad_clamp_fusion.5), kind=kCustom, calls=%fused_computation.2 | custom fusion | bytes 2097664 | tf_op jit(solution)/shard_map/jit(_take)/gather | solution.py:84
  40.8 0.6 fusion.22
  41.4 3.6 %collective-permute-done.3 = bf16[4,32,1024]{2,1,0:T(8,128)(2,1)} collective-permute-done((bf16[4,32,1024]{2,1,0:T(8,128)(2,1)}, bf16[4,32,1024]{2,1,0:T(8,128)(2,1)}, u32[]{:S(2)}, u32[]{:S(2)}) %collective-permute-start.3) | collective-permute-done | bytes 262176 | tf_op jit(solution)/shard_map/ppermute | solution.py:106
  45.0 3.2 %collective-permute-done.5 = bf16[4,32,1024]{2,1,0:T(8,128)(2,1)} collective-permute-done((bf16[4,32,1024]{2,1,0:T(8,128)(2,1)}, bf16[4,32,1024]{2,1,0:T(8,128)(2,1)}, u32[]{:S(2)}, u32[]{:S(2)}) %collective-permute-start.5) | collective-permute-done | bytes 262176 | tf_op jit(solution)/shard_map/ppermute | solution.py:106
  48.2 11.8 %collective-permute-done.4 = bf16[4,32,1024]{2,1,0:T(8,128)(2,1)} collective-permute-done((bf16[4,32,1024]{2,1,0:T(8,128)(2,1)S(1)}, bf16[4,32,1024]{2,1,0:T(8,128)(2,1)}, u32[]{:S(2)}, u32[]{:S(2)}) %collective-permute-start.4) | collective-permute-done | bytes 262176 | tf_op jit(solution)/shard_map/ppermute | solution.py:106
  59.9 2.3 %fusion.37 = (bf16[4,32,1024]{2,1,0:T(8,128)(2,1)}, f32[4,32,1024]{2,1,0:T(8,128)}) fusion(bf16[4,32,1024]{2,1,0:T(8,128)(2,1)} %collective-permute-done.5, bf16[4,32,1024]{2,1,0:T(8,128)(2,1)} %collective-permute-done.4, bf16[4,32,1024]{2,1,0:T(8,128)(2,1)} %collective-permute-done.3, bf16[4,4,32,1024]{3,2,1,0:T(8,128)(2,1)} %bitcast.157, s32[]{:T(128)S(6)} %select_n.206), kind=kLoop, calls=%fused_computation.138 | loop fusion | flops 1048576 | bytes 1835012 | tf_op jit(solution)/shard_map/convert.13
  62.2 4.1 %all-to-all-start = ((bf16[16,8,4096]{2,1,0:T(8,128)(2,1)}), bf16[16,8,4096]{2,1,0:T(8,128)(2,1)S(1)}, u32[]{:S(2)}, u32[]{:S(2)}) async-start(bf16[16,8,4096]{2,1,0:T(8,128)(2,1)} %bitcast.147), calls=%async_computation | async-start | bytes 2097152 | tf_op jit(solution)/shard_map/all_to_all | solution.py:89
  66.5 0.8 stack.72
  67.9 0.6 maximum_bitcast_fusion
  68.5 0.6 pad_clamp_fusion.4
  69.1 0.6 pad_clamp_fusion.3
  70.3 0.9 fusion.10
  71.2 0.8 reshape_reshape.2.decay_ref
  72.0 0.9 slice.91
  73.0 1.6 %slice_convert_fusion = (f32[1,32,1024]{2,1,0:T(8,128)}, f32[1,32,1024]{2,1,0:T(8,128)}, f32[1,32,1024]{2,1,0:T(8,128)S(1)}) fusion(bf16[4,32,1024]{2,1,0:T(8,128)(2,1)} %get-tuple-element.27), kind=kLoop, calls=%fused_computation.61 | loop fusion | flops 98304 | bytes 589824 | tf_op jit(solution)/shard_map/convert_element_type | solution.py:164
  74.7 1.7 %reshape.467.value_ref = f32[4,128,64]{2,1,0:T(8,128)} reshape(f32[1,32,1024]{2,1,0:T(8,128)} %get-tuple-element.45) | data formatting | bytes 262144 | tf_op jit(solution)/shard_map/convert_element_type | solution.py:164
  76.4 1.7 %reshape.466.key_ref = f32[4,128,64]{2,1,0:T(8,128)} reshape(f32[1,32,1024]{2,1,0:T(8,128)} %get-tuple-element.46) | data formatting | bytes 262144 | tf_op jit(solution)/shard_map/convert_element_type | solution.py:164
  78.1 0.8 reshape.465.recept_ref
  78.9 0.8 divide_multiply_fusion.gate_ref
  79.7 1.4 %broadcast_in_dim.56 = f32[3,8,16,64]{3,2,1,0:T(8,128)} broadcast(f32[3,16,64]{2,1,0:T(8,128)} %maximum_bitcast_fusion), dimensions={0,2,3} | broadcast | bytes 110592 | tf_op jit(solution)/shard_map/broadcast_in_dim | solution.py:412
  81.1 6.4 %shard_map.166 = (bf16[4,128,64]{2,1,0:T(8,128)(2,1)}, bf16[9,128,64]{2,1,0:T(8,128)(2,1)}) custom-call(f32[4,128,64]{2,1,0:T(8,128)} %reshape.465.recept_ref, f32[4,128,64]{2,1,0:T(8,128)} %reshape.466.key_ref, f32[4,128,64]{2,1,0:T(8,128)} %reshape.467.value_ref, f32[4,128,64]{2,1,0:T(8,128)} %reshape_reshape.2.decay_ref, ...), custom_call_target="tpu_custom_call" | custom-call | flops 805306368 | bytes 3063808 | tf_op jit(solution)/shard_map/pallas_call | solution.py:252
  87.5 1.7 %all-to-all-done = bf16[16,8,4096]{2,1,0:T(8,128)(2,1)S(1)} async-done(((bf16[16,8,4096]{2,1,0:T(8,128)(2,1)}), bf16[16,8,4096]{2,1,0:T(8,128)(2,1)S(1)}, u32[]{:S(2)}, u32[]{:S(2)}) %all-to-all-start) | async-done | bytes 1048608 | tf_op jit(solution)/shard_map/all_to_all | solution.py:89
  89.3 2.2 %gather_fusion.3 = bf16[128,4096]{1,0:T(8,128)(2,1)} fusion(bf16[128,4096]{1,0:T(8,128)(2,1)S(1)} %bitcast.143, s32[1024]{0:T(1024)S(1)} %pad_clamp_fusion.4), kind=kCustom, calls=%fused_computation.3 | custom fusion | bytes 2097664 | tf_op jit(solution)/shard_map/jit(_take)/gather | solution.py:90
  91.4 1.7 %gather_fusion.6 = bf16[8,9,16,64]{3,2,1,0:T(8,128)(2,1)S(1)} fusion(bf16[9,8,16,64]{3,2,1,0:T(8,128)(2,1)} %bitcast.165, s32[1024]{0:T(1024)} %pad_clamp_fusion.2), kind=kCustom, calls=%fused_computation.6 | custom fusion | bytes 294944 | tf_op jit(solution)/shard_map/jit(_take)/gather | solution.py:430
  93.2 3.2 %collective-permute-start.17 = (bf16[9,2,16,64]{3,2,1,0:T(8,128)(2,1)S(1)}, bf16[9,2,16,64]{3,2,1,0:T(8,128)(2,1)S(1)}, u32[]{:S(2)}, u32[]{:S(2)}) collective-permute-start(bf16[9,2,16,64]{3,2,1,0:T(8,128)(2,1)S(1)} %bitcast.178), channel_id=1, source_target_pairs={{0,12},{4,0},{8,4},{12,8},{1,13},{5,1},{9,5},{13,9},{2,14},{6,2},{... | collective-permute-start | bytes 110600 | tf_op jit(solution)/shard_map/ppermute | solution.py:135
  96.5 3.8 %collective-permute-start.16 = (bf16[9,2,16,64]{3,2,1,0:T(8,128)(2,1)S(1)}, bf16[9,2,16,64]{3,2,1,0:T(8,128)(2,1)S(1)}, u32[]{:S(2)}, u32[]{:S(2)}) collective-permute-start(bf16[9,2,16,64]{3,2,1,0:T(8,128)(2,1)S(1)} %bitcast.176), channel_id=1, source_target_pairs={{0,8},{4,12},{8,0},{12,4},{1,9},{5,13},{9,1},{13,5},{2,10},{6,14},... | collective-permute-start | bytes 110600 | tf_op jit(solution)/shard_map/ppermute | solution.py:135
  100.7 1.0 collective-permute-start.11
  101.7 1.0 collective-permute-start.10
  102.8 1.8 %collective-permute-done.15 = bf16[9,2,16,64]{3,2,1,0:T(8,128)(2,1)S(1)} collective-permute-done((bf16[9,2,16,64]{3,2,1,0:T(8,128)(2,1)S(1)}, bf16[9,2,16,64]{3,2,1,0:T(8,128)(2,1)S(1)}, u32[]{:S(2)}, u32[]{:S(2)}) %collective-permute-start.15) | collective-permute-done | bytes 36896 | tf_op jit(solution)/shard_map/ppermute | solution.py:135
  104.6 0.8 collective-permute-done.16
  105.5 0.6 gather_fusion.7
  106.3 5.1 %collective-permute-start.19 = (bf16[4,9,2,4,64]{4,3,2,1,0:T(4,128)(2,1)S(1)}, bf16[4,9,2,4,64]{4,3,2,1,0:T(4,128)(2,1)S(1)}, u32[]{:S(2)}, u32[]{:S(2)}) collective-permute-start(bf16[4,9,2,4,64]{4,3,2,1,0:T(4,128)(2,1)S(1)} %get-tuple-element.34), channel_id=1, source_target_pairs={{0,2},{1,3},{2,0},{3,1},{4,6},{5,7},{6,4},{7,5},{8,10},{9,11},{10,... | collective-permute-start | bytes 110600 | tf_op jit(solution)/shard_map/ppermute | solution.py:150
  112.4 0.8 gather_fusion.5
  113.8 0.7 dynamic-slice_bitcast_fusion.9
  114.5 1.7 %collective-permute-start.14 = (bf16[4,8,1024]{2,1,0:T(8,128)(2,1)}, bf16[4,8,1024]{2,1,0:T(8,128)(2,1)}, u32[]{:S(2)}, u32[]{:S(2)}) collective-permute-start(bf16[4,8,1024]{2,1,0:T(8,128)(2,1)} %get-tuple-element.41), channel_id=1, source_target_pairs={{0,3},{1,0},{2,1},{3,2},{4,7},{5,4},{6,5},{7,6},{8,11},{9,8},{10,9... | collective-permute-start | bytes 196616 | tf_op jit(solution)/shard_map/ppermute | solution.py:150
  116.2 1.7 %collective-permute-start.13 = (bf16[4,8,1024]{2,1,0:T(8,128)(2,1)}, bf16[4,8,1024]{2,1,0:T(8,128)(2,1)S(1)}, u32[]{:S(2)}, u32[]{:S(2)}) collective-permute-start(bf16[4,8,1024]{2,1,0:T(8,128)(2,1)} %get-tuple-element.42), channel_id=1, source_target_pairs={{0,2},{1,3},{2,0},{3,1},{4,6},{5,7},{6,4},{7,5},{8,10},{9,11},{10,... | collective-permute-start | bytes 196616 | tf_op jit(solution)/shard_map/ppermute | solution.py:150
  118.2 0.9 gather_fusion.8
  119.2 0.6 gather_fusion.9
  119.9 0.7 copy.79
  120.6 5.0 %shard_map.167 = f32[128,4096]{1,0:T(8,128)} custom-call(bf16[128,4096]{1,0:T(8,128)(2,1)} %gather_fusion.3, bf16[9,128,64]{2,1,0:T(8,128)(2,1)} %bitcast.154), custom_call_target="tpu_custom_call" | custom-call | flops 603979776 | bytes 3293184 | tf_op jit(solution)/shard_map/pallas_call | solution.py:296
  125.6 0.9 fusion.20
  126.5 0.6 fusion.40
  (113 shorter events, 7.1 us)
Async XLA Ops:
  0.6 112.7 %copy-start = (bf16[1024,1024]{1,0:T(8,128)(2,1)S(1)}, bf16[1024,1024]{1,0:T(8,128)(2,1)}, u32[]{:S(2)}) copy-start(bf16[1024,1024]{1,0:T(8,128)(2,1)} %param.29) | copy-start | bytes 6291460
  2.7 1.9 %copy-start.4 = (bf16[1024,320]{0,1:T(8,128)(2,1)S(1)}, bf16[1024,320]{0,1:T(8,128)(2,1)}, u32[]{:S(2)}) copy-start(bf16[1024,320]{0,1:T(8,128)(2,1)} %param.20) | copy-start | bytes 1966084
  2.8 1.9 %slice-start = ((f32[6,1024]{1,0:T(8,128)}), f32[1,1024]{1,0:T(1,128)S(1)}, s32[]{:S(2)}) async-start(f32[6,1024]{1,0:T(8,128)} %param.19), calls=%async_computation.1 | async-start | bytes 8192 | tf_op jit(solution)/shard_map/slice | solution.py:355
  3.8 7.4 %copy-start.17 = (s32[32]{0:T(128)S(1)}, s32[32]{0:T(128)}, u32[]{:S(2)}) copy-start(s32[32]{0:T(128)} %param.18) | copy-start | bytes 388
  3.8 7.5 %copy-start.11 = (f32[6,1024]{1,0:T(8,128)S(1)}, f32[6,1024]{1,0:T(8,128)}, u32[]{:S(2)}) copy-start(f32[6,1024]{1,0:T(8,128)} %param.19) | copy-start | bytes 73732
  3.8 0.8 copy-start.1
  3.9 1.1 copy-start.2
  5.0 8.5 %copy-start.6 = (bf16[128,320]{0,1:T(8,128)(2,1)}, bf16[128,320]{0,1:T(8,128)(2,1)S(1)}, u32[]{:S(2)}) copy-start(bf16[128,320]{0,1:T(8,128)(2,1)S(1)} %convolution_convert_fusion.1) | copy-start | bytes 245764
  5.0 11.4 %collective-permute-start.2 = (bf16[128,320]{0,1:T(8,128)(2,1)S(1)}, bf16[128,320]{0,1:T(8,128)(2,1)S(1)}, u32[]{:S(2)}, u32[]{:S(2)}) collective-permute-start(bf16[128,320]{0,1:T(8,128)(2,1)S(1)} %convolution_convert_fusion.1), channel_id=1, source_target_pairs={{0,12},{4,0},{8,4},{12,8},{1,13},{5,1},{9,5},{13,9},{2,14},{6,2},{... | collective-permute-start | bytes 245768 | tf_op jit(solution)/shard_map/ppermute | solution.py:118
  10.1 7.5 %collective-permute-start.1 = (bf16[128,320]{0,1:T(8,128)(2,1)S(1)}, bf16[128,320]{0,1:T(8,128)(2,1)S(1)}, u32[]{:S(2)}, u32[]{:S(2)}) collective-permute-start(bf16[128,320]{0,1:T(8,128)(2,1)S(1)} %convolution_convert_fusion.1), channel_id=1, source_target_pairs={{0,8},{4,12},{8,0},{12,4},{1,9},{5,13},{9,1},{13,5},{2,10},{6,14},... | collective-permute-start | bytes 245768 | tf_op jit(solution)/shard_map/ppermute | solution.py:118
  10.1 7.5 %collective-permute-start = (bf16[128,320]{0,1:T(8,128)(2,1)S(1)}, bf16[128,320]{0,1:T(8,128)(2,1)}, u32[]{:S(2)}, u32[]{:S(2)}) collective-permute-start(bf16[128,320]{0,1:T(8,128)(2,1)S(1)} %convolution_convert_fusion.1), channel_id=1, source_target_pairs={{0,4},{4,8},{8,12},{12,0},{1,5},{5,9},{9,13},{13,1},{2,6},{6,10},{... | collective-permute-start | bytes 245768 | tf_op jit(solution)/shard_map/ppermute | solution.py:118
  11.2 0.5 copy-start.16
  12.0 0.6 copy-start.14
  16.4 1.2 copy-start.9
  17.6 0.6 copy-start.10
  20.7 3.1 %copy-start.7 = (bf16[1024,128]{1,0:T(8,128)(2,1)S(1)}, bf16[1024,128]{1,0:T(8,128)(2,1)}, u32[]{:S(2)}) copy-start(bf16[1024,128]{1,0:T(8,128)(2,1)} %param.23) | copy-start | bytes 786436
  28.8 3.9 %copy-start.3 = (bf16[4,128,1024]{2,1,0:T(8,128)(2,1)}, bf16[4,128,1024]{2,1,0:T(8,128)(2,1)S(1)}, u32[]{:S(2)}) copy-start(bf16[4,128,1024]{2,1,0:T(8,128)(2,1)S(1)} %convolution_convert_fusion) | copy-start | bytes 3145732
  28.9 8.6 %collective-permute-start.6 = (bf16[32,128]{1,0:T(8,128)(2,1)S(1)}, bf16[32,128]{1,0:T(8,128)(2,1)S(1)}, u32[]{:S(2)}, u32[]{:S(2)}) collective-permute-start(bf16[32,128]{1,0:T(8,128)(2,1)S(1)} %get-tuple-element.50), channel_id=1, source_target_pairs={{0,4},{4,8},{8,12},{12,0},{1,5},{5,9},{9,13},{13,1},{2,6},{6,10},{... | collective-permute-start | bytes 24584 | tf_op jit(solution)/shard_map/ppermute | solution.py:106
  30.2 10.5 %collective-permute-start.8 = (bf16[32,128]{1,0:T(8,128)(2,1)S(1)}, bf16[32,128]{1,0:T(8,128)(2,1)S(1)}, u32[]{:S(2)}, u32[]{:S(2)}) collective-permute-start(bf16[32,128]{1,0:T(8,128)(2,1)S(1)} %get-tuple-element.51), channel_id=1, source_target_pairs={{0,12},{4,0},{8,4},{12,8},{1,13},{5,1},{9,5},{13,9},{2,14},{6,2},{... | collective-permute-start | bytes 24584 | tf_op jit(solution)/shard_map/ppermute | solution.py:106
  32.7 8.0 %collective-permute-start.7 = (bf16[32,128]{1,0:T(8,128)(2,1)S(1)}, bf16[32,128]{1,0:T(8,128)(2,1)S(1)}, u32[]{:S(2)}, u32[]{:S(2)}) collective-permute-start(bf16[32,128]{1,0:T(8,128)(2,1)S(1)} %get-tuple-element.52), channel_id=1, source_target_pairs={{0,8},{4,12},{8,0},{12,4},{1,9},{5,13},{9,1},{13,5},{2,10},{6,14},... | collective-permute-start | bytes 24584 | tf_op jit(solution)/shard_map/ppermute | solution.py:106
  33.6 11.4 %collective-permute-start.3 = (bf16[4,32,1024]{2,1,0:T(8,128)(2,1)}, bf16[4,32,1024]{2,1,0:T(8,128)(2,1)}, u32[]{:S(2)}, u32[]{:S(2)}) collective-permute-start(bf16[4,32,1024]{2,1,0:T(8,128)(2,1)} %get-tuple-element.29), channel_id=1, source_target_pairs={{0,4},{4,8},{8,12},{12,0},{1,5},{5,9},{9,13},{13,1},{2,6},{6,10},{... | collective-permute-start | bytes 786440 | tf_op jit(solution)/shard_map/ppermute | solution.py:106
  34.5 13.7 %collective-permute-start.5 = (bf16[4,32,1024]{2,1,0:T(8,128)(2,1)}, bf16[4,32,1024]{2,1,0:T(8,128)(2,1)}, u32[]{:S(2)}, u32[]{:S(2)}) collective-permute-start(bf16[4,32,1024]{2,1,0:T(8,128)(2,1)} %get-tuple-element.30), channel_id=1, source_target_pairs={{0,12},{4,0},{8,4},{12,8},{1,13},{5,1},{9,5},{13,9},{2,14},{6,2},{... | collective-permute-start | bytes 786440 | tf_op jit(solution)/shard_map/ppermute | solution.py:106
  37.4 22.5 %collective-permute-start.4 = (bf16[4,32,1024]{2,1,0:T(8,128)(2,1)S(1)}, bf16[4,32,1024]{2,1,0:T(8,128)(2,1)}, u32[]{:S(2)}, u32[]{:S(2)}) collective-permute-start(bf16[4,32,1024]{2,1,0:T(8,128)(2,1)S(1)} %get-tuple-element.31), channel_id=1, source_target_pairs={{0,8},{4,12},{8,0},{12,4},{1,9},{5,13},{9,1},{13,5},{2,10},{6,14},... | collective-permute-start | bytes 786440 | tf_op jit(solution)/shard_map/ppermute | solution.py:106
  40.7 25.6 %copy-start.12 = (f32[1024]{0:T(1024)S(1)}, f32[1024]{0:T(1024)}, u32[]{:S(2)}) copy-start(f32[1024]{0:T(1024)} %param.26) | copy-start | bytes 12292
  40.7 25.7 %copy-start.13 = (f32[1024]{0:T(1024)S(1)}, f32[1024]{0:T(1024)}, u32[]{:S(2)}) copy-start(f32[1024]{0:T(1024)} %param.27) | copy-start | bytes 12292
  59.9 10.4 %copy-start.8 = (bf16[128,1024]{1,0:T(8,128)(2,1)S(1)}, bf16[128,1024]{1,0:T(8,128)(2,1)}, u32[]{:S(2)}) copy-start(bf16[128,1024]{1,0:T(8,128)(2,1)} %param.24) | copy-start | bytes 786436
  62.2 27.0 %all-to-all-start = ((bf16[16,8,4096]{2,1,0:T(8,128)(2,1)}), bf16[16,8,4096]{2,1,0:T(8,128)(2,1)S(1)}, u32[]{:S(2)}, u32[]{:S(2)}) async-start(bf16[16,8,4096]{2,1,0:T(8,128)(2,1)} %bitcast.147), calls=%async_computation | async-start | bytes 2097152 | tf_op jit(solution)/shard_map/all_to_all | solution.py:89
  89.3 11.1 %copy-start.15 = (s32[8]{0:T(128)S(1)}, s32[8]{0:T(128)}, u32[]{:S(2)}) copy-start(s32[8]{0:T(128)} %copy-done.14) | copy-start | bytes 100
  89.3 11.1 %copy-start.5 = (bf16[4,128,64]{2,1,0:T(8,128)(2,1)S(1)}, bf16[4,128,64]{2,1,0:T(8,128)(2,1)}, u32[]{:S(2)}) copy-start(bf16[4,128,64]{2,1,0:T(8,128)(2,1)} %get-tuple-element.21) | copy-start | bytes 196612
  93.2 9.5 %collective-permute-start.17 = (bf16[9,2,16,64]{3,2,1,0:T(8,128)(2,1)S(1)}, bf16[9,2,16,64]{3,2,1,0:T(8,128)(2,1)S(1)}, u32[]{:S(2)}, u32[]{:S(2)}) collective-permute-start(bf16[9,2,16,64]{3,2,1,0:T(8,128)(2,1)S(1)} %bitcast.178), channel_id=1, source_target_pairs={{0,12},{4,0},{8,4},{12,8},{1,13},{5,1},{9,5},{13,9},{2,14},{6,2},{... | collective-permute-start | bytes 110600 | tf_op jit(solution)/shard_map/ppermute | solution.py:135
  96.5 8.1 %collective-permute-start.15 = (bf16[9,2,16,64]{3,2,1,0:T(8,128)(2,1)S(1)}, bf16[9,2,16,64]{3,2,1,0:T(8,128)(2,1)S(1)}, u32[]{:S(2)}, u32[]{:S(2)}) collective-permute-start(bf16[9,2,16,64]{3,2,1,0:T(8,128)(2,1)S(1)} %bitcast.177), channel_id=1, source_target_pairs={{0,4},{4,8},{8,12},{12,0},{1,5},{5,9},{9,13},{13,1},{2,6},{6,10},{... | collective-permute-start | bytes 110600 | tf_op jit(solution)/shard_map/ppermute | solution.py:135
  96.5 8.9 %collective-permute-start.16 = (bf16[9,2,16,64]{3,2,1,0:T(8,128)(2,1)S(1)}, bf16[9,2,16,64]{3,2,1,0:T(8,128)(2,1)S(1)}, u32[]{:S(2)}, u32[]{:S(2)}) collective-permute-start(bf16[9,2,16,64]{3,2,1,0:T(8,128)(2,1)S(1)} %bitcast.176), channel_id=1, source_target_pairs={{0,8},{4,12},{8,0},{12,4},{1,9},{5,13},{9,1},{13,5},{2,10},{6,14},... | collective-permute-start | bytes 110600 | tf_op jit(solution)/shard_map/ppermute | solution.py:135
  100.7 10.8 %collective-permute-start.11 = (bf16[4,8,1024]{2,1,0:T(8,128)(2,1)S(1)}, bf16[4,8,1024]{2,1,0:T(8,128)(2,1)S(1)}, u32[]{:S(2)}, u32[]{:S(2)}) collective-permute-start(bf16[4,8,1024]{2,1,0:T(8,128)(2,1)S(1)} %reshape.452), channel_id=1, source_target_pairs={{0,12},{4,0},{8,4},{12,8},{1,13},{5,1},{9,5},{13,9},{2,14},{6,2},{... | collective-permute-start | bytes 196616 | tf_op jit(solution)/shard_map/ppermute | solution.py:135
  101.7 9.9 %collective-permute-start.10 = (bf16[4,8,1024]{2,1,0:T(8,128)(2,1)S(1)}, bf16[4,8,1024]{2,1,0:T(8,128)(2,1)S(1)}, u32[]{:S(2)}, u32[]{:S(2)}) collective-permute-start(bf16[4,8,1024]{2,1,0:T(8,128)(2,1)S(1)} %reshape.452), channel_id=1, source_target_pairs={{0,8},{4,12},{8,0},{12,4},{1,9},{5,13},{9,1},{13,5},{2,10},{6,14},... | collective-permute-start | bytes 196616 | tf_op jit(solution)/shard_map/ppermute | solution.py:135
  102.7 8.9 %collective-permute-start.9 = (bf16[4,8,1024]{2,1,0:T(8,128)(2,1)S(1)}, bf16[4,8,1024]{2,1,0:T(8,128)(2,1)S(1)}, u32[]{:S(2)}, u32[]{:S(2)}) collective-permute-start(bf16[4,8,1024]{2,1,0:T(8,128)(2,1)S(1)} %reshape.452), channel_id=1, source_target_pairs={{0,4},{4,8},{8,12},{12,0},{1,5},{5,9},{9,13},{13,1},{2,6},{6,10},{... | collective-permute-start | bytes 196616 | tf_op jit(solution)/shard_map/ppermute | solution.py:135
  106.3 9.9 %collective-permute-start.20 = (bf16[4,9,2,4,64]{4,3,2,1,0:T(4,128)(2,1)S(1)}, bf16[4,9,2,4,64]{4,3,2,1,0:T(4,128)(2,1)S(1)}, u32[]{:S(2)}, u32[]{:S(2)}) collective-permute-start(bf16[4,9,2,4,64]{4,3,2,1,0:T(4,128)(2,1)S(1)} %get-tuple-element.33), channel_id=1, source_target_pairs={{0,3},{1,0},{2,1},{3,2},{4,7},{5,4},{6,5},{7,6},{8,11},{9,8},{10,9... | collective-permute-start | bytes 110600 | tf_op jit(solution)/shard_map/ppermute | solution.py:150
  106.3 11.6 %collective-permute-start.19 = (bf16[4,9,2,4,64]{4,3,2,1,0:T(4,128)(2,1)S(1)}, bf16[4,9,2,4,64]{4,3,2,1,0:T(4,128)(2,1)S(1)}, u32[]{:S(2)}, u32[]{:S(2)}) collective-permute-start(bf16[4,9,2,4,64]{4,3,2,1,0:T(4,128)(2,1)S(1)} %get-tuple-element.34), channel_id=1, source_target_pairs={{0,2},{1,3},{2,0},{3,1},{4,6},{5,7},{6,4},{7,5},{8,10},{9,11},{10,... | collective-permute-start | bytes 110600 | tf_op jit(solution)/shard_map/ppermute | solution.py:150
  111.4 6.5 %collective-permute-start.18 = (bf16[4,9,2,4,64]{4,3,2,1,0:T(4,128)(2,1)S(1)}, bf16[4,9,2,4,64]{4,3,2,1,0:T(4,128)(2,1)S(1)}, u32[]{:S(2)}, u32[]{:S(2)}) collective-permute-start(bf16[4,9,2,4,64]{4,3,2,1,0:T(4,128)(2,1)S(1)} %get-tuple-element.35), channel_id=1, source_target_pairs={{0,1},{1,2},{2,3},{3,0},{4,5},{5,6},{6,7},{7,4},{8,9},{9,10},{10,1... | collective-permute-start | bytes 110600 | tf_op jit(solution)/shard_map/ppermute | solution.py:150
  114.5 11.2 %collective-permute-start.12 = (bf16[4,8,1024]{2,1,0:T(8,128)(2,1)}, bf16[4,8,1024]{2,1,0:T(8,128)(2,1)S(1)}, u32[]{:S(2)}, u32[]{:S(2)}) collective-permute-start(bf16[4,8,1024]{2,1,0:T(8,128)(2,1)} %get-tuple-element.40), channel_id=1, source_target_pairs={{0,1},{1,2},{2,3},{3,0},{4,5},{5,6},{6,7},{7,4},{8,9},{9,10},{10,1... | collective-permute-start | bytes 196616 | tf_op jit(solution)/shard_map/ppermute | solution.py:150
  114.5 11.1 %collective-permute-start.14 = (bf16[4,8,1024]{2,1,0:T(8,128)(2,1)}, bf16[4,8,1024]{2,1,0:T(8,128)(2,1)}, u32[]{:S(2)}, u32[]{:S(2)}) collective-permute-start(bf16[4,8,1024]{2,1,0:T(8,128)(2,1)} %get-tuple-element.41), channel_id=1, source_target_pairs={{0,3},{1,0},{2,1},{3,2},{4,7},{5,4},{6,5},{7,6},{8,11},{9,8},{10,9... | collective-permute-start | bytes 196616 | tf_op jit(solution)/shard_map/ppermute | solution.py:150
  116.2 9.4 %collective-permute-start.13 = (bf16[4,8,1024]{2,1,0:T(8,128)(2,1)}, bf16[4,8,1024]{2,1,0:T(8,128)(2,1)S(1)}, u32[]{:S(2)}, u32[]{:S(2)}) collective-permute-start(bf16[4,8,1024]{2,1,0:T(8,128)(2,1)} %get-tuple-element.42), channel_id=1, source_target_pairs={{0,2},{1,3},{2,0},{3,1},{4,6},{5,7},{6,4},{7,5},{8,10},{9,11},{10,... | collective-permute-start | bytes 196616 | tf_op jit(solution)/shard_map/ppermute | solution.py:150

commit v15 on v13

--- a/solution.py
+++ b/solution.py
@@ -227,7 +227,7 @@
 
 
 def row_block(rows):
-    return 64 if rows % 64 == 0 else rows
+    return 128 if rows % 128 == 0 else rows
 
 
 def run_recurrence(projected, params, state):

time: 128 us -> 128 us (level)
  no operation moved by 1% of the time
where the time goes in v15:
time: 128 us; the launch traced here: 127 us
  starting transfers between devices  33.7 us (26%)
  local copies, waits for them, and re-layouts  28.4 us (22%)
  waiting for transfers between devices  25.6 us (20%)
  other arithmetic  18.1 us (14%)
  Pallas kernels  11.7 us (9%)
  matrix products  8.39 us (7%)
    ppermute x6, waiting for transfers between devices, exchange_sum(): lax.ppermute(own(shift), axis_name, [(i, (i + shift) % count) for i in ra...  17.5 us
    ppermute x6, starting transfers between devices, gather_with_parts(): lax.ppermute((value, sent), axis_name, [(i, (i + shift) % count) for i in...  9.74 us
    ppermute x6, starting transfers between devices, exchange_sum(): lax.ppermute(own(shift), axis_name, [(i, (i + shift) % count) for i in ra...  8.82 us
    pallas_call x1, Pallas kernels, run_recurrence(): pl.pallas_call(functools.partial(recurrence_kernel, steps), grid=(rows //...  6.38 us
    ppermute x3, starting transfers between devices, exchange_copies(): lax.ppermute(value, axis_name, [(i, (i + shift) % count) for i in range(c...  6.12 us
    pallas_call x1, Pallas kernels, rebuild_state(): pl.pallas_call(functools.partial(rebuild_kernel, steps), grid=(rows // bl...  5.27 us
    ppermute x6, starting transfers between devices, sum_with_parts(): lax.ppermute((lax.dynamic_index_in_dim(pieces, target, keepdims=False), l...  4.96 us
    dot_general x1, matrix products, per_device(): jnp.einsum('inf,ifc->inc', mixed[:4], fourfold_linear_maps, preferred_ele...  4.83 us
  transfers between devices with their start and end apart: 22, of which 7 were waited for; matrix products, arithmetic and copies ran while one was open for 26% of the time, Pallas kernels for 9%

profile of v15, /device:TPU:0, one launch (start us, length us, event | category | flops | bytes accessed | tf_op | source)
XLA Modules:
  0.0 127.2 jit_solution(5522730653288425888)
XLA Ops:
  0.6 1.1 slice_bitcast_fusion.2
  1.7 1.0 convert_bitcast_fusion
  2.8 0.9 convert_bitcast_fusion.1
  4.3 5.1 %collective-permute-start.2 = (bf16[128,320]{0,1:T(8,128)(2,1)S(1)}, bf16[128,320]{0,1:T(8,128)(2,1)S(1)}, u32[]{:S(2)}, u32[]{:S(2)}) collective-permute-start(bf16[128,320]{0,1:T(8,128)(2,1)S(1)} %convolution_convert_fusion.1), channel_id=1, source_target_pairs={{0,12},{4,0},{8,4},{12,8},{1,13},{5,1},{9,5},{13,9},{2,14},{6,2},{... | collective-permute-start | bytes 245768 | tf_op jit(solution)/shard_map/ppermute | solution.py:104
  9.4 1.0 collective-permute-start
  11.3 0.6 fusion.35
  12.4 0.7 gather_fusion
  13.5 3.4 %collective-permute-done.1 = bf16[128,320]{0,1:T(8,128)(2,1)S(1)} collective-permute-done((bf16[128,320]{0,1:T(8,128)(2,1)S(1)}, bf16[128,320]{0,1:T(8,128)(2,1)S(1)}, u32[]{:S(2)}, u32[]{:S(2)}) %collective-permute-start.1) | collective-permute-done | bytes 81952 | tf_op jit(solution)/shard_map/ppermute | solution.py:104
  16.9 0.6 copy-done.8
  17.5 1.0 pad_maximum_fusion
  18.6 1.3 %gather_fusion.2 = bf16[4,128,320]{1,2,0:T(8,128)(2,1)} fusion(bf16[4,128,320]{1,2,0:T(8,128)(2,1)S(1)} %pad_maximum_fusion, s32[1024]{0:T(1024)S(1)} %pad_clamp_fusion.5), kind=kCustom, calls=%fused_computation.2 | custom fusion | bytes 655376 | tf_op jit(solution)/shard_map/jit(_take)/gather | solution.py:107
  19.9 1.1 convert_reduce_fusion
  21.0 1.7 %add_convert_fusion = bf16[5,128,1024]{2,1,0:T(8,128)(2,1)S(1)} fusion(bf16[128,5,64]{0,2,1:T(8,128)(2,1)S(1)} %bitcast.163, bf16[5,64,1024]{2,1,0:T(8,128)(2,1)} %param.21, f32[5,1024]{1,0:T(8,128)S(1)} %slice.53, f32[128,1024]{1,0:T(8,128)S(1)} %bitcast_subtract_fusion, f32[128,1024]{1,0:T(8,128)S(1)} %bitcast.146), kind=kOutput, calls=%fused_computation.10 | convolution fusion | flops 86507520 | bytes 3117056 | tf_op jit(solution)/shard_map/nim,imd->ind/dot_general | solution.py:347
  22.9 4.8 %convolution_convert_fusion = bf16[4,128,1024]{2,1,0:T(8,128)(2,1)S(1)} fusion(bf16[5,128,1024]{2,1,0:T(8,128)(2,1)S(1)} %add_convert_fusion, bf16[4,1024,1024]{2,1,0:T(8,128)(2,1)} %param.22), kind=kOutput, calls=%fused_computation.13 | convolution fusion | flops 1074266112 | bytes 10747904 | tf_op jit(solution)/shard_map/inf,ifc->inc/dot_general | solution.py:353
  27.9 3.8 %collective-permute-start.8 = (bf16[32,128]{1,0:T(8,128)(2,1)S(1)}, bf16[32,128]{1,0:T(8,128)(2,1)S(1)}, u32[]{:S(2)}, u32[]{:S(2)}) collective-permute-start(bf16[32,128]{1,0:T(8,128)(2,1)S(1)} %get-tuple-element.39), channel_id=1, source_target_pairs={{0,12},{4,0},{8,4},{12,8},{1,13},{5,1},{9,5},{13,9},{2,14},{6,2},{... | collective-permute-start | bytes 24584 | tf_op jit(solution)/shard_map/ppermute | solution.py:92
  31.7 0.9 dynamic-slice_bitcast_fusion.2
  32.5 0.9 collective-permute-start.3
  33.4 2.9 %collective-permute-start.5 = (bf16[4,32,1024]{2,1,0:T(8,128)(2,1)}, bf16[4,32,1024]{2,1,0:T(8,128)(2,1)}, u32[]{:S(2)}, u32[]{:S(2)}) collective-permute-start(bf16[4,32,1024]{2,1,0:T(8,128)(2,1)} %get-tuple-element.18), channel_id=1, source_target_pairs={{0,12},{4,0},{8,4},{12,8},{1,13},{5,1},{9,5},{13,9},{2,14},{6,2},{... | collective-permute-start | bytes 786440 | tf_op jit(solution)/shard_map/ppermute | solution.py:92
  36.4 1.1 collective-permute-start.4
  37.5 1.7 %convert_element_type.155 = bf16[8,16,4096]{2,1,0:T(8,128)(2,1)S(1)} convert(f32[8,16,4096]{2,1,0:T(8,128)} %param.17) | non-fusion elementwise | flops 524288 | bytes 3145728 | tf_op jit(solution)/shard_map/convert_element_type | solution.py:368
  39.2 2.2 %gather_fusion.1 = bf16[128,4096]{1,0:T(8,128)(2,1)} fusion(bf16[128,4096]{1,0:T(8,128)(2,1)S(1)} %bitcast.142, s32[1024]{0:T(1024)S(1)} %pad_clamp_fusion.6), kind=kCustom, calls=%fused_computation.1 | custom fusion | bytes 2097664 | tf_op jit(solution)/shard_map/jit(_take)/gather | solution.py:52
  41.4 2.5 %collective-permute-done.3 = bf16[4,32,1024]{2,1,0:T(8,128)(2,1)} collective-permute-done((bf16[4,32,1024]{2,1,0:T(8,128)(2,1)}, bf16[4,32,1024]{2,1,0:T(8,128)(2,1)}, u32[]{:S(2)}, u32[]{:S(2)}) %collective-permute-start.3) | collective-permute-done | bytes 262176 | tf_op jit(solution)/shard_map/ppermute | solution.py:92
  44.0 3.2 %collective-permute-done.5 = bf16[4,32,1024]{2,1,0:T(8,128)(2,1)} collective-permute-done((bf16[4,32,1024]{2,1,0:T(8,128)(2,1)}, bf16[4,32,1024]{2,1,0:T(8,128)(2,1)}, u32[]{:S(2)}, u32[]{:S(2)}) %collective-permute-start.5) | collective-permute-done | bytes 262176 | tf_op jit(solution)/shard_map/ppermute | solution.py:92
  47.1 11.8 %collective-permute-done.4 = bf16[4,32,1024]{2,1,0:T(8,128)(2,1)} collective-permute-done((bf16[4,32,1024]{2,1,0:T(8,128)(2,1)S(1)}, bf16[4,32,1024]{2,1,0:T(8,128)(2,1)}, u32[]{:S(2)}, u32[]{:S(2)}) %collective-permute-start.4) | collective-permute-done | bytes 262176 | tf_op jit(solution)/shard_map/ppermute | solution.py:92
  58.9 2.3 %fusion.37 = (bf16[4,32,1024]{2,1,0:T(8,128)(2,1)}, f32[4,32,1024]{2,1,0:T(8,128)}) fusion(bf16[4,32,1024]{2,1,0:T(8,128)(2,1)} %collective-permute-done.5, bf16[4,32,1024]{2,1,0:T(8,128)(2,1)} %collective-permute-done.4, bf16[4,32,1024]{2,1,0:T(8,128)(2,1)} %collective-permute-done.3, bf16[4,4,32,1024]{3,2,1,0:T(8,128)(2,1)} %bitcast.157, s32[]{:T(128)S(6)} %select_n.203), kind=kLoop, calls=%fused_computation.138 | loop fusion | flops 1048576 | bytes 1835012 | tf_op jit(solution)/shard_map/convert.13
  61.2 4.1 %all-to-all-start = ((bf16[16,8,4096]{2,1,0:T(8,128)(2,1)}), bf16[16,8,4096]{2,1,0:T(8,128)(2,1)S(1)}, u32[]{:S(2)}, u32[]{:S(2)}) async-start(bf16[16,8,4096]{2,1,0:T(8,128)(2,1)} %bitcast.147), calls=%async_computation | async-start | bytes 2097152 | tf_op jit(solution)/shard_map/all_to_all | solution.py:57
  65.3 0.8 stack.70
  66.0 0.8 stack.71
  66.8 0.8 stack.72
  67.5 0.7 add_multiply_fusion
  69.0 1.2 pad_clamp_fusion
  70.2 1.3 pad_clamp_fusion.3
  72.1 0.6 pad_clamp_fusion.4
  72.6 0.6 maximum_bitcast_fusion
  73.3 0.9 fusion.10
  74.1 0.8 reshape_reshape.2.decay_ref
  74.9 0.9 slice.91
  76.0 1.6 %slice_convert_fusion = (f32[1,32,1024]{2,1,0:T(8,128)}, f32[1,32,1024]{2,1,0:T(8,128)}, f32[1,32,1024]{2,1,0:T(8,128)S(1)}) fusion(bf16[4,32,1024]{2,1,0:T(8,128)(2,1)} %get-tuple-element.15), kind=kLoop, calls=%fused_computation.61 | loop fusion | flops 98304 | bytes 589824 | tf_op jit(solution)/shard_map/convert_element_type | solution.py:150
  77.6 1.7 %reshape.507.value_ref = f32[4,128,64]{2,1,0:T(8,128)} reshape(f32[1,32,1024]{2,1,0:T(8,128)} %get-tuple-element.33) | data formatting | bytes 262144 | tf_op jit(solution)/shard_map/convert_element_type | solution.py:150
  79.3 1.7 %reshape.506.key_ref = f32[4,128,64]{2,1,0:T(8,128)} reshape(f32[1,32,1024]{2,1,0:T(8,128)} %get-tuple-element.34) | data formatting | bytes 262144 | tf_op jit(solution)/shard_map/convert_element_type | solution.py:150
  81.0 0.8 reshape.505.recept_ref
  81.8 0.8 divide_multiply_fusion.gate_ref
  82.6 1.4 %broadcast_in_dim.57 = f32[3,8,16,64]{3,2,1,0:T(8,128)} broadcast(f32[3,16,64]{2,1,0:T(8,128)} %maximum_bitcast_fusion), dimensions={0,2,3} | broadcast | bytes 110592 | tf_op jit(solution)/shard_map/broadcast_in_dim | solution.py:398
  84.0 6.4 %shard_map.166 = (bf16[4,128,64]{2,1,0:T(8,128)(2,1)}, bf16[9,128,64]{2,1,0:T(8,128)(2,1)}) custom-call(f32[4,128,64]{2,1,0:T(8,128)} %reshape.505.recept_ref, f32[4,128,64]{2,1,0:T(8,128)} %reshape.506.key_ref, f32[4,128,64]{2,1,0:T(8,128)} %reshape.507.value_ref, f32[4,128,64]{2,1,0:T(8,128)} %reshape_reshape.2.decay_ref, ...), custom_call_target="tpu_custom_call" | custom-call | flops 805306368 | bytes 3063808 | tf_op jit(solution)/shard_map/pallas_call | solution.py:238
  90.4 2.4 %gather_fusion.3 = bf16[128,4096]{1,0:T(8,128)(2,1)} fusion(bf16[128,4096]{1,0:T(8,128)(2,1)S(1)} %bitcast.143, s32[1024]{0:T(1024)} %pad_clamp_fusion.4), kind=kCustom, calls=%fused_computation.3 | custom fusion | bytes 2097664 | tf_op jit(solution)/shard_map/jit(_take)/gather | solution.py:76
  92.8 1.7 %gather_fusion.6 = bf16[8,9,16,64]{3,2,1,0:T(8,128)(2,1)S(1)} fusion(bf16[9,8,16,64]{3,2,1,0:T(8,128)(2,1)} %bitcast.165, s32[1024]{0:T(1024)} %pad_clamp_fusion.2), kind=kCustom, calls=%fused_computation.6 | custom fusion | bytes 294944 | tf_op jit(solution)/shard_map/jit(_take)/gather | solution.py:424
  94.6 3.8 %collective-permute-start.17 = (bf16[9,2,16,64]{3,2,1,0:T(8,128)(2,1)S(1)}, bf16[9,2,16,64]{3,2,1,0:T(8,128)(2,1)S(1)}, u32[]{:S(2)}, u32[]{:S(2)}) collective-permute-start(bf16[9,2,16,64]{3,2,1,0:T(8,128)(2,1)S(1)} %bitcast.178), channel_id=1, source_target_pairs={{0,12},{4,0},{8,4},{12,8},{1,13},{5,1},{9,5},{13,9},{2,14},{6,2},{... | collective-permute-start | bytes 110600 | tf_op jit(solution)/shard_map/ppermute | solution.py:121
  98.4 1.1 collective-permute-start.16
  99.9 2.7 %collective-permute-start.11 = (bf16[4,8,1024]{2,1,0:T(8,128)(2,1)S(1)}, bf16[4,8,1024]{2,1,0:T(8,128)(2,1)S(1)}, u32[]{:S(2)}, u32[]{:S(2)}) collective-permute-start(bf16[4,8,1024]{2,1,0:T(8,128)(2,1)S(1)} %reshape.492), channel_id=1, source_target_pairs={{0,12},{4,0},{8,4},{12,8},{1,13},{5,1},{9,5},{13,9},{2,14},{6,2},{... | collective-permute-start | bytes 196616 | tf_op jit(solution)/shard_map/ppermute | solution.py:121
  102.6 2.0 %collective-permute-start.10 = (bf16[4,8,1024]{2,1,0:T(8,128)(2,1)S(1)}, bf16[4,8,1024]{2,1,0:T(8,128)(2,1)S(1)}, u32[]{:S(2)}, u32[]{:S(2)}) collective-permute-start(bf16[4,8,1024]{2,1,0:T(8,128)(2,1)S(1)} %reshape.492), channel_id=1, source_target_pairs={{0,8},{4,12},{8,0},{12,4},{1,9},{5,13},{9,1},{13,5},{2,10},{6,14},... | collective-permute-start | bytes 196616 | tf_op jit(solution)/shard_map/ppermute | solution.py:121
  104.8 0.6 collective-permute-done.15
  105.4 4.0 %collective-permute-done.16 = bf16[9,2,16,64]{3,2,1,0:T(8,128)(2,1)S(1)} collective-permute-done((bf16[9,2,16,64]{3,2,1,0:T(8,128)(2,1)S(1)}, bf16[9,2,16,64]{3,2,1,0:T(8,128)(2,1)S(1)}, u32[]{:S(2)}, u32[]{:S(2)}) %collective-permute-start.16) | collective-permute-done | bytes 36896 | tf_op jit(solution)/shard_map/ppermute | solution.py:121
  109.5 0.7 gather_fusion.7
  110.4 1.5 %collective-permute-start.19 = (bf16[4,9,2,4,64]{4,3,2,1,0:T(4,128)(2,1)S(1)}, bf16[4,9,2,4,64]{4,3,2,1,0:T(4,128)(2,1)S(1)}, u32[]{:S(2)}, u32[]{:S(2)}) collective-permute-start(bf16[4,9,2,4,64]{4,3,2,1,0:T(4,128)(2,1)S(1)} %get-tuple-element.22), channel_id=1, source_target_pairs={{0,2},{1,3},{2,0},{3,1},{4,6},{5,7},{6,4},{7,5},{8,10},{9,11},{10,... | collective-permute-start | bytes 110600 | tf_op jit(solution)/shard_map/ppermute | solution.py:136
  112.3 0.7 gather_fusion.4
  113.2 0.9 gather_fusion.5
  114.6 0.7 dynamic-slice_bitcast_fusion.9
  115.7 1.3 %collective-permute-start.14 = (bf16[4,8,1024]{2,1,0:T(8,128)(2,1)}, bf16[4,8,1024]{2,1,0:T(8,128)(2,1)S(1)}, u32[]{:S(2)}, u32[]{:S(2)}) collective-permute-start(bf16[4,8,1024]{2,1,0:T(8,128)(2,1)} %get-tuple-element.29), channel_id=1, source_target_pairs={{0,3},{1,0},{2,1},{3,2},{4,7},{5,4},{6,5},{7,6},{8,11},{9,8},{10,9... | collective-permute-start | bytes 196616 | tf_op jit(solution)/shard_map/ppermute | solution.py:136
  117.1 1.5 %collective-permute-start.13 = (bf16[4,8,1024]{2,1,0:T(8,128)(2,1)S(1)}, bf16[4,8,1024]{2,1,0:T(8,128)(2,1)S(1)}, u32[]{:S(2)}, u32[]{:S(2)}) collective-permute-start(bf16[4,8,1024]{2,1,0:T(8,128)(2,1)S(1)} %get-tuple-element.30), channel_id=1, source_target_pairs={{0,2},{1,3},{2,0},{3,1},{4,6},{5,7},{6,4},{7,5},{8,10},{9,11},{10,... | collective-permute-start | bytes 196616 | tf_op jit(solution)/shard_map/ppermute | solution.py:136
  118.8 0.8 gather_fusion.8
  119.8 0.7 gather_fusion.9
  120.5 0.7 copy.79
  121.2 5.3 %shard_map.167 = f32[128,4096]{1,0:T(8,128)} custom-call(bf16[128,4096]{1,0:T(8,128)(2,1)} %gather_fusion.3, bf16[9,128,64]{2,1,0:T(8,128)(2,1)} %bitcast.154), custom_call_target="tpu_custom_call" | custom-call | flops 603979776 | bytes 3293184 | tf_op jit(solution)/shard_map/pallas_call | solution.py:282
  126.6 0.6 fusion.40
  (107 shorter events, 6.6 us)
Async XLA Ops:
  0.6 113.5 %copy-start = (bf16[1024,1024]{1,0:T(8,128)(2,1)S(1)}, bf16[1024,1024]{1,0:T(8,128)(2,1)}, u32[]{:S(2)}) copy-start(bf16[1024,1024]{1,0:T(8,128)(2,1)} %param.29) | copy-start | bytes 6291460
  2.7 1.2 copy-start.2
  2.8 1.2 slice-start
  3.8 6.6 %copy-start.14 = (s32[32]{0:T(128)S(1)}, s32[32]{0:T(128)}, u32[]{:S(2)}) copy-start(s32[32]{0:T(128)} %param.18) | copy-start | bytes 388
  3.8 6.8 %copy-start.9 = (f32[6,1024]{1,0:T(8,128)S(1)}, f32[6,1024]{1,0:T(8,128)}, u32[]{:S(2)}) copy-start(f32[6,1024]{1,0:T(8,128)} %param.19) | copy-start | bytes 73732
  4.3 8.8 %copy-start.4 = (bf16[128,320]{0,1:T(8,128)(2,1)}, bf16[128,320]{0,1:T(8,128)(2,1)S(1)}, u32[]{:S(2)}) copy-start(bf16[128,320]{0,1:T(8,128)(2,1)S(1)} %convolution_convert_fusion.1) | copy-start | bytes 245764
  4.3 9.2 %collective-permute-start.2 = (bf16[128,320]{0,1:T(8,128)(2,1)S(1)}, bf16[128,320]{0,1:T(8,128)(2,1)S(1)}, u32[]{:S(2)}, u32[]{:S(2)}) collective-permute-start(bf16[128,320]{0,1:T(8,128)(2,1)S(1)} %convolution_convert_fusion.1), channel_id=1, source_target_pairs={{0,12},{4,0},{8,4},{12,8},{1,13},{5,1},{9,5},{13,9},{2,14},{6,2},{... | collective-permute-start | bytes 245768 | tf_op jit(solution)/shard_map/ppermute | solution.py:104
  9.4 7.5 %collective-permute-start.1 = (bf16[128,320]{0,1:T(8,128)(2,1)S(1)}, bf16[128,320]{0,1:T(8,128)(2,1)S(1)}, u32[]{:S(2)}, u32[]{:S(2)}) collective-permute-start(bf16[128,320]{0,1:T(8,128)(2,1)S(1)} %convolution_convert_fusion.1), channel_id=1, source_target_pairs={{0,8},{4,12},{8,0},{12,4},{1,9},{5,13},{9,1},{13,5},{2,10},{6,14},... | collective-permute-start | bytes 245768 | tf_op jit(solution)/shard_map/ppermute | solution.py:104
  9.4 7.5 %collective-permute-start = (bf16[128,320]{0,1:T(8,128)(2,1)S(1)}, bf16[128,320]{0,1:T(8,128)(2,1)}, u32[]{:S(2)}, u32[]{:S(2)}) collective-permute-start(bf16[128,320]{0,1:T(8,128)(2,1)S(1)} %convolution_convert_fusion.1), channel_id=1, source_target_pairs={{0,4},{4,8},{8,12},{12,0},{1,5},{5,9},{9,13},{13,1},{2,6},{6,10},{... | collective-permute-start | bytes 245768 | tf_op jit(solution)/shard_map/ppermute | solution.py:104
  10.5 0.5 copy-start.12
  11.3 0.6 copy-start.11
  13.5 9.2 %copy-start.10 = (s32[1024]{0:T(1024)}, s32[1024]{0:T(1024)S(1)}, u32[]{:S(2)}) copy-start(s32[1024]{0:T(1024)S(1)} %pad_clamp_fusion.5) | copy-start | bytes 12292
  13.5 3.4 %copy-start.7 = (bf16[128,320]{0,1:T(8,128)(2,1)}, bf16[128,320]{0,1:T(8,128)(2,1)S(1)}, u32[]{:S(2)}) copy-start(bf16[128,320]{0,1:T(8,128)(2,1)S(1)} %collective-permute-done.2) | copy-start | bytes 245764
  16.9 0.6 copy-start.8
  19.9 2.8 %copy-start.5 = (bf16[1024,128]{1,0:T(8,128)(2,1)S(1)}, bf16[1024,128]{1,0:T(8,128)(2,1)}, u32[]{:S(2)}) copy-start(bf16[1024,128]{1,0:T(8,128)(2,1)} %param.23) | copy-start | bytes 786436
  27.8 3.9 %copy-start.1 = (bf16[4,128,1024]{2,1,0:T(8,128)(2,1)}, bf16[4,128,1024]{2,1,0:T(8,128)(2,1)S(1)}, u32[]{:S(2)}) copy-start(bf16[4,128,1024]{2,1,0:T(8,128)(2,1)S(1)} %convolution_convert_fusion) | copy-start | bytes 3145732
  27.8 8.6 %collective-permute-start.6 = (bf16[32,128]{1,0:T(8,128)(2,1)S(1)}, bf16[32,128]{1,0:T(8,128)(2,1)S(1)}, u32[]{:S(2)}, u32[]{:S(2)}) collective-permute-start(bf16[32,128]{1,0:T(8,128)(2,1)S(1)} %get-tuple-element.38), channel_id=1, source_target_pairs={{0,4},{4,8},{8,12},{12,0},{1,5},{5,9},{9,13},{13,1},{2,6},{6,10},{... | collective-permute-start | bytes 24584 | tf_op jit(solution)/shard_map/ppermute | solution.py:92
  27.9 13.5 %collective-permute-start.8 = (bf16[32,128]{1,0:T(8,128)(2,1)S(1)}, bf16[32,128]{1,0:T(8,128)(2,1)S(1)}, u32[]{:S(2)}, u32[]{:S(2)}) collective-permute-start(bf16[32,128]{1,0:T(8,128)(2,1)S(1)} %get-tuple-element.39), channel_id=1, source_target_pairs={{0,12},{4,0},{8,4},{12,8},{1,13},{5,1},{9,5},{13,9},{2,14},{6,2},{... | collective-permute-start | bytes 24584 | tf_op jit(solution)/shard_map/ppermute | solution.py:92
  31.7 9.7 %collective-permute-start.7 = (bf16[32,128]{1,0:T(8,128)(2,1)S(1)}, bf16[32,128]{1,0:T(8,128)(2,1)S(1)}, u32[]{:S(2)}, u32[]{:S(2)}) collective-permute-start(bf16[32,128]{1,0:T(8,128)(2,1)S(1)} %get-tuple-element.40), channel_id=1, source_target_pairs={{0,8},{4,12},{8,0},{12,4},{1,9},{5,13},{9,1},{13,5},{2,10},{6,14},... | collective-permute-start | bytes 24584 | tf_op jit(solution)/shard_map/ppermute | solution.py:92
  32.5 11.4 %collective-permute-start.3 = (bf16[4,32,1024]{2,1,0:T(8,128)(2,1)}, bf16[4,32,1024]{2,1,0:T(8,128)(2,1)}, u32[]{:S(2)}, u32[]{:S(2)}) collective-permute-start(bf16[4,32,1024]{2,1,0:T(8,128)(2,1)} %get-tuple-element.17), channel_id=1, source_target_pairs={{0,4},{4,8},{8,12},{12,0},{1,5},{5,9},{9,13},{13,1},{2,6},{6,10},{... | collective-permute-start | bytes 786440 | tf_op jit(solution)/shard_map/ppermute | solution.py:92
  33.4 13.7 %collective-permute-start.5 = (bf16[4,32,1024]{2,1,0:T(8,128)(2,1)}, bf16[4,32,1024]{2,1,0:T(8,128)(2,1)}, u32[]{:S(2)}, u32[]{:S(2)}) collective-permute-start(bf16[4,32,1024]{2,1,0:T(8,128)(2,1)} %get-tuple-element.18), channel_id=1, source_target_pairs={{0,12},{4,0},{8,4},{12,8},{1,13},{5,1},{9,5},{13,9},{2,14},{6,2},{... | collective-permute-start | bytes 786440 | tf_op jit(solution)/shard_map/ppermute | solution.py:92
  36.4 22.5 %collective-permute-start.4 = (bf16[4,32,1024]{2,1,0:T(8,128)(2,1)S(1)}, bf16[4,32,1024]{2,1,0:T(8,128)(2,1)}, u32[]{:S(2)}, u32[]{:S(2)}) collective-permute-start(bf16[4,32,1024]{2,1,0:T(8,128)(2,1)S(1)} %get-tuple-element.19), channel_id=1, source_target_pairs={{0,8},{4,12},{8,0},{12,4},{1,9},{5,13},{9,1},{13,5},{2,10},{6,14},... | collective-permute-start | bytes 786440 | tf_op jit(solution)/shard_map/ppermute | solution.py:92
  58.9 14.4 %copy-start.6 = (bf16[128,1024]{1,0:T(8,128)(2,1)S(1)}, bf16[128,1024]{1,0:T(8,128)(2,1)}, u32[]{:S(2)}) copy-start(bf16[128,1024]{1,0:T(8,128)(2,1)} %param.24) | copy-start | bytes 786436
  61.2 29.2 %all-to-all-start = ((bf16[16,8,4096]{2,1,0:T(8,128)(2,1)}), bf16[16,8,4096]{2,1,0:T(8,128)(2,1)S(1)}, u32[]{:S(2)}, u32[]{:S(2)}) async-start(bf16[16,8,4096]{2,1,0:T(8,128)(2,1)} %bitcast.147), calls=%async_computation | async-start | bytes 2097152 | tf_op jit(solution)/shard_map/all_to_all | solution.py:57
  90.4 9.2 %copy-start.13 = (s32[4]{0:T(128)S(1)}, s32[4]{0:T(128)}, u32[]{:S(2)}) copy-start(s32[4]{0:T(128)} %fusion.31) | copy-start | bytes 52
  90.4 9.2 %copy-start.3 = (bf16[4,128,64]{2,1,0:T(8,128)(2,1)S(1)}, bf16[4,128,64]{2,1,0:T(8,128)(2,1)}, u32[]{:S(2)}) copy-start(bf16[4,128,64]{2,1,0:T(8,128)(2,1)} %get-tuple-element.12) | copy-start | bytes 196612
  94.6 10.0 %collective-permute-start.17 = (bf16[9,2,16,64]{3,2,1,0:T(8,128)(2,1)S(1)}, bf16[9,2,16,64]{3,2,1,0:T(8,128)(2,1)S(1)}, u32[]{:S(2)}, u32[]{:S(2)}) collective-permute-start(bf16[9,2,16,64]{3,2,1,0:T(8,128)(2,1)S(1)} %bitcast.178), channel_id=1, source_target_pairs={{0,12},{4,0},{8,4},{12,8},{1,13},{5,1},{9,5},{13,9},{2,14},{6,2},{... | collective-permute-start | bytes 110600 | tf_op jit(solution)/shard_map/ppermute | solution.py:121
  98.4 7.0 %collective-permute-start.15 = (bf16[9,2,16,64]{3,2,1,0:T(8,128)(2,1)S(1)}, bf16[9,2,16,64]{3,2,1,0:T(8,128)(2,1)S(1)}, u32[]{:S(2)}, u32[]{:S(2)}) collective-permute-start(bf16[9,2,16,64]{3,2,1,0:T(8,128)(2,1)S(1)} %bitcast.177), channel_id=1, source_target_pairs={{0,4},{4,8},{8,12},{12,0},{1,5},{5,9},{9,13},{13,1},{2,6},{6,10},{... | collective-permute-start | bytes 110600 | tf_op jit(solution)/shard_map/ppermute | solution.py:121
  98.4 11.0 %collective-permute-start.16 = (bf16[9,2,16,64]{3,2,1,0:T(8,128)(2,1)S(1)}, bf16[9,2,16,64]{3,2,1,0:T(8,128)(2,1)S(1)}, u32[]{:S(2)}, u32[]{:S(2)}) collective-permute-start(bf16[9,2,16,64]{3,2,1,0:T(8,128)(2,1)S(1)} %bitcast.176), channel_id=1, source_target_pairs={{0,8},{4,12},{8,0},{12,4},{1,9},{5,13},{9,1},{13,5},{2,10},{6,14},... | collective-permute-start | bytes 110600 | tf_op jit(solution)/shard_map/ppermute | solution.py:121
  99.9 12.0 %collective-permute-start.11 = (bf16[4,8,1024]{2,1,0:T(8,128)(2,1)S(1)}, bf16[4,8,1024]{2,1,0:T(8,128)(2,1)S(1)}, u32[]{:S(2)}, u32[]{:S(2)}) collective-permute-start(bf16[4,8,1024]{2,1,0:T(8,128)(2,1)S(1)} %reshape.492), channel_id=1, source_target_pairs={{0,12},{4,0},{8,4},{12,8},{1,13},{5,1},{9,5},{13,9},{2,14},{6,2},{... | collective-permute-start | bytes 196616 | tf_op jit(solution)/shard_map/ppermute | solution.py:121
  102.6 9.6 %collective-permute-start.10 = (bf16[4,8,1024]{2,1,0:T(8,128)(2,1)S(1)}, bf16[4,8,1024]{2,1,0:T(8,128)(2,1)S(1)}, u32[]{:S(2)}, u32[]{:S(2)}) collective-permute-start(bf16[4,8,1024]{2,1,0:T(8,128)(2,1)S(1)} %reshape.492), channel_id=1, source_target_pairs={{0,8},{4,12},{8,0},{12,4},{1,9},{5,13},{9,1},{13,5},{2,10},{6,14},... | collective-permute-start | bytes 196616 | tf_op jit(solution)/shard_map/ppermute | solution.py:121
  104.7 7.6 %collective-permute-start.9 = (bf16[4,8,1024]{2,1,0:T(8,128)(2,1)S(1)}, bf16[4,8,1024]{2,1,0:T(8,128)(2,1)S(1)}, u32[]{:S(2)}, u32[]{:S(2)}) collective-permute-start(bf16[4,8,1024]{2,1,0:T(8,128)(2,1)S(1)} %reshape.492), channel_id=1, source_target_pairs={{0,4},{4,8},{8,12},{12,0},{1,5},{5,9},{9,13},{13,1},{2,6},{6,10},{... | collective-permute-start | bytes 196616 | tf_op jit(solution)/shard_map/ppermute | solution.py:121
  110.4 6.7 %collective-permute-start.20 = (bf16[4,9,2,4,64]{4,3,2,1,0:T(4,128)(2,1)S(1)}, bf16[4,9,2,4,64]{4,3,2,1,0:T(4,128)(2,1)S(1)}, u32[]{:S(2)}, u32[]{:S(2)}) collective-permute-start(bf16[4,9,2,4,64]{4,3,2,1,0:T(4,128)(2,1)S(1)} %get-tuple-element.21), channel_id=1, source_target_pairs={{0,3},{1,0},{2,1},{3,2},{4,7},{5,4},{6,5},{7,6},{8,11},{9,8},{10,9... | collective-permute-start | bytes 110600 | tf_op jit(solution)/shard_map/ppermute | solution.py:136
  110.4 8.1 %collective-permute-start.19 = (bf16[4,9,2,4,64]{4,3,2,1,0:T(4,128)(2,1)S(1)}, bf16[4,9,2,4,64]{4,3,2,1,0:T(4,128)(2,1)S(1)}, u32[]{:S(2)}, u32[]{:S(2)}) collective-permute-start(bf16[4,9,2,4,64]{4,3,2,1,0:T(4,128)(2,1)S(1)} %get-tuple-element.22), channel_id=1, source_target_pairs={{0,2},{1,3},{2,0},{3,1},{4,6},{5,7},{6,4},{7,5},{8,10},{9,11},{10,... | collective-permute-start | bytes 110600 | tf_op jit(solution)/shard_map/ppermute | solution.py:136
  112.0 6.6 %collective-permute-start.18 = (bf16[4,9,2,4,64]{4,3,2,1,0:T(4,128)(2,1)S(1)}, bf16[4,9,2,4,64]{4,3,2,1,0:T(4,128)(2,1)S(1)}, u32[]{:S(2)}, u32[]{:S(2)}) collective-permute-start(bf16[4,9,2,4,64]{4,3,2,1,0:T(4,128)(2,1)S(1)} %get-tuple-element.23), channel_id=1, source_target_pairs={{0,1},{1,2},{2,3},{3,0},{4,5},{5,6},{6,7},{7,4},{8,9},{9,10},{10,1... | collective-permute-start | bytes 110600 | tf_op jit(solution)/shard_map/ppermute | solution.py:136
  115.3 11.2 %collective-permute-start.12 = (bf16[4,8,1024]{2,1,0:T(8,128)(2,1)}, bf16[4,8,1024]{2,1,0:T(8,128)(2,1)S(1)}, u32[]{:S(2)}, u32[]{:S(2)}) collective-permute-start(bf16[4,8,1024]{2,1,0:T(8,128)(2,1)} %get-tuple-element.28), channel_id=1, source_target_pairs={{0,1},{1,2},{2,3},{3,0},{4,5},{5,6},{6,7},{7,4},{8,9},{9,10},{10,1... | collective-permute-start | bytes 196616 | tf_op jit(solution)/shard_map/ppermute | solution.py:136
  115.7 10.8 %collective-permute-start.14 = (bf16[4,8,1024]{2,1,0:T(8,128)(2,1)}, bf16[4,8,1024]{2,1,0:T(8,128)(2,1)S(1)}, u32[]{:S(2)}, u32[]{:S(2)}) collective-permute-start(bf16[4,8,1024]{2,1,0:T(8,128)(2,1)} %get-tuple-element.29), channel_id=1, source_target_pairs={{0,3},{1,0},{2,1},{3,2},{4,7},{5,4},{6,5},{7,6},{8,11},{9,8},{10,9... | collective-permute-start | bytes 196616 | tf_op jit(solution)/shard_map/ppermute | solution.py:136
  117.1 9.5 %collective-permute-start.13 = (bf16[4,8,1024]{2,1,0:T(8,128)(2,1)S(1)}, bf16[4,8,1024]{2,1,0:T(8,128)(2,1)S(1)}, u32[]{:S(2)}, u32[]{:S(2)}) collective-permute-start(bf16[4,8,1024]{2,1,0:T(8,128)(2,1)S(1)} %get-tuple-element.30), channel_id=1, source_target_pairs={{0,2},{1,3},{2,0},{3,1},{4,6},{5,7},{6,4},{7,5},{8,10},{9,11},{10,... | collective-permute-start | bytes 196616 | tf_op jit(solution)/shard_map/ppermute | solution.py:136

commit v16 on v13

--- a/solution.py
+++ b/solution.py
@@ -240,7 +240,7 @@
         grid=(rows // block,),
         in_specs=[
             *[pl.BlockSpec((steps, block, extent), lambda n: (0, n, 0))] * pieces,
-            pl.BlockSpec((3, block, extent), lambda n: (0, n, 0)),
+            pl.BlockSpec((3, block, extent), lambda n: (0, 0, 0)),
             pl.BlockSpec((block, flat), lambda n: (n, 0)),
         ],
         out_specs=[
@@ -395,12 +395,12 @@
         return value.reshape(steps, rows_here, SUBSPACE_EXTENT)
 
     projected = tuple(by_row(value) for value in (recept, key_vec, valued, decay_rate, gate_act))
-    params = jnp.broadcast_to(
+    params = jnp.tile(
         jnp.stack([instant_premium, norming_multiplier, norming_intercept]).reshape(
-            3, 1, heads_here, SUBSPACE_EXTENT
+            3, heads_here, SUBSPACE_EXTENT
         ),
-        (3, local_rows, heads_here, SUBSPACE_EXTENT),
-    ).reshape(3, rows_here, SUBSPACE_EXTENT)
+        (1, row_block(rows_here) // heads_here, 1),
+    )
     mixed_rows, payload = run_recurrence(
         projected, params, stream_kept_tableaux.reshape(rows_here, -1)
     )

time: 128 us -> 128 us (level)
    broadcast_in_dim x1 -> x0, local copies, waits for them, and re-layouts: 1.44 us -> none  [per_device(): jnp.broadcast_to(jnp.stack([instant_premium, norming_multiplier, norming_...]
    another operation x1 -> x2, local copies, waits for them, and re-layouts: 0.03 us -> 1.41 us  [the longest x1 1.38 us: per_device(): jnp.tile(jnp.stack([instant_premium, norming_multiplier, norming_intercep...]
    another operation x1 -> x2, other arithmetic: 2.31 us -> 2.92 us
where the time goes in v16:
time: 128 us; the launch traced here: 127 us
  starting transfers between devices  33.7 us (26%)
  local copies, waits for them, and re-layouts  28.4 us (22%)
  waiting for transfers between devices  25.7 us (20%)
  other arithmetic  18 us (14%)
  Pallas kernels  11.4 us (9%)
  matrix products  8.39 us (7%)
  between operations  1.28 us (1%)
    ppermute x6, waiting for transfers between devices, exchange_sum(): lax.ppermute(own(shift), axis_name, [(i, (i + shift) % count) for i in ra...  17.5 us
    ppermute x6, starting transfers between devices, gather_with_parts(): lax.ppermute((value, sent), axis_name, [(i, (i + shift) % count) for i in...  9.73 us
    ppermute x6, starting transfers between devices, exchange_sum(): lax.ppermute(own(shift), axis_name, [(i, (i + shift) % count) for i in ra...  8.82 us
    pallas_call x1, Pallas kernels, run_recurrence(): pl.pallas_call(functools.partial(recurrence_kernel, steps), grid=(rows //...  6.38 us
    ppermute x3, starting transfers between devices, exchange_copies(): lax.ppermute(value, axis_name, [(i, (i + shift) % count) for i in range(c...  6.12 us
    pallas_call x1, Pallas kernels, rebuild_state(): pl.pallas_call(functools.partial(rebuild_kernel, steps), grid=(rows // bl...  5 us
    ppermute x6, starting transfers between devices, sum_with_parts(): lax.ppermute((lax.dynamic_index_in_dim(pieces, target, keepdims=False), l...  4.94 us
    dot_general x1, matrix products, per_device(): jnp.einsum('inf,ifc->inc', mixed[:4], fourfold_linear_maps, preferred_ele...  4.83 us
  transfers between devices with their start and end apart: 22, of which 7 were waited for; matrix products, arithmetic and copies ran while one was open for 26% of the time, Pallas kernels for 9%

profile of v16, /device:TPU:0, one launch (start us, length us, event | category | flops | bytes accessed | tf_op | source)
XLA Modules:
  0.0 126.8 jit_solution(1787818034434846715)
XLA Ops:
  0.6 1.1 slice_bitcast_fusion.2
  1.7 1.0 convert_bitcast_fusion
  2.8 0.9 convert_bitcast_fusion.1
  4.3 5.1 %collective-permute-start.2 = (bf16[128,320]{0,1:T(8,128)(2,1)S(1)}, bf16[128,320]{0,1:T(8,128)(2,1)S(1)}, u32[]{:S(2)}, u32[]{:S(2)}) collective-permute-start(bf16[128,320]{0,1:T(8,128)(2,1)S(1)} %convolution_convert_fusion.1), channel_id=1, source_target_pairs={{0,12},{4,0},{8,4},{12,8},{1,13},{5,1},{9,5},{13,9},{2,14},{6,2},{... | collective-permute-start | bytes 245768 | tf_op jit(solution)/shard_map/ppermute | solution.py:104
  9.4 1.0 collective-permute-start
  12.4 0.7 gather_fusion
  13.5 3.4 %collective-permute-done.1 = bf16[128,320]{0,1:T(8,128)(2,1)S(1)} collective-permute-done((bf16[128,320]{0,1:T(8,128)(2,1)S(1)}, bf16[128,320]{0,1:T(8,128)(2,1)S(1)}, u32[]{:S(2)}, u32[]{:S(2)}) %collective-permute-start.1) | collective-permute-done | bytes 81952 | tf_op jit(solution)/shard_map/ppermute | solution.py:104
  16.9 0.6 copy-done.8
  17.5 1.0 pad_maximum_fusion
  18.6 1.3 %gather_fusion.2 = bf16[4,128,320]{1,2,0:T(8,128)(2,1)} fusion(bf16[4,128,320]{1,2,0:T(8,128)(2,1)S(1)} %pad_maximum_fusion, s32[1024]{0:T(1024)S(1)} %pad_clamp_fusion.5), kind=kCustom, calls=%fused_computation.2 | custom fusion | bytes 655376 | tf_op jit(solution)/shard_map/jit(_take)/gather | solution.py:107
  19.9 1.1 convert_reduce_fusion
  21.0 1.7 %add_convert_fusion = bf16[5,128,1024]{2,1,0:T(8,128)(2,1)S(1)} fusion(bf16[128,5,64]{0,2,1:T(8,128)(2,1)S(1)} %bitcast.163, bf16[5,64,1024]{2,1,0:T(8,128)(2,1)} %param.21, f32[5,1024]{1,0:T(8,128)S(1)} %slice.53, f32[128,1024]{1,0:T(8,128)S(1)} %bitcast_subtract_fusion, f32[128,1024]{1,0:T(8,128)S(1)} %bitcast.145), kind=kOutput, calls=%fused_computation.10 | convolution fusion | flops 86507520 | bytes 3117056 | tf_op jit(solution)/shard_map/nim,imd->ind/dot_general | solution.py:347
  22.9 4.8 %convolution_convert_fusion = bf16[4,128,1024]{2,1,0:T(8,128)(2,1)S(1)} fusion(bf16[5,128,1024]{2,1,0:T(8,128)(2,1)S(1)} %add_convert_fusion, bf16[4,1024,1024]{2,1,0:T(8,128)(2,1)} %param.22), kind=kOutput, calls=%fused_computation.13 | convolution fusion | flops 1074266112 | bytes 10747904 | tf_op jit(solution)/shard_map/inf,ifc->inc/dot_general | solution.py:353
  27.9 3.8 %collective-permute-start.8 = (bf16[32,128]{1,0:T(8,128)(2,1)S(1)}, bf16[32,128]{1,0:T(8,128)(2,1)S(1)}, u32[]{:S(2)}, u32[]{:S(2)}) collective-permute-start(bf16[32,128]{1,0:T(8,128)(2,1)S(1)} %get-tuple-element.39), channel_id=1, source_target_pairs={{0,12},{4,0},{8,4},{12,8},{1,13},{5,1},{9,5},{13,9},{2,14},{6,2},{... | collective-permute-start | bytes 24584 | tf_op jit(solution)/shard_map/ppermute | solution.py:92
  31.7 0.9 dynamic-slice_bitcast_fusion.2
  32.5 0.9 collective-permute-start.3
  33.4 2.9 %collective-permute-start.5 = (bf16[4,32,1024]{2,1,0:T(8,128)(2,1)}, bf16[4,32,1024]{2,1,0:T(8,128)(2,1)}, u32[]{:S(2)}, u32[]{:S(2)}) collective-permute-start(bf16[4,32,1024]{2,1,0:T(8,128)(2,1)} %get-tuple-element.18), channel_id=1, source_target_pairs={{0,12},{4,0},{8,4},{12,8},{1,13},{5,1},{9,5},{13,9},{2,14},{6,2},{... | collective-permute-start | bytes 786440 | tf_op jit(solution)/shard_map/ppermute | solution.py:92
  36.4 1.1 collective-permute-start.4
  37.5 1.7 %convert_element_type.155 = bf16[8,16,4096]{2,1,0:T(8,128)(2,1)S(1)} convert(f32[8,16,4096]{2,1,0:T(8,128)} %param.17) | non-fusion elementwise | flops 524288 | bytes 3145728 | tf_op jit(solution)/shard_map/convert_element_type | solution.py:368
  39.2 2.2 %gather_fusion.1 = bf16[128,4096]{1,0:T(8,128)(2,1)} fusion(bf16[128,4096]{1,0:T(8,128)(2,1)S(1)} %bitcast.142, s32[1024]{0:T(1024)S(1)} %pad_clamp_fusion.6), kind=kCustom, calls=%fused_computation.1 | custom fusion | bytes 2097664 | tf_op jit(solution)/shard_map/jit(_take)/gather | solution.py:52
  41.4 2.5 %collective-permute-done.3 = bf16[4,32,1024]{2,1,0:T(8,128)(2,1)} collective-permute-done((bf16[4,32,1024]{2,1,0:T(8,128)(2,1)}, bf16[4,32,1024]{2,1,0:T(8,128)(2,1)}, u32[]{:S(2)}, u32[]{:S(2)}) %collective-permute-start.3) | collective-permute-done | bytes 262176 | tf_op jit(solution)/shard_map/ppermute | solution.py:92
  44.0 3.2 %collective-permute-done.5 = bf16[4,32,1024]{2,1,0:T(8,128)(2,1)} collective-permute-done((bf16[4,32,1024]{2,1,0:T(8,128)(2,1)}, bf16[4,32,1024]{2,1,0:T(8,128)(2,1)}, u32[]{:S(2)}, u32[]{:S(2)}) %collective-permute-start.5) | collective-permute-done | bytes 262176 | tf_op jit(solution)/shard_map/ppermute | solution.py:92
  47.1 11.8 %collective-permute-done.4 = bf16[4,32,1024]{2,1,0:T(8,128)(2,1)} collective-permute-done((bf16[4,32,1024]{2,1,0:T(8,128)(2,1)S(1)}, bf16[4,32,1024]{2,1,0:T(8,128)(2,1)}, u32[]{:S(2)}, u32[]{:S(2)}) %collective-permute-start.4) | collective-permute-done | bytes 262176 | tf_op jit(solution)/shard_map/ppermute | solution.py:92
  58.9 2.3 %fusion.37 = (bf16[4,32,1024]{2,1,0:T(8,128)(2,1)}, f32[4,32,1024]{2,1,0:T(8,128)}) fusion(bf16[4,32,1024]{2,1,0:T(8,128)(2,1)} %collective-permute-done.5, bf16[4,32,1024]{2,1,0:T(8,128)(2,1)} %collective-permute-done.4, bf16[4,32,1024]{2,1,0:T(8,128)(2,1)} %collective-permute-done.3, bf16[4,4,32,1024]{3,2,1,0:T(8,128)(2,1)} %bitcast.157, s32[]{:T(128)S(6)} %select_n.203), kind=kLoop, calls=%fused_computation.138 | loop fusion | flops 1048576 | bytes 1835012 | tf_op jit(solution)/shard_map/convert.13
  61.2 4.1 %all-to-all-start = ((bf16[16,8,4096]{2,1,0:T(8,128)(2,1)}), bf16[16,8,4096]{2,1,0:T(8,128)(2,1)S(1)}, u32[]{:S(2)}, u32[]{:S(2)}) async-start(bf16[16,8,4096]{2,1,0:T(8,128)(2,1)} %bitcast.147), calls=%async_computation | async-start | bytes 2097152 | tf_op jit(solution)/shard_map/all_to_all | solution.py:57
  65.3 0.8 stack.70
  66.0 0.8 stack.71
  66.8 0.8 stack.72
  67.5 0.7 add_multiply_fusion
  68.9 1.3 %pad_clamp_fusion = s32[1024]{0:T(1024)} fusion(s32[8]{0:T(128)} %copy-done.11), kind=kLoop, calls=%fused_computation.85 | loop fusion | flops 1024 | bytes 4128 | tf_op jit(solution)/shard_map/jit(_take)/gather | solution.py:463
  70.2 1.2 pad_clamp_fusion.3
  71.4 0.6 pad_clamp_fusion.2
  72.0 0.6 pad_clamp_fusion.4
  72.6 0.6 maximum_bitcast_fusion
  73.2 0.9 fusion.10
  74.1 0.8 reshape_reshape.2.decay_ref
  74.9 0.9 slice.91
  75.9 1.6 %slice_convert_fusion = (f32[1,32,1024]{2,1,0:T(8,128)}, f32[1,32,1024]{2,1,0:T(8,128)}, f32[1,32,1024]{2,1,0:T(8,128)S(1)}) fusion(bf16[4,32,1024]{2,1,0:T(8,128)(2,1)} %get-tuple-element.15), kind=kLoop, calls=%fused_computation.61 | loop fusion | flops 98304 | bytes 589824 | tf_op jit(solution)/shard_map/convert_element_type | solution.py:150
  77.6 1.7 %reshape.505.value_ref = f32[4,128,64]{2,1,0:T(8,128)} reshape(f32[1,32,1024]{2,1,0:T(8,128)} %get-tuple-element.33) | data formatting | bytes 262144 | tf_op jit(solution)/shard_map/convert_element_type | solution.py:150
  79.2 1.7 %reshape.504.key_ref = f32[4,128,64]{2,1,0:T(8,128)} reshape(f32[1,32,1024]{2,1,0:T(8,128)} %get-tuple-element.34) | data formatting | bytes 262144 | tf_op jit(solution)/shard_map/convert_element_type | solution.py:150
  81.0 0.8 reshape.503.recept_ref
  81.8 0.8 divide_multiply_fusion.gate_ref
  82.5 1.4 %tile.11 = f32[3,4,16,64]{3,2,1,0:T(8,128)} broadcast(f32[3,16,64]{2,1,0:T(8,128)} %maximum_bitcast_fusion), dimensions={0,2,3} | broadcast | bytes 61440 | tf_op jit(solution)/shard_map/tile | solution.py:398
  83.9 6.4 %shard_map.166 = (bf16[4,128,64]{2,1,0:T(8,128)(2,1)}, bf16[9,128,64]{2,1,0:T(8,128)(2,1)}) custom-call(f32[4,128,64]{2,1,0:T(8,128)} %reshape.503.recept_ref, f32[4,128,64]{2,1,0:T(8,128)} %reshape.504.key_ref, f32[4,128,64]{2,1,0:T(8,128)} %reshape.505.value_ref, f32[4,128,64]{2,1,0:T(8,128)} %reshape_reshape.2.decay_ref, ...), custom_call_target="tpu_custom_call" | custom-call | flops 805306368 | bytes 3063808 | tf_op jit(solution)/shard_map/pallas_call | solution.py:238
  90.3 2.4 %gather_fusion.3 = bf16[128,4096]{1,0:T(8,128)(2,1)} fusion(bf16[128,4096]{1,0:T(8,128)(2,1)S(1)} %bitcast.143, s32[1024]{0:T(1024)} %pad_clamp_fusion.4), kind=kCustom, calls=%fused_computation.3 | custom fusion | bytes 2097664 | tf_op jit(solution)/shard_map/jit(_take)/gather | solution.py:76
  92.7 1.7 %gather_fusion.6 = bf16[8,9,16,64]{3,2,1,0:T(8,128)(2,1)S(1)} fusion(bf16[9,8,16,64]{3,2,1,0:T(8,128)(2,1)} %bitcast.165, s32[1024]{0:T(1024)} %pad_clamp_fusion.2), kind=kCustom, calls=%fused_computation.6 | custom fusion | bytes 294944 | tf_op jit(solution)/shard_map/jit(_take)/gather | solution.py:424
  94.5 3.8 %collective-permute-start.17 = (bf16[9,2,16,64]{3,2,1,0:T(8,128)(2,1)S(1)}, bf16[9,2,16,64]{3,2,1,0:T(8,128)(2,1)S(1)}, u32[]{:S(2)}, u32[]{:S(2)}) collective-permute-start(bf16[9,2,16,64]{3,2,1,0:T(8,128)(2,1)S(1)} %bitcast.178), channel_id=1, source_target_pairs={{0,12},{4,0},{8,4},{12,8},{1,13},{5,1},{9,5},{13,9},{2,14},{6,2},{... | collective-permute-start | bytes 110600 | tf_op jit(solution)/shard_map/ppermute | solution.py:121
  98.3 1.2 collective-permute-start.16
  99.9 2.6 %collective-permute-start.11 = (bf16[4,8,1024]{2,1,0:T(8,128)(2,1)S(1)}, bf16[4,8,1024]{2,1,0:T(8,128)(2,1)S(1)}, u32[]{:S(2)}, u32[]{:S(2)}) collective-permute-start(bf16[4,8,1024]{2,1,0:T(8,128)(2,1)S(1)} %reshape.490), channel_id=1, source_target_pairs={{0,12},{4,0},{8,4},{12,8},{1,13},{5,1},{9,5},{13,9},{2,14},{6,2},{... | collective-permute-start | bytes 196616 | tf_op jit(solution)/shard_map/ppermute | solution.py:121
  102.6 2.0 %collective-permute-start.10 = (bf16[4,8,1024]{2,1,0:T(8,128)(2,1)S(1)}, bf16[4,8,1024]{2,1,0:T(8,128)(2,1)S(1)}, u32[]{:S(2)}, u32[]{:S(2)}) collective-permute-start(bf16[4,8,1024]{2,1,0:T(8,128)(2,1)S(1)} %reshape.490), channel_id=1, source_target_pairs={{0,8},{4,12},{8,0},{12,4},{1,9},{5,13},{9,1},{13,5},{2,10},{6,14},... | collective-permute-start | bytes 196616 | tf_op jit(solution)/shard_map/ppermute | solution.py:121
  104.7 0.6 collective-permute-done.15
  105.3 4.0 %collective-permute-done.16 = bf16[9,2,16,64]{3,2,1,0:T(8,128)(2,1)S(1)} collective-permute-done((bf16[9,2,16,64]{3,2,1,0:T(8,128)(2,1)S(1)}, bf16[9,2,16,64]{3,2,1,0:T(8,128)(2,1)S(1)}, u32[]{:S(2)}, u32[]{:S(2)}) %collective-permute-start.16) | collective-permute-done | bytes 36896 | tf_op jit(solution)/shard_map/ppermute | solution.py:121
  109.4 0.7 gather_fusion.7
  110.3 1.5 %collective-permute-start.19 = (bf16[4,9,2,4,64]{4,3,2,1,0:T(4,128)(2,1)S(1)}, bf16[4,9,2,4,64]{4,3,2,1,0:T(4,128)(2,1)S(1)}, u32[]{:S(2)}, u32[]{:S(2)}) collective-permute-start(bf16[4,9,2,4,64]{4,3,2,1,0:T(4,128)(2,1)S(1)} %get-tuple-element.22), channel_id=1, source_target_pairs={{0,2},{1,3},{2,0},{3,1},{4,6},{5,7},{6,4},{7,5},{8,10},{9,11},{10,... | collective-permute-start | bytes 110600 | tf_op jit(solution)/shard_map/ppermute | solution.py:136
  112.2 0.7 gather_fusion.4
  113.1 0.9 gather_fusion.5
  114.5 0.7 dynamic-slice_bitcast_fusion.9
  115.6 1.3 %collective-permute-start.14 = (bf16[4,8,1024]{2,1,0:T(8,128)(2,1)}, bf16[4,8,1024]{2,1,0:T(8,128)(2,1)S(1)}, u32[]{:S(2)}, u32[]{:S(2)}) collective-permute-start(bf16[4,8,1024]{2,1,0:T(8,128)(2,1)} %get-tuple-element.29), channel_id=1, source_target_pairs={{0,3},{1,0},{2,1},{3,2},{4,7},{5,4},{6,5},{7,6},{8,11},{9,8},{10,9... | collective-permute-start | bytes 196616 | tf_op jit(solution)/shard_map/ppermute | solution.py:136
  117.0 1.5 %collective-permute-start.13 = (bf16[4,8,1024]{2,1,0:T(8,128)(2,1)S(1)}, bf16[4,8,1024]{2,1,0:T(8,128)(2,1)S(1)}, u32[]{:S(2)}, u32[]{:S(2)}) collective-permute-start(bf16[4,8,1024]{2,1,0:T(8,128)(2,1)S(1)} %get-tuple-element.30), channel_id=1, source_target_pairs={{0,2},{1,3},{2,0},{3,1},{4,6},{5,7},{6,4},{7,5},{8,10},{9,11},{10,... | collective-permute-start | bytes 196616 | tf_op jit(solution)/shard_map/ppermute | solution.py:136
  118.7 0.8 gather_fusion.8
  119.7 0.7 gather_fusion.9
  120.4 0.7 copy.79
  121.1 5.0 %shard_map.167 = f32[128,4096]{1,0:T(8,128)} custom-call(bf16[128,4096]{1,0:T(8,128)(2,1)} %gather_fusion.3, bf16[9,128,64]{2,1,0:T(8,128)(2,1)} %bitcast.154), custom_call_target="tpu_custom_call" | custom-call | flops 603979776 | bytes 3293184 | tf_op jit(solution)/shard_map/pallas_call | solution.py:282
  126.2 0.6 fusion.40
  (107 shorter events, 6.5 us)
Async XLA Ops:
  0.6 113.4 %copy-start = (bf16[1024,1024]{1,0:T(8,128)(2,1)S(1)}, bf16[1024,1024]{1,0:T(8,128)(2,1)}, u32[]{:S(2)}) copy-start(bf16[1024,1024]{1,0:T(8,128)(2,1)} %param.29) | copy-start | bytes 6291460
  2.7 1.2 copy-start.2
  2.8 1.2 slice-start
  3.8 6.6 %copy-start.14 = (s32[32]{0:T(128)S(1)}, s32[32]{0:T(128)}, u32[]{:S(2)}) copy-start(s32[32]{0:T(128)} %param.18) | copy-start | bytes 388
  3.8 6.8 %copy-start.9 = (f32[6,1024]{1,0:T(8,128)S(1)}, f32[6,1024]{1,0:T(8,128)}, u32[]{:S(2)}) copy-start(f32[6,1024]{1,0:T(8,128)} %param.19) | copy-start | bytes 73732
  4.3 8.8 %copy-start.4 = (bf16[128,320]{0,1:T(8,128)(2,1)}, bf16[128,320]{0,1:T(8,128)(2,1)S(1)}, u32[]{:S(2)}) copy-start(bf16[128,320]{0,1:T(8,128)(2,1)S(1)} %convolution_convert_fusion.1) | copy-start | bytes 245764
  4.3 9.2 %collective-permute-start.2 = (bf16[128,320]{0,1:T(8,128)(2,1)S(1)}, bf16[128,320]{0,1:T(8,128)(2,1)S(1)}, u32[]{:S(2)}, u32[]{:S(2)}) collective-permute-start(bf16[128,320]{0,1:T(8,128)(2,1)S(1)} %convolution_convert_fusion.1), channel_id=1, source_target_pairs={{0,12},{4,0},{8,4},{12,8},{1,13},{5,1},{9,5},{13,9},{2,14},{6,2},{... | collective-permute-start | bytes 245768 | tf_op jit(solution)/shard_map/ppermute | solution.py:104
  9.4 7.5 %collective-permute-start.1 = (bf16[128,320]{0,1:T(8,128)(2,1)S(1)}, bf16[128,320]{0,1:T(8,128)(2,1)S(1)}, u32[]{:S(2)}, u32[]{:S(2)}) collective-permute-start(bf16[128,320]{0,1:T(8,128)(2,1)S(1)} %convolution_convert_fusion.1), channel_id=1, source_target_pairs={{0,8},{4,12},{8,0},{12,4},{1,9},{5,13},{9,1},{13,5},{2,10},{6,14},... | collective-permute-start | bytes 245768 | tf_op jit(solution)/shard_map/ppermute | solution.py:104
  9.4 7.5 %collective-permute-start = (bf16[128,320]{0,1:T(8,128)(2,1)S(1)}, bf16[128,320]{0,1:T(8,128)(2,1)}, u32[]{:S(2)}, u32[]{:S(2)}) collective-permute-start(bf16[128,320]{0,1:T(8,128)(2,1)S(1)} %convolution_convert_fusion.1), channel_id=1, source_target_pairs={{0,4},{4,8},{8,12},{12,0},{1,5},{5,9},{9,13},{13,1},{2,6},{6,10},{... | collective-permute-start | bytes 245768 | tf_op jit(solution)/shard_map/ppermute | solution.py:104
  10.5 0.5 copy-start.12
  11.3 0.6 copy-start.11
  13.5 9.2 %copy-start.10 = (s32[1024]{0:T(1024)}, s32[1024]{0:T(1024)S(1)}, u32[]{:S(2)}) copy-start(s32[1024]{0:T(1024)S(1)} %pad_clamp_fusion.5) | copy-start | bytes 12292
  13.5 3.4 %copy-start.7 = (bf16[128,320]{0,1:T(8,128)(2,1)}, bf16[128,320]{0,1:T(8,128)(2,1)S(1)}, u32[]{:S(2)}) copy-start(bf16[128,320]{0,1:T(8,128)(2,1)S(1)} %collective-permute-done.2) | copy-start | bytes 245764
  16.9 0.6 copy-start.8
  19.9 2.8 %copy-start.5 = (bf16[1024,128]{1,0:T(8,128)(2,1)S(1)}, bf16[1024,128]{1,0:T(8,128)(2,1)}, u32[]{:S(2)}) copy-start(bf16[1024,128]{1,0:T(8,128)(2,1)} %param.23) | copy-start | bytes 786436
  27.8 3.9 %copy-start.1 = (bf16[4,128,1024]{2,1,0:T(8,128)(2,1)}, bf16[4,128,1024]{2,1,0:T(8,128)(2,1)S(1)}, u32[]{:S(2)}) copy-start(bf16[4,128,1024]{2,1,0:T(8,128)(2,1)S(1)} %convolution_convert_fusion) | copy-start | bytes 3145732
  27.8 8.6 %collective-permute-start.6 = (bf16[32,128]{1,0:T(8,128)(2,1)S(1)}, bf16[32,128]{1,0:T(8,128)(2,1)S(1)}, u32[]{:S(2)}, u32[]{:S(2)}) collective-permute-start(bf16[32,128]{1,0:T(8,128)(2,1)S(1)} %get-tuple-element.38), channel_id=1, source_target_pairs={{0,4},{4,8},{8,12},{12,0},{1,5},{5,9},{9,13},{13,1},{2,6},{6,10},{... | collective-permute-start | bytes 24584 | tf_op jit(solution)/shard_map/ppermute | solution.py:92
  27.9 13.5 %collective-permute-start.8 = (bf16[32,128]{1,0:T(8,128)(2,1)S(1)}, bf16[32,128]{1,0:T(8,128)(2,1)S(1)}, u32[]{:S(2)}, u32[]{:S(2)}) collective-permute-start(bf16[32,128]{1,0:T(8,128)(2,1)S(1)} %get-tuple-element.39), channel_id=1, source_target_pairs={{0,12},{4,0},{8,4},{12,8},{1,13},{5,1},{9,5},{13,9},{2,14},{6,2},{... | collective-permute-start | bytes 24584 | tf_op jit(solution)/shard_map/ppermute | solution.py:92
  31.7 9.7 %collective-permute-start.7 = (bf16[32,128]{1,0:T(8,128)(2,1)S(1)}, bf16[32,128]{1,0:T(8,128)(2,1)S(1)}, u32[]{:S(2)}, u32[]{:S(2)}) collective-permute-start(bf16[32,128]{1,0:T(8,128)(2,1)S(1)} %get-tuple-element.40), channel_id=1, source_target_pairs={{0,8},{4,12},{8,0},{12,4},{1,9},{5,13},{9,1},{13,5},{2,10},{6,14},... | collective-permute-start | bytes 24584 | tf_op jit(solution)/shard_map/ppermute | solution.py:92
  32.5 11.4 %collective-permute-start.3 = (bf16[4,32,1024]{2,1,0:T(8,128)(2,1)}, bf16[4,32,1024]{2,1,0:T(8,128)(2,1)}, u32[]{:S(2)}, u32[]{:S(2)}) collective-permute-start(bf16[4,32,1024]{2,1,0:T(8,128)(2,1)} %get-tuple-element.17), channel_id=1, source_target_pairs={{0,4},{4,8},{8,12},{12,0},{1,5},{5,9},{9,13},{13,1},{2,6},{6,10},{... | collective-permute-start | bytes 786440 | tf_op jit(solution)/shard_map/ppermute | solution.py:92
  33.4 13.7 %collective-permute-start.5 = (bf16[4,32,1024]{2,1,0:T(8,128)(2,1)}, bf16[4,32,1024]{2,1,0:T(8,128)(2,1)}, u32[]{:S(2)}, u32[]{:S(2)}) collective-permute-start(bf16[4,32,1024]{2,1,0:T(8,128)(2,1)} %get-tuple-element.18), channel_id=1, source_target_pairs={{0,12},{4,0},{8,4},{12,8},{1,13},{5,1},{9,5},{13,9},{2,14},{6,2},{... | collective-permute-start | bytes 786440 | tf_op jit(solution)/shard_map/ppermute | solution.py:92
  36.4 22.5 %collective-permute-start.4 = (bf16[4,32,1024]{2,1,0:T(8,128)(2,1)S(1)}, bf16[4,32,1024]{2,1,0:T(8,128)(2,1)}, u32[]{:S(2)}, u32[]{:S(2)}) collective-permute-start(bf16[4,32,1024]{2,1,0:T(8,128)(2,1)S(1)} %get-tuple-element.19), channel_id=1, source_target_pairs={{0,8},{4,12},{8,0},{12,4},{1,9},{5,13},{9,1},{13,5},{2,10},{6,14},... | collective-permute-start | bytes 786440 | tf_op jit(solution)/shard_map/ppermute | solution.py:92
  58.9 14.4 %copy-start.6 = (bf16[128,1024]{1,0:T(8,128)(2,1)S(1)}, bf16[128,1024]{1,0:T(8,128)(2,1)}, u32[]{:S(2)}) copy-start(bf16[128,1024]{1,0:T(8,128)(2,1)} %param.24) | copy-start | bytes 786436
  61.2 29.1 %all-to-all-start = ((bf16[16,8,4096]{2,1,0:T(8,128)(2,1)}), bf16[16,8,4096]{2,1,0:T(8,128)(2,1)S(1)}, u32[]{:S(2)}, u32[]{:S(2)}) async-start(bf16[16,8,4096]{2,1,0:T(8,128)(2,1)} %bitcast.147), calls=%async_computation | async-start | bytes 2097152 | tf_op jit(solution)/shard_map/all_to_all | solution.py:57
  90.3 9.3 %copy-start.13 = (s32[4]{0:T(128)S(1)}, s32[4]{0:T(128)}, u32[]{:S(2)}) copy-start(s32[4]{0:T(128)} %fusion.31) | copy-start | bytes 52
  90.3 9.3 %copy-start.3 = (bf16[4,128,64]{2,1,0:T(8,128)(2,1)S(1)}, bf16[4,128,64]{2,1,0:T(8,128)(2,1)}, u32[]{:S(2)}) copy-start(bf16[4,128,64]{2,1,0:T(8,128)(2,1)} %get-tuple-element.12) | copy-start | bytes 196612
  94.5 10.0 %collective-permute-start.17 = (bf16[9,2,16,64]{3,2,1,0:T(8,128)(2,1)S(1)}, bf16[9,2,16,64]{3,2,1,0:T(8,128)(2,1)S(1)}, u32[]{:S(2)}, u32[]{:S(2)}) collective-permute-start(bf16[9,2,16,64]{3,2,1,0:T(8,128)(2,1)S(1)} %bitcast.178), channel_id=1, source_target_pairs={{0,12},{4,0},{8,4},{12,8},{1,13},{5,1},{9,5},{13,9},{2,14},{6,2},{... | collective-permute-start | bytes 110600 | tf_op jit(solution)/shard_map/ppermute | solution.py:121
  98.3 7.0 %collective-permute-start.15 = (bf16[9,2,16,64]{3,2,1,0:T(8,128)(2,1)S(1)}, bf16[9,2,16,64]{3,2,1,0:T(8,128)(2,1)S(1)}, u32[]{:S(2)}, u32[]{:S(2)}) collective-permute-start(bf16[9,2,16,64]{3,2,1,0:T(8,128)(2,1)S(1)} %bitcast.177), channel_id=1, source_target_pairs={{0,4},{4,8},{8,12},{12,0},{1,5},{5,9},{9,13},{13,1},{2,6},{6,10},{... | collective-permute-start | bytes 110600 | tf_op jit(solution)/shard_map/ppermute | solution.py:121
  98.3 11.0 %collective-permute-start.16 = (bf16[9,2,16,64]{3,2,1,0:T(8,128)(2,1)S(1)}, bf16[9,2,16,64]{3,2,1,0:T(8,128)(2,1)S(1)}, u32[]{:S(2)}, u32[]{:S(2)}) collective-permute-start(bf16[9,2,16,64]{3,2,1,0:T(8,128)(2,1)S(1)} %bitcast.176), channel_id=1, source_target_pairs={{0,8},{4,12},{8,0},{12,4},{1,9},{5,13},{9,1},{13,5},{2,10},{6,14},... | collective-permute-start | bytes 110600 | tf_op jit(solution)/shard_map/ppermute | solution.py:121
  99.9 11.9 %collective-permute-start.11 = (bf16[4,8,1024]{2,1,0:T(8,128)(2,1)S(1)}, bf16[4,8,1024]{2,1,0:T(8,128)(2,1)S(1)}, u32[]{:S(2)}, u32[]{:S(2)}) collective-permute-start(bf16[4,8,1024]{2,1,0:T(8,128)(2,1)S(1)} %reshape.490), channel_id=1, source_target_pairs={{0,12},{4,0},{8,4},{12,8},{1,13},{5,1},{9,5},{13,9},{2,14},{6,2},{... | collective-permute-start | bytes 196616 | tf_op jit(solution)/shard_map/ppermute | solution.py:121
  102.6 9.6 %collective-permute-start.10 = (bf16[4,8,1024]{2,1,0:T(8,128)(2,1)S(1)}, bf16[4,8,1024]{2,1,0:T(8,128)(2,1)S(1)}, u32[]{:S(2)}, u32[]{:S(2)}) collective-permute-start(bf16[4,8,1024]{2,1,0:T(8,128)(2,1)S(1)} %reshape.490), channel_id=1, source_target_pairs={{0,8},{4,12},{8,0},{12,4},{1,9},{5,13},{9,1},{13,5},{2,10},{6,14},... | collective-permute-start | bytes 196616 | tf_op jit(solution)/shard_map/ppermute | solution.py:121
  104.6 7.6 %collective-permute-start.9 = (bf16[4,8,1024]{2,1,0:T(8,128)(2,1)S(1)}, bf16[4,8,1024]{2,1,0:T(8,128)(2,1)S(1)}, u32[]{:S(2)}, u32[]{:S(2)}) collective-permute-start(bf16[4,8,1024]{2,1,0:T(8,128)(2,1)S(1)} %reshape.490), channel_id=1, source_target_pairs={{0,4},{4,8},{8,12},{12,0},{1,5},{5,9},{9,13},{13,1},{2,6},{6,10},{... | collective-permute-start | bytes 196616 | tf_op jit(solution)/shard_map/ppermute | solution.py:121
  110.3 6.7 %collective-permute-start.20 = (bf16[4,9,2,4,64]{4,3,2,1,0:T(4,128)(2,1)S(1)}, bf16[4,9,2,4,64]{4,3,2,1,0:T(4,128)(2,1)S(1)}, u32[]{:S(2)}, u32[]{:S(2)}) collective-permute-start(bf16[4,9,2,4,64]{4,3,2,1,0:T(4,128)(2,1)S(1)} %get-tuple-element.21), channel_id=1, source_target_pairs={{0,3},{1,0},{2,1},{3,2},{4,7},{5,4},{6,5},{7,6},{8,11},{9,8},{10,9... | collective-permute-start | bytes 110600 | tf_op jit(solution)/shard_map/ppermute | solution.py:136
  110.3 8.1 %collective-permute-start.19 = (bf16[4,9,2,4,64]{4,3,2,1,0:T(4,128)(2,1)S(1)}, bf16[4,9,2,4,64]{4,3,2,1,0:T(4,128)(2,1)S(1)}, u32[]{:S(2)}, u32[]{:S(2)}) collective-permute-start(bf16[4,9,2,4,64]{4,3,2,1,0:T(4,128)(2,1)S(1)} %get-tuple-element.22), channel_id=1, source_target_pairs={{0,2},{1,3},{2,0},{3,1},{4,6},{5,7},{6,4},{7,5},{8,10},{9,11},{10,... | collective-permute-start | bytes 110600 | tf_op jit(solution)/shard_map/ppermute | solution.py:136
  111.9 6.6 %collective-permute-start.18 = (bf16[4,9,2,4,64]{4,3,2,1,0:T(4,128)(2,1)S(1)}, bf16[4,9,2,4,64]{4,3,2,1,0:T(4,128)(2,1)S(1)}, u32[]{:S(2)}, u32[]{:S(2)}) collective-permute-start(bf16[4,9,2,4,64]{4,3,2,1,0:T(4,128)(2,1)S(1)} %get-tuple-element.23), channel_id=1, source_target_pairs={{0,1},{1,2},{2,3},{3,0},{4,5},{5,6},{6,7},{7,4},{8,9},{9,10},{10,1... | collective-permute-start | bytes 110600 | tf_op jit(solution)/shard_map/ppermute | solution.py:136
  115.2 10.9 %collective-permute-start.12 = (bf16[4,8,1024]{2,1,0:T(8,128)(2,1)}, bf16[4,8,1024]{2,1,0:T(8,128)(2,1)S(1)}, u32[]{:S(2)}, u32[]{:S(2)}) collective-permute-start(bf16[4,8,1024]{2,1,0:T(8,128)(2,1)} %get-tuple-element.28), channel_id=1, source_target_pairs={{0,1},{1,2},{2,3},{3,0},{4,5},{5,6},{6,7},{7,4},{8,9},{9,10},{10,1... | collective-permute-start | bytes 196616 | tf_op jit(solution)/shard_map/ppermute | solution.py:136
  115.6 10.5 %collective-permute-start.14 = (bf16[4,8,1024]{2,1,0:T(8,128)(2,1)}, bf16[4,8,1024]{2,1,0:T(8,128)(2,1)S(1)}, u32[]{:S(2)}, u32[]{:S(2)}) collective-permute-start(bf16[4,8,1024]{2,1,0:T(8,128)(2,1)} %get-tuple-element.29), channel_id=1, source_target_pairs={{0,3},{1,0},{2,1},{3,2},{4,7},{5,4},{6,5},{7,6},{8,11},{9,8},{10,9... | collective-permute-start | bytes 196616 | tf_op jit(solution)/shard_map/ppermute | solution.py:136
  117.0 9.2 %collective-permute-start.13 = (bf16[4,8,1024]{2,1,0:T(8,128)(2,1)S(1)}, bf16[4,8,1024]{2,1,0:T(8,128)(2,1)S(1)}, u32[]{:S(2)}, u32[]{:S(2)}) collective-permute-start(bf16[4,8,1024]{2,1,0:T(8,128)(2,1)S(1)} %get-tuple-element.30), channel_id=1, source_target_pairs={{0,2},{1,3},{2,0},{3,1},{4,6},{5,7},{6,4},{7,5},{8,10},{9,11},{10,... | collective-permute-start | bytes 196616 | tf_op jit(solution)/shard_map/ppermute | solution.py:136

commit v17 on v16

--- a/solution.py
+++ b/solution.py
@@ -194,10 +194,12 @@
         rest = query - high.astype(jnp.float32)
         middle = rest.astype(jnp.bfloat16)
         low = (rest - middle.astype(jnp.float32)).astype(jnp.bfloat16)
+        rows = query.shape[0]
+        spread_parts = jnp.dot(
+            jnp.concatenate([high, middle, low], axis=0), spread, preferred_element_type=jnp.float32
+        )
         spread_query = (
-            jnp.dot(high, spread, preferred_element_type=jnp.float32)
-            + jnp.dot(middle, spread, preferred_element_type=jnp.float32)
-            + jnp.dot(low, spread, preferred_element_type=jnp.float32)
+            spread_parts[:rows] + spread_parts[rows : 2 * rows] + spread_parts[2 * rows :]
         )
         weighted = spread_query * state
         folded = weighted[:, 0:128]

time: 128 us -> 128 us (level)
  no operation moved by 1% of the time
where the time goes in v17:
time: 128 us; the launch traced here: 127 us
  starting transfers between devices  33.7 us (26%)
  local copies, waits for them, and re-layouts  28.4 us (22%)
  waiting for transfers between devices  25.7 us (20%)
  other arithmetic  18 us (14%)
  Pallas kernels  11.4 us (9%)
  matrix products  8.39 us (7%)
  between operations  1.28 us (1%)
    ppermute x6, waiting for transfers between devices, exchange_sum(): lax.ppermute(own(shift), axis_name, [(i, (i + shift) % count) for i in ra...  17.5 us
    ppermute x6, starting transfers between devices, gather_with_parts(): lax.ppermute((value, sent), axis_name, [(i, (i + shift) % count) for i in...  9.74 us
    ppermute x6, starting transfers between devices, exchange_sum(): lax.ppermute(own(shift), axis_name, [(i, (i + shift) % count) for i in ra...  8.82 us
    pallas_call x1, Pallas kernels, run_recurrence(): pl.pallas_call(functools.partial(recurrence_kernel, steps), grid=(rows //...  6.37 us
    ppermute x3, starting transfers between devices, exchange_copies(): lax.ppermute(value, axis_name, [(i, (i + shift) % count) for i in range(c...  6.12 us
    pallas_call x1, Pallas kernels, rebuild_state(): pl.pallas_call(functools.partial(rebuild_kernel, steps), grid=(rows // bl...  5 us
    ppermute x6, starting transfers between devices, sum_with_parts(): lax.ppermute((lax.dynamic_index_in_dim(pieces, target, keepdims=False), l...  4.97 us
    dot_general x1, matrix products, per_device(): jnp.einsum('inf,ifc->inc', mixed[:4], fourfold_linear_maps, preferred_ele...  4.83 us
  transfers between devices with their start and end apart: 22, of which 7 were waited for; matrix products, arithmetic and copies ran while one was open for 26% of the time, Pallas kernels for 9%

profile of v17, /device:TPU:0, one launch (start us, length us, event | category | flops | bytes accessed | tf_op | source)
XLA Modules:
  0.0 126.8 jit_solution(4878928392644094232)
XLA Ops:
  0.6 1.1 slice_bitcast_fusion.2
  1.7 1.0 convert_bitcast_fusion
  2.8 0.9 convert_bitcast_fusion.1
  4.3 5.1 %collective-permute-start.2 = (bf16[128,320]{0,1:T(8,128)(2,1)S(1)}, bf16[128,320]{0,1:T(8,128)(2,1)S(1)}, u32[]{:S(2)}, u32[]{:S(2)}) collective-permute-start(bf16[128,320]{0,1:T(8,128)(2,1)S(1)} %convolution_convert_fusion.1), channel_id=1, source_target_pairs={{0,12},{4,0},{8,4},{12,8},{1,13},{5,1},{9,5},{13,9},{2,14},{6,2},{... | collective-permute-start | bytes 245768 | tf_op jit(solution)/shard_map/ppermute | solution.py:104
  9.4 1.0 collective-permute-start
  12.4 0.7 gather_fusion
  13.5 3.4 %collective-permute-done.1 = bf16[128,320]{0,1:T(8,128)(2,1)S(1)} collective-permute-done((bf16[128,320]{0,1:T(8,128)(2,1)S(1)}, bf16[128,320]{0,1:T(8,128)(2,1)S(1)}, u32[]{:S(2)}, u32[]{:S(2)}) %collective-permute-start.1) | collective-permute-done | bytes 81952 | tf_op jit(solution)/shard_map/ppermute | solution.py:104
  16.9 0.6 copy-done.8
  17.5 1.0 pad_maximum_fusion
  18.6 1.3 %gather_fusion.2 = bf16[4,128,320]{1,2,0:T(8,128)(2,1)} fusion(bf16[4,128,320]{1,2,0:T(8,128)(2,1)S(1)} %pad_maximum_fusion, s32[1024]{0:T(1024)S(1)} %pad_clamp_fusion.5), kind=kCustom, calls=%fused_computation.2 | custom fusion | bytes 655376 | tf_op jit(solution)/shard_map/jit(_take)/gather | solution.py:107
  19.9 1.1 convert_reduce_fusion
  21.0 1.7 %add_convert_fusion = bf16[5,128,1024]{2,1,0:T(8,128)(2,1)S(1)} fusion(bf16[128,5,64]{0,2,1:T(8,128)(2,1)S(1)} %bitcast.163, bf16[5,64,1024]{2,1,0:T(8,128)(2,1)} %param.21, f32[5,1024]{1,0:T(8,128)S(1)} %slice.53, f32[128,1024]{1,0:T(8,128)S(1)} %bitcast_subtract_fusion, f32[128,1024]{1,0:T(8,128)S(1)} %bitcast.145), kind=kOutput, calls=%fused_computation.10 | convolution fusion | flops 86507520 | bytes 3117056 | tf_op jit(solution)/shard_map/nim,imd->ind/dot_general | solution.py:349
  22.9 4.8 %convolution_convert_fusion = bf16[4,128,1024]{2,1,0:T(8,128)(2,1)S(1)} fusion(bf16[5,128,1024]{2,1,0:T(8,128)(2,1)S(1)} %add_convert_fusion, bf16[4,1024,1024]{2,1,0:T(8,128)(2,1)} %param.22), kind=kOutput, calls=%fused_computation.13 | convolution fusion | flops 1074266112 | bytes 10747904 | tf_op jit(solution)/shard_map/inf,ifc->inc/dot_general | solution.py:355
  27.9 3.8 %collective-permute-start.8 = (bf16[32,128]{1,0:T(8,128)(2,1)S(1)}, bf16[32,128]{1,0:T(8,128)(2,1)S(1)}, u32[]{:S(2)}, u32[]{:S(2)}) collective-permute-start(bf16[32,128]{1,0:T(8,128)(2,1)S(1)} %get-tuple-element.39), channel_id=1, source_target_pairs={{0,12},{4,0},{8,4},{12,8},{1,13},{5,1},{9,5},{13,9},{2,14},{6,2},{... | collective-permute-start | bytes 24584 | tf_op jit(solution)/shard_map/ppermute | solution.py:92
  31.7 0.9 dynamic-slice_bitcast_fusion.2
  32.5 0.9 collective-permute-start.3
  33.4 2.9 %collective-permute-start.5 = (bf16[4,32,1024]{2,1,0:T(8,128)(2,1)}, bf16[4,32,1024]{2,1,0:T(8,128)(2,1)}, u32[]{:S(2)}, u32[]{:S(2)}) collective-permute-start(bf16[4,32,1024]{2,1,0:T(8,128)(2,1)} %get-tuple-element.18), channel_id=1, source_target_pairs={{0,12},{4,0},{8,4},{12,8},{1,13},{5,1},{9,5},{13,9},{2,14},{6,2},{... | collective-permute-start | bytes 786440 | tf_op jit(solution)/shard_map/ppermute | solution.py:92
  36.4 1.1 collective-permute-start.4
  37.5 1.7 %convert_element_type.155 = bf16[8,16,4096]{2,1,0:T(8,128)(2,1)S(1)} convert(f32[8,16,4096]{2,1,0:T(8,128)} %param.17) | non-fusion elementwise | flops 524288 | bytes 3145728 | tf_op jit(solution)/shard_map/convert_element_type | solution.py:370
  39.2 2.2 %gather_fusion.1 = bf16[128,4096]{1,0:T(8,128)(2,1)} fusion(bf16[128,4096]{1,0:T(8,128)(2,1)S(1)} %bitcast.142, s32[1024]{0:T(1024)S(1)} %pad_clamp_fusion.6), kind=kCustom, calls=%fused_computation.1 | custom fusion | bytes 2097664 | tf_op jit(solution)/shard_map/jit(_take)/gather | solution.py:52
  41.4 2.5 %collective-permute-done.3 = bf16[4,32,1024]{2,1,0:T(8,128)(2,1)} collective-permute-done((bf16[4,32,1024]{2,1,0:T(8,128)(2,1)}, bf16[4,32,1024]{2,1,0:T(8,128)(2,1)}, u32[]{:S(2)}, u32[]{:S(2)}) %collective-permute-start.3) | collective-permute-done | bytes 262176 | tf_op jit(solution)/shard_map/ppermute | solution.py:92
  44.0 3.2 %collective-permute-done.5 = bf16[4,32,1024]{2,1,0:T(8,128)(2,1)} collective-permute-done((bf16[4,32,1024]{2,1,0:T(8,128)(2,1)}, bf16[4,32,1024]{2,1,0:T(8,128)(2,1)}, u32[]{:S(2)}, u32[]{:S(2)}) %collective-permute-start.5) | collective-permute-done | bytes 262176 | tf_op jit(solution)/shard_map/ppermute | solution.py:92
  47.1 11.8 %collective-permute-done.4 = bf16[4,32,1024]{2,1,0:T(8,128)(2,1)} collective-permute-done((bf16[4,32,1024]{2,1,0:T(8,128)(2,1)S(1)}, bf16[4,32,1024]{2,1,0:T(8,128)(2,1)}, u32[]{:S(2)}, u32[]{:S(2)}) %collective-permute-start.4) | collective-permute-done | bytes 262176 | tf_op jit(solution)/shard_map/ppermute | solution.py:92
  58.9 2.3 %fusion.37 = (bf16[4,32,1024]{2,1,0:T(8,128)(2,1)}, f32[4,32,1024]{2,1,0:T(8,128)}) fusion(bf16[4,32,1024]{2,1,0:T(8,128)(2,1)} %collective-permute-done.5, bf16[4,32,1024]{2,1,0:T(8,128)(2,1)} %collective-permute-done.4, bf16[4,32,1024]{2,1,0:T(8,128)(2,1)} %collective-permute-done.3, bf16[4,4,32,1024]{3,2,1,0:T(8,128)(2,1)} %bitcast.157, s32[]{:T(128)S(6)} %select_n.203), kind=kLoop, calls=%fused_computation.138 | loop fusion | flops 1048576 | bytes 1835012 | tf_op jit(solution)/shard_map/convert.13
  61.2 4.1 %all-to-all-start = ((bf16[16,8,4096]{2,1,0:T(8,128)(2,1)}), bf16[16,8,4096]{2,1,0:T(8,128)(2,1)S(1)}, u32[]{:S(2)}, u32[]{:S(2)}) async-start(bf16[16,8,4096]{2,1,0:T(8,128)(2,1)} %bitcast.147), calls=%async_computation | async-start | bytes 2097152 | tf_op jit(solution)/shard_map/all_to_all | solution.py:57
  65.3 0.8 stack.70
  66.0 0.8 stack.71
  66.8 0.8 stack.72
  67.5 0.7 add_multiply_fusion
  68.9 1.3 %pad_clamp_fusion = s32[1024]{0:T(1024)} fusion(s32[8]{0:T(128)} %copy-done.11), kind=kLoop, calls=%fused_computation.85 | loop fusion | flops 1024 | bytes 4128 | tf_op jit(solution)/shard_map/jit(_take)/gather | solution.py:465
  70.2 1.2 pad_clamp_fusion.3
  71.4 0.6 pad_clamp_fusion.2
  72.0 0.6 pad_clamp_fusion.4
  72.6 0.6 maximum_bitcast_fusion
  73.2 0.9 fusion.10
  74.1 0.8 reshape_reshape.2.decay_ref
  74.9 0.9 slice.91
  75.9 1.6 %slice_convert_fusion = (f32[1,32,1024]{2,1,0:T(8,128)}, f32[1,32,1024]{2,1,0:T(8,128)}, f32[1,32,1024]{2,1,0:T(8,128)S(1)}) fusion(bf16[4,32,1024]{2,1,0:T(8,128)(2,1)} %get-tuple-element.15), kind=kLoop, calls=%fused_computation.61 | loop fusion | flops 98304 | bytes 589824 | tf_op jit(solution)/shard_map/convert_element_type | solution.py:150
  77.6 1.7 %reshape.505.value_ref = f32[4,128,64]{2,1,0:T(8,128)} reshape(f32[1,32,1024]{2,1,0:T(8,128)} %get-tuple-element.33) | data formatting | bytes 262144 | tf_op jit(solution)/shard_map/convert_element_type | solution.py:150
  79.2 1.7 %reshape.504.key_ref = f32[4,128,64]{2,1,0:T(8,128)} reshape(f32[1,32,1024]{2,1,0:T(8,128)} %get-tuple-element.34) | data formatting | bytes 262144 | tf_op jit(solution)/shard_map/convert_element_type | solution.py:150
  81.0 0.8 reshape.503.recept_ref
  81.8 0.8 divide_multiply_fusion.gate_ref
  82.5 1.4 %tile.11 = f32[3,4,16,64]{3,2,1,0:T(8,128)} broadcast(f32[3,16,64]{2,1,0:T(8,128)} %maximum_bitcast_fusion), dimensions={0,2,3} | broadcast | bytes 61440 | tf_op jit(solution)/shard_map/tile | solution.py:400
  83.9 6.4 %shard_map.166 = (bf16[4,128,64]{2,1,0:T(8,128)(2,1)}, bf16[9,128,64]{2,1,0:T(8,128)(2,1)}) custom-call(f32[4,128,64]{2,1,0:T(8,128)} %reshape.503.recept_ref, f32[4,128,64]{2,1,0:T(8,128)} %reshape.504.key_ref, f32[4,128,64]{2,1,0:T(8,128)} %reshape.505.value_ref, f32[4,128,64]{2,1,0:T(8,128)} %reshape_reshape.2.decay_ref, ...), custom_call_target="tpu_custom_call" | custom-call | flops 805306368 | bytes 3063808 | tf_op jit(solution)/shard_map/pallas_call | solution.py:240
  90.3 2.4 %gather_fusion.3 = bf16[128,4096]{1,0:T(8,128)(2,1)} fusion(bf16[128,4096]{1,0:T(8,128)(2,1)S(1)} %bitcast.143, s32[1024]{0:T(1024)} %pad_clamp_fusion.4), kind=kCustom, calls=%fused_computation.3 | custom fusion | bytes 2097664 | tf_op jit(solution)/shard_map/jit(_take)/gather | solution.py:76
  92.7 1.7 %gather_fusion.6 = bf16[8,9,16,64]{3,2,1,0:T(8,128)(2,1)S(1)} fusion(bf16[9,8,16,64]{3,2,1,0:T(8,128)(2,1)} %bitcast.165, s32[1024]{0:T(1024)} %pad_clamp_fusion.2), kind=kCustom, calls=%fused_computation.6 | custom fusion | bytes 294944 | tf_op jit(solution)/shard_map/jit(_take)/gather | solution.py:426
  94.5 3.8 %collective-permute-start.17 = (bf16[9,2,16,64]{3,2,1,0:T(8,128)(2,1)S(1)}, bf16[9,2,16,64]{3,2,1,0:T(8,128)(2,1)S(1)}, u32[]{:S(2)}, u32[]{:S(2)}) collective-permute-start(bf16[9,2,16,64]{3,2,1,0:T(8,128)(2,1)S(1)} %bitcast.178), channel_id=1, source_target_pairs={{0,12},{4,0},{8,4},{12,8},{1,13},{5,1},{9,5},{13,9},{2,14},{6,2},{... | collective-permute-start | bytes 110600 | tf_op jit(solution)/shard_map/ppermute | solution.py:121
  98.3 1.3 collective-permute-start.16
  99.9 2.6 %collective-permute-start.11 = (bf16[4,8,1024]{2,1,0:T(8,128)(2,1)S(1)}, bf16[4,8,1024]{2,1,0:T(8,128)(2,1)S(1)}, u32[]{:S(2)}, u32[]{:S(2)}) collective-permute-start(bf16[4,8,1024]{2,1,0:T(8,128)(2,1)S(1)} %reshape.490), channel_id=1, source_target_pairs={{0,12},{4,0},{8,4},{12,8},{1,13},{5,1},{9,5},{13,9},{2,14},{6,2},{... | collective-permute-start | bytes 196616 | tf_op jit(solution)/shard_map/ppermute | solution.py:121
  102.5 2.0 %collective-permute-start.10 = (bf16[4,8,1024]{2,1,0:T(8,128)(2,1)S(1)}, bf16[4,8,1024]{2,1,0:T(8,128)(2,1)S(1)}, u32[]{:S(2)}, u32[]{:S(2)}) collective-permute-start(bf16[4,8,1024]{2,1,0:T(8,128)(2,1)S(1)} %reshape.490), channel_id=1, source_target_pairs={{0,8},{4,12},{8,0},{12,4},{1,9},{5,13},{9,1},{13,5},{2,10},{6,14},... | collective-permute-start | bytes 196616 | tf_op jit(solution)/shard_map/ppermute | solution.py:121
  104.6 0.6 collective-permute-done.15
  105.3 4.0 %collective-permute-done.16 = bf16[9,2,16,64]{3,2,1,0:T(8,128)(2,1)S(1)} collective-permute-done((bf16[9,2,16,64]{3,2,1,0:T(8,128)(2,1)S(1)}, bf16[9,2,16,64]{3,2,1,0:T(8,128)(2,1)S(1)}, u32[]{:S(2)}, u32[]{:S(2)}) %collective-permute-start.16) | collective-permute-done | bytes 36896 | tf_op jit(solution)/shard_map/ppermute | solution.py:121
  109.4 0.7 gather_fusion.7
  110.3 1.5 %collective-permute-start.19 = (bf16[4,9,2,4,64]{4,3,2,1,0:T(4,128)(2,1)S(1)}, bf16[4,9,2,4,64]{4,3,2,1,0:T(4,128)(2,1)S(1)}, u32[]{:S(2)}, u32[]{:S(2)}) collective-permute-start(bf16[4,9,2,4,64]{4,3,2,1,0:T(4,128)(2,1)S(1)} %get-tuple-element.22), channel_id=1, source_target_pairs={{0,2},{1,3},{2,0},{3,1},{4,6},{5,7},{6,4},{7,5},{8,10},{9,11},{10,... | collective-permute-start | bytes 110600 | tf_op jit(solution)/shard_map/ppermute | solution.py:136
  112.2 0.7 gather_fusion.4
  113.1 0.9 gather_fusion.5
  114.5 0.7 dynamic-slice_bitcast_fusion.9
  115.6 1.3 %collective-permute-start.14 = (bf16[4,8,1024]{2,1,0:T(8,128)(2,1)}, bf16[4,8,1024]{2,1,0:T(8,128)(2,1)S(1)}, u32[]{:S(2)}, u32[]{:S(2)}) collective-permute-start(bf16[4,8,1024]{2,1,0:T(8,128)(2,1)} %get-tuple-element.29), channel_id=1, source_target_pairs={{0,3},{1,0},{2,1},{3,2},{4,7},{5,4},{6,5},{7,6},{8,11},{9,8},{10,9... | collective-permute-start | bytes 196616 | tf_op jit(solution)/shard_map/ppermute | solution.py:136
  117.0 1.5 %collective-permute-start.13 = (bf16[4,8,1024]{2,1,0:T(8,128)(2,1)S(1)}, bf16[4,8,1024]{2,1,0:T(8,128)(2,1)S(1)}, u32[]{:S(2)}, u32[]{:S(2)}) collective-permute-start(bf16[4,8,1024]{2,1,0:T(8,128)(2,1)S(1)} %get-tuple-element.30), channel_id=1, source_target_pairs={{0,2},{1,3},{2,0},{3,1},{4,6},{5,7},{6,4},{7,5},{8,10},{9,11},{10,... | collective-permute-start | bytes 196616 | tf_op jit(solution)/shard_map/ppermute | solution.py:136
  118.7 0.8 gather_fusion.8
  119.7 0.7 gather_fusion.9
  120.4 0.7 copy.79
  121.1 5.0 %shard_map.167 = f32[128,4096]{1,0:T(8,128)} custom-call(bf16[128,4096]{1,0:T(8,128)(2,1)} %gather_fusion.3, bf16[9,128,64]{2,1,0:T(8,128)(2,1)} %bitcast.154), custom_call_target="tpu_custom_call" | custom-call | flops 603979776 | bytes 3293184 | tf_op jit(solution)/shard_map/pallas_call | solution.py:284
  126.2 0.6 fusion.40
  (107 shorter events, 6.5 us)
Async XLA Ops:
  0.6 113.4 %copy-start = (bf16[1024,1024]{1,0:T(8,128)(2,1)S(1)}, bf16[1024,1024]{1,0:T(8,128)(2,1)}, u32[]{:S(2)}) copy-start(bf16[1024,1024]{1,0:T(8,128)(2,1)} %param.29) | copy-start | bytes 6291460
  2.7 1.2 copy-start.2
  2.8 1.2 slice-start
  3.8 6.6 %copy-start.14 = (s32[32]{0:T(128)S(1)}, s32[32]{0:T(128)}, u32[]{:S(2)}) copy-start(s32[32]{0:T(128)} %param.18) | copy-start | bytes 388
  3.8 6.8 %copy-start.9 = (f32[6,1024]{1,0:T(8,128)S(1)}, f32[6,1024]{1,0:T(8,128)}, u32[]{:S(2)}) copy-start(f32[6,1024]{1,0:T(8,128)} %param.19) | copy-start | bytes 73732
  4.3 8.8 %copy-start.4 = (bf16[128,320]{0,1:T(8,128)(2,1)}, bf16[128,320]{0,1:T(8,128)(2,1)S(1)}, u32[]{:S(2)}) copy-start(bf16[128,320]{0,1:T(8,128)(2,1)S(1)} %convolution_convert_fusion.1) | copy-start | bytes 245764
  4.3 9.2 %collective-permute-start.2 = (bf16[128,320]{0,1:T(8,128)(2,1)S(1)}, bf16[128,320]{0,1:T(8,128)(2,1)S(1)}, u32[]{:S(2)}, u32[]{:S(2)}) collective-permute-start(bf16[128,320]{0,1:T(8,128)(2,1)S(1)} %convolution_convert_fusion.1), channel_id=1, source_target_pairs={{0,12},{4,0},{8,4},{12,8},{1,13},{5,1},{9,5},{13,9},{2,14},{6,2},{... | collective-permute-start | bytes 245768 | tf_op jit(solution)/shard_map/ppermute | solution.py:104
  9.4 7.5 %collective-permute-start.1 = (bf16[128,320]{0,1:T(8,128)(2,1)S(1)}, bf16[128,320]{0,1:T(8,128)(2,1)S(1)}, u32[]{:S(2)}, u32[]{:S(2)}) collective-permute-start(bf16[128,320]{0,1:T(8,128)(2,1)S(1)} %convolution_convert_fusion.1), channel_id=1, source_target_pairs={{0,8},{4,12},{8,0},{12,4},{1,9},{5,13},{9,1},{13,5},{2,10},{6,14},... | collective-permute-start | bytes 245768 | tf_op jit(solution)/shard_map/ppermute | solution.py:104
  9.4 7.5 %collective-permute-start = (bf16[128,320]{0,1:T(8,128)(2,1)S(1)}, bf16[128,320]{0,1:T(8,128)(2,1)}, u32[]{:S(2)}, u32[]{:S(2)}) collective-permute-start(bf16[128,320]{0,1:T(8,128)(2,1)S(1)} %convolution_convert_fusion.1), channel_id=1, source_target_pairs={{0,4},{4,8},{8,12},{12,0},{1,5},{5,9},{9,13},{13,1},{2,6},{6,10},{... | collective-permute-start | bytes 245768 | tf_op jit(solution)/shard_map/ppermute | solution.py:104
  10.5 0.5 copy-start.12
  11.3 0.6 copy-start.11
  13.5 9.2 %copy-start.10 = (s32[1024]{0:T(1024)}, s32[1024]{0:T(1024)S(1)}, u32[]{:S(2)}) copy-start(s32[1024]{0:T(1024)S(1)} %pad_clamp_fusion.5) | copy-start | bytes 12292
  13.5 3.4 %copy-start.7 = (bf16[128,320]{0,1:T(8,128)(2,1)}, bf16[128,320]{0,1:T(8,128)(2,1)S(1)}, u32[]{:S(2)}) copy-start(bf16[128,320]{0,1:T(8,128)(2,1)S(1)} %collective-permute-done.2) | copy-start | bytes 245764
  16.9 0.6 copy-start.8
  19.9 2.8 %copy-start.5 = (bf16[1024,128]{1,0:T(8,128)(2,1)S(1)}, bf16[1024,128]{1,0:T(8,128)(2,1)}, u32[]{:S(2)}) copy-start(bf16[1024,128]{1,0:T(8,128)(2,1)} %param.23) | copy-start | bytes 786436
  27.8 3.9 %copy-start.1 = (bf16[4,128,1024]{2,1,0:T(8,128)(2,1)}, bf16[4,128,1024]{2,1,0:T(8,128)(2,1)S(1)}, u32[]{:S(2)}) copy-start(bf16[4,128,1024]{2,1,0:T(8,128)(2,1)S(1)} %convolution_convert_fusion) | copy-start | bytes 3145732
  27.8 8.6 %collective-permute-start.6 = (bf16[32,128]{1,0:T(8,128)(2,1)S(1)}, bf16[32,128]{1,0:T(8,128)(2,1)S(1)}, u32[]{:S(2)}, u32[]{:S(2)}) collective-permute-start(bf16[32,128]{1,0:T(8,128)(2,1)S(1)} %get-tuple-element.38), channel_id=1, source_target_pairs={{0,4},{4,8},{8,12},{12,0},{1,5},{5,9},{9,13},{13,1},{2,6},{6,10},{... | collective-permute-start | bytes 24584 | tf_op jit(solution)/shard_map/ppermute | solution.py:92
  27.9 13.5 %collective-permute-start.8 = (bf16[32,128]{1,0:T(8,128)(2,1)S(1)}, bf16[32,128]{1,0:T(8,128)(2,1)S(1)}, u32[]{:S(2)}, u32[]{:S(2)}) collective-permute-start(bf16[32,128]{1,0:T(8,128)(2,1)S(1)} %get-tuple-element.39), channel_id=1, source_target_pairs={{0,12},{4,0},{8,4},{12,8},{1,13},{5,1},{9,5},{13,9},{2,14},{6,2},{... | collective-permute-start | bytes 24584 | tf_op jit(solution)/shard_map/ppermute | solution.py:92
  31.7 9.7 %collective-permute-start.7 = (bf16[32,128]{1,0:T(8,128)(2,1)S(1)}, bf16[32,128]{1,0:T(8,128)(2,1)S(1)}, u32[]{:S(2)}, u32[]{:S(2)}) collective-permute-start(bf16[32,128]{1,0:T(8,128)(2,1)S(1)} %get-tuple-element.40), channel_id=1, source_target_pairs={{0,8},{4,12},{8,0},{12,4},{1,9},{5,13},{9,1},{13,5},{2,10},{6,14},... | collective-permute-start | bytes 24584 | tf_op jit(solution)/shard_map/ppermute | solution.py:92
  32.5 11.4 %collective-permute-start.3 = (bf16[4,32,1024]{2,1,0:T(8,128)(2,1)}, bf16[4,32,1024]{2,1,0:T(8,128)(2,1)}, u32[]{:S(2)}, u32[]{:S(2)}) collective-permute-start(bf16[4,32,1024]{2,1,0:T(8,128)(2,1)} %get-tuple-element.17), channel_id=1, source_target_pairs={{0,4},{4,8},{8,12},{12,0},{1,5},{5,9},{9,13},{13,1},{2,6},{6,10},{... | collective-permute-start | bytes 786440 | tf_op jit(solution)/shard_map/ppermute | solution.py:92
  33.4 13.7 %collective-permute-start.5 = (bf16[4,32,1024]{2,1,0:T(8,128)(2,1)}, bf16[4,32,1024]{2,1,0:T(8,128)(2,1)}, u32[]{:S(2)}, u32[]{:S(2)}) collective-permute-start(bf16[4,32,1024]{2,1,0:T(8,128)(2,1)} %get-tuple-element.18), channel_id=1, source_target_pairs={{0,12},{4,0},{8,4},{12,8},{1,13},{5,1},{9,5},{13,9},{2,14},{6,2},{... | collective-permute-start | bytes 786440 | tf_op jit(solution)/shard_map/ppermute | solution.py:92
  36.4 22.5 %collective-permute-start.4 = (bf16[4,32,1024]{2,1,0:T(8,128)(2,1)S(1)}, bf16[4,32,1024]{2,1,0:T(8,128)(2,1)}, u32[]{:S(2)}, u32[]{:S(2)}) collective-permute-start(bf16[4,32,1024]{2,1,0:T(8,128)(2,1)S(1)} %get-tuple-element.19), channel_id=1, source_target_pairs={{0,8},{4,12},{8,0},{12,4},{1,9},{5,13},{9,1},{13,5},{2,10},{6,14},... | collective-permute-start | bytes 786440 | tf_op jit(solution)/shard_map/ppermute | solution.py:92
  58.9 14.4 %copy-start.6 = (bf16[128,1024]{1,0:T(8,128)(2,1)S(1)}, bf16[128,1024]{1,0:T(8,128)(2,1)}, u32[]{:S(2)}) copy-start(bf16[128,1024]{1,0:T(8,128)(2,1)} %param.24) | copy-start | bytes 786436
  61.2 29.1 %all-to-all-start = ((bf16[16,8,4096]{2,1,0:T(8,128)(2,1)}), bf16[16,8,4096]{2,1,0:T(8,128)(2,1)S(1)}, u32[]{:S(2)}, u32[]{:S(2)}) async-start(bf16[16,8,4096]{2,1,0:T(8,128)(2,1)} %bitcast.147), calls=%async_computation | async-start | bytes 2097152 | tf_op jit(solution)/shard_map/all_to_all | solution.py:57
  90.3 9.3 %copy-start.13 = (s32[4]{0:T(128)S(1)}, s32[4]{0:T(128)}, u32[]{:S(2)}) copy-start(s32[4]{0:T(128)} %fusion.31) | copy-start | bytes 52
  90.3 9.3 %copy-start.3 = (bf16[4,128,64]{2,1,0:T(8,128)(2,1)S(1)}, bf16[4,128,64]{2,1,0:T(8,128)(2,1)}, u32[]{:S(2)}) copy-start(bf16[4,128,64]{2,1,0:T(8,128)(2,1)} %get-tuple-element.12) | copy-start | bytes 196612
  94.5 10.0 %collective-permute-start.17 = (bf16[9,2,16,64]{3,2,1,0:T(8,128)(2,1)S(1)}, bf16[9,2,16,64]{3,2,1,0:T(8,128)(2,1)S(1)}, u32[]{:S(2)}, u32[]{:S(2)}) collective-permute-start(bf16[9,2,16,64]{3,2,1,0:T(8,128)(2,1)S(1)} %bitcast.178), channel_id=1, source_target_pairs={{0,12},{4,0},{8,4},{12,8},{1,13},{5,1},{9,5},{13,9},{2,14},{6,2},{... | collective-permute-start | bytes 110600 | tf_op jit(solution)/shard_map/ppermute | solution.py:121
  98.3 7.0 %collective-permute-start.15 = (bf16[9,2,16,64]{3,2,1,0:T(8,128)(2,1)S(1)}, bf16[9,2,16,64]{3,2,1,0:T(8,128)(2,1)S(1)}, u32[]{:S(2)}, u32[]{:S(2)}) collective-permute-start(bf16[9,2,16,64]{3,2,1,0:T(8,128)(2,1)S(1)} %bitcast.177), channel_id=1, source_target_pairs={{0,4},{4,8},{8,12},{12,0},{1,5},{5,9},{9,13},{13,1},{2,6},{6,10},{... | collective-permute-start | bytes 110600 | tf_op jit(solution)/shard_map/ppermute | solution.py:121
  98.3 11.0 %collective-permute-start.16 = (bf16[9,2,16,64]{3,2,1,0:T(8,128)(2,1)S(1)}, bf16[9,2,16,64]{3,2,1,0:T(8,128)(2,1)S(1)}, u32[]{:S(2)}, u32[]{:S(2)}) collective-permute-start(bf16[9,2,16,64]{3,2,1,0:T(8,128)(2,1)S(1)} %bitcast.176), channel_id=1, source_target_pairs={{0,8},{4,12},{8,0},{12,4},{1,9},{5,13},{9,1},{13,5},{2,10},{6,14},... | collective-permute-start | bytes 110600 | tf_op jit(solution)/shard_map/ppermute | solution.py:121
  99.9 11.9 %collective-permute-start.11 = (bf16[4,8,1024]{2,1,0:T(8,128)(2,1)S(1)}, bf16[4,8,1024]{2,1,0:T(8,128)(2,1)S(1)}, u32[]{:S(2)}, u32[]{:S(2)}) collective-permute-start(bf16[4,8,1024]{2,1,0:T(8,128)(2,1)S(1)} %reshape.490), channel_id=1, source_target_pairs={{0,12},{4,0},{8,4},{12,8},{1,13},{5,1},{9,5},{13,9},{2,14},{6,2},{... | collective-permute-start | bytes 196616 | tf_op jit(solution)/shard_map/ppermute | solution.py:121
  102.5 9.6 %collective-permute-start.10 = (bf16[4,8,1024]{2,1,0:T(8,128)(2,1)S(1)}, bf16[4,8,1024]{2,1,0:T(8,128)(2,1)S(1)}, u32[]{:S(2)}, u32[]{:S(2)}) collective-permute-start(bf16[4,8,1024]{2,1,0:T(8,128)(2,1)S(1)} %reshape.490), channel_id=1, source_target_pairs={{0,8},{4,12},{8,0},{12,4},{1,9},{5,13},{9,1},{13,5},{2,10},{6,14},... | collective-permute-start | bytes 196616 | tf_op jit(solution)/shard_map/ppermute | solution.py:121
  104.6 7.6 %collective-permute-start.9 = (bf16[4,8,1024]{2,1,0:T(8,128)(2,1)S(1)}, bf16[4,8,1024]{2,1,0:T(8,128)(2,1)S(1)}, u32[]{:S(2)}, u32[]{:S(2)}) collective-permute-start(bf16[4,8,1024]{2,1,0:T(8,128)(2,1)S(1)} %reshape.490), channel_id=1, source_target_pairs={{0,4},{4,8},{8,12},{12,0},{1,5},{5,9},{9,13},{13,1},{2,6},{6,10},{... | collective-permute-start | bytes 196616 | tf_op jit(solution)/shard_map/ppermute | solution.py:121
  110.3 6.7 %collective-permute-start.20 = (bf16[4,9,2,4,64]{4,3,2,1,0:T(4,128)(2,1)S(1)}, bf16[4,9,2,4,64]{4,3,2,1,0:T(4,128)(2,1)S(1)}, u32[]{:S(2)}, u32[]{:S(2)}) collective-permute-start(bf16[4,9,2,4,64]{4,3,2,1,0:T(4,128)(2,1)S(1)} %get-tuple-element.21), channel_id=1, source_target_pairs={{0,3},{1,0},{2,1},{3,2},{4,7},{5,4},{6,5},{7,6},{8,11},{9,8},{10,9... | collective-permute-start | bytes 110600 | tf_op jit(solution)/shard_map/ppermute | solution.py:136
  110.3 8.1 %collective-permute-start.19 = (bf16[4,9,2,4,64]{4,3,2,1,0:T(4,128)(2,1)S(1)}, bf16[4,9,2,4,64]{4,3,2,1,0:T(4,128)(2,1)S(1)}, u32[]{:S(2)}, u32[]{:S(2)}) collective-permute-start(bf16[4,9,2,4,64]{4,3,2,1,0:T(4,128)(2,1)S(1)} %get-tuple-element.22), channel_id=1, source_target_pairs={{0,2},{1,3},{2,0},{3,1},{4,6},{5,7},{6,4},{7,5},{8,10},{9,11},{10,... | collective-permute-start | bytes 110600 | tf_op jit(solution)/shard_map/ppermute | solution.py:136
  111.9 6.6 %collective-permute-start.18 = (bf16[4,9,2,4,64]{4,3,2,1,0:T(4,128)(2,1)S(1)}, bf16[4,9,2,4,64]{4,3,2,1,0:T(4,128)(2,1)S(1)}, u32[]{:S(2)}, u32[]{:S(2)}) collective-permute-start(bf16[4,9,2,4,64]{4,3,2,1,0:T(4,128)(2,1)S(1)} %get-tuple-element.23), channel_id=1, source_target_pairs={{0,1},{1,2},{2,3},{3,0},{4,5},{5,6},{6,7},{7,4},{8,9},{9,10},{10,1... | collective-permute-start | bytes 110600 | tf_op jit(solution)/shard_map/ppermute | solution.py:136
  115.2 10.9 %collective-permute-start.12 = (bf16[4,8,1024]{2,1,0:T(8,128)(2,1)}, bf16[4,8,1024]{2,1,0:T(8,128)(2,1)S(1)}, u32[]{:S(2)}, u32[]{:S(2)}) collective-permute-start(bf16[4,8,1024]{2,1,0:T(8,128)(2,1)} %get-tuple-element.28), channel_id=1, source_target_pairs={{0,1},{1,2},{2,3},{3,0},{4,5},{5,6},{6,7},{7,4},{8,9},{9,10},{10,1... | collective-permute-start | bytes 196616 | tf_op jit(solution)/shard_map/ppermute | solution.py:136
  115.6 10.5 %collective-permute-start.14 = (bf16[4,8,1024]{2,1,0:T(8,128)(2,1)}, bf16[4,8,1024]{2,1,0:T(8,128)(2,1)S(1)}, u32[]{:S(2)}, u32[]{:S(2)}) collective-permute-start(bf16[4,8,1024]{2,1,0:T(8,128)(2,1)} %get-tuple-element.29), channel_id=1, source_target_pairs={{0,3},{1,0},{2,1},{3,2},{4,7},{5,4},{6,5},{7,6},{8,11},{9,8},{10,9... | collective-permute-start | bytes 196616 | tf_op jit(solution)/shard_map/ppermute | solution.py:136
  117.0 9.2 %collective-permute-start.13 = (bf16[4,8,1024]{2,1,0:T(8,128)(2,1)S(1)}, bf16[4,8,1024]{2,1,0:T(8,128)(2,1)S(1)}, u32[]{:S(2)}, u32[]{:S(2)}) collective-permute-start(bf16[4,8,1024]{2,1,0:T(8,128)(2,1)S(1)} %get-tuple-element.30), channel_id=1, source_target_pairs={{0,2},{1,3},{2,0},{3,1},{4,6},{5,7},{6,4},{7,5},{8,10},{9,11},{10,... | collective-permute-start | bytes 196616 | tf_op jit(solution)/shard_map/ppermute | solution.py:136
